TPU v7x, 512 devices: a whole 4x8x8 slice. The times are simulated.
512 devices in a mesh: req: 64 (over z, x, core), tp: 8 (over y).
Axes of the slice: x: 4, y: 8, z: 8, core: 2. Of those that a mesh axis runs over, the one named last changes fastest.
Arguments:
- queries: bfloat16 [16384, 7168], P('req', 'tp'), may hold values from -200 to 200
- key_value: bfloat16 [2, 16384, 1024], P(None, 'req', 'tp'), may hold values from -8 to 8
- segment: int32 [16384], P('req'), may hold values from 0 to 31, never falling along the last dimension, each value on 1 to 1024 neighbouring positions
- residual: bfloat16 [16384, 7168], P('req', 'tp'), may hold values from -4 to 4
- out_weight: bfloat16 [7168, 7168], P('tp', 'req'), may hold values from -0.0625 to 0.0625
- head_gain: bfloat16 [7168], P('tp'), may hold values from 0.099609375 to 1.8984375
- vocab_weight: bfloat16 [7168, 64000], P('tp', 'req'), may hold values from -0.21875 to 0.21875
Outputs:
- hidden: bfloat16 [16384, 7168], P('req', 'tp')
- key_cache: bfloat16 [16384, 1024], P('req', 'tp')
- last_norm: float32 [32], replicated
- top_logit: float32 [32], replicated
Inputs may be any that keep to these rules, and one draw needn't show every extreme that they name: `segment`: ids never fall; each of the 32 requests has 1 to 1024 tokens, one has exactly 1024.
All inputs are finite; a program needn't handle non-finite values.
Results may differ from a plain program's by a relative error of at most 0.013.
Values may be sent and summed in bfloat16 or wider, within the bound.
No kernel may reach another device: no remote copies, remote signals or barrier semaphores. Data moves between devices by JAX's collectives and lax.ppermute only.
A program may use at most 128 MiB of HBM per device.

v0:
```python
import jax
import jax.numpy as jnp
from jax import lax
from jax.sharding import PartitionSpec as P

D = 7168
HD = 128
GROUP = 7
REACH = 4


theta = 5000000.0
eps = 1e-05
masked_score = -1e30


def from_behind(value, axis, steps):
    count = lax.axis_size(axis)
    initial, last = (max(0, -steps), min(count, count - steps))
    return lax.ppermute(value, axis, [(source, source + steps) for source in range(initial, last)])


def rope_tables(positions, width):
    half_width = width // 2
    frequency = theta ** (-(jnp.arange(half_width, dtype=jnp.float32) * 2.0 / width))
    angles = positions[:, None] * frequency[None, :]
    return (jnp.cos(angles), jnp.sin(angles))


def rotate(values, cosine, sine_table):
    half_width = values.shape[-1] // 2
    first_half = values[..., :half_width]
    second_half = values[..., half_width:]
    table_shape = (cosine.shape[0],) + (1,) * (values.ndim - 2) + (half_width,)
    cosine = cosine.reshape(table_shape)
    sine_table = sine_table.reshape(table_shape)
    return jnp.concatenate(
        [
            first_half * cosine - second_half * sine_table,
            second_half * cosine + first_half * sine_table,
        ],
        axis=-1,
    )


def local(queries, key_value, segment, residual, out_weight, head_gain, vocab_weight):
    tok_rows = segment.shape[0]
    heads_kv = key_value.shape[2] // HD
    requests = lax.axis_size("req") // 2
    device = lax.axis_index("req")
    request_ids = jnp.arange(requests, dtype=jnp.int32)
    member = segment[:, None] == request_ids[None, :]
    counts = jnp.sum(member.astype(jnp.float32), axis=0)
    lengths = lax.psum(counts, "req")
    starts = jnp.cumsum(lengths) - lengths
    tok_index = (device * tok_rows).astype(jnp.float32) + jnp.arange(tok_rows, dtype=jnp.float32)
    own_start = jnp.sum(jnp.where(member, starts[None, :], 0.0), axis=1)
    positions = tok_index - own_start
    cosine, sine_table = rope_tables(positions, HD)
    rot_query = rotate(
        queries.astype(jnp.float32).reshape(tok_rows, heads_kv, GROUP, HD), cosine, sine_table
    ).astype(jnp.bfloat16)
    rot_key = rotate(
        key_value[0].astype(jnp.float32).reshape(tok_rows, heads_kv, HD), cosine, sine_table
    ).astype(jnp.bfloat16)
    key_cache = rot_key.reshape(tok_rows, heads_kv * HD)
    own_block = jnp.stack([key_cache, key_value[1]])
    blocks = [own_block]
    moving = own_block
    for offset in range(REACH):
        moving = from_behind(moving, "req", 1)
        blocks.insert(0, moving)
    window = jnp.concatenate(blocks, axis=1)
    span = window.shape[1]
    key_rows = window[0].reshape(span, heads_kv, HD)
    value_rows = window[1].reshape(span, heads_kv, HD)
    key_index = ((device - REACH) * tok_rows).astype(jnp.float32) + jnp.arange(
        span, dtype=jnp.float32
    )
    allowed = (key_index[None, :] >= own_start[:, None]) & (
        key_index[None, :] <= tok_index[:, None]
    )
    scale = HD ** (-0.5)
    scores_part = (
        jnp.einsum("qhgd,khd->hgqk", rot_query, key_rows, preferred_element_type=jnp.float32)
        * scale
    )
    scores = jnp.where(allowed[None, None], scores_part, masked_score)
    peak = jnp.max(scores, axis=3, keepdims=True)
    weights = jnp.exp(scores - peak)
    total = jnp.sum(weights, axis=3)
    context = jnp.einsum(
        "hgqk,khd->qhgd",
        weights.astype(jnp.bfloat16),
        value_rows,
        preferred_element_type=jnp.float32,
    )
    context = context / jnp.transpose(total, (2, 0, 1))[..., None]
    attended = context.astype(jnp.bfloat16).reshape(tok_rows, heads_kv * GROUP * HD)
    projected = jnp.dot(
        attended,
        lax.all_gather(out_weight, "req", axis=1, tiled=True),
        preferred_element_type=jnp.float32,
    )
    width_dev = residual.shape[1]
    summed = lax.psum(projected.astype(jnp.bfloat16), "tp").astype(jnp.float32)
    own_share = lax.dynamic_slice_in_dim(summed, lax.axis_index("tp") * width_dev, width_dev, 1)
    hidden = (residual.astype(jnp.float32) + own_share).astype(jnp.bfloat16)
    ends = starts + lengths - 1.0
    select = (tok_index[:, None] == ends[None, :]).astype(jnp.bfloat16)
    local_last = lax.dot_general(
        select, hidden, (((0,), (0,)), ((), ())), preferred_element_type=jnp.float32
    )
    last_state = lax.psum(local_last, "req")
    scaled = (last_state * head_gain.astype(jnp.float32)).astype(jnp.bfloat16)
    square_part = jnp.sum(last_state * last_state, axis=1)
    logit_part = jnp.dot(scaled, vocab_weight, preferred_element_type=jnp.float32)
    square_sum, raw_logits = (
        lax.psum(square_part.astype(jnp.bfloat16), "tp").astype(jnp.float32),
        lax.psum(logit_part.astype(jnp.bfloat16), "tp").astype(jnp.float32),
    )
    mean_square = square_sum / D
    last_norm = jnp.sqrt(mean_square)
    local_top = jnp.max(raw_logits * lax.rsqrt(mean_square + eps)[:, None], axis=1)
    top_logit = lax.pmax(local_top, "req")
    return (hidden, key_cache, last_norm, top_logit)


def solution(mesh):
    placed = (
        P("req", "tp"),
        P(None, "req", "tp"),
        P("req"),
        P("req", "tp"),
        P("tp", "req"),
        P("tp"),
        P("tp", "req"),
    )
    return jax.shard_map(
        local,
        mesh=mesh,
        in_specs=placed,
        out_specs=(P("req", "tp"), P("req", "tp"), P(), P()),
        check_vma=False,
    )
```

profile of v0, /device:TPU:56, one launch (start us, length us, event | category | flops | bytes accessed | tf_op | source)
XLA Modules:
  0.0 656.0 jit_solution(12627300125974174510)
XLA Ops:
  7.2 0.7 all-gather.2.cloned.1.call-update
  8.0 0.8 convert_reduce_fusion
  8.8 135.4 %psum.35 = f32[32]{0:T(128)S(1)} all-reduce(f32[32]{0:T(128)S(1)} %convert_reduce_fusion), channel_id=1, replica_groups=mesh['req'=64,'tp'=8] {'req'}, use_global_device_ids=true, to_apply=%region_1.0 | all-reduce | flops 32 | bytes 256 | tf_op jit(solution)/shard_map/psum | solution.py:54
  144.5 0.8 select_reduce_fusion
  145.2 0.9 bitcast_convert_fusion
  146.7 0.6 copy-done.2
  147.5 2.0 collective-permute-start
  149.8 1.2 copy.21
  151.0 1.9 collective-permute-start.1
  152.9 0.9 fusion.40
  153.8 1.3 copy.29
  155.1 1.3 copy.30
  156.4 1.3 collective-permute-start.2
  158.2 0.6 collective-permute-done.2
  158.9 4.3 collective-permute-start.3
  163.2 1.5 fusion.16
  164.8 0.9 constant_dynamic-update-slice_fusion.2
  165.7 0.9 constant_dynamic-update-slice_fusion.1
  166.7 1.0 constant_dynamic-update-slice_fusion
  167.7 1.8 fusion.2
  169.5 1.9 fusion
  171.4 2.5 fusion.13
  173.9 14.7 %convolution_convert_fusion = bf16[256,7168]{1,0:T(8,128)(2,1)} fusion(bf16[256,896]{0,1:T(8,128)(2,1)S(1)} %bitcast.80, bf16[896,7168]{0,1:T(8,128)(2,1)} %all-gather.2.cloned.1.call-done), kind=kOutput, calls=%fused_computation.2 | convolution fusion | flops 3290169344 | bytes 16973824 | tf_op jit(solution)/shard_map/dot_general | solution.py:100
  188.7 117.3 %all-reduce.4.cloned.1.call-done = bf16[256,7168]{1,0:T(8,128)(2,1)} async-done(((bf16[256,7168]{1,0:T(8,128)(2,1)}), bf16[256,7168]{1,0:T(8,128)(2,1)}) %all-reduce.4.cloned.1.call-update) | async-done | bytes 3670032 | tf_op jit(solution)/shard_map/psum | solution.py:106
  306.0 1.2 add_convert_fusion
  307.2 0.9 fusion.30
  308.2 0.7 pad_maximum_fusion.1
  308.9 183.8 %all-reduce.6.cloned.1.call-done = f32[32,896]{1,0:T(8,128)} async-done(((f32[32,896]{1,0:T(8,128)}), f32[32,896]{1,0:T(8,128)}) %all-reduce.6.cloned.1.call-update) | async-done | bytes 114704 | tf_op jit(solution)/shard_map/psum | solution.py:114
  492.7 1.0 multiply_reduce_fusion.1
  493.8 1.5 convolution_convert_fusion.1
  495.3 28.9 %all-reduce = (bf16[32]{0:T(256)(128)(2,1)S(1)}, bf16[32,1000]{1,0:T(8,128)(2,1)S(1)}) all-reduce(bf16[32]{0:T(256)(128)(2,1)S(1)} %multiply_reduce_fusion.1, bf16[32,1000]{1,0:T(8,128)(2,1)S(1)} %convolution_convert_fusion.1), channel_id=1, replica_groups=mesh['req'=64,'tp'=8] {'tp'}, use_global_device_ids=true, to_apply=%region_9.10 | all-reduce | flops 32032 | bytes 128128 | tf_op jit(solution)/shard_map/psum | solution.py:119
  524.9 124.6 %pmax.7 = f32[32]{0:T(128)} all-reduce(f32[32]{0:T(128)S(1)} %multiply_reduce_fusion), channel_id=1, replica_groups=mesh['req'=64,'tp'=8] {'req'}, use_global_device_ids=true, to_apply=%region_12.13 | all-reduce | flops 32 | bytes 256 | tf_op jit(solution)/shard_map/pmax | solution.py:125
  (43 shorter events, 2.8 us)
Async XLA Ops:
  7.2 486.6 %copy-start = (bf16[896,1000]{0,1:T(8,128)(2,1)S(1)}, bf16[896,1000]{0,1:T(8,128)(2,1)}, u32[]{:S(2)}) copy-start(bf16[896,1000]{0,1:T(8,128)(2,1)} %param.13) | copy-start | bytes 5376004
  7.2 166.7 %all-gather.2.cloned.1.call-start = ((), (), s32[]{:S(2)}) async-start(), calls=%async_computation | async-start | bytes 13045760 | tf_op jit(solution)/shard_map/all_gather | solution.py:102
  7.9 298.1 %all-reduce.4.cloned.1.call-start = ((), (), s32[]{:S(2)}) async-start(), calls=%async_computation.1 | async-start | bytes 7340032 | tf_op jit(solution)/shard_map/psum | solution.py:106
  146.1 1.3 copy-start.6
  146.7 0.6 copy-start.2
  146.7 0.7 copy-start.4
  147.5 3.5 collective-permute-start
  151.0 5.4 collective-permute-start.1
  156.4 2.5 collective-permute-start.2
  158.9 5.9 collective-permute-start.3
  173.9 14.9 %copy-start.8 = (bf16[896]{0:T(1024)(128)(2,1)S(1)}, bf16[896]{0:T(1024)(128)(2,1)}, u32[]{:S(2)}) copy-start(bf16[896]{0:T(1024)(128)(2,1)} %param.12) | copy-start | bytes 5380
  173.9 132.1 %copy-start.7 = (bf16[256,896]{1,0:T(8,128)(2,1)S(1)}, bf16[256,896]{1,0:T(8,128)(2,1)}, u32[]{:S(2)}) copy-start(bf16[256,896]{1,0:T(8,128)(2,1)} %param.10) | copy-start | bytes 1376260
  173.9 134.3 %copy-start.3 = (bf16[256,1,64]{2,0,1:T(8,128)(2,1)S(1)}, bf16[256,1,64]{2,0,1:T(8,128)(2,1)}, u32[]{:S(2)}) copy-start(bf16[256,1,64]{2,0,1:T(8,128)(2,1)} %copy-done.2) | copy-start | bytes 98308
  173.9 134.3 %copy-start.5 = (bf16[256,1,64]{2,0,1:T(8,128)(2,1)S(1)}, bf16[256,1,64]{2,0,1:T(8,128)(2,1)}, u32[]{:S(2)}) copy-start(bf16[256,1,64]{2,0,1:T(8,128)(2,1)} %copy-done.4) | copy-start | bytes 98308
  188.7 304.1 %all-reduce.6.cloned.1.call-start = ((), (), s32[]{:S(2)}) async-start(), calls=%async_computation.2 | async-start | bytes 229376 | tf_op jit(solution)/shard_map/psum | solution.py:114
  307.2 342.3 %copy-start.1 = (bf16[256,896]{1,0:T(8,128)(2,1)}, bf16[256,896]{1,0:T(8,128)(2,1)S(1)}, u32[]{:S(2)}) copy-start(bf16[256,896]{1,0:T(8,128)(2,1)S(1)} %add_convert_fusion) | copy-start | bytes 1376260
Sparse Core Ops, SparseCore 0:
  11.3 100.7 all-gather.1
  188.8 117.1 all-reduce.3
  309.5 183.1 all-reduce.5
where the time goes:
time: 660 us; the launch traced here: 656 us
  waiting for transfers between devices  302 us (46%)
  blocking collectives  289 us (44%)
  matrix products  21.5 us (3%)
  between operations  14 us (2%)
  other arithmetic  12.2 us (2%)
  starting transfers between devices  9.64 us (1%)
  local copies, waits for them, and re-layouts  7.31 us (1%)
    psum x1, waiting for transfers between devices, local(): last_state = lax.psum(local_last, 'req')  184 us
    psum x1, blocking collectives, local(): lengths = lax.psum(counts, 'req')  135 us
    pmax x1, blocking collectives, local(): top_logit = lax.pmax(local_top, 'req')  125 us
    psum x1, waiting for transfers between devices, local(): summed = lax.psum(projected.astype(jnp.bfloat16), 'tp').astype(jnp.float32)  117 us
    psum x1, blocking collectives, local(): lax.psum(square_part.astype(jnp.bfloat16), 'tp').astype(jnp.float32)  28.9 us
    dot_general x1, matrix products, local(): jnp.dot(attended, lax.all_gather(out_weight, 'req', axis=1, tiled=True),...  14.7 us
  transfers between devices with their start and end apart: 7, of which 3 were waited for; matrix products, arithmetic and copies ran while one was open for 3% of the time, Pallas kernels for 0%

commit v1 on v0

--- a/solution.py
+++ b/solution.py
@@ -18,6 +18,16 @@
     count = lax.axis_size(axis)
     initial, last = (max(0, -steps), min(count, count - steps))
     return lax.ppermute(value, axis, [(source, source + steps) for source in range(initial, last)])
+
+
+def butterfly(value, axis, combine):
+    count = lax.axis_size(axis)
+    stride = 1
+    while stride < count:
+        other = lax.ppermute(value, axis, [(source, source ^ stride) for source in range(count)])
+        value = combine(value, other)
+        stride *= 2
+    return value
 
 
 def rope_tables(positions, width):
@@ -47,38 +57,49 @@
     tok_rows = segment.shape[0]
     heads_kv = key_value.shape[2] // HD
     requests = lax.axis_size("req") // 2
+    devices_req = lax.axis_size("req")
     device = lax.axis_index("req")
     request_ids = jnp.arange(requests, dtype=jnp.int32)
-    member = segment[:, None] == request_ids[None, :]
-    counts = jnp.sum(member.astype(jnp.float32), axis=0)
-    lengths = lax.psum(counts, "req")
-    starts = jnp.cumsum(lengths) - lengths
-    tok_index = (device * tok_rows).astype(jnp.float32) + jnp.arange(tok_rows, dtype=jnp.float32)
-    own_start = jnp.sum(jnp.where(member, starts[None, :], 0.0), axis=1)
-    positions = tok_index - own_start
-    cosine, sine_table = rope_tables(positions, HD)
+
+    own_kv = key_value
+    parts_kv, parts_seg = [], []
+    for back in range(REACH, 0, -1):
+        kv_b, seg_b = from_behind((own_kv, segment), "req", back)
+        parts_kv.append(kv_b)
+        parts_seg.append(seg_b)
+    parts_kv.append(own_kv)
+    parts_seg.append(segment)
+    next_first = from_behind(segment[:1], "req", -1)
+    window = jnp.concatenate(parts_kv, axis=1)
+    seg_window = jnp.concatenate(parts_seg, axis=0)
+    span = window.shape[1]
+    key_index_i = (device - REACH) * tok_rows + jnp.arange(span, dtype=jnp.int32)
+    valid = key_index_i >= 0
+    same = (seg_window[:, None] == seg_window[None, :]) & valid[None, :]
+    start_i = jnp.min(jnp.where(same, key_index_i[None, :], jnp.int32(2**30)), axis=1)
+    key_index = key_index_i.astype(jnp.float32)
+    win_start = start_i.astype(jnp.float32)
+    win_pos = key_index - win_start
+    own_start = win_start[span - tok_rows:]
+    tok_index = key_index[span - tok_rows:]
+    positions = win_pos[span - tok_rows:]
+
+    cosine, sine_table = rope_tables(win_pos, HD)
+    rot_keys = rotate(
+        window[0].astype(jnp.float32).reshape(span, heads_kv, HD), cosine, sine_table
+    ).astype(jnp.bfloat16)
+    q_cos, q_sin = cosine[span - tok_rows:], sine_table[span - tok_rows:]
     rot_query = rotate(
-        queries.astype(jnp.float32).reshape(tok_rows, heads_kv, GROUP, HD), cosine, sine_table
+        queries.astype(jnp.float32).reshape(tok_rows, heads_kv, GROUP, HD), q_cos, q_sin
     ).astype(jnp.bfloat16)
-    rot_key = rotate(
-        key_value[0].astype(jnp.float32).reshape(tok_rows, heads_kv, HD), cosine, sine_table
-    ).astype(jnp.bfloat16)
-    key_cache = rot_key.reshape(tok_rows, heads_kv * HD)
-    own_block = jnp.stack([key_cache, key_value[1]])
-    blocks = [own_block]
-    moving = own_block
-    for offset in range(REACH):
-        moving = from_behind(moving, "req", 1)
-        blocks.insert(0, moving)
-    window = jnp.concatenate(blocks, axis=1)
-    span = window.shape[1]
-    key_rows = window[0].reshape(span, heads_kv, HD)
+    key_cache = rot_keys[span - tok_rows:].reshape(tok_rows, heads_kv * HD)
+    key_rows = rot_keys
     value_rows = window[1].reshape(span, heads_kv, HD)
-    key_index = ((device - REACH) * tok_rows).astype(jnp.float32) + jnp.arange(
-        span, dtype=jnp.float32
-    )
-    allowed = (key_index[None, :] >= own_start[:, None]) & (
-        key_index[None, :] <= tok_index[:, None]
+    q_seg = segment
+    allowed = (
+        (seg_window[None, :] == q_seg[:, None])
+        & valid[None, :]
+        & (key_index[None, :] <= tok_index[:, None])
     )
     scale = HD ** (-0.5)
     scores_part = (
@@ -102,16 +123,20 @@
         lax.all_gather(out_weight, "req", axis=1, tiled=True),
         preferred_element_type=jnp.float32,
     )
-    width_dev = residual.shape[1]
-    summed = lax.psum(projected.astype(jnp.bfloat16), "tp").astype(jnp.float32)
-    own_share = lax.dynamic_slice_in_dim(summed, lax.axis_index("tp") * width_dev, width_dev, 1)
+    own_share = lax.psum_scatter(
+        projected.astype(jnp.bfloat16), "tp", scatter_dimension=1, tiled=True
+    ).astype(jnp.float32)
     hidden = (residual.astype(jnp.float32) + own_share).astype(jnp.bfloat16)
-    ends = starts + lengths - 1.0
-    select = (tok_index[:, None] == ends[None, :]).astype(jnp.bfloat16)
+
+    following = jnp.concatenate([segment[1:], next_first])
+    is_last_dev = device == devices_req - 1
+    is_end = following != segment
+    is_end = is_end.at[tok_rows - 1].set(is_end[tok_rows - 1] | is_last_dev)
+    select = (is_end[:, None] & (segment[:, None] == request_ids[None, :])).astype(jnp.bfloat16)
     local_last = lax.dot_general(
         select, hidden, (((0,), (0,)), ((), ())), preferred_element_type=jnp.float32
     )
-    last_state = lax.psum(local_last, "req")
+    last_state = butterfly(local_last.astype(jnp.bfloat16), "req", jnp.add).astype(jnp.float32)
     scaled = (last_state * head_gain.astype(jnp.float32)).astype(jnp.bfloat16)
     square_part = jnp.sum(last_state * last_state, axis=1)
     logit_part = jnp.dot(scaled, vocab_weight, preferred_element_type=jnp.float32)
@@ -122,7 +147,7 @@
     mean_square = square_sum / D
     last_norm = jnp.sqrt(mean_square)
     local_top = jnp.max(raw_logits * lax.rsqrt(mean_square + eps)[:, None], axis=1)
-    top_logit = lax.pmax(local_top, "req")
+    top_logit = butterfly(local_top, "req", jnp.maximum)
     return (hidden, key_cache, last_norm, top_logit)
 
 

time: 660 us -> 302 us (0.46)
  blocking collectives: 289 us -> 28.4 us
  waiting for transfers between devices: 302 us -> 124 us
  starting transfers between devices: 9.64 us -> 82.2 us
  local copies, waits for them, and re-layouts: 7.31 us -> 14.5 us
    psum x2 -> x0, waiting for transfers between devices: 301 us -> none  [the longest x1 184 us: local(): last_state = lax.psum(local_last, 'req')]
    psum x1 -> x0, blocking collectives: 135 us -> none  [local(): lengths = lax.psum(counts, 'req')]
    pmax x1 -> x0, blocking collectives: 125 us -> none  [local(): top_logit = lax.pmax(local_top, 'req')]
    all_gather x1, waiting for transfers between devices: 0.02 us -> 54.7 us  [local(): lax.all_gather(out_weight, 'req', axis=1, tiled=True)]
    ppermute x0 -> x12, starting transfers between devices: none -> 52.3 us  [butterfly(): lax.ppermute(value, axis, [(source, source ^ stride) for source in range(...]
    unnamed x3, waiting for transfers between devices: 0.71 us -> 42.9 us
    ppermute x0 -> x12, waiting for transfers between devices: none -> 24.1 us  [butterfly(): lax.ppermute(value, axis, [(source, source ^ stride) for source in range(...]
    ppermute x4 -> x9, starting transfers between devices: 9.52 us -> 29.9 us  [from_behind(): lax.ppermute(value, axis, [(source, source + steps) for source in range(i...]
  transfers between devices with their start and end apart: 7 -> 23, of which waited for: 3 -> 15; matrix products, arithmetic and copies ran while one was open for 3% -> 8% of each run, Pallas kernels for 0% -> 0%
where the time goes in v1:
time: 302 us; the launch traced here: 298 us
  waiting for transfers between devices  124 us (41%)
  starting transfers between devices  82.2 us (27%)
  blocking collectives  28.4 us (9%)
  matrix products  20 us (7%)
  between operations  15.2 us (5%)
  local copies, waits for them, and re-layouts  14.5 us (5%)
  other arithmetic  14.2 us (5%)
    all_gather x1, waiting for transfers between devices, local(): lax.all_gather(out_weight, 'req', axis=1, tiled=True)  54.7 us
    ppermute x12, starting transfers between devices, butterfly(): lax.ppermute(value, axis, [(source, source ^ stride) for source in range(...  52.3 us
    unnamed x3, waiting for transfers between devices  42.9 us
    ppermute x9, starting transfers between devices, from_behind(): lax.ppermute(value, axis, [(source, source + steps) for source in range(i...  29.9 us
    psum x1, blocking collectives, local(): lax.psum(square_part.astype(jnp.bfloat16), 'tp').astype(jnp.float32)  28.4 us
    ppermute x12, waiting for transfers between devices, butterfly(): lax.ppermute(value, axis, [(source, source ^ stride) for source in range(...  24.1 us
    dot_general x1, matrix products, local(): jnp.dot(attended, lax.all_gather(out_weight, 'req', axis=1, tiled=True),...  14.7 us
    unnamed x23, local copies, waits for them, and re-layouts  11.1 us
  transfers between devices with their start and end apart: 23, of which 15 were waited for; matrix products, arithmetic and copies ran while one was open for 8% of the time, Pallas kernels for 0%

profile of v1, /device:TPU:56, one launch (start us, length us, event | category | flops | bytes accessed | tf_op | source)
XLA Modules:
  0.0 298.0 jit_solution(13777661090446029314)
XLA Ops:
  8.0 4.9 %collective-permute-start.4 = (s32[256]{0:T(256)}, s32[256]{0:T(256)S(1)}, u32[]{:S(2)}, u32[]{:S(2)}) collective-permute-start(s32[256]{0:T(256)} %param.11), channel_id=1, source_target_pairs={{0,32},{8,40},{16,48},{24,56},{32,64},{40,72},{48,80},{56,88},{64,... | collective-permute-start | bytes 3080 | tf_op jit(solution)/shard_map/ppermute | solution.py:20
  14.6 3.6 %collective-permute-start.6 = (s32[256]{0:T(256)}, s32[256]{0:T(256)S(1)}, u32[]{:S(2)}, u32[]{:S(2)}) collective-permute-start(s32[256]{0:T(256)} %param.11), channel_id=1, source_target_pairs={{0,16},{8,24},{16,32},{24,40},{32,48},{40,56},{48,64},{56,72},{64,... | collective-permute-start | bytes 3080 | tf_op jit(solution)/shard_map/ppermute | solution.py:20
  18.2 4.1 %collective-permute-start.7 = (s32[256]{0:T(256)}, s32[256]{0:T(256)S(1)}, u32[]{:S(2)}, u32[]{:S(2)}) collective-permute-start(s32[256]{0:T(256)} %param.11), channel_id=1, source_target_pairs={{0,8},{8,16},{16,24},{24,32},{32,40},{40,48},{48,56},{56,64},{64,7... | collective-permute-start | bytes 3080 | tf_op jit(solution)/shard_map/ppermute | solution.py:20
  22.3 4.7 %collective-permute-start = (bf16[2,256,128]{2,1,0:T(8,128)(2,1)}, bf16[2,256,128]{2,1,0:T(8,128)(2,1)S(1)}, u32[]{:S(2)}, u32[]{:S(2)}) collective-permute-start(bf16[2,256,128]{2,1,0:T(8,128)(2,1)} %param.10), channel_id=1, source_target_pairs={{0,32},{8,40},{16,48},{24,56},{32,64},{40,72},{48,80},{56,88},{64,... | collective-permute-start | bytes 393224 | tf_op jit(solution)/shard_map/ppermute | solution.py:20
  31.7 2.9 collective-permute-start.1
  34.7 2.8 collective-permute-start.2
  37.5 4.0 %collective-permute-start.3 = (bf16[2,256,128]{2,1,0:T(8,128)(2,1)}, bf16[2,256,128]{2,1,0:T(8,128)(2,1)S(1)}, u32[]{:S(2)}, u32[]{:S(2)}) collective-permute-start(bf16[2,256,128]{2,1,0:T(8,128)(2,1)} %param.10), channel_id=1, source_target_pairs={{0,8},{8,16},{16,24},{24,32},{32,40},{40,48},{48,56},{56,64},{64,7... | collective-permute-start | bytes 393224 | tf_op jit(solution)/shard_map/ppermute | solution.py:20
  48.2 3.0 %fusion.21 = (bf16[1280,1,64]{2,0,1:T(8,128)(2,1)S(1)}, bf16[1280,1,64]{2,0,1:T(8,128)(2,1)S(1)}) fusion(f32[1280,1,128]{2,0,1:T(8,128)S(1)} %fusion.30, f32[64]{0:T(128)S(1)} %negate_power_fusion, f32[1280]{0:T(1024)S(1)} %convert_subtract_fusion), kind=kLoop, calls=%fused_computation.26 | loop fusion | flops 737280 | bytes 988416 | tf_op jit(solution)/shard_map/convert.11
  55.0 2.5 fusion.13
  57.5 54.7 %all-gather.2.cloned.1.call-done = bf16[896,7168]{0,1:T(8,128)(2,1)} async-done(((bf16[896,112]{0,1:T(8,128)(2,1)}), bf16[896,7168]{0,1:T(8,128)(2,1)}) %all-gather.2.cloned.1.call-update) | async-done | bytes 12845072 | tf_op jit(solution)/shard_map/all_gather | solution.py:123
  112.2 14.7 %convolution_convert_fusion = bf16[256,7168]{1,0:T(8,128)(2,1)} fusion(bf16[256,896]{0,1:T(8,128)(2,1)S(1)} %bitcast.81, bf16[896,7168]{0,1:T(8,128)(2,1)} %all-gather.2.cloned.1.call-done), kind=kOutput, calls=%fused_computation.2 | convolution fusion | flops 3290169344 | bytes 16973824 | tf_op jit(solution)/shard_map/dot_general | solution.py:121
  126.8 5.9 %copy.31 = bf16[256,7168]{0,1:T(8,128)(2,1)} copy(bf16[256,7168]{1,0:T(8,128)(2,1)} %convolution_convert_fusion) | data formatting | bytes 7340032
  138.6 42.2 %reduce-scatter.4.cloned.1.call-done = bf16[896,256]{1,0:T(8,128)(2,1)} async-done(((bf16[7168,256]{1,0:T(8,128)(2,1)}), bf16[896,256]{1,0:T(8,128)(2,1)}) %reduce-scatter.4.cloned.1.call-update) | async-done | bytes 458768
  186.7 3.4 %collective-permute-start.10 = (bf16[32,896]{1,0:T(8,128)(2,1)S(1)}, bf16[32,896]{1,0:T(8,128)(2,1)S(1)}, u32[]{:S(2)}, u32[]{:S(2)}) collective-permute-start(bf16[32,896]{1,0:T(8,128)(2,1)S(1)} %add.67), channel_id=1, source_target_pairs={{0,16},{8,24},{16,0},{24,8},{32,48},{40,56},{48,32},{56,40},{64,80... | collective-permute-start | bytes 172040 | tf_op jit(solution)/shard_map/ppermute | solution.py:27
  190.1 2.7 collective-permute-done.10
  192.8 4.9 %collective-permute-start.11 = (bf16[32,896]{1,0:T(8,128)(2,1)S(1)}, bf16[32,896]{1,0:T(8,128)(2,1)S(1)}, u32[]{:S(2)}, u32[]{:S(2)}) collective-permute-start(bf16[32,896]{1,0:T(8,128)(2,1)S(1)} %add.68), channel_id=1, source_target_pairs={{0,32},{8,40},{16,48},{24,56},{32,0},{40,8},{48,16},{56,24},{64,96... | collective-permute-start | bytes 172040 | tf_op jit(solution)/shard_map/ppermute | solution.py:27
  197.6 2.7 collective-permute-done.11
  200.4 3.6 %collective-permute-start.12 = (bf16[32,896]{1,0:T(8,128)(2,1)S(1)}, bf16[32,896]{1,0:T(8,128)(2,1)S(1)}, u32[]{:S(2)}, u32[]{:S(2)}) collective-permute-start(bf16[32,896]{1,0:T(8,128)(2,1)S(1)} %add.69), channel_id=1, source_target_pairs={{0,64},{8,72},{16,80},{24,88},{32,96},{40,104},{48,112},{56,120},{... | collective-permute-start | bytes 172040 | tf_op jit(solution)/shard_map/ppermute | solution.py:27
  203.9 2.5 collective-permute-done.12
  206.5 4.6 %collective-permute-start.13 = (bf16[32,896]{1,0:T(8,128)(2,1)S(1)}, bf16[32,896]{1,0:T(8,128)(2,1)S(1)}, u32[]{:S(2)}, u32[]{:S(2)}) collective-permute-start(bf16[32,896]{1,0:T(8,128)(2,1)S(1)} %add.70), channel_id=1, source_target_pairs={{0,128},{8,136},{16,144},{24,152},{32,160},{40,168},{48,176},{56,1... | collective-permute-start | bytes 172040 | tf_op jit(solution)/shard_map/ppermute | solution.py:27
  211.1 2.3 collective-permute-done.13
  213.4 8.6 %collective-permute-start.14 = (bf16[32,896]{1,0:T(8,128)(2,1)S(1)}, bf16[32,896]{1,0:T(8,128)(2,1)S(1)}, u32[]{:S(2)}, u32[]{:S(2)}) collective-permute-start(bf16[32,896]{1,0:T(8,128)(2,1)S(1)} %add.71), channel_id=1, source_target_pairs={{0,256},{8,264},{16,272},{24,280},{32,288},{40,296},{48,304},{56,3... | collective-permute-start | bytes 172040 | tf_op jit(solution)/shard_map/ppermute | solution.py:27
  222.1 2.2 collective-permute-done.14
  225.1 28.4 %all-reduce = (bf16[32]{0:T(256)(128)(2,1)S(1)}, bf16[32,1000]{1,0:T(8,128)(2,1)S(1)}) all-reduce(bf16[32]{0:T(256)(128)(2,1)S(1)} %fusion.35, bf16[32,1000]{1,0:T(8,128)(2,1)S(1)} %convolution_convert_fusion.1), channel_id=1, replica_groups=mesh['req'=64,'tp'=8] {'tp'}, use_global_device_ids=true, to_apply=%region_5.6 | all-reduce | flops 32032 | bytes 128128 | tf_op jit(solution)/shard_map/psum | solution.py:144
  257.2 3.4 %collective-permute-start.16 = (f32[32]{0:T(128)S(1)}, f32[32]{0:T(128)S(1)}, u32[]{:S(2)}, u32[]{:S(2)}) collective-permute-start(f32[32]{0:T(128)S(1)} %max.18), channel_id=1, source_target_pairs={{0,16},{8,24},{16,0},{24,8},{32,48},{40,56},{48,32},{56,40},{64,80... | collective-permute-start | bytes 392 | tf_op jit(solution)/shard_map/ppermute | solution.py:27
  260.6 2.0 collective-permute-done.16
  262.7 4.9 %collective-permute-start.17 = (f32[32]{0:T(128)S(1)}, f32[32]{0:T(128)S(1)}, u32[]{:S(2)}, u32[]{:S(2)}) collective-permute-start(f32[32]{0:T(128)S(1)} %max.19), channel_id=1, source_target_pairs={{0,32},{8,40},{16,48},{24,56},{32,0},{40,8},{48,16},{56,24},{64,96... | collective-permute-start | bytes 392 | tf_op jit(solution)/shard_map/ppermute | solution.py:27
  267.6 2.0 collective-permute-done.17
  269.6 2.7 collective-permute-start.18
  272.3 2.7 collective-permute-done.18
  275.0 4.5 %collective-permute-start.19 = (f32[32]{0:T(128)S(1)}, f32[32]{0:T(128)S(1)}, u32[]{:S(2)}, u32[]{:S(2)}) collective-permute-start(f32[32]{0:T(128)S(1)} %max.21), channel_id=1, source_target_pairs={{0,128},{8,136},{16,144},{24,152},{32,160},{40,168},{48,176},{56,1... | collective-permute-start | bytes 392 | tf_op jit(solution)/shard_map/ppermute | solution.py:27
  281.4 7.8 %collective-permute-start.20 = (f32[32]{0:T(128)S(1)}, f32[32]{0:T(128)S(1)}, u32[]{:S(2)}, u32[]{:S(2)}) collective-permute-start(f32[32]{0:T(128)S(1)} %max.22), channel_id=1, source_target_pairs={{0,256},{8,264},{16,272},{24,280},{32,288},{40,296},{48,304},{56,3... | collective-permute-start | bytes 392 | tf_op jit(solution)/shard_map/ppermute | solution.py:27
  (85 shorter events, 36.9 us)
Async XLA Ops:
  7.2 217.3 %copy-start = (bf16[896,1000]{0,1:T(8,128)(2,1)S(1)}, bf16[896,1000]{0,1:T(8,128)(2,1)}, u32[]{:S(2)}) copy-start(bf16[896,1000]{0,1:T(8,128)(2,1)} %param.15) | copy-start | bytes 5376004
  7.2 40.9 %copy-start.2 = (bf16[2,256,128]{2,1,0:T(8,128)(2,1)S(1)}, bf16[2,256,128]{2,1,0:T(8,128)(2,1)}, u32[]{:S(2)}) copy-start(bf16[2,256,128]{2,1,0:T(8,128)(2,1)} %param.10) | copy-start | bytes 393220
  7.2 105.0 %all-gather.2.cloned.1.call-start = ((), (), s32[]{:S(2)}) async-start(), calls=%async_computation.1 | async-start | bytes 13045760 | tf_op jit(solution)/shard_map/all_gather | solution.py:123
  7.9 172.8 %reduce-scatter.4.cloned.1.call-start = ((), (), s32[]{:S(2)}) async-start(), calls=%async_computation.2 | async-start | bytes 4128768
  8.0 23.8 %collective-permute-start.4 = (s32[256]{0:T(256)}, s32[256]{0:T(256)S(1)}, u32[]{:S(2)}, u32[]{:S(2)}) collective-permute-start(s32[256]{0:T(256)} %param.11), channel_id=1, source_target_pairs={{0,32},{8,40},{16,48},{24,56},{32,64},{40,72},{48,80},{56,88},{64,... | collective-permute-start | bytes 3080 | tf_op jit(solution)/shard_map/ppermute | solution.py:20
  12.9 21.8 %collective-permute-start.5 = (s32[256]{0:T(256)}, s32[256]{0:T(256)S(1)}, u32[]{:S(2)}, u32[]{:S(2)}) collective-permute-start(s32[256]{0:T(256)} %param.11), channel_id=1, source_target_pairs={{0,24},{8,32},{16,40},{24,48},{32,56},{40,64},{48,72},{56,80},{64,... | collective-permute-start | bytes 3080 | tf_op jit(solution)/shard_map/ppermute | solution.py:20
  14.6 22.9 %collective-permute-start.6 = (s32[256]{0:T(256)}, s32[256]{0:T(256)S(1)}, u32[]{:S(2)}, u32[]{:S(2)}) collective-permute-start(s32[256]{0:T(256)} %param.11), channel_id=1, source_target_pairs={{0,16},{8,24},{16,32},{24,40},{32,48},{40,56},{48,64},{56,72},{64,... | collective-permute-start | bytes 3080 | tf_op jit(solution)/shard_map/ppermute | solution.py:20
  18.2 23.3 %collective-permute-start.7 = (s32[256]{0:T(256)}, s32[256]{0:T(256)S(1)}, u32[]{:S(2)}, u32[]{:S(2)}) collective-permute-start(s32[256]{0:T(256)} %param.11), channel_id=1, source_target_pairs={{0,8},{8,16},{16,24},{24,32},{32,40},{40,48},{48,56},{56,64},{64,7... | collective-permute-start | bytes 3080 | tf_op jit(solution)/shard_map/ppermute | solution.py:20
  22.3 25.7 %collective-permute-start = (bf16[2,256,128]{2,1,0:T(8,128)(2,1)}, bf16[2,256,128]{2,1,0:T(8,128)(2,1)S(1)}, u32[]{:S(2)}, u32[]{:S(2)}) collective-permute-start(bf16[2,256,128]{2,1,0:T(8,128)(2,1)} %param.10), channel_id=1, source_target_pairs={{0,32},{8,40},{16,48},{24,56},{32,64},{40,72},{48,80},{56,88},{64,... | collective-permute-start | bytes 393224 | tf_op jit(solution)/shard_map/ppermute | solution.py:20
  31.7 16.3 %collective-permute-start.1 = (bf16[2,256,128]{2,1,0:T(8,128)(2,1)}, bf16[2,256,128]{2,1,0:T(8,128)(2,1)S(1)}, u32[]{:S(2)}, u32[]{:S(2)}) collective-permute-start(bf16[2,256,128]{2,1,0:T(8,128)(2,1)} %param.10), channel_id=1, source_target_pairs={{0,24},{8,32},{16,40},{24,48},{32,56},{40,64},{48,72},{56,80},{64,... | collective-permute-start | bytes 393224 | tf_op jit(solution)/shard_map/ppermute | solution.py:20
  34.7 13.4 %collective-permute-start.2 = (bf16[2,256,128]{2,1,0:T(8,128)(2,1)}, bf16[2,256,128]{2,1,0:T(8,128)(2,1)S(1)}, u32[]{:S(2)}, u32[]{:S(2)}) collective-permute-start(bf16[2,256,128]{2,1,0:T(8,128)(2,1)} %param.10), channel_id=1, source_target_pairs={{0,16},{8,24},{16,32},{24,40},{32,48},{40,56},{48,64},{56,72},{64,... | collective-permute-start | bytes 393224 | tf_op jit(solution)/shard_map/ppermute | solution.py:20
  37.5 10.6 %collective-permute-start.3 = (bf16[2,256,128]{2,1,0:T(8,128)(2,1)}, bf16[2,256,128]{2,1,0:T(8,128)(2,1)S(1)}, u32[]{:S(2)}, u32[]{:S(2)}) collective-permute-start(bf16[2,256,128]{2,1,0:T(8,128)(2,1)} %param.10), channel_id=1, source_target_pairs={{0,8},{8,16},{16,24},{24,32},{32,40},{40,48},{48,56},{56,64},{64,7... | collective-permute-start | bytes 393224 | tf_op jit(solution)/shard_map/ppermute | solution.py:20
  126.8 6.0 %copy-start.3 = (s32[256]{0:T(256)S(1)}, s32[256]{0:T(256)}, u32[]{:S(2)}) copy-start(s32[256]{0:T(256)} %param.11) | copy-start | bytes 3076
  126.8 95.3 %copy-start.4 = (bf16[896]{0:T(1024)(128)(2,1)S(1)}, bf16[896]{0:T(1024)(128)(2,1)}, u32[]{:S(2)}) copy-start(bf16[896]{0:T(1024)(128)(2,1)} %param.14) | copy-start | bytes 5380
  133.3 3.3 %collective-permute-start.8 = (s32[1]{0:T(128)}, s32[1]{0:T(128)}, u32[]{:S(2)}, u32[]{:S(2)}) collective-permute-start(s32[1]{0:T(128)} %slice.60), channel_id=1, source_target_pairs={{8,0},{16,8},{24,16},{32,24},{40,32},{48,40},{56,48},{64,56},{72,6... | collective-permute-start | bytes 20 | tf_op jit(solution)/shard_map/ppermute | solution.py:20
  183.2 108.0 %copy-start.1 = (bf16[256,896]{1,0:T(8,128)(2,1)}, bf16[256,896]{1,0:T(8,128)(2,1)S(1)}, u32[]{:S(2)}) copy-start(bf16[256,896]{1,0:T(8,128)(2,1)S(1)} %add_convert_fusion) | copy-start | bytes 1376260
  183.5 3.1 %collective-permute-start.9 = (bf16[32,896]{1,0:T(8,128)(2,1)S(1)}, bf16[32,896]{1,0:T(8,128)(2,1)S(1)}, u32[]{:S(2)}, u32[]{:S(2)}) collective-permute-start(bf16[32,896]{1,0:T(8,128)(2,1)S(1)} %convolution_convert_fusion.2), channel_id=1, source_target_pairs={{0,8},{8,0},{16,24},{24,16},{32,40},{40,32},{48,56},{56,48},{64,72... | collective-permute-start | bytes 172040 | tf_op jit(solution)/shard_map/ppermute | solution.py:27
  186.7 6.1 %collective-permute-start.10 = (bf16[32,896]{1,0:T(8,128)(2,1)S(1)}, bf16[32,896]{1,0:T(8,128)(2,1)S(1)}, u32[]{:S(2)}, u32[]{:S(2)}) collective-permute-start(bf16[32,896]{1,0:T(8,128)(2,1)S(1)} %add.67), channel_id=1, source_target_pairs={{0,16},{8,24},{16,0},{24,8},{32,48},{40,56},{48,32},{56,40},{64,80... | collective-permute-start | bytes 172040 | tf_op jit(solution)/shard_map/ppermute | solution.py:27
  192.8 7.6 %collective-permute-start.11 = (bf16[32,896]{1,0:T(8,128)(2,1)S(1)}, bf16[32,896]{1,0:T(8,128)(2,1)S(1)}, u32[]{:S(2)}, u32[]{:S(2)}) collective-permute-start(bf16[32,896]{1,0:T(8,128)(2,1)S(1)} %add.68), channel_id=1, source_target_pairs={{0,32},{8,40},{16,48},{24,56},{32,0},{40,8},{48,16},{56,24},{64,96... | collective-permute-start | bytes 172040 | tf_op jit(solution)/shard_map/ppermute | solution.py:27
  200.4 6.1 %collective-permute-start.12 = (bf16[32,896]{1,0:T(8,128)(2,1)S(1)}, bf16[32,896]{1,0:T(8,128)(2,1)S(1)}, u32[]{:S(2)}, u32[]{:S(2)}) collective-permute-start(bf16[32,896]{1,0:T(8,128)(2,1)S(1)} %add.69), channel_id=1, source_target_pairs={{0,64},{8,72},{16,80},{24,88},{32,96},{40,104},{48,112},{56,120},{... | collective-permute-start | bytes 172040 | tf_op jit(solution)/shard_map/ppermute | solution.py:27
  206.5 7.0 %collective-permute-start.13 = (bf16[32,896]{1,0:T(8,128)(2,1)S(1)}, bf16[32,896]{1,0:T(8,128)(2,1)S(1)}, u32[]{:S(2)}, u32[]{:S(2)}) collective-permute-start(bf16[32,896]{1,0:T(8,128)(2,1)S(1)} %add.70), channel_id=1, source_target_pairs={{0,128},{8,136},{16,144},{24,152},{32,160},{40,168},{48,176},{56,1... | collective-permute-start | bytes 172040 | tf_op jit(solution)/shard_map/ppermute | solution.py:27
  213.4 10.9 %collective-permute-start.14 = (bf16[32,896]{1,0:T(8,128)(2,1)S(1)}, bf16[32,896]{1,0:T(8,128)(2,1)S(1)}, u32[]{:S(2)}, u32[]{:S(2)}) collective-permute-start(bf16[32,896]{1,0:T(8,128)(2,1)S(1)} %add.71), channel_id=1, source_target_pairs={{0,256},{8,264},{16,272},{24,280},{32,288},{40,296},{48,304},{56,3... | collective-permute-start | bytes 172040 | tf_op jit(solution)/shard_map/ppermute | solution.py:27
  254.2 3.0 %collective-permute-start.15 = (f32[32]{0:T(128)S(1)}, f32[32]{0:T(128)S(1)}, u32[]{:S(2)}, u32[]{:S(2)}) collective-permute-start(f32[32]{0:T(128)S(1)} %multiply_reduce_fusion), channel_id=1, source_target_pairs={{0,8},{8,0},{16,24},{24,16},{32,40},{40,32},{48,56},{56,48},{64,72... | collective-permute-start | bytes 392 | tf_op jit(solution)/shard_map/ppermute | solution.py:27
  257.2 5.4 %collective-permute-start.16 = (f32[32]{0:T(128)S(1)}, f32[32]{0:T(128)S(1)}, u32[]{:S(2)}, u32[]{:S(2)}) collective-permute-start(f32[32]{0:T(128)S(1)} %max.18), channel_id=1, source_target_pairs={{0,16},{8,24},{16,0},{24,8},{32,48},{40,56},{48,32},{56,40},{64,80... | collective-permute-start | bytes 392 | tf_op jit(solution)/shard_map/ppermute | solution.py:27
  262.7 6.9 %collective-permute-start.17 = (f32[32]{0:T(128)S(1)}, f32[32]{0:T(128)S(1)}, u32[]{:S(2)}, u32[]{:S(2)}) collective-permute-start(f32[32]{0:T(128)S(1)} %max.19), channel_id=1, source_target_pairs={{0,32},{8,40},{16,48},{24,56},{32,0},{40,8},{48,16},{56,24},{64,96... | collective-permute-start | bytes 392 | tf_op jit(solution)/shard_map/ppermute | solution.py:27
  269.6 5.4 %collective-permute-start.18 = (f32[32]{0:T(128)S(1)}, f32[32]{0:T(128)S(1)}, u32[]{:S(2)}, u32[]{:S(2)}) collective-permute-start(f32[32]{0:T(128)S(1)} %max.20), channel_id=1, source_target_pairs={{0,64},{8,72},{16,80},{24,88},{32,96},{40,104},{48,112},{56,120},{... | collective-permute-start | bytes 392 | tf_op jit(solution)/shard_map/ppermute | solution.py:27
  275.0 6.3 %collective-permute-start.19 = (f32[32]{0:T(128)S(1)}, f32[32]{0:T(128)S(1)}, u32[]{:S(2)}, u32[]{:S(2)}) collective-permute-start(f32[32]{0:T(128)S(1)} %max.21), channel_id=1, source_target_pairs={{0,128},{8,136},{16,144},{24,152},{32,160},{40,168},{48,176},{56,1... | collective-permute-start | bytes 392 | tf_op jit(solution)/shard_map/ppermute | solution.py:27
  281.4 9.3 %collective-permute-start.20 = (f32[32]{0:T(128)S(1)}, f32[32]{0:T(128)S(1)}, u32[]{:S(2)}, u32[]{:S(2)}) collective-permute-start(f32[32]{0:T(128)S(1)} %max.22), channel_id=1, source_target_pairs={{0,256},{8,264},{16,272},{24,280},{32,288},{40,296},{48,304},{56,3... | collective-permute-start | bytes 392 | tf_op jit(solution)/shard_map/ppermute | solution.py:27
Sparse Core Ops, SparseCore 0:
  11.3 100.8 all-gather.1
  132.9 47.7 reduce-scatter.3

commit v2 on v1

--- a/solution.py
+++ b/solution.py
@@ -28,6 +28,22 @@
         value = combine(value, other)
         stride *= 2
     return value
+
+
+def halving_scatter(value, axis):
+    count = lax.axis_size(axis)
+    index = lax.axis_index(axis)
+    rows = value.shape[0]
+    held = value.reshape(rows, count, value.shape[1] // count)
+    bit = count // 2
+    while bit >= 1:
+        half = held.shape[1] // 2
+        mine = (index // bit) % 2
+        keep = lax.dynamic_slice_in_dim(held, mine * half, half, 1)
+        give = lax.dynamic_slice_in_dim(held, (1 - mine) * half, half, 1)
+        held = keep + lax.ppermute(give, axis, [(source, source ^ bit) for source in range(count)])
+        bit //= 2
+    return held.reshape(rows, -1)
 
 
 def rope_tables(positions, width):
@@ -118,32 +134,38 @@
     )
     context = context / jnp.transpose(total, (2, 0, 1))[..., None]
     attended = context.astype(jnp.bfloat16).reshape(tok_rows, heads_kv * GROUP * HD)
-    projected = jnp.dot(
-        attended,
-        lax.all_gather(out_weight, "req", axis=1, tiled=True),
+    following = jnp.concatenate([segment[1:], next_first])
+    is_last_dev = device == devices_req - 1
+    is_end = following != segment
+    is_end = is_end.at[tok_rows - 1].set(is_end[tok_rows - 1] | is_last_dev)
+    select = (is_end[:, None] & (segment[:, None] == request_ids[None, :])).astype(jnp.bfloat16)
+    end_rows = lax.dot_general(
+        select,
+        jnp.concatenate([attended, residual], axis=1),
+        (((0,), (0,)), ((), ())),
         preferred_element_type=jnp.float32,
-    )
+    ).astype(jnp.bfloat16)
+    end_rows = butterfly(end_rows, "req", jnp.add)
+    end_att, end_res = end_rows[:, : attended.shape[1]], end_rows[:, attended.shape[1] :]
+
+    full_weight = lax.all_gather(out_weight, "req", axis=1, tiled=True)
+    projected = jnp.dot(attended, full_weight, preferred_element_type=jnp.float32)
     own_share = lax.psum_scatter(
         projected.astype(jnp.bfloat16), "tp", scatter_dimension=1, tiled=True
     ).astype(jnp.float32)
     hidden = (residual.astype(jnp.float32) + own_share).astype(jnp.bfloat16)
 
-    following = jnp.concatenate([segment[1:], next_first])
-    is_last_dev = device == devices_req - 1
-    is_end = following != segment
-    is_end = is_end.at[tok_rows - 1].set(is_end[tok_rows - 1] | is_last_dev)
-    select = (is_end[:, None] & (segment[:, None] == request_ids[None, :])).astype(jnp.bfloat16)
-    local_last = lax.dot_general(
-        select, hidden, (((0,), (0,)), ((), ())), preferred_element_type=jnp.float32
-    )
-    last_state = butterfly(local_last.astype(jnp.bfloat16), "req", jnp.add).astype(jnp.float32)
+    end_part = jnp.dot(end_att, full_weight, preferred_element_type=jnp.float32)
+    end_part = end_part.astype(jnp.bfloat16).astype(jnp.float32)
+    end_sum = halving_scatter(end_part, "tp")
+    last_state = (end_res.astype(jnp.float32) + end_sum).astype(jnp.bfloat16).astype(jnp.float32)
     scaled = (last_state * head_gain.astype(jnp.float32)).astype(jnp.bfloat16)
     square_part = jnp.sum(last_state * last_state, axis=1)
     logit_part = jnp.dot(scaled, vocab_weight, preferred_element_type=jnp.float32)
-    square_sum, raw_logits = (
-        lax.psum(square_part.astype(jnp.bfloat16), "tp").astype(jnp.float32),
-        lax.psum(logit_part.astype(jnp.bfloat16), "tp").astype(jnp.float32),
+    summed = butterfly(
+        jnp.concatenate([logit_part, square_part[:, None]], axis=1), "tp", jnp.add
     )
+    raw_logits, square_sum = summed[:, :-1], summed[:, -1]
     mean_square = square_sum / D
     last_norm = jnp.sqrt(mean_square)
     local_top = jnp.max(raw_logits * lax.rsqrt(mean_square + eps)[:, None], axis=1)

time: 302 us -> 323 us (1.070)
  blocking collectives: 28.4 us -> 0 us
  waiting for transfers between devices: 124 us -> 146 us
  starting transfers between devices: 82.2 us -> 96.2 us
  matrix products: 20 us -> 29.6 us
    unnamed x3, waiting for transfers between devices: 42.9 us -> 0.7 us
    ppermute x12 -> x15, waiting for transfers between devices: 24.1 us -> 57.2 us  [butterfly(): lax.ppermute(value, axis, [(source, source ^ stride) for source in range(...]
    ppermute x0 -> x3, waiting for transfers between devices: none -> 31.7 us  [halving_scatter(): lax.ppermute(give, axis, [(source, source ^ bit) for source in range(coun...]
    psum x1 -> x0, blocking collectives: 28.4 us -> none  [local(): lax.psum(square_part.astype(jnp.bfloat16), 'tp').astype(jnp.float32)]
    dot_general x2 -> x3, matrix products: 15 us -> 24.6 us  [the longest x1 14.7 us: local(): jnp.dot(attended, full_weight, preferred_element_type=jnp.float32)]
    ppermute x0 -> x3, starting transfers between devices: none -> 8.92 us  [halving_scatter(): lax.ppermute(give, axis, [(source, source ^ bit) for source in range(coun...]
    ppermute x12 -> x15, starting transfers between devices: 52.3 us -> 57.3 us  [butterfly(): lax.ppermute(value, axis, [(source, source ^ stride) for source in range(...]
  transfers between devices with their start and end apart: 23 -> 29, of which waited for: 15 -> 20; matrix products, arithmetic and copies ran while one was open for 8% -> 12% of each run, Pallas kernels for 0% -> 0%
where the time goes in v2:
time: 323 us; the launch traced here: 319 us
  waiting for transfers between devices  146 us (45%)
  starting transfers between devices  96.2 us (30%)
  matrix products  29.6 us (9%)
  other arithmetic  16.7 us (5%)
  between operations  15.4 us (5%)
  local copies, waits for them, and re-layouts  15.2 us (5%)
    ppermute x15, starting transfers between devices, butterfly(): lax.ppermute(value, axis, [(source, source ^ stride) for source in range(...  57.3 us
    ppermute x15, waiting for transfers between devices, butterfly(): lax.ppermute(value, axis, [(source, source ^ stride) for source in range(...  57.2 us
    all_gather x1, waiting for transfers between devices, local(): full_weight = lax.all_gather(out_weight, 'req', axis=1, tiled=True)  54.7 us
    ppermute x3, waiting for transfers between devices, halving_scatter(): lax.ppermute(give, axis, [(source, source ^ bit) for source in range(coun...  31.7 us
    ppermute x9, starting transfers between devices, from_behind(): lax.ppermute(value, axis, [(source, source + steps) for source in range(i...  29.9 us
    dot_general x1, matrix products, local(): jnp.dot(attended, full_weight, preferred_element_type=jnp.float32)  14.7 us
    unnamed x23, local copies, waits for them, and re-layouts  11.3 us
    ppermute x3, starting transfers between devices, halving_scatter(): lax.ppermute(give, axis, [(source, source ^ bit) for source in range(coun...  8.92 us
  transfers between devices with their start and end apart: 29, of which 20 were waited for; matrix products, arithmetic and copies ran while one was open for 12% of the time, Pallas kernels for 0%

profile of v2, /device:TPU:56, one launch (start us, length us, event | category | flops | bytes accessed | tf_op | source)
XLA Modules:
  0.0 319.2 jit_solution(86178037567882648)
XLA Ops:
  8.0 4.9 %collective-permute-start.4 = (s32[256]{0:T(256)}, s32[256]{0:T(256)S(1)}, u32[]{:S(2)}, u32[]{:S(2)}) collective-permute-start(s32[256]{0:T(256)} %param.11), channel_id=1, source_target_pairs={{0,32},{8,40},{16,48},{24,56},{32,64},{40,72},{48,80},{56,88},{64,... | collective-permute-start | bytes 3080 | tf_op jit(solution)/shard_map/ppermute | solution.py:20
  14.6 3.6 %collective-permute-start.6 = (s32[256]{0:T(256)}, s32[256]{0:T(256)S(1)}, u32[]{:S(2)}, u32[]{:S(2)}) collective-permute-start(s32[256]{0:T(256)} %param.11), channel_id=1, source_target_pairs={{0,16},{8,24},{16,32},{24,40},{32,48},{40,56},{48,64},{56,72},{64,... | collective-permute-start | bytes 3080 | tf_op jit(solution)/shard_map/ppermute | solution.py:20
  18.2 4.1 %collective-permute-start.7 = (s32[256]{0:T(256)}, s32[256]{0:T(256)S(1)}, u32[]{:S(2)}, u32[]{:S(2)}) collective-permute-start(s32[256]{0:T(256)} %param.11), channel_id=1, source_target_pairs={{0,8},{8,16},{16,24},{24,32},{32,40},{40,48},{48,56},{56,64},{64,7... | collective-permute-start | bytes 3080 | tf_op jit(solution)/shard_map/ppermute | solution.py:20
  22.3 4.7 %collective-permute-start = (bf16[2,256,128]{2,1,0:T(8,128)(2,1)}, bf16[2,256,128]{2,1,0:T(8,128)(2,1)S(1)}, u32[]{:S(2)}, u32[]{:S(2)}) collective-permute-start(bf16[2,256,128]{2,1,0:T(8,128)(2,1)} %param.10), channel_id=1, source_target_pairs={{0,32},{8,40},{16,48},{24,56},{32,64},{40,72},{48,80},{56,88},{64,... | collective-permute-start | bytes 393224 | tf_op jit(solution)/shard_map/ppermute | solution.py:20
  37.5 4.0 %collective-permute-start.3 = (bf16[2,256,128]{2,1,0:T(8,128)(2,1)}, bf16[2,256,128]{2,1,0:T(8,128)(2,1)S(1)}, u32[]{:S(2)}, u32[]{:S(2)}) collective-permute-start(bf16[2,256,128]{2,1,0:T(8,128)(2,1)} %param.10), channel_id=1, source_target_pairs={{0,8},{8,16},{16,24},{24,32},{32,40},{40,48},{48,56},{56,64},{64,7... | collective-permute-start | bytes 393224 | tf_op jit(solution)/shard_map/ppermute | solution.py:20
  48.2 3.0 fusion.25
  57.5 54.7 %all-gather.2.cloned.1.call-done = bf16[896,7168]{0,1:T(8,128)(2,1)} async-done(((bf16[896,112]{0,1:T(8,128)(2,1)}), bf16[896,7168]{0,1:T(8,128)(2,1)}) %all-gather.2.cloned.1.call-update) | async-done | bytes 12845072 | tf_op jit(solution)/shard_map/all_gather | solution.py:151
  112.2 14.7 %convolution_convert_fusion = bf16[256,7168]{1,0:T(8,128)(2,1)} fusion(bf16[256,896]{0,1:T(8,128)(2,1)S(1)} %bitcast.90, bf16[896,7168]{0,1:T(8,128)(2,1)} %all-gather.2.cloned.1.call-done), kind=kOutput, calls=%fused_computation.2 | convolution fusion | flops 3290169344 | bytes 16973824 | tf_op jit(solution)/shard_map/dot_general | solution.py:152
  126.8 5.9 %copy.45 = bf16[256,7168]{0,1:T(8,128)(2,1)} copy(bf16[256,7168]{1,0:T(8,128)(2,1)} %convolution_convert_fusion) | data formatting | bytes 7340032
  140.3 4.1 %collective-permute-start.9 = (bf16[32,1792]{1,0:T(8,128)(2,1)S(1)}, bf16[32,1792]{1,0:T(8,128)(2,1)S(1)}, u32[]{:S(2)}, u32[]{:S(2)}) collective-permute-start(bf16[32,1792]{1,0:T(8,128)(2,1)S(1)} %convolution_convert_fusion.2), channel_id=1, source_target_pairs={{0,8},{8,0},{16,24},{24,16},{32,40},{40,32},{48,56},{56,48},{64,72... | collective-permute-start | bytes 344072 | tf_op jit(solution)/shard_map/ppermute | solution.py:27
  147.5 5.2 %collective-permute-done.10 = bf16[32,1792]{1,0:T(8,128)(2,1)S(1)} collective-permute-done((bf16[32,1792]{1,0:T(8,128)(2,1)S(1)}, bf16[32,1792]{1,0:T(8,128)(2,1)S(1)}, u32[]{:S(2)}, u32[]{:S(2)}) %collective-permute-start.10) | collective-permute-done | bytes 114720 | tf_op jit(solution)/shard_map/ppermute | solution.py:27
  152.7 4.6 %collective-permute-start.11 = (bf16[32,1792]{1,0:T(8,128)(2,1)S(1)}, bf16[32,1792]{1,0:T(8,128)(2,1)S(1)}, u32[]{:S(2)}, u32[]{:S(2)}) collective-permute-start(bf16[32,1792]{1,0:T(8,128)(2,1)S(1)} %add.118), channel_id=1, source_target_pairs={{0,32},{8,40},{16,48},{24,56},{32,0},{40,8},{48,16},{56,24},{64,96... | collective-permute-start | bytes 344072 | tf_op jit(solution)/shard_map/ppermute | solution.py:27
  157.3 3.6 %collective-permute-done.11 = bf16[32,1792]{1,0:T(8,128)(2,1)S(1)} collective-permute-done((bf16[32,1792]{1,0:T(8,128)(2,1)S(1)}, bf16[32,1792]{1,0:T(8,128)(2,1)S(1)}, u32[]{:S(2)}, u32[]{:S(2)}) %collective-permute-start.11) | collective-permute-done | bytes 114720 | tf_op jit(solution)/shard_map/ppermute | solution.py:27
  163.9 3.7 %collective-permute-done.12 = bf16[32,1792]{1,0:T(8,128)(2,1)S(1)} collective-permute-done((bf16[32,1792]{1,0:T(8,128)(2,1)S(1)}, bf16[32,1792]{1,0:T(8,128)(2,1)S(1)}, u32[]{:S(2)}, u32[]{:S(2)}) %collective-permute-start.12) | collective-permute-done | bytes 114720 | tf_op jit(solution)/shard_map/ppermute | solution.py:27
  167.7 3.7 %collective-permute-start.13 = (bf16[32,1792]{1,0:T(8,128)(2,1)S(1)}, bf16[32,1792]{1,0:T(8,128)(2,1)S(1)}, u32[]{:S(2)}, u32[]{:S(2)}) collective-permute-start(bf16[32,1792]{1,0:T(8,128)(2,1)S(1)} %add.120), channel_id=1, source_target_pairs={{0,128},{8,136},{16,144},{24,152},{32,160},{40,168},{48,176},{56,1... | collective-permute-start | bytes 344072 | tf_op jit(solution)/shard_map/ppermute | solution.py:27
  171.3 5.1 %collective-permute-done.13 = bf16[32,1792]{1,0:T(8,128)(2,1)S(1)} collective-permute-done((bf16[32,1792]{1,0:T(8,128)(2,1)S(1)}, bf16[32,1792]{1,0:T(8,128)(2,1)S(1)}, u32[]{:S(2)}, u32[]{:S(2)}) %collective-permute-start.13) | collective-permute-done | bytes 114720 | tf_op jit(solution)/shard_map/ppermute | solution.py:27
  176.5 5.5 %collective-permute-start.14 = (bf16[32,1792]{1,0:T(8,128)(2,1)S(1)}, bf16[32,1792]{1,0:T(8,128)(2,1)S(1)}, u32[]{:S(2)}, u32[]{:S(2)}) collective-permute-start(bf16[32,1792]{1,0:T(8,128)(2,1)S(1)} %add.121), channel_id=1, source_target_pairs={{0,256},{8,264},{16,272},{24,280},{32,288},{40,296},{48,304},{56,3... | collective-permute-start | bytes 344072 | tf_op jit(solution)/shard_map/ppermute | solution.py:27
  182.0 6.3 %collective-permute-done.14 = bf16[32,1792]{1,0:T(8,128)(2,1)S(1)} collective-permute-done((bf16[32,1792]{1,0:T(8,128)(2,1)S(1)}, bf16[32,1792]{1,0:T(8,128)(2,1)S(1)}, u32[]{:S(2)}, u32[]{:S(2)}) %collective-permute-start.14) | collective-permute-done | bytes 114720 | tf_op jit(solution)/shard_map/ppermute | solution.py:27
  188.4 8.5 %fusion.2 = f32[32,7168]{1,0:T(8,128)S(1)} fusion(bf16[896,7168]{0,1:T(8,128)(2,1)} %all-gather.2.cloned.1.call-done, bf16[32,1792]{1,0:T(8,128)(2,1)S(1)} %add.122), kind=kOutput, calls=%fused_computation.6 | convolution fusion | flops 411500544 | bytes 13819904 | tf_op jit(solution)/shard_map/dot_general | solution.py:158
  197.3 5.1 %collective-permute-start.15 = (f32[32,4,896]{2,0,1:T(8,128)S(1)}, f32[32,4,896]{2,0,1:T(8,128)}, u32[]{:S(2)}, u32[]{:S(2)}) collective-permute-start(f32[32,4,896]{2,0,1:T(8,128)S(1)} %copy.50), channel_id=1, source_target_pairs={{0,4},{1,5},{2,6},{3,7},{4,0},{5,1},{6,2},{7,3},{8,12},{9,13},{10,... | collective-permute-start | bytes 1376264 | tf_op jit(solution)/shard_map/ppermute | solution.py:44
  202.4 18.1 %collective-permute-done.15 = f32[32,4,896]{2,0,1:T(8,128)} collective-permute-done((f32[32,4,896]{2,0,1:T(8,128)S(1)}, f32[32,4,896]{2,0,1:T(8,128)}, u32[]{:S(2)}, u32[]{:S(2)}) %collective-permute-start.15) | collective-permute-done | bytes 458784 | tf_op jit(solution)/shard_map/ppermute | solution.py:44
  223.6 8.8 %collective-permute-done.16 = f32[32,2,896]{2,0,1:T(8,128)S(1)} collective-permute-done((f32[32,2,896]{2,0,1:T(8,128)S(1)}, f32[32,2,896]{2,0,1:T(8,128)S(1)}, u32[]{:S(2)}, u32[]{:S(2)}) %collective-permute-start.16) | collective-permute-done | bytes 229408 | tf_op jit(solution)/shard_map/ppermute | solution.py:44
  234.5 4.7 %collective-permute-done.17 = f32[32,1,896]{2,0,1:T(8,128)S(1)} collective-permute-done((f32[32,1,896]{2,0,1:T(8,128)S(1)}, f32[32,1,896]{2,0,1:T(8,128)S(1)}, u32[]{:S(2)}, u32[]{:S(2)}) %collective-permute-start.17) | collective-permute-done | bytes 114720 | tf_op jit(solution)/shard_map/ppermute | solution.py:44
  242.1 4.9 %collective-permute-done.18 = f32[32,1001]{1,0:T(8,128)S(1)} collective-permute-done((f32[32,1001]{1,0:T(8,128)S(1)}, f32[32,1001]{1,0:T(8,128)S(1)}, u32[]{:S(2)}, u32[]{:S(2)}) %collective-permute-start.18) | collective-permute-done | bytes 128160 | tf_op jit(solution)/shard_map/ppermute | solution.py:27
  249.0 8.1 %collective-permute-done.19 = f32[32,1001]{1,0:T(8,128)S(1)} collective-permute-done((f32[32,1001]{1,0:T(8,128)S(1)}, f32[32,1001]{1,0:T(8,128)S(1)}, u32[]{:S(2)}, u32[]{:S(2)}) %collective-permute-start.19) | collective-permute-done | bytes 128160 | tf_op jit(solution)/shard_map/ppermute | solution.py:27
  257.1 5.1 %collective-permute-start.20 = (f32[32,1001]{1,0:T(8,128)S(1)}, f32[32,1001]{1,0:T(8,128)S(1)}, u32[]{:S(2)}, u32[]{:S(2)}) collective-permute-start(f32[32,1001]{1,0:T(8,128)S(1)} %add.137), channel_id=1, source_target_pairs={{0,4},{1,5},{2,6},{3,7},{4,0},{5,1},{6,2},{7,3},{8,12},{9,13},{10,... | collective-permute-start | bytes 384392 | tf_op jit(solution)/shard_map/ppermute | solution.py:27
  262.1 6.9 %collective-permute-done.20 = f32[32,1001]{1,0:T(8,128)S(1)} collective-permute-done((f32[32,1001]{1,0:T(8,128)S(1)}, f32[32,1001]{1,0:T(8,128)S(1)}, u32[]{:S(2)}, u32[]{:S(2)}) %collective-permute-start.20) | collective-permute-done | bytes 128160 | tf_op jit(solution)/shard_map/ppermute | solution.py:27
  278.4 5.3 %collective-permute-start.23 = (f32[32]{0:T(128)S(1)}, f32[32]{0:T(128)S(1)}, u32[]{:S(2)}, u32[]{:S(2)}) collective-permute-start(f32[32]{0:T(128)S(1)} %max.19), channel_id=1, source_target_pairs={{0,32},{8,40},{16,48},{24,56},{32,0},{40,8},{48,16},{56,24},{64,96... | collective-permute-start | bytes 392 | tf_op jit(solution)/shard_map/ppermute | solution.py:27
  285.3 3.9 %collective-permute-start.24 = (f32[32]{0:T(128)S(1)}, f32[32]{0:T(128)S(1)}, u32[]{:S(2)}, u32[]{:S(2)}) collective-permute-start(f32[32]{0:T(128)S(1)} %max.20), channel_id=1, source_target_pairs={{0,64},{8,72},{16,80},{24,88},{32,96},{40,104},{48,112},{56,120},{... | collective-permute-start | bytes 392 | tf_op jit(solution)/shard_map/ppermute | solution.py:27
  290.8 7.0 %collective-permute-start.25 = (f32[32]{0:T(128)S(1)}, f32[32]{0:T(128)S(1)}, u32[]{:S(2)}, u32[]{:S(2)}) collective-permute-start(f32[32]{0:T(128)S(1)} %max.21), channel_id=1, source_target_pairs={{0,128},{8,136},{16,144},{24,152},{32,160},{40,168},{48,176},{56,1... | collective-permute-start | bytes 392 | tf_op jit(solution)/shard_map/ppermute | solution.py:27
  299.3 4.3 %collective-permute-start.26 = (f32[32]{0:T(128)S(1)}, f32[32]{0:T(128)S(1)}, u32[]{:S(2)}, u32[]{:S(2)}) collective-permute-start(f32[32]{0:T(128)S(1)} %max.22), channel_id=1, source_target_pairs={{0,256},{8,264},{16,272},{24,280},{32,288},{40,296},{48,304},{56,3... | collective-permute-start | bytes 392 | tf_op jit(solution)/shard_map/ppermute | solution.py:27
  304.4 4.3 %collective-permute-done.26 = f32[32]{0:T(128)S(1)} collective-permute-done((f32[32]{0:T(128)S(1)}, f32[32]{0:T(128)S(1)}, u32[]{:S(2)}, u32[]{:S(2)}) %collective-permute-start.26) | collective-permute-done | bytes 160 | tf_op jit(solution)/shard_map/ppermute | solution.py:27
  (109 shorter events, 67.3 us)
Async XLA Ops:
  7.2 232.2 %copy-start = (bf16[896,1000]{0,1:T(8,128)(2,1)S(1)}, bf16[896,1000]{0,1:T(8,128)(2,1)}, u32[]{:S(2)}) copy-start(bf16[896,1000]{0,1:T(8,128)(2,1)} %param.15) | copy-start | bytes 5376004
  7.2 40.9 %copy-start.1 = (bf16[2,256,128]{2,1,0:T(8,128)(2,1)S(1)}, bf16[2,256,128]{2,1,0:T(8,128)(2,1)}, u32[]{:S(2)}) copy-start(bf16[2,256,128]{2,1,0:T(8,128)(2,1)} %param.10) | copy-start | bytes 393220
  7.2 105.0 %all-gather.2.cloned.1.call-start = ((), (), s32[]{:S(2)}) async-start(), calls=%async_computation.1 | async-start | bytes 13045760 | tf_op jit(solution)/shard_map/all_gather | solution.py:151
  7.9 301.2 %reduce-scatter.4.cloned.1.call-start = ((), (), s32[]{:S(2)}) async-start(), calls=%async_computation.2 | async-start | bytes 4128768
  8.0 23.7 %collective-permute-start.4 = (s32[256]{0:T(256)}, s32[256]{0:T(256)S(1)}, u32[]{:S(2)}, u32[]{:S(2)}) collective-permute-start(s32[256]{0:T(256)} %param.11), channel_id=1, source_target_pairs={{0,32},{8,40},{16,48},{24,56},{32,64},{40,72},{48,80},{56,88},{64,... | collective-permute-start | bytes 3080 | tf_op jit(solution)/shard_map/ppermute | solution.py:20
  12.9 21.7 %collective-permute-start.5 = (s32[256]{0:T(256)}, s32[256]{0:T(256)S(1)}, u32[]{:S(2)}, u32[]{:S(2)}) collective-permute-start(s32[256]{0:T(256)} %param.11), channel_id=1, source_target_pairs={{0,24},{8,32},{16,40},{24,48},{32,56},{40,64},{48,72},{56,80},{64,... | collective-permute-start | bytes 3080 | tf_op jit(solution)/shard_map/ppermute | solution.py:20
  14.6 22.9 %collective-permute-start.6 = (s32[256]{0:T(256)}, s32[256]{0:T(256)S(1)}, u32[]{:S(2)}, u32[]{:S(2)}) collective-permute-start(s32[256]{0:T(256)} %param.11), channel_id=1, source_target_pairs={{0,16},{8,24},{16,32},{24,40},{32,48},{40,56},{48,64},{56,72},{64,... | collective-permute-start | bytes 3080 | tf_op jit(solution)/shard_map/ppermute | solution.py:20
  18.2 23.3 %collective-permute-start.7 = (s32[256]{0:T(256)}, s32[256]{0:T(256)S(1)}, u32[]{:S(2)}, u32[]{:S(2)}) collective-permute-start(s32[256]{0:T(256)} %param.11), channel_id=1, source_target_pairs={{0,8},{8,16},{16,24},{24,32},{32,40},{40,48},{48,56},{56,64},{64,7... | collective-permute-start | bytes 3080 | tf_op jit(solution)/shard_map/ppermute | solution.py:20
  22.3 25.7 %collective-permute-start = (bf16[2,256,128]{2,1,0:T(8,128)(2,1)}, bf16[2,256,128]{2,1,0:T(8,128)(2,1)S(1)}, u32[]{:S(2)}, u32[]{:S(2)}) collective-permute-start(bf16[2,256,128]{2,1,0:T(8,128)(2,1)} %param.10), channel_id=1, source_target_pairs={{0,32},{8,40},{16,48},{24,56},{32,64},{40,72},{48,80},{56,88},{64,... | collective-permute-start | bytes 393224 | tf_op jit(solution)/shard_map/ppermute | solution.py:20
  31.7 16.3 %collective-permute-start.1 = (bf16[2,256,128]{2,1,0:T(8,128)(2,1)}, bf16[2,256,128]{2,1,0:T(8,128)(2,1)S(1)}, u32[]{:S(2)}, u32[]{:S(2)}) collective-permute-start(bf16[2,256,128]{2,1,0:T(8,128)(2,1)} %param.10), channel_id=1, source_target_pairs={{0,24},{8,32},{16,40},{24,48},{32,56},{40,64},{48,72},{56,80},{64,... | collective-permute-start | bytes 393224 | tf_op jit(solution)/shard_map/ppermute | solution.py:20
  34.6 13.4 %collective-permute-start.2 = (bf16[2,256,128]{2,1,0:T(8,128)(2,1)}, bf16[2,256,128]{2,1,0:T(8,128)(2,1)S(1)}, u32[]{:S(2)}, u32[]{:S(2)}) collective-permute-start(bf16[2,256,128]{2,1,0:T(8,128)(2,1)} %param.10), channel_id=1, source_target_pairs={{0,16},{8,24},{16,32},{24,40},{32,48},{40,56},{48,64},{56,72},{64,... | collective-permute-start | bytes 393224 | tf_op jit(solution)/shard_map/ppermute | solution.py:20
  37.5 10.6 %collective-permute-start.3 = (bf16[2,256,128]{2,1,0:T(8,128)(2,1)}, bf16[2,256,128]{2,1,0:T(8,128)(2,1)S(1)}, u32[]{:S(2)}, u32[]{:S(2)}) collective-permute-start(bf16[2,256,128]{2,1,0:T(8,128)(2,1)} %param.10), channel_id=1, source_target_pairs={{0,8},{8,16},{16,24},{24,32},{32,40},{40,48},{48,56},{56,64},{64,7... | collective-permute-start | bytes 393224 | tf_op jit(solution)/shard_map/ppermute | solution.py:20
  133.3 3.1 collective-permute-start.8
  140.3 5.1 %collective-permute-start.9 = (bf16[32,1792]{1,0:T(8,128)(2,1)S(1)}, bf16[32,1792]{1,0:T(8,128)(2,1)S(1)}, u32[]{:S(2)}, u32[]{:S(2)}) collective-permute-start(bf16[32,1792]{1,0:T(8,128)(2,1)S(1)} %convolution_convert_fusion.2), channel_id=1, source_target_pairs={{0,8},{8,0},{16,24},{24,16},{32,40},{40,32},{48,56},{56,48},{64,72... | collective-permute-start | bytes 344072 | tf_op jit(solution)/shard_map/ppermute | solution.py:27
  145.4 7.3 %collective-permute-start.10 = (bf16[32,1792]{1,0:T(8,128)(2,1)S(1)}, bf16[32,1792]{1,0:T(8,128)(2,1)S(1)}, u32[]{:S(2)}, u32[]{:S(2)}) collective-permute-start(bf16[32,1792]{1,0:T(8,128)(2,1)S(1)} %add.117), channel_id=1, source_target_pairs={{0,16},{8,24},{16,0},{24,8},{32,48},{40,56},{48,32},{56,40},{64,80... | collective-permute-start | bytes 344072 | tf_op jit(solution)/shard_map/ppermute | solution.py:27
  152.7 8.2 %collective-permute-start.11 = (bf16[32,1792]{1,0:T(8,128)(2,1)S(1)}, bf16[32,1792]{1,0:T(8,128)(2,1)S(1)}, u32[]{:S(2)}, u32[]{:S(2)}) collective-permute-start(bf16[32,1792]{1,0:T(8,128)(2,1)S(1)} %add.118), channel_id=1, source_target_pairs={{0,32},{8,40},{16,48},{24,56},{32,0},{40,8},{48,16},{56,24},{64,96... | collective-permute-start | bytes 344072 | tf_op jit(solution)/shard_map/ppermute | solution.py:27
  160.9 6.7 %collective-permute-start.12 = (bf16[32,1792]{1,0:T(8,128)(2,1)S(1)}, bf16[32,1792]{1,0:T(8,128)(2,1)S(1)}, u32[]{:S(2)}, u32[]{:S(2)}) collective-permute-start(bf16[32,1792]{1,0:T(8,128)(2,1)S(1)} %add.119), channel_id=1, source_target_pairs={{0,64},{8,72},{16,80},{24,88},{32,96},{40,104},{48,112},{56,120},{... | collective-permute-start | bytes 344072 | tf_op jit(solution)/shard_map/ppermute | solution.py:27
  167.7 8.8 %collective-permute-start.13 = (bf16[32,1792]{1,0:T(8,128)(2,1)S(1)}, bf16[32,1792]{1,0:T(8,128)(2,1)S(1)}, u32[]{:S(2)}, u32[]{:S(2)}) collective-permute-start(bf16[32,1792]{1,0:T(8,128)(2,1)S(1)} %add.120), channel_id=1, source_target_pairs={{0,128},{8,136},{16,144},{24,152},{32,160},{40,168},{48,176},{56,1... | collective-permute-start | bytes 344072 | tf_op jit(solution)/shard_map/ppermute | solution.py:27
  176.5 11.8 %collective-permute-start.14 = (bf16[32,1792]{1,0:T(8,128)(2,1)S(1)}, bf16[32,1792]{1,0:T(8,128)(2,1)S(1)}, u32[]{:S(2)}, u32[]{:S(2)}) collective-permute-start(bf16[32,1792]{1,0:T(8,128)(2,1)S(1)} %add.121), channel_id=1, source_target_pairs={{0,256},{8,264},{16,272},{24,280},{32,288},{40,296},{48,304},{56,3... | collective-permute-start | bytes 344072 | tf_op jit(solution)/shard_map/ppermute | solution.py:27
  188.4 46.1 %copy-start.3 = (bf16[896]{0:T(1024)(128)(2,1)S(1)}, bf16[896]{0:T(1024)(128)(2,1)}, u32[]{:S(2)}) copy-start(bf16[896]{0:T(1024)(128)(2,1)} %param.14) | copy-start | bytes 5380
  197.3 23.3 %collective-permute-start.15 = (f32[32,4,896]{2,0,1:T(8,128)S(1)}, f32[32,4,896]{2,0,1:T(8,128)}, u32[]{:S(2)}, u32[]{:S(2)}) collective-permute-start(f32[32,4,896]{2,0,1:T(8,128)S(1)} %copy.50), channel_id=1, source_target_pairs={{0,4},{1,5},{2,6},{3,7},{4,0},{5,1},{6,2},{7,3},{8,12},{9,13},{10,... | collective-permute-start | bytes 1376264 | tf_op jit(solution)/shard_map/ppermute | solution.py:44
  221.7 10.8 %collective-permute-start.16 = (f32[32,2,896]{2,0,1:T(8,128)S(1)}, f32[32,2,896]{2,0,1:T(8,128)S(1)}, u32[]{:S(2)}, u32[]{:S(2)}) collective-permute-start(f32[32,2,896]{2,0,1:T(8,128)S(1)} %constant_dynamic-slice_fusion.1), channel_id=1, source_target_pairs={{0,2},{1,3},{2,0},{3,1},{4,6},{5,7},{6,4},{7,5},{8,10},{9,11},{10,... | collective-permute-start | bytes 688136 | tf_op jit(solution)/shard_map/ppermute | solution.py:44
  232.5 6.7 %collective-permute-start.17 = (f32[32,1,896]{2,0,1:T(8,128)S(1)}, f32[32,1,896]{2,0,1:T(8,128)S(1)}, u32[]{:S(2)}, u32[]{:S(2)}) collective-permute-start(f32[32,1,896]{2,0,1:T(8,128)S(1)} %constant_dynamic-slice_fusion), channel_id=1, source_target_pairs={{0,1},{1,0},{2,3},{3,2},{4,5},{5,4},{6,7},{7,6},{8,9},{9,8},{10,11... | collective-permute-start | bytes 344072 | tf_op jit(solution)/shard_map/ppermute | solution.py:44
  240.1 6.9 %collective-permute-start.18 = (f32[32,1001]{1,0:T(8,128)S(1)}, f32[32,1001]{1,0:T(8,128)S(1)}, u32[]{:S(2)}, u32[]{:S(2)}) collective-permute-start(f32[32,1001]{1,0:T(8,128)S(1)} %pad_maximum_fusion), channel_id=1, source_target_pairs={{0,1},{1,0},{2,3},{3,2},{4,5},{5,4},{6,7},{7,6},{8,9},{9,8},{10,11... | collective-permute-start | bytes 384392 | tf_op jit(solution)/shard_map/ppermute | solution.py:27
  247.1 10.0 %collective-permute-start.19 = (f32[32,1001]{1,0:T(8,128)S(1)}, f32[32,1001]{1,0:T(8,128)S(1)}, u32[]{:S(2)}, u32[]{:S(2)}) collective-permute-start(f32[32,1001]{1,0:T(8,128)S(1)} %fusion.62), channel_id=1, source_target_pairs={{0,2},{1,3},{2,0},{3,1},{4,6},{5,7},{6,4},{7,5},{8,10},{9,11},{10,... | collective-permute-start | bytes 384392 | tf_op jit(solution)/shard_map/ppermute | solution.py:27
  257.1 11.9 %collective-permute-start.20 = (f32[32,1001]{1,0:T(8,128)S(1)}, f32[32,1001]{1,0:T(8,128)S(1)}, u32[]{:S(2)}, u32[]{:S(2)}) collective-permute-start(f32[32,1001]{1,0:T(8,128)S(1)} %add.137), channel_id=1, source_target_pairs={{0,4},{1,5},{2,6},{3,7},{4,0},{5,1},{6,2},{7,3},{8,12},{9,13},{10,... | collective-permute-start | bytes 384392 | tf_op jit(solution)/shard_map/ppermute | solution.py:27
  269.9 3.0 collective-permute-start.21
  272.9 5.4 %collective-permute-start.22 = (f32[32]{0:T(128)S(1)}, f32[32]{0:T(128)S(1)}, u32[]{:S(2)}, u32[]{:S(2)}) collective-permute-start(f32[32]{0:T(128)S(1)} %max.18), channel_id=1, source_target_pairs={{0,16},{8,24},{16,0},{24,8},{32,48},{40,56},{48,32},{56,40},{64,80... | collective-permute-start | bytes 392 | tf_op jit(solution)/shard_map/ppermute | solution.py:27
  278.4 6.9 %collective-permute-start.23 = (f32[32]{0:T(128)S(1)}, f32[32]{0:T(128)S(1)}, u32[]{:S(2)}, u32[]{:S(2)}) collective-permute-start(f32[32]{0:T(128)S(1)} %max.19), channel_id=1, source_target_pairs={{0,32},{8,40},{16,48},{24,56},{32,0},{40,8},{48,16},{56,24},{64,96... | collective-permute-start | bytes 392 | tf_op jit(solution)/shard_map/ppermute | solution.py:27
  285.3 5.5 %collective-permute-start.24 = (f32[32]{0:T(128)S(1)}, f32[32]{0:T(128)S(1)}, u32[]{:S(2)}, u32[]{:S(2)}) collective-permute-start(f32[32]{0:T(128)S(1)} %max.20), channel_id=1, source_target_pairs={{0,64},{8,72},{16,80},{24,88},{32,96},{40,104},{48,112},{56,120},{... | collective-permute-start | bytes 392 | tf_op jit(solution)/shard_map/ppermute | solution.py:27
  290.8 8.6 %collective-permute-start.25 = (f32[32]{0:T(128)S(1)}, f32[32]{0:T(128)S(1)}, u32[]{:S(2)}, u32[]{:S(2)}) collective-permute-start(f32[32]{0:T(128)S(1)} %max.21), channel_id=1, source_target_pairs={{0,128},{8,136},{16,144},{24,152},{32,160},{40,168},{48,176},{56,1... | collective-permute-start | bytes 392 | tf_op jit(solution)/shard_map/ppermute | solution.py:27
  299.3 9.3 %collective-permute-start.26 = (f32[32]{0:T(128)S(1)}, f32[32]{0:T(128)S(1)}, u32[]{:S(2)}, u32[]{:S(2)}) collective-permute-start(f32[32]{0:T(128)S(1)} %max.22), channel_id=1, source_target_pairs={{0,256},{8,264},{16,272},{24,280},{32,288},{40,296},{48,304},{56,3... | collective-permute-start | bytes 392 | tf_op jit(solution)/shard_map/ppermute | solution.py:27
  (1 other events, 6.0 us)
Sparse Core Ops, SparseCore 0:
  11.3 100.8 all-gather.1
  132.9 47.7 reduce-scatter.3

commit v3 on v2

--- a/solution.py
+++ b/solution.py
@@ -37,11 +37,13 @@
     held = value.reshape(rows, count, value.shape[1] // count)
     bit = count // 2
     while bit >= 1:
+        if bit < count // 2:
+            held = held.astype(jnp.float32)
         half = held.shape[1] // 2
         mine = (index // bit) % 2
         keep = lax.dynamic_slice_in_dim(held, mine * half, half, 1)
         give = lax.dynamic_slice_in_dim(held, (1 - mine) * half, half, 1)
-        held = keep + lax.ppermute(give, axis, [(source, source ^ bit) for source in range(count)])
+        held = keep.astype(jnp.float32) + lax.ppermute(give, axis, [(source, source ^ bit) for source in range(count)]).astype(jnp.float32)
         bit //= 2
     return held.reshape(rows, -1)
 
@@ -146,17 +148,19 @@
         preferred_element_type=jnp.float32,
     ).astype(jnp.bfloat16)
     end_rows = butterfly(end_rows, "req", jnp.add)
+    attended, end_rows = lax.optimization_barrier((attended, end_rows))
     end_att, end_res = end_rows[:, : attended.shape[1]], end_rows[:, attended.shape[1] :]
 
     full_weight = lax.all_gather(out_weight, "req", axis=1, tiled=True)
+    end_part = jnp.dot(end_att, full_weight, preferred_element_type=jnp.float32)
+    end_part = end_part.astype(jnp.bfloat16)
+    attended, end_part = lax.optimization_barrier((attended, end_part))
     projected = jnp.dot(attended, full_weight, preferred_element_type=jnp.float32)
     own_share = lax.psum_scatter(
         projected.astype(jnp.bfloat16), "tp", scatter_dimension=1, tiled=True
     ).astype(jnp.float32)
     hidden = (residual.astype(jnp.float32) + own_share).astype(jnp.bfloat16)
 
-    end_part = jnp.dot(end_att, full_weight, preferred_element_type=jnp.float32)
-    end_part = end_part.astype(jnp.bfloat16).astype(jnp.float32)
     end_sum = halving_scatter(end_part, "tp")
     last_state = (end_res.astype(jnp.float32) + end_sum).astype(jnp.bfloat16).astype(jnp.float32)
     scaled = (last_state * head_gain.astype(jnp.float32)).astype(jnp.bfloat16)

time: 323 us -> 287 us (0.89)
  waiting for transfers between devices: 146 us -> 109 us
    all_gather x1, waiting for transfers between devices: 54.7 us -> 0.02 us  [local(): full_weight = lax.all_gather(out_weight, 'req', axis=1, tiled=True)]
    ppermute x15, waiting for transfers between devices: 57.2 us -> 75.6 us  [butterfly(): lax.ppermute(value, axis, [(source, source ^ stride) for source in range(...]
  transfers between devices with their start and end apart: 29 -> 29, of which waited for: 20 -> 18; matrix products, arithmetic and copies ran while one was open for 12% -> 11% of each run, Pallas kernels for 0% -> 0%
where the time goes in v3:
time: 287 us; the launch traced here: 285 us
  waiting for transfers between devices  109 us (38%)
  starting transfers between devices  97.4 us (34%)
  matrix products  29.6 us (10%)
  local copies, waits for them, and re-layouts  17.4 us (6%)
  other arithmetic  16.1 us (6%)
  between operations  15.4 us (5%)
    ppermute x15, waiting for transfers between devices, butterfly(): lax.ppermute(value, axis, [(source, source ^ stride) for source in range(...  75.6 us
    ppermute x15, starting transfers between devices, butterfly(): lax.ppermute(value, axis, [(source, source ^ stride) for source in range(...  57.5 us
    ppermute x3, waiting for transfers between devices, halving_scatter(): lax.ppermute(give, axis, [(source, source ^ bit) for source in range(coun...  32.4 us
    ppermute x9, starting transfers between devices, from_behind(): lax.ppermute(value, axis, [(source, source + steps) for source in range(i...  31 us
    dot_general x1, matrix products, local(): jnp.dot(attended, full_weight, preferred_element_type=jnp.float32)  14.7 us
    unnamed x23, local copies, waits for them, and re-layouts  12.1 us
    ppermute x3, starting transfers between devices, halving_scatter(): lax.ppermute(give, axis, [(source, source ^ bit) for source in range(coun...  8.88 us
    dot_general x1, matrix products, local(): end_part = jnp.dot(end_att, full_weight, preferred_element_type=jnp.float32)  8.51 us
  transfers between devices with their start and end apart: 29, of which 18 were waited for; matrix products, arithmetic and copies ran while one was open for 11% of the time, Pallas kernels for 0%

profile of v3, /device:TPU:56, one launch (start us, length us, event | category | flops | bytes accessed | tf_op | source)
XLA Modules:
  0.0 284.7 jit_solution(18056748036821165008)
XLA Ops:
  8.0 4.9 %collective-permute-start.4 = (s32[256]{0:T(256)}, s32[256]{0:T(256)S(1)}, u32[]{:S(2)}, u32[]{:S(2)}) collective-permute-start(s32[256]{0:T(256)} %param.11), channel_id=1, source_target_pairs={{0,32},{8,40},{16,48},{24,56},{32,64},{40,72},{48,80},{56,88},{64,... | collective-permute-start | bytes 3080 | tf_op jit(solution)/shard_map/ppermute | solution.py:20
  14.6 3.6 %collective-permute-start.6 = (s32[256]{0:T(256)}, s32[256]{0:T(256)S(1)}, u32[]{:S(2)}, u32[]{:S(2)}) collective-permute-start(s32[256]{0:T(256)} %param.11), channel_id=1, source_target_pairs={{0,16},{8,24},{16,32},{24,40},{32,48},{40,56},{48,64},{56,72},{64,... | collective-permute-start | bytes 3080 | tf_op jit(solution)/shard_map/ppermute | solution.py:20
  18.2 4.1 %collective-permute-start.7 = (s32[256]{0:T(256)}, s32[256]{0:T(256)S(1)}, u32[]{:S(2)}, u32[]{:S(2)}) collective-permute-start(s32[256]{0:T(256)} %param.11), channel_id=1, source_target_pairs={{0,8},{8,16},{16,24},{24,32},{32,40},{40,48},{48,56},{56,64},{64,7... | collective-permute-start | bytes 3080 | tf_op jit(solution)/shard_map/ppermute | solution.py:20
  30.3 7.0 %collective-permute-start = (bf16[2,256,128]{2,1,0:T(8,128)(2,1)}, bf16[2,256,128]{2,1,0:T(8,128)(2,1)}, u32[]{:S(2)}, u32[]{:S(2)}) collective-permute-start(bf16[2,256,128]{2,1,0:T(8,128)(2,1)} %param.10), channel_id=1, source_target_pairs={{0,32},{8,40},{16,48},{24,56},{32,64},{40,72},{48,80},{56,88},{64,... | collective-permute-start | bytes 393224 | tf_op jit(solution)/shard_map/ppermute | solution.py:20
  44.6 3.9 %collective-permute-start.3 = (bf16[2,256,128]{2,1,0:T(8,128)(2,1)}, bf16[2,256,128]{2,1,0:T(8,128)(2,1)S(1)}, u32[]{:S(2)}, u32[]{:S(2)}) collective-permute-start(bf16[2,256,128]{2,1,0:T(8,128)(2,1)} %param.10), channel_id=1, source_target_pairs={{0,8},{8,16},{16,24},{24,32},{32,40},{40,48},{48,56},{56,64},{64,7... | collective-permute-start | bytes 393224 | tf_op jit(solution)/shard_map/ppermute | solution.py:20
  70.4 3.5 %collective-permute-start.10 = (bf16[32,1792]{1,0:T(8,128)(2,1)S(1)}, bf16[32,1792]{1,0:T(8,128)(2,1)S(1)}, u32[]{:S(2)}, u32[]{:S(2)}) collective-permute-start(bf16[32,1792]{1,0:T(8,128)(2,1)S(1)} %add.116), channel_id=1, source_target_pairs={{0,16},{8,24},{16,0},{24,8},{32,48},{40,56},{48,32},{56,40},{64,80... | collective-permute-start | bytes 344072 | tf_op jit(solution)/shard_map/ppermute | solution.py:27
  73.9 6.6 %collective-permute-done.10 = bf16[32,1792]{1,0:T(8,128)(2,1)S(1)} collective-permute-done((bf16[32,1792]{1,0:T(8,128)(2,1)S(1)}, bf16[32,1792]{1,0:T(8,128)(2,1)S(1)}, u32[]{:S(2)}, u32[]{:S(2)}) %collective-permute-start.10) | collective-permute-done | bytes 114720 | tf_op jit(solution)/shard_map/ppermute | solution.py:27
  80.5 6.7 %collective-permute-start.11 = (bf16[32,1792]{1,0:T(8,128)(2,1)S(1)}, bf16[32,1792]{1,0:T(8,128)(2,1)S(1)}, u32[]{:S(2)}, u32[]{:S(2)}) collective-permute-start(bf16[32,1792]{1,0:T(8,128)(2,1)S(1)} %add.117), channel_id=1, source_target_pairs={{0,32},{8,40},{16,48},{24,56},{32,0},{40,8},{48,16},{56,24},{64,96... | collective-permute-start | bytes 344072 | tf_op jit(solution)/shard_map/ppermute | solution.py:27
  87.3 6.1 %collective-permute-done.11 = bf16[32,1792]{1,0:T(8,128)(2,1)S(1)} collective-permute-done((bf16[32,1792]{1,0:T(8,128)(2,1)S(1)}, bf16[32,1792]{1,0:T(8,128)(2,1)S(1)}, u32[]{:S(2)}, u32[]{:S(2)}) %collective-permute-start.11) | collective-permute-done | bytes 114720 | tf_op jit(solution)/shard_map/ppermute | solution.py:27
  93.4 5.3 %collective-permute-start.12 = (bf16[32,1792]{1,0:T(8,128)(2,1)S(1)}, bf16[32,1792]{1,0:T(8,128)(2,1)S(1)}, u32[]{:S(2)}, u32[]{:S(2)}) collective-permute-start(bf16[32,1792]{1,0:T(8,128)(2,1)S(1)} %add.118), channel_id=1, source_target_pairs={{0,64},{8,72},{16,80},{24,88},{32,96},{40,104},{48,112},{56,120},{... | collective-permute-start | bytes 344072 | tf_op jit(solution)/shard_map/ppermute | solution.py:27
  98.7 5.3 %collective-permute-done.12 = bf16[32,1792]{1,0:T(8,128)(2,1)S(1)} collective-permute-done((bf16[32,1792]{1,0:T(8,128)(2,1)S(1)}, bf16[32,1792]{1,0:T(8,128)(2,1)S(1)}, u32[]{:S(2)}, u32[]{:S(2)}) %collective-permute-start.12) | collective-permute-done | bytes 114720 | tf_op jit(solution)/shard_map/ppermute | solution.py:27
  104.1 6.2 %collective-permute-start.13 = (bf16[32,1792]{1,0:T(8,128)(2,1)S(1)}, bf16[32,1792]{1,0:T(8,128)(2,1)S(1)}, u32[]{:S(2)}, u32[]{:S(2)}) collective-permute-start(bf16[32,1792]{1,0:T(8,128)(2,1)S(1)} %add.119), channel_id=1, source_target_pairs={{0,128},{8,136},{16,144},{24,152},{32,160},{40,168},{48,176},{56,1... | collective-permute-start | bytes 344072 | tf_op jit(solution)/shard_map/ppermute | solution.py:27
  110.2 7.3 %collective-permute-done.13 = bf16[32,1792]{1,0:T(8,128)(2,1)S(1)} collective-permute-done((bf16[32,1792]{1,0:T(8,128)(2,1)S(1)}, bf16[32,1792]{1,0:T(8,128)(2,1)S(1)}, u32[]{:S(2)}, u32[]{:S(2)}) %collective-permute-start.13) | collective-permute-done | bytes 114720 | tf_op jit(solution)/shard_map/ppermute | solution.py:27
  117.6 5.6 %collective-permute-start.14 = (bf16[32,1792]{1,0:T(8,128)(2,1)S(1)}, bf16[32,1792]{1,0:T(8,128)(2,1)S(1)}, u32[]{:S(2)}, u32[]{:S(2)}) collective-permute-start(bf16[32,1792]{1,0:T(8,128)(2,1)S(1)} %add.120), channel_id=1, source_target_pairs={{0,256},{8,264},{16,272},{24,280},{32,288},{40,296},{48,304},{56,3... | collective-permute-start | bytes 344072 | tf_op jit(solution)/shard_map/ppermute | solution.py:27
  123.2 6.2 %collective-permute-done.14 = bf16[32,1792]{1,0:T(8,128)(2,1)S(1)} collective-permute-done((bf16[32,1792]{1,0:T(8,128)(2,1)S(1)}, bf16[32,1792]{1,0:T(8,128)(2,1)S(1)}, u32[]{:S(2)}, u32[]{:S(2)}) %collective-permute-start.14) | collective-permute-done | bytes 114720 | tf_op jit(solution)/shard_map/ppermute | solution.py:27
  129.5 8.5 %convolution_convert_fusion.1 = bf16[32,7168]{1,0:T(8,128)(2,1)S(1)} fusion(bf16[896,7168]{0,1:T(8,128)(2,1)} %all-gather.2.cloned.1.call-done, bf16[32,1792]{1,0:T(8,128)(2,1)S(1)} %add.121), kind=kOutput, calls=%fused_computation.5 | convolution fusion | flops 411271168 | bytes 13361152 | tf_op jit(solution)/shard_map/dot_general | solution.py:155
  138.0 14.7 %convolution_convert_fusion = bf16[256,7168]{1,0:T(8,128)(2,1)} fusion(bf16[256,896]{0,1:T(8,128)(2,1)S(1)} %bitcast.91, bf16[896,7168]{0,1:T(8,128)(2,1)} %all-gather.2.cloned.1.call-done), kind=kOutput, calls=%fused_computation.2 | convolution fusion | flops 3290169344 | bytes 16973824 | tf_op jit(solution)/shard_map/dot_general | solution.py:158
  152.7 5.9 %copy.45 = bf16[256,7168]{0,1:T(8,128)(2,1)} copy(bf16[256,7168]{1,0:T(8,128)(2,1)} %convolution_convert_fusion) | data formatting | bytes 7340032
  159.0 5.0 %collective-permute-start.15 = (bf16[32,4,896]{2,0,1:T(8,128)(2,1)S(1)}, bf16[32,4,896]{2,0,1:T(8,128)(2,1)S(1)}, u32[]{:S(2)}, u32[]{:S(2)}) collective-permute-start(bf16[32,4,896]{2,0,1:T(8,128)(2,1)S(1)} %copy.50), channel_id=1, source_target_pairs={{0,4},{1,5},{2,6},{3,7},{4,0},{5,1},{6,2},{7,3},{8,12},{9,13},{10,... | collective-permute-start | bytes 688136 | tf_op jit(solution)/shard_map/ppermute | solution.py:46
  164.1 10.0 %collective-permute-done.15 = bf16[32,4,896]{2,0,1:T(8,128)(2,1)S(1)} collective-permute-done((bf16[32,4,896]{2,0,1:T(8,128)(2,1)S(1)}, bf16[32,4,896]{2,0,1:T(8,128)(2,1)S(1)}, u32[]{:S(2)}, u32[]{:S(2)}) %collective-permute-start.15) | collective-permute-done | bytes 229408 | tf_op jit(solution)/shard_map/ppermute | solution.py:46
  176.1 14.8 %collective-permute-done.16 = f32[32,2,896]{2,0,1:T(8,128)S(1)} collective-permute-done((f32[32,2,896]{2,0,1:T(8,128)S(1)}, f32[32,2,896]{2,0,1:T(8,128)S(1)}, u32[]{:S(2)}, u32[]{:S(2)}) %collective-permute-start.16) | collective-permute-done | bytes 229408 | tf_op jit(solution)/shard_map/ppermute | solution.py:46
  192.9 7.6 %collective-permute-done.17 = f32[32,1,896]{2,0,1:T(8,128)S(1)} collective-permute-done((f32[32,1,896]{2,0,1:T(8,128)S(1)}, f32[32,1,896]{2,0,1:T(8,128)S(1)}, u32[]{:S(2)}, u32[]{:S(2)}) %collective-permute-start.17) | collective-permute-done | bytes 114720 | tf_op jit(solution)/shard_map/ppermute | solution.py:46
  203.4 8.6 %collective-permute-done.18 = f32[32,1001]{1,0:T(8,128)S(1)} collective-permute-done((f32[32,1001]{1,0:T(8,128)S(1)}, f32[32,1001]{1,0:T(8,128)S(1)}, u32[]{:S(2)}, u32[]{:S(2)}) %collective-permute-start.18) | collective-permute-done | bytes 128160 | tf_op jit(solution)/shard_map/ppermute | solution.py:27
  212.1 3.2 %collective-permute-start.19 = (f32[32,1001]{1,0:T(8,128)S(1)}, f32[32,1001]{1,0:T(8,128)S(1)}, u32[]{:S(2)}, u32[]{:S(2)}) collective-permute-start(f32[32,1001]{1,0:T(8,128)S(1)} %fusion.61), channel_id=1, source_target_pairs={{0,2},{1,3},{2,0},{3,1},{4,6},{5,7},{6,4},{7,5},{8,10},{9,11},{10,... | collective-permute-start | bytes 384392 | tf_op jit(solution)/shard_map/ppermute | solution.py:27
  215.3 10.0 %collective-permute-done.19 = f32[32,1001]{1,0:T(8,128)S(1)} collective-permute-done((f32[32,1001]{1,0:T(8,128)S(1)}, f32[32,1001]{1,0:T(8,128)S(1)}, u32[]{:S(2)}, u32[]{:S(2)}) %collective-permute-start.19) | collective-permute-done | bytes 128160 | tf_op jit(solution)/shard_map/ppermute | solution.py:27
  225.4 4.9 %collective-permute-start.20 = (f32[32,1001]{1,0:T(8,128)S(1)}, f32[32,1001]{1,0:T(8,128)S(1)}, u32[]{:S(2)}, u32[]{:S(2)}) collective-permute-start(f32[32,1001]{1,0:T(8,128)S(1)} %add.137), channel_id=1, source_target_pairs={{0,4},{1,5},{2,6},{3,7},{4,0},{5,1},{6,2},{7,3},{8,12},{9,13},{10,... | collective-permute-start | bytes 384392 | tf_op jit(solution)/shard_map/ppermute | solution.py:27
  230.3 6.5 %collective-permute-done.20 = f32[32,1001]{1,0:T(8,128)S(1)} collective-permute-done((f32[32,1001]{1,0:T(8,128)S(1)}, f32[32,1001]{1,0:T(8,128)S(1)}, u32[]{:S(2)}, u32[]{:S(2)}) %collective-permute-start.20) | collective-permute-done | bytes 128160 | tf_op jit(solution)/shard_map/ppermute | solution.py:27
  246.1 4.6 %collective-permute-start.23 = (f32[32]{0:T(128)S(1)}, f32[32]{0:T(128)S(1)}, u32[]{:S(2)}, u32[]{:S(2)}) collective-permute-start(f32[32]{0:T(128)S(1)} %max.19), channel_id=1, source_target_pairs={{0,32},{8,40},{16,48},{24,56},{32,0},{40,8},{48,16},{56,24},{64,96... | collective-permute-start | bytes 392 | tf_op jit(solution)/shard_map/ppermute | solution.py:27
  255.0 3.5 %collective-permute-done.24 = f32[32]{0:T(128)S(1)} collective-permute-done((f32[32]{0:T(128)S(1)}, f32[32]{0:T(128)S(1)}, u32[]{:S(2)}, u32[]{:S(2)}) %collective-permute-start.24) | collective-permute-done | bytes 160 | tf_op jit(solution)/shard_map/ppermute | solution.py:27
  260.4 4.4 %collective-permute-done.25 = f32[32]{0:T(128)S(1)} collective-permute-done((f32[32]{0:T(128)S(1)}, f32[32]{0:T(128)S(1)}, u32[]{:S(2)}, u32[]{:S(2)}) %collective-permute-start.25) | collective-permute-done | bytes 160 | tf_op jit(solution)/shard_map/ppermute | solution.py:27
  264.8 4.2 %collective-permute-start.26 = (f32[32]{0:T(128)S(1)}, f32[32]{0:T(128)S(1)}, u32[]{:S(2)}, u32[]{:S(2)}) collective-permute-start(f32[32]{0:T(128)S(1)} %max.22), channel_id=1, source_target_pairs={{0,256},{8,264},{16,272},{24,280},{32,288},{40,296},{48,304},{56,3... | collective-permute-start | bytes 392 | tf_op jit(solution)/shard_map/ppermute | solution.py:27
  269.7 4.4 %collective-permute-done.26 = f32[32]{0:T(128)S(1)} collective-permute-done((f32[32]{0:T(128)S(1)}, f32[32]{0:T(128)S(1)}, u32[]{:S(2)}, u32[]{:S(2)}) %collective-permute-start.26) | collective-permute-done | bytes 160 | tf_op jit(solution)/shard_map/ppermute | solution.py:27
  (109 shorter events, 66.1 us)
Async XLA Ops:
  7.2 193.6 %copy-start = (bf16[896,1000]{0,1:T(8,128)(2,1)S(1)}, bf16[896,1000]{0,1:T(8,128)(2,1)}, u32[]{:S(2)}) copy-start(bf16[896,1000]{0,1:T(8,128)(2,1)} %param.15) | copy-start | bytes 5376004
  7.2 48.7 %copy-start.1 = (bf16[2,256,128]{2,1,0:T(8,128)(2,1)S(1)}, bf16[2,256,128]{2,1,0:T(8,128)(2,1)}, u32[]{:S(2)}) copy-start(bf16[2,256,128]{2,1,0:T(8,128)(2,1)} %param.10) | copy-start | bytes 393220
  7.2 122.3 %all-gather.2.cloned.1.call-start = ((), (), s32[]{:S(2)}) async-start(), calls=%async_computation.1 | async-start | bytes 13045760 | tf_op jit(solution)/shard_map/all_gather | solution.py:154
  7.9 266.7 %reduce-scatter.4.cloned.1.call-start = ((), (), s32[]{:S(2)}) async-start(), calls=%async_computation.2 | async-start | bytes 4128768
  8.0 32.0 %collective-permute-start.4 = (s32[256]{0:T(256)}, s32[256]{0:T(256)S(1)}, u32[]{:S(2)}, u32[]{:S(2)}) collective-permute-start(s32[256]{0:T(256)} %param.11), channel_id=1, source_target_pairs={{0,32},{8,40},{16,48},{24,56},{32,64},{40,72},{48,80},{56,88},{64,... | collective-permute-start | bytes 3080 | tf_op jit(solution)/shard_map/ppermute | solution.py:20
  12.9 29.5 %collective-permute-start.5 = (s32[256]{0:T(256)}, s32[256]{0:T(256)S(1)}, u32[]{:S(2)}, u32[]{:S(2)}) collective-permute-start(s32[256]{0:T(256)} %param.11), channel_id=1, source_target_pairs={{0,24},{8,32},{16,40},{24,48},{32,56},{40,64},{48,72},{56,80},{64,... | collective-permute-start | bytes 3080 | tf_op jit(solution)/shard_map/ppermute | solution.py:20
  14.6 30.0 %collective-permute-start.6 = (s32[256]{0:T(256)}, s32[256]{0:T(256)S(1)}, u32[]{:S(2)}, u32[]{:S(2)}) collective-permute-start(s32[256]{0:T(256)} %param.11), channel_id=1, source_target_pairs={{0,16},{8,24},{16,32},{24,40},{32,48},{40,56},{48,64},{56,72},{64,... | collective-permute-start | bytes 3080 | tf_op jit(solution)/shard_map/ppermute | solution.py:20
  18.2 30.3 %collective-permute-start.7 = (s32[256]{0:T(256)}, s32[256]{0:T(256)S(1)}, u32[]{:S(2)}, u32[]{:S(2)}) collective-permute-start(s32[256]{0:T(256)} %param.11), channel_id=1, source_target_pairs={{0,8},{8,16},{16,24},{24,32},{32,40},{40,48},{48,56},{56,64},{64,7... | collective-permute-start | bytes 3080 | tf_op jit(solution)/shard_map/ppermute | solution.py:20
  23.5 6.8 %collective-permute-start.8 = (s32[1]{0:T(128)}, s32[1]{0:T(128)}, u32[]{:S(2)}, u32[]{:S(2)}) collective-permute-start(s32[1]{0:T(128)} %slice.71), channel_id=1, source_target_pairs={{8,0},{16,8},{24,16},{32,24},{40,32},{48,40},{56,48},{64,56},{72,6... | collective-permute-start | bytes 20 | tf_op jit(solution)/shard_map/ppermute | solution.py:20
  30.3 24.5 %collective-permute-start = (bf16[2,256,128]{2,1,0:T(8,128)(2,1)}, bf16[2,256,128]{2,1,0:T(8,128)(2,1)}, u32[]{:S(2)}, u32[]{:S(2)}) collective-permute-start(bf16[2,256,128]{2,1,0:T(8,128)(2,1)} %param.10), channel_id=1, source_target_pairs={{0,32},{8,40},{16,48},{24,56},{32,64},{40,72},{48,80},{56,88},{64,... | collective-permute-start | bytes 393224 | tf_op jit(solution)/shard_map/ppermute | solution.py:20
  40.0 15.8 %collective-permute-start.1 = (bf16[2,256,128]{2,1,0:T(8,128)(2,1)}, bf16[2,256,128]{2,1,0:T(8,128)(2,1)S(1)}, u32[]{:S(2)}, u32[]{:S(2)}) collective-permute-start(bf16[2,256,128]{2,1,0:T(8,128)(2,1)} %param.10), channel_id=1, source_target_pairs={{0,24},{8,32},{16,40},{24,48},{32,56},{40,64},{48,72},{56,80},{64,... | collective-permute-start | bytes 393224 | tf_op jit(solution)/shard_map/ppermute | solution.py:20
  42.4 13.4 %collective-permute-start.2 = (bf16[2,256,128]{2,1,0:T(8,128)(2,1)}, bf16[2,256,128]{2,1,0:T(8,128)(2,1)S(1)}, u32[]{:S(2)}, u32[]{:S(2)}) collective-permute-start(bf16[2,256,128]{2,1,0:T(8,128)(2,1)} %param.10), channel_id=1, source_target_pairs={{0,16},{8,24},{16,32},{24,40},{32,48},{40,56},{48,64},{56,72},{64,... | collective-permute-start | bytes 393224 | tf_op jit(solution)/shard_map/ppermute | solution.py:20
  44.6 11.2 %collective-permute-start.3 = (bf16[2,256,128]{2,1,0:T(8,128)(2,1)}, bf16[2,256,128]{2,1,0:T(8,128)(2,1)S(1)}, u32[]{:S(2)}, u32[]{:S(2)}) collective-permute-start(bf16[2,256,128]{2,1,0:T(8,128)(2,1)} %param.10), channel_id=1, source_target_pairs={{0,8},{8,16},{16,24},{24,32},{32,40},{40,48},{48,56},{56,64},{64,7... | collective-permute-start | bytes 393224 | tf_op jit(solution)/shard_map/ppermute | solution.py:20
  66.9 3.4 %collective-permute-start.9 = (bf16[32,1792]{1,0:T(8,128)(2,1)S(1)}, bf16[32,1792]{1,0:T(8,128)(2,1)S(1)}, u32[]{:S(2)}, u32[]{:S(2)}) collective-permute-start(bf16[32,1792]{1,0:T(8,128)(2,1)S(1)} %convolution_convert_fusion.2), channel_id=1, source_target_pairs={{0,8},{8,0},{16,24},{24,16},{32,40},{40,32},{48,56},{56,48},{64,72... | collective-permute-start | bytes 344072 | tf_op jit(solution)/shard_map/ppermute | solution.py:27
  70.4 10.1 %collective-permute-start.10 = (bf16[32,1792]{1,0:T(8,128)(2,1)S(1)}, bf16[32,1792]{1,0:T(8,128)(2,1)S(1)}, u32[]{:S(2)}, u32[]{:S(2)}) collective-permute-start(bf16[32,1792]{1,0:T(8,128)(2,1)S(1)} %add.116), channel_id=1, source_target_pairs={{0,16},{8,24},{16,0},{24,8},{32,48},{40,56},{48,32},{56,40},{64,80... | collective-permute-start | bytes 344072 | tf_op jit(solution)/shard_map/ppermute | solution.py:27
  80.5 12.8 %collective-permute-start.11 = (bf16[32,1792]{1,0:T(8,128)(2,1)S(1)}, bf16[32,1792]{1,0:T(8,128)(2,1)S(1)}, u32[]{:S(2)}, u32[]{:S(2)}) collective-permute-start(bf16[32,1792]{1,0:T(8,128)(2,1)S(1)} %add.117), channel_id=1, source_target_pairs={{0,32},{8,40},{16,48},{24,56},{32,0},{40,8},{48,16},{56,24},{64,96... | collective-permute-start | bytes 344072 | tf_op jit(solution)/shard_map/ppermute | solution.py:27
  93.4 10.7 %collective-permute-start.12 = (bf16[32,1792]{1,0:T(8,128)(2,1)S(1)}, bf16[32,1792]{1,0:T(8,128)(2,1)S(1)}, u32[]{:S(2)}, u32[]{:S(2)}) collective-permute-start(bf16[32,1792]{1,0:T(8,128)(2,1)S(1)} %add.118), channel_id=1, source_target_pairs={{0,64},{8,72},{16,80},{24,88},{32,96},{40,104},{48,112},{56,120},{... | collective-permute-start | bytes 344072 | tf_op jit(solution)/shard_map/ppermute | solution.py:27
  104.1 13.5 %collective-permute-start.13 = (bf16[32,1792]{1,0:T(8,128)(2,1)S(1)}, bf16[32,1792]{1,0:T(8,128)(2,1)S(1)}, u32[]{:S(2)}, u32[]{:S(2)}) collective-permute-start(bf16[32,1792]{1,0:T(8,128)(2,1)S(1)} %add.119), channel_id=1, source_target_pairs={{0,128},{8,136},{16,144},{24,152},{32,160},{40,168},{48,176},{56,1... | collective-permute-start | bytes 344072 | tf_op jit(solution)/shard_map/ppermute | solution.py:27
  117.6 11.8 %collective-permute-start.14 = (bf16[32,1792]{1,0:T(8,128)(2,1)S(1)}, bf16[32,1792]{1,0:T(8,128)(2,1)S(1)}, u32[]{:S(2)}, u32[]{:S(2)}) collective-permute-start(bf16[32,1792]{1,0:T(8,128)(2,1)S(1)} %add.120), channel_id=1, source_target_pairs={{0,256},{8,264},{16,272},{24,280},{32,288},{40,296},{48,304},{56,3... | collective-permute-start | bytes 344072 | tf_op jit(solution)/shard_map/ppermute | solution.py:27
  152.7 40.2 %copy-start.3 = (bf16[896]{0:T(1024)(128)(2,1)S(1)}, bf16[896]{0:T(1024)(128)(2,1)}, u32[]{:S(2)}) copy-start(bf16[896]{0:T(1024)(128)(2,1)} %param.14) | copy-start | bytes 5380
  159.0 15.1 %collective-permute-start.15 = (bf16[32,4,896]{2,0,1:T(8,128)(2,1)S(1)}, bf16[32,4,896]{2,0,1:T(8,128)(2,1)S(1)}, u32[]{:S(2)}, u32[]{:S(2)}) collective-permute-start(bf16[32,4,896]{2,0,1:T(8,128)(2,1)S(1)} %copy.50), channel_id=1, source_target_pairs={{0,4},{1,5},{2,6},{3,7},{4,0},{5,1},{6,2},{7,3},{8,12},{9,13},{10,... | collective-permute-start | bytes 688136 | tf_op jit(solution)/shard_map/ppermute | solution.py:46
  174.1 16.8 %collective-permute-start.16 = (f32[32,2,896]{2,0,1:T(8,128)S(1)}, f32[32,2,896]{2,0,1:T(8,128)S(1)}, u32[]{:S(2)}, u32[]{:S(2)}) collective-permute-start(f32[32,2,896]{2,0,1:T(8,128)S(1)} %constant_dynamic-slice_fusion.1), channel_id=1, source_target_pairs={{0,2},{1,3},{2,0},{3,1},{4,6},{5,7},{6,4},{7,5},{8,10},{9,11},{10,... | collective-permute-start | bytes 688136 | tf_op jit(solution)/shard_map/ppermute | solution.py:46
  191.0 9.5 %collective-permute-start.17 = (f32[32,1,896]{2,0,1:T(8,128)S(1)}, f32[32,1,896]{2,0,1:T(8,128)S(1)}, u32[]{:S(2)}, u32[]{:S(2)}) collective-permute-start(f32[32,1,896]{2,0,1:T(8,128)S(1)} %constant_dynamic-slice_fusion), channel_id=1, source_target_pairs={{0,1},{1,0},{2,3},{3,2},{4,5},{5,4},{6,7},{7,6},{8,9},{9,8},{10,11... | collective-permute-start | bytes 344072 | tf_op jit(solution)/shard_map/ppermute | solution.py:46
  201.5 10.5 %collective-permute-start.18 = (f32[32,1001]{1,0:T(8,128)S(1)}, f32[32,1001]{1,0:T(8,128)S(1)}, u32[]{:S(2)}, u32[]{:S(2)}) collective-permute-start(f32[32,1001]{1,0:T(8,128)S(1)} %pad_maximum_fusion), channel_id=1, source_target_pairs={{0,1},{1,0},{2,3},{3,2},{4,5},{5,4},{6,7},{7,6},{8,9},{9,8},{10,11... | collective-permute-start | bytes 384392 | tf_op jit(solution)/shard_map/ppermute | solution.py:27
  212.1 13.3 %collective-permute-start.19 = (f32[32,1001]{1,0:T(8,128)S(1)}, f32[32,1001]{1,0:T(8,128)S(1)}, u32[]{:S(2)}, u32[]{:S(2)}) collective-permute-start(f32[32,1001]{1,0:T(8,128)S(1)} %fusion.61), channel_id=1, source_target_pairs={{0,2},{1,3},{2,0},{3,1},{4,6},{5,7},{6,4},{7,5},{8,10},{9,11},{10,... | collective-permute-start | bytes 384392 | tf_op jit(solution)/shard_map/ppermute | solution.py:27
  225.4 11.4 %collective-permute-start.20 = (f32[32,1001]{1,0:T(8,128)S(1)}, f32[32,1001]{1,0:T(8,128)S(1)}, u32[]{:S(2)}, u32[]{:S(2)}) collective-permute-start(f32[32,1001]{1,0:T(8,128)S(1)} %add.137), channel_id=1, source_target_pairs={{0,4},{1,5},{2,6},{3,7},{4,0},{5,1},{6,2},{7,3},{8,12},{9,13},{10,... | collective-permute-start | bytes 384392 | tf_op jit(solution)/shard_map/ppermute | solution.py:27
  237.7 3.0 %collective-permute-start.21 = (f32[32]{0:T(128)S(1)}, f32[32]{0:T(128)S(1)}, u32[]{:S(2)}, u32[]{:S(2)}) collective-permute-start(f32[32]{0:T(128)S(1)} %fusion.36), channel_id=1, source_target_pairs={{0,8},{8,0},{16,24},{24,16},{32,40},{40,32},{48,56},{56,48},{64,72... | collective-permute-start | bytes 392 | tf_op jit(solution)/shard_map/ppermute | solution.py:27
  240.7 5.4 %collective-permute-start.22 = (f32[32]{0:T(128)S(1)}, f32[32]{0:T(128)S(1)}, u32[]{:S(2)}, u32[]{:S(2)}) collective-permute-start(f32[32]{0:T(128)S(1)} %max.18), channel_id=1, source_target_pairs={{0,16},{8,24},{16,0},{24,8},{32,48},{40,56},{48,32},{56,40},{64,80... | collective-permute-start | bytes 392 | tf_op jit(solution)/shard_map/ppermute | solution.py:27
  246.1 6.9 %collective-permute-start.23 = (f32[32]{0:T(128)S(1)}, f32[32]{0:T(128)S(1)}, u32[]{:S(2)}, u32[]{:S(2)}) collective-permute-start(f32[32]{0:T(128)S(1)} %max.19), channel_id=1, source_target_pairs={{0,32},{8,40},{16,48},{24,56},{32,0},{40,8},{48,16},{56,24},{64,96... | collective-permute-start | bytes 392 | tf_op jit(solution)/shard_map/ppermute | solution.py:27
  253.1 5.4 %collective-permute-start.24 = (f32[32]{0:T(128)S(1)}, f32[32]{0:T(128)S(1)}, u32[]{:S(2)}, u32[]{:S(2)}) collective-permute-start(f32[32]{0:T(128)S(1)} %max.20), channel_id=1, source_target_pairs={{0,64},{8,72},{16,80},{24,88},{32,96},{40,104},{48,112},{56,120},{... | collective-permute-start | bytes 392 | tf_op jit(solution)/shard_map/ppermute | solution.py:27
  258.5 6.3 %collective-permute-start.25 = (f32[32]{0:T(128)S(1)}, f32[32]{0:T(128)S(1)}, u32[]{:S(2)}, u32[]{:S(2)}) collective-permute-start(f32[32]{0:T(128)S(1)} %max.21), channel_id=1, source_target_pairs={{0,128},{8,136},{16,144},{24,152},{32,160},{40,168},{48,176},{56,1... | collective-permute-start | bytes 392 | tf_op jit(solution)/shard_map/ppermute | solution.py:27
  264.8 9.3 %collective-permute-start.26 = (f32[32]{0:T(128)S(1)}, f32[32]{0:T(128)S(1)}, u32[]{:S(2)}, u32[]{:S(2)}) collective-permute-start(f32[32]{0:T(128)S(1)} %max.22), channel_id=1, source_target_pairs={{0,256},{8,264},{16,272},{24,280},{32,288},{40,296},{48,304},{56,3... | collective-permute-start | bytes 392 | tf_op jit(solution)/shard_map/ppermute | solution.py:27
  (1 other events, 2.7 us)
Sparse Core Ops, SparseCore 0:
  11.3 107.2 all-gather.1
  158.7 67.7 reduce-scatter.3

commit v4 on v3

--- a/solution.py
+++ b/solution.py
@@ -30,22 +30,30 @@
     return value
 
 
-def halving_scatter(value, axis):
+def direct_scatter(value, axis):
     count = lax.axis_size(axis)
     index = lax.axis_index(axis)
     rows = value.shape[0]
     held = value.reshape(rows, count, value.shape[1] // count)
-    bit = count // 2
-    while bit >= 1:
-        if bit < count // 2:
-            held = held.astype(jnp.float32)
-        half = held.shape[1] // 2
-        mine = (index // bit) % 2
-        keep = lax.dynamic_slice_in_dim(held, mine * half, half, 1)
-        give = lax.dynamic_slice_in_dim(held, (1 - mine) * half, half, 1)
-        held = keep.astype(jnp.float32) + lax.ppermute(give, axis, [(source, source ^ bit) for source in range(count)]).astype(jnp.float32)
-        bit //= 2
-    return held.reshape(rows, -1)
+    total = lax.dynamic_index_in_dim(held, index, 1, keepdims=False).astype(jnp.float32)
+    for shift in range(1, count):
+        piece = lax.dynamic_index_in_dim(held, (index + shift) % count, 1, keepdims=False)
+        moved = lax.ppermute(piece, axis, [(source, (source + shift) % count) for source in range(count)])
+        total = total + moved.astype(jnp.float32)
+    return total
+
+
+def direct_sum(value, axis):
+    count = lax.axis_size(axis)
+    index = lax.axis_index(axis)
+    pieces = [value]
+    for shift in range(1, count):
+        pieces.append(
+            lax.ppermute(value, axis, [(source, (source + shift) % count) for source in range(count)])
+        )
+    stacked = jnp.stack(pieces)
+    by_source = jnp.take(stacked, (index - jnp.arange(count)) % count, axis=0)
+    return jnp.sum(by_source, axis=0)
 
 
 def rope_tables(positions, width):
@@ -161,14 +169,12 @@
     ).astype(jnp.float32)
     hidden = (residual.astype(jnp.float32) + own_share).astype(jnp.bfloat16)
 
-    end_sum = halving_scatter(end_part, "tp")
+    end_sum = direct_scatter(end_part, "tp")
     last_state = (end_res.astype(jnp.float32) + end_sum).astype(jnp.bfloat16).astype(jnp.float32)
     scaled = (last_state * head_gain.astype(jnp.float32)).astype(jnp.bfloat16)
     square_part = jnp.sum(last_state * last_state, axis=1)
     logit_part = jnp.dot(scaled, vocab_weight, preferred_element_type=jnp.float32)
-    summed = butterfly(
-        jnp.concatenate([logit_part, square_part[:, None]], axis=1), "tp", jnp.add
-    )
+    summed = direct_sum(jnp.concatenate([logit_part, square_part[:, None]], axis=1), "tp")
     raw_logits, square_sum = summed[:, :-1], summed[:, -1]
     mean_square = square_sum / D
     last_norm = jnp.sqrt(mean_square)

time: 287 us -> 294 us (1.024)
  waiting for transfers between devices: 109 us -> 69.8 us
  starting transfers between devices: 97.4 us -> 135 us
  local copies, waits for them, and re-layouts: 17.4 us -> 24.6 us
    ppermute x3 -> x14, starting transfers between devices: 8.88 us -> 51.7 us  [the longest x7 27.1 us: direct_scatter(): lax.ppermute(piece, axis, [(source, (source + shift) % count) for source...]
    ppermute x15 -> x12, waiting for transfers between devices: 75.6 us -> 46.2 us  [butterfly(): lax.ppermute(value, axis, [(source, source ^ stride) for source in range(...]
    ppermute x3 -> x14, waiting for transfers between devices: 32.4 us -> 22.8 us  [the longest x7 16.1 us: direct_sum(): lax.ppermute(value, axis, [(source, (source + shift) % count) for source...]
    ppermute x15 -> x12, starting transfers between devices: 57.5 us -> 51.9 us  [butterfly(): lax.ppermute(value, axis, [(source, source ^ stride) for source in range(...]
    unnamed x23 -> x35, local copies, waits for them, and re-layouts: 12.1 us -> 16.1 us
  transfers between devices with their start and end apart: 29 -> 37, of which waited for: 18 -> 19; matrix products, arithmetic and copies ran while one was open for 11% -> 13% of each run, Pallas kernels for 0% -> 0%
where the time goes in v4:
time: 294 us; the launch traced here: 291 us
  starting transfers between devices  135 us (46%)
  waiting for transfers between devices  69.8 us (24%)
  matrix products  29.6 us (10%)
  local copies, waits for them, and re-layouts  24.6 us (8%)
  other arithmetic  16.8 us (6%)
  between operations  15.5 us (5%)
    ppermute x12, starting transfers between devices, butterfly(): lax.ppermute(value, axis, [(source, source ^ stride) for source in range(...  51.9 us
    ppermute x12, waiting for transfers between devices, butterfly(): lax.ppermute(value, axis, [(source, source ^ stride) for source in range(...  46.2 us
    ppermute x9, starting transfers between devices, from_behind(): lax.ppermute(value, axis, [(source, source + steps) for source in range(i...  31 us
    ppermute x7, starting transfers between devices, direct_scatter(): lax.ppermute(piece, axis, [(source, (source + shift) % count) for source...  27.1 us
    ppermute x7, starting transfers between devices, direct_sum(): lax.ppermute(value, axis, [(source, (source + shift) % count) for source...  24.6 us
    ppermute x7, waiting for transfers between devices, direct_sum(): lax.ppermute(value, axis, [(source, (source + shift) % count) for source...  16.1 us
    unnamed x35, local copies, waits for them, and re-layouts  16.1 us
    dot_general x1, matrix products, local(): jnp.dot(attended, full_weight, preferred_element_type=jnp.float32)  14.7 us
  transfers between devices with their start and end apart: 37, of which 19 were waited for; matrix products, arithmetic and copies ran while one was open for 13% of the time, Pallas kernels for 0%

profile of v4, /device:TPU:56, one launch (start us, length us, event | category | flops | bytes accessed | tf_op | source)
XLA Modules:
  0.0 291.0 jit_solution(9558656254620721252)
XLA Ops:
  8.0 4.9 %collective-permute-start.4 = (s32[256]{0:T(256)}, s32[256]{0:T(256)S(1)}, u32[]{:S(2)}, u32[]{:S(2)}) collective-permute-start(s32[256]{0:T(256)} %param.11), channel_id=1, source_target_pairs={{0,32},{8,40},{16,48},{24,56},{32,64},{40,72},{48,80},{56,88},{64,... | collective-permute-start | bytes 3080 | tf_op jit(solution)/shard_map/ppermute | solution.py:20
  14.6 3.6 %collective-permute-start.6 = (s32[256]{0:T(256)}, s32[256]{0:T(256)S(1)}, u32[]{:S(2)}, u32[]{:S(2)}) collective-permute-start(s32[256]{0:T(256)} %param.11), channel_id=1, source_target_pairs={{0,16},{8,24},{16,32},{24,40},{32,48},{40,56},{48,64},{56,72},{64,... | collective-permute-start | bytes 3080 | tf_op jit(solution)/shard_map/ppermute | solution.py:20
  18.2 4.1 %collective-permute-start.7 = (s32[256]{0:T(256)}, s32[256]{0:T(256)S(1)}, u32[]{:S(2)}, u32[]{:S(2)}) collective-permute-start(s32[256]{0:T(256)} %param.11), channel_id=1, source_target_pairs={{0,8},{8,16},{16,24},{24,32},{32,40},{40,48},{48,56},{56,64},{64,7... | collective-permute-start | bytes 3080 | tf_op jit(solution)/shard_map/ppermute | solution.py:20
  30.2 7.0 %collective-permute-start = (bf16[2,256,128]{2,1,0:T(8,128)(2,1)}, bf16[2,256,128]{2,1,0:T(8,128)(2,1)}, u32[]{:S(2)}, u32[]{:S(2)}) collective-permute-start(bf16[2,256,128]{2,1,0:T(8,128)(2,1)} %param.10), channel_id=1, source_target_pairs={{0,32},{8,40},{16,48},{24,56},{32,64},{40,72},{48,80},{56,88},{64,... | collective-permute-start | bytes 393224 | tf_op jit(solution)/shard_map/ppermute | solution.py:20
  44.5 3.9 %collective-permute-start.3 = (bf16[2,256,128]{2,1,0:T(8,128)(2,1)}, bf16[2,256,128]{2,1,0:T(8,128)(2,1)S(1)}, u32[]{:S(2)}, u32[]{:S(2)}) collective-permute-start(bf16[2,256,128]{2,1,0:T(8,128)(2,1)} %param.10), channel_id=1, source_target_pairs={{0,8},{8,16},{16,24},{24,32},{32,40},{40,48},{48,56},{56,64},{64,7... | collective-permute-start | bytes 393224 | tf_op jit(solution)/shard_map/ppermute | solution.py:20
  70.3 3.5 %collective-permute-start.10 = (bf16[32,1792]{1,0:T(8,128)(2,1)S(1)}, bf16[32,1792]{1,0:T(8,128)(2,1)S(1)}, u32[]{:S(2)}, u32[]{:S(2)}) collective-permute-start(bf16[32,1792]{1,0:T(8,128)(2,1)S(1)} %add.187), channel_id=1, source_target_pairs={{0,16},{8,24},{16,0},{24,8},{32,48},{40,56},{48,32},{56,40},{64,80... | collective-permute-start | bytes 344072 | tf_op jit(solution)/shard_map/ppermute | solution.py:27
  73.8 6.6 %collective-permute-done.10 = bf16[32,1792]{1,0:T(8,128)(2,1)S(1)} collective-permute-done((bf16[32,1792]{1,0:T(8,128)(2,1)S(1)}, bf16[32,1792]{1,0:T(8,128)(2,1)S(1)}, u32[]{:S(2)}, u32[]{:S(2)}) %collective-permute-start.10) | collective-permute-done | bytes 114720 | tf_op jit(solution)/shard_map/ppermute | solution.py:27
  80.5 6.7 %collective-permute-start.11 = (bf16[32,1792]{1,0:T(8,128)(2,1)S(1)}, bf16[32,1792]{1,0:T(8,128)(2,1)S(1)}, u32[]{:S(2)}, u32[]{:S(2)}) collective-permute-start(bf16[32,1792]{1,0:T(8,128)(2,1)S(1)} %add.188), channel_id=1, source_target_pairs={{0,32},{8,40},{16,48},{24,56},{32,0},{40,8},{48,16},{56,24},{64,96... | collective-permute-start | bytes 344072 | tf_op jit(solution)/shard_map/ppermute | solution.py:27
  87.2 6.1 %collective-permute-done.11 = bf16[32,1792]{1,0:T(8,128)(2,1)S(1)} collective-permute-done((bf16[32,1792]{1,0:T(8,128)(2,1)S(1)}, bf16[32,1792]{1,0:T(8,128)(2,1)S(1)}, u32[]{:S(2)}, u32[]{:S(2)}) %collective-permute-start.11) | collective-permute-done | bytes 114720 | tf_op jit(solution)/shard_map/ppermute | solution.py:27
  93.3 5.3 %collective-permute-start.12 = (bf16[32,1792]{1,0:T(8,128)(2,1)S(1)}, bf16[32,1792]{1,0:T(8,128)(2,1)S(1)}, u32[]{:S(2)}, u32[]{:S(2)}) collective-permute-start(bf16[32,1792]{1,0:T(8,128)(2,1)S(1)} %add.189), channel_id=1, source_target_pairs={{0,64},{8,72},{16,80},{24,88},{32,96},{40,104},{48,112},{56,120},{... | collective-permute-start | bytes 344072 | tf_op jit(solution)/shard_map/ppermute | solution.py:27
  98.6 5.4 %collective-permute-done.12 = bf16[32,1792]{1,0:T(8,128)(2,1)S(1)} collective-permute-done((bf16[32,1792]{1,0:T(8,128)(2,1)S(1)}, bf16[32,1792]{1,0:T(8,128)(2,1)S(1)}, u32[]{:S(2)}, u32[]{:S(2)}) %collective-permute-start.12) | collective-permute-done | bytes 114720 | tf_op jit(solution)/shard_map/ppermute | solution.py:27
  104.1 6.1 %collective-permute-start.13 = (bf16[32,1792]{1,0:T(8,128)(2,1)S(1)}, bf16[32,1792]{1,0:T(8,128)(2,1)S(1)}, u32[]{:S(2)}, u32[]{:S(2)}) collective-permute-start(bf16[32,1792]{1,0:T(8,128)(2,1)S(1)} %add.190), channel_id=1, source_target_pairs={{0,128},{8,136},{16,144},{24,152},{32,160},{40,168},{48,176},{56,1... | collective-permute-start | bytes 344072 | tf_op jit(solution)/shard_map/ppermute | solution.py:27
  110.2 7.4 %collective-permute-done.13 = bf16[32,1792]{1,0:T(8,128)(2,1)S(1)} collective-permute-done((bf16[32,1792]{1,0:T(8,128)(2,1)S(1)}, bf16[32,1792]{1,0:T(8,128)(2,1)S(1)}, u32[]{:S(2)}, u32[]{:S(2)}) %collective-permute-start.13) | collective-permute-done | bytes 114720 | tf_op jit(solution)/shard_map/ppermute | solution.py:27
  117.6 5.6 %collective-permute-start.14 = (bf16[32,1792]{1,0:T(8,128)(2,1)S(1)}, bf16[32,1792]{1,0:T(8,128)(2,1)S(1)}, u32[]{:S(2)}, u32[]{:S(2)}) collective-permute-start(bf16[32,1792]{1,0:T(8,128)(2,1)S(1)} %add.191), channel_id=1, source_target_pairs={{0,256},{8,264},{16,272},{24,280},{32,288},{40,296},{48,304},{56,3... | collective-permute-start | bytes 344072 | tf_op jit(solution)/shard_map/ppermute | solution.py:27
  123.2 6.3 %collective-permute-done.14 = bf16[32,1792]{1,0:T(8,128)(2,1)S(1)} collective-permute-done((bf16[32,1792]{1,0:T(8,128)(2,1)S(1)}, bf16[32,1792]{1,0:T(8,128)(2,1)S(1)}, u32[]{:S(2)}, u32[]{:S(2)}) %collective-permute-start.14) | collective-permute-done | bytes 114720 | tf_op jit(solution)/shard_map/ppermute | solution.py:27
  129.5 8.5 %convolution_convert_fusion.1 = bf16[32,7168]{1,0:T(8,128)(2,1)S(1)} fusion(bf16[896,7168]{0,1:T(8,128)(2,1)} %all-gather.2.cloned.1.call-done, bf16[32,1792]{1,0:T(8,128)(2,1)S(1)} %add.192), kind=kOutput, calls=%fused_computation.6 | convolution fusion | flops 411271168 | bytes 13361152 | tf_op jit(solution)/shard_map/dot_general | solution.py:163
  138.0 14.7 %convolution_convert_fusion = bf16[256,7168]{1,0:T(8,128)(2,1)} fusion(bf16[256,896]{0,1:T(8,128)(2,1)S(1)} %bitcast.131, bf16[896,7168]{0,1:T(8,128)(2,1)} %all-gather.2.cloned.1.call-done), kind=kOutput, calls=%fused_computation.3 | convolution fusion | flops 3290169344 | bytes 16973824 | tf_op jit(solution)/shard_map/dot_general | solution.py:166
  152.7 5.9 %copy.58 = bf16[256,7168]{0,1:T(8,128)(2,1)} copy(bf16[256,7168]{1,0:T(8,128)(2,1)} %convolution_convert_fusion) | data formatting | bytes 7340032
  161.9 4.6 %collective-permute-start.16 = (bf16[32,896]{1,0:T(8,128)(2,1)S(1)}, bf16[32,896]{1,0:T(8,128)(2,1)S(1)}, u32[]{:S(2)}, u32[]{:S(2)}) collective-permute-start(bf16[32,896]{1,0:T(8,128)(2,1)S(1)} %bitcast.133), channel_id=1, source_target_pairs={{0,2},{1,3},{2,4},{3,5},{4,6},{5,7},{6,0},{7,1},{8,10},{9,11},{10,... | collective-permute-start | bytes 172040 | tf_op jit(solution)/shard_map/ppermute | solution.py:41
  166.5 5.6 %collective-permute-start.17 = (bf16[32,896]{1,0:T(8,128)(2,1)S(1)}, bf16[32,896]{1,0:T(8,128)(2,1)S(1)}, u32[]{:S(2)}, u32[]{:S(2)}) collective-permute-start(bf16[32,896]{1,0:T(8,128)(2,1)S(1)} %bitcast.132), channel_id=1, source_target_pairs={{0,3},{1,4},{2,5},{3,6},{4,7},{5,0},{6,1},{7,2},{8,11},{9,12},{10,... | collective-permute-start | bytes 172040 | tf_op jit(solution)/shard_map/ppermute | solution.py:41
  175.2 4.7 %collective-permute-start.19 = (bf16[32,896]{1,0:T(8,128)(2,1)S(1)}, bf16[32,896]{1,0:T(8,128)(2,1)S(1)}, u32[]{:S(2)}, u32[]{:S(2)}) collective-permute-start(bf16[32,896]{1,0:T(8,128)(2,1)S(1)} %bitcast.136), channel_id=1, source_target_pairs={{0,5},{1,6},{2,7},{3,0},{4,1},{5,2},{6,3},{7,4},{8,13},{9,14},{10,... | collective-permute-start | bytes 172040 | tf_op jit(solution)/shard_map/ppermute | solution.py:41
  179.9 5.4 %collective-permute-start.20 = (bf16[32,896]{1,0:T(8,128)(2,1)S(1)}, bf16[32,896]{1,0:T(8,128)(2,1)S(1)}, u32[]{:S(2)}, u32[]{:S(2)}) collective-permute-start(bf16[32,896]{1,0:T(8,128)(2,1)S(1)} %bitcast.138), channel_id=1, source_target_pairs={{0,6},{1,7},{2,0},{3,1},{4,2},{5,3},{6,4},{7,5},{8,14},{9,15},{10,... | collective-permute-start | bytes 172040 | tf_op jit(solution)/shard_map/ppermute | solution.py:41
  190.6 3.4 %collective-permute-done.21 = bf16[32,896]{1,0:T(8,128)(2,1)S(1)} collective-permute-done((bf16[32,896]{1,0:T(8,128)(2,1)S(1)}, bf16[32,896]{1,0:T(8,128)(2,1)S(1)}, u32[]{:S(2)}, u32[]{:S(2)}) %collective-permute-start.21) | collective-permute-done | bytes 57376 | tf_op jit(solution)/shard_map/ppermute | solution.py:41
  200.2 4.9 %collective-permute-start.24 = (f32[32,1001]{1,0:T(8,128)S(1)}, f32[32,1001]{1,0:T(8,128)S(1)}, u32[]{:S(2)}, u32[]{:S(2)}) collective-permute-start(f32[32,1001]{1,0:T(8,128)S(1)} %get-tuple-element.27), channel_id=1, source_target_pairs={{0,3},{1,4},{2,5},{3,6},{4,7},{5,0},{6,1},{7,2},{8,11},{9,12},{10,... | collective-permute-start | bytes 384392 | tf_op jit(solution)/shard_map/ppermute | solution.py:52
  205.1 4.8 %collective-permute-start.25 = (f32[32,1001]{1,0:T(8,128)S(1)}, f32[32,1001]{1,0:T(8,128)S(1)}, u32[]{:S(2)}, u32[]{:S(2)}) collective-permute-start(f32[32,1001]{1,0:T(8,128)S(1)} %get-tuple-element.27), channel_id=1, source_target_pairs={{0,4},{1,5},{2,6},{3,7},{4,0},{5,1},{6,2},{7,3},{8,12},{9,13},{10,... | collective-permute-start | bytes 384392 | tf_op jit(solution)/shard_map/ppermute | solution.py:52
  209.9 3.5 %collective-permute-start.26 = (f32[32,1001]{1,0:T(8,128)S(1)}, f32[32,1001]{1,0:T(8,128)S(1)}, u32[]{:S(2)}, u32[]{:S(2)}) collective-permute-start(f32[32,1001]{1,0:T(8,128)S(1)} %get-tuple-element.27), channel_id=1, source_target_pairs={{0,5},{1,6},{2,7},{3,0},{4,1},{5,2},{6,3},{7,4},{8,13},{9,14},{10,... | collective-permute-start | bytes 384392 | tf_op jit(solution)/shard_map/ppermute | solution.py:52
  213.4 4.7 %collective-permute-start.27 = (f32[32,1001]{1,0:T(8,128)S(1)}, f32[32,1001]{1,0:T(8,128)S(1)}, u32[]{:S(2)}, u32[]{:S(2)}) collective-permute-start(f32[32,1001]{1,0:T(8,128)S(1)} %get-tuple-element.27), channel_id=1, source_target_pairs={{0,6},{1,7},{2,0},{3,1},{4,2},{5,3},{6,4},{7,5},{8,14},{9,15},{10,... | collective-permute-start | bytes 384392 | tf_op jit(solution)/shard_map/ppermute | solution.py:52
  229.8 8.2 %collective-permute-done.27 = f32[32,1001]{1,0:T(8,128)S(1)} collective-permute-done((f32[32,1001]{1,0:T(8,128)S(1)}, f32[32,1001]{1,0:T(8,128)S(1)}, u32[]{:S(2)}, u32[]{:S(2)}) %collective-permute-start.27) | collective-permute-done | bytes 128160 | tf_op jit(solution)/shard_map/ppermute | solution.py:52
  252.4 5.1 %collective-permute-start.31 = (f32[32]{0:T(128)S(1)}, f32[32]{0:T(128)S(1)}, u32[]{:S(2)}, u32[]{:S(2)}) collective-permute-start(f32[32]{0:T(128)S(1)} %max.19), channel_id=1, source_target_pairs={{0,32},{8,40},{16,48},{24,56},{32,0},{40,8},{48,16},{56,24},{64,96... | collective-permute-start | bytes 392 | tf_op jit(solution)/shard_map/ppermute | solution.py:27
  261.3 3.5 %collective-permute-done.32 = f32[32]{0:T(128)S(1)} collective-permute-done((f32[32]{0:T(128)S(1)}, f32[32]{0:T(128)S(1)}, u32[]{:S(2)}, u32[]{:S(2)}) %collective-permute-start.32) | collective-permute-done | bytes 160 | tf_op jit(solution)/shard_map/ppermute | solution.py:27
  264.8 4.3 %collective-permute-start.33 = (f32[32]{0:T(128)S(1)}, f32[32]{0:T(128)S(1)}, u32[]{:S(2)}, u32[]{:S(2)}) collective-permute-start(f32[32]{0:T(128)S(1)} %max.21), channel_id=1, source_target_pairs={{0,128},{8,136},{16,144},{24,152},{32,160},{40,168},{48,176},{56,1... | collective-permute-start | bytes 392 | tf_op jit(solution)/shard_map/ppermute | solution.py:27
  271.1 6.2 %collective-permute-start.34 = (f32[32]{0:T(128)S(1)}, f32[32]{0:T(128)S(1)}, u32[]{:S(2)}, u32[]{:S(2)}) collective-permute-start(f32[32]{0:T(128)S(1)} %max.22), channel_id=1, source_target_pairs={{0,256},{8,264},{16,272},{24,280},{32,288},{40,296},{48,304},{56,3... | collective-permute-start | bytes 392 | tf_op jit(solution)/shard_map/ppermute | solution.py:27
  (136 shorter events, 94.9 us)
Async XLA Ops:
  7.2 122.3 %all-gather.2.cloned.1.call-start = ((), (), s32[]{:S(2)}) async-start(), calls=%async_computation.1 | async-start | bytes 13045760 | tf_op jit(solution)/shard_map/all_gather | solution.py:162
  7.9 273.0 %reduce-scatter.4.cloned.1.call-start = ((), (), s32[]{:S(2)}) async-start(), calls=%async_computation.2 | async-start | bytes 4128768
  8.0 31.9 %collective-permute-start.4 = (s32[256]{0:T(256)}, s32[256]{0:T(256)S(1)}, u32[]{:S(2)}, u32[]{:S(2)}) collective-permute-start(s32[256]{0:T(256)} %param.11), channel_id=1, source_target_pairs={{0,32},{8,40},{16,48},{24,56},{32,64},{40,72},{48,80},{56,88},{64,... | collective-permute-start | bytes 3080 | tf_op jit(solution)/shard_map/ppermute | solution.py:20
  12.9 29.4 %collective-permute-start.5 = (s32[256]{0:T(256)}, s32[256]{0:T(256)S(1)}, u32[]{:S(2)}, u32[]{:S(2)}) collective-permute-start(s32[256]{0:T(256)} %param.11), channel_id=1, source_target_pairs={{0,24},{8,32},{16,40},{24,48},{32,56},{40,64},{48,72},{56,80},{64,... | collective-permute-start | bytes 3080 | tf_op jit(solution)/shard_map/ppermute | solution.py:20
  14.6 29.9 %collective-permute-start.6 = (s32[256]{0:T(256)}, s32[256]{0:T(256)S(1)}, u32[]{:S(2)}, u32[]{:S(2)}) collective-permute-start(s32[256]{0:T(256)} %param.11), channel_id=1, source_target_pairs={{0,16},{8,24},{16,32},{24,40},{32,48},{40,56},{48,64},{56,72},{64,... | collective-permute-start | bytes 3080 | tf_op jit(solution)/shard_map/ppermute | solution.py:20
  18.2 30.2 %collective-permute-start.7 = (s32[256]{0:T(256)}, s32[256]{0:T(256)S(1)}, u32[]{:S(2)}, u32[]{:S(2)}) collective-permute-start(s32[256]{0:T(256)} %param.11), channel_id=1, source_target_pairs={{0,8},{8,16},{16,24},{24,32},{32,40},{40,48},{48,56},{56,64},{64,7... | collective-permute-start | bytes 3080 | tf_op jit(solution)/shard_map/ppermute | solution.py:20
  23.5 6.7 %collective-permute-start.8 = (s32[1]{0:T(128)}, s32[1]{0:T(128)}, u32[]{:S(2)}, u32[]{:S(2)}) collective-permute-start(s32[1]{0:T(128)} %slice.71), channel_id=1, source_target_pairs={{8,0},{16,8},{24,16},{32,24},{40,32},{48,40},{56,48},{64,56},{72,6... | collective-permute-start | bytes 20 | tf_op jit(solution)/shard_map/ppermute | solution.py:20
  30.2 24.5 %collective-permute-start = (bf16[2,256,128]{2,1,0:T(8,128)(2,1)}, bf16[2,256,128]{2,1,0:T(8,128)(2,1)}, u32[]{:S(2)}, u32[]{:S(2)}) collective-permute-start(bf16[2,256,128]{2,1,0:T(8,128)(2,1)} %param.10), channel_id=1, source_target_pairs={{0,32},{8,40},{16,48},{24,56},{32,64},{40,72},{48,80},{56,88},{64,... | collective-permute-start | bytes 393224 | tf_op jit(solution)/shard_map/ppermute | solution.py:20
  39.9 15.8 %collective-permute-start.1 = (bf16[2,256,128]{2,1,0:T(8,128)(2,1)}, bf16[2,256,128]{2,1,0:T(8,128)(2,1)S(1)}, u32[]{:S(2)}, u32[]{:S(2)}) collective-permute-start(bf16[2,256,128]{2,1,0:T(8,128)(2,1)} %param.10), channel_id=1, source_target_pairs={{0,24},{8,32},{16,40},{24,48},{32,56},{40,64},{48,72},{56,80},{64,... | collective-permute-start | bytes 393224 | tf_op jit(solution)/shard_map/ppermute | solution.py:20
  42.3 13.4 %collective-permute-start.2 = (bf16[2,256,128]{2,1,0:T(8,128)(2,1)}, bf16[2,256,128]{2,1,0:T(8,128)(2,1)S(1)}, u32[]{:S(2)}, u32[]{:S(2)}) collective-permute-start(bf16[2,256,128]{2,1,0:T(8,128)(2,1)} %param.10), channel_id=1, source_target_pairs={{0,16},{8,24},{16,32},{24,40},{32,48},{40,56},{48,64},{56,72},{64,... | collective-permute-start | bytes 393224 | tf_op jit(solution)/shard_map/ppermute | solution.py:20
  44.5 11.2 %collective-permute-start.3 = (bf16[2,256,128]{2,1,0:T(8,128)(2,1)}, bf16[2,256,128]{2,1,0:T(8,128)(2,1)S(1)}, u32[]{:S(2)}, u32[]{:S(2)}) collective-permute-start(bf16[2,256,128]{2,1,0:T(8,128)(2,1)} %param.10), channel_id=1, source_target_pairs={{0,8},{8,16},{16,24},{24,32},{32,40},{40,48},{48,56},{56,64},{64,7... | collective-permute-start | bytes 393224 | tf_op jit(solution)/shard_map/ppermute | solution.py:20
  70.3 10.1 %collective-permute-start.10 = (bf16[32,1792]{1,0:T(8,128)(2,1)S(1)}, bf16[32,1792]{1,0:T(8,128)(2,1)S(1)}, u32[]{:S(2)}, u32[]{:S(2)}) collective-permute-start(bf16[32,1792]{1,0:T(8,128)(2,1)S(1)} %add.187), channel_id=1, source_target_pairs={{0,16},{8,24},{16,0},{24,8},{32,48},{40,56},{48,32},{56,40},{64,80... | collective-permute-start | bytes 344072 | tf_op jit(solution)/shard_map/ppermute | solution.py:27
  80.5 12.8 %collective-permute-start.11 = (bf16[32,1792]{1,0:T(8,128)(2,1)S(1)}, bf16[32,1792]{1,0:T(8,128)(2,1)S(1)}, u32[]{:S(2)}, u32[]{:S(2)}) collective-permute-start(bf16[32,1792]{1,0:T(8,128)(2,1)S(1)} %add.188), channel_id=1, source_target_pairs={{0,32},{8,40},{16,48},{24,56},{32,0},{40,8},{48,16},{56,24},{64,96... | collective-permute-start | bytes 344072 | tf_op jit(solution)/shard_map/ppermute | solution.py:27
  93.3 10.8 %collective-permute-start.12 = (bf16[32,1792]{1,0:T(8,128)(2,1)S(1)}, bf16[32,1792]{1,0:T(8,128)(2,1)S(1)}, u32[]{:S(2)}, u32[]{:S(2)}) collective-permute-start(bf16[32,1792]{1,0:T(8,128)(2,1)S(1)} %add.189), channel_id=1, source_target_pairs={{0,64},{8,72},{16,80},{24,88},{32,96},{40,104},{48,112},{56,120},{... | collective-permute-start | bytes 344072 | tf_op jit(solution)/shard_map/ppermute | solution.py:27
  104.1 13.5 %collective-permute-start.13 = (bf16[32,1792]{1,0:T(8,128)(2,1)S(1)}, bf16[32,1792]{1,0:T(8,128)(2,1)S(1)}, u32[]{:S(2)}, u32[]{:S(2)}) collective-permute-start(bf16[32,1792]{1,0:T(8,128)(2,1)S(1)} %add.190), channel_id=1, source_target_pairs={{0,128},{8,136},{16,144},{24,152},{32,160},{40,168},{48,176},{56,1... | collective-permute-start | bytes 344072 | tf_op jit(solution)/shard_map/ppermute | solution.py:27
  117.6 11.8 %collective-permute-start.14 = (bf16[32,1792]{1,0:T(8,128)(2,1)S(1)}, bf16[32,1792]{1,0:T(8,128)(2,1)S(1)}, u32[]{:S(2)}, u32[]{:S(2)}) collective-permute-start(bf16[32,1792]{1,0:T(8,128)(2,1)S(1)} %add.191), channel_id=1, source_target_pairs={{0,256},{8,264},{16,272},{24,280},{32,288},{40,296},{48,304},{56,3... | collective-permute-start | bytes 344072 | tf_op jit(solution)/shard_map/ppermute | solution.py:27
  159.9 20.0 %collective-permute-start.15 = (bf16[32,896]{1,0:T(8,128)(2,1)S(1)}, bf16[32,896]{1,0:T(8,128)(2,1)S(1)}, u32[]{:S(2)}, u32[]{:S(2)}) collective-permute-start(bf16[32,896]{1,0:T(8,128)(2,1)S(1)} %bitcast.135), channel_id=1, source_target_pairs={{0,1},{1,2},{2,3},{3,4},{4,5},{5,6},{6,7},{7,0},{8,9},{9,10},{10,1... | collective-permute-start | bytes 172040 | tf_op jit(solution)/shard_map/ppermute | solution.py:41
  161.9 23.4 %collective-permute-start.16 = (bf16[32,896]{1,0:T(8,128)(2,1)S(1)}, bf16[32,896]{1,0:T(8,128)(2,1)S(1)}, u32[]{:S(2)}, u32[]{:S(2)}) collective-permute-start(bf16[32,896]{1,0:T(8,128)(2,1)S(1)} %bitcast.133), channel_id=1, source_target_pairs={{0,2},{1,3},{2,4},{3,5},{4,6},{5,7},{6,0},{7,1},{8,10},{9,11},{10,... | collective-permute-start | bytes 172040 | tf_op jit(solution)/shard_map/ppermute | solution.py:41
  166.5 20.8 %collective-permute-start.17 = (bf16[32,896]{1,0:T(8,128)(2,1)S(1)}, bf16[32,896]{1,0:T(8,128)(2,1)S(1)}, u32[]{:S(2)}, u32[]{:S(2)}) collective-permute-start(bf16[32,896]{1,0:T(8,128)(2,1)S(1)} %bitcast.132), channel_id=1, source_target_pairs={{0,3},{1,4},{2,5},{3,6},{4,7},{5,0},{6,1},{7,2},{8,11},{9,12},{10,... | collective-permute-start | bytes 172040 | tf_op jit(solution)/shard_map/ppermute | solution.py:41
  172.2 15.1 %collective-permute-start.18 = (bf16[32,896]{1,0:T(8,128)(2,1)S(1)}, bf16[32,896]{1,0:T(8,128)(2,1)S(1)}, u32[]{:S(2)}, u32[]{:S(2)}) collective-permute-start(bf16[32,896]{1,0:T(8,128)(2,1)S(1)} %bitcast.134), channel_id=1, source_target_pairs={{0,4},{1,5},{2,6},{3,7},{4,0},{5,1},{6,2},{7,3},{8,12},{9,13},{10,... | collective-permute-start | bytes 172040 | tf_op jit(solution)/shard_map/ppermute | solution.py:41
  175.2 12.3 %collective-permute-start.19 = (bf16[32,896]{1,0:T(8,128)(2,1)S(1)}, bf16[32,896]{1,0:T(8,128)(2,1)S(1)}, u32[]{:S(2)}, u32[]{:S(2)}) collective-permute-start(bf16[32,896]{1,0:T(8,128)(2,1)S(1)} %bitcast.136), channel_id=1, source_target_pairs={{0,5},{1,6},{2,7},{3,0},{4,1},{5,2},{6,3},{7,4},{8,13},{9,14},{10,... | collective-permute-start | bytes 172040 | tf_op jit(solution)/shard_map/ppermute | solution.py:41
  179.9 10.6 %collective-permute-start.20 = (bf16[32,896]{1,0:T(8,128)(2,1)S(1)}, bf16[32,896]{1,0:T(8,128)(2,1)S(1)}, u32[]{:S(2)}, u32[]{:S(2)}) collective-permute-start(bf16[32,896]{1,0:T(8,128)(2,1)S(1)} %bitcast.138), channel_id=1, source_target_pairs={{0,6},{1,7},{2,0},{3,1},{4,2},{5,3},{6,4},{7,5},{8,14},{9,15},{10,... | collective-permute-start | bytes 172040 | tf_op jit(solution)/shard_map/ppermute | solution.py:41
  185.3 8.7 %collective-permute-start.21 = (bf16[32,896]{1,0:T(8,128)(2,1)S(1)}, bf16[32,896]{1,0:T(8,128)(2,1)S(1)}, u32[]{:S(2)}, u32[]{:S(2)}) collective-permute-start(bf16[32,896]{1,0:T(8,128)(2,1)S(1)} %bitcast.137), channel_id=1, source_target_pairs={{0,7},{1,0},{2,1},{3,2},{4,3},{5,4},{6,5},{7,6},{8,15},{9,8},{10,9... | collective-permute-start | bytes 172040 | tf_op jit(solution)/shard_map/ppermute | solution.py:41
  195.6 17.8 %collective-permute-start.22 = (f32[32,1001]{1,0:T(8,128)S(1)}, f32[32,1001]{1,0:T(8,128)S(1)}, u32[]{:S(2)}, u32[]{:S(2)}) collective-permute-start(f32[32,1001]{1,0:T(8,128)S(1)} %get-tuple-element.27), channel_id=1, source_target_pairs={{0,1},{1,2},{2,3},{3,4},{4,5},{5,6},{6,7},{7,0},{8,9},{9,10},{10,1... | collective-permute-start | bytes 384392 | tf_op jit(solution)/shard_map/ppermute | solution.py:52
  198.2 20.6 %collective-permute-start.23 = (f32[32,1001]{1,0:T(8,128)S(1)}, f32[32,1001]{1,0:T(8,128)S(1)}, u32[]{:S(2)}, u32[]{:S(2)}) collective-permute-start(f32[32,1001]{1,0:T(8,128)S(1)} %get-tuple-element.27), channel_id=1, source_target_pairs={{0,2},{1,3},{2,4},{3,5},{4,6},{5,7},{6,0},{7,1},{8,10},{9,11},{10,... | collective-permute-start | bytes 384392 | tf_op jit(solution)/shard_map/ppermute | solution.py:52
  200.2 24.5 %collective-permute-start.24 = (f32[32,1001]{1,0:T(8,128)S(1)}, f32[32,1001]{1,0:T(8,128)S(1)}, u32[]{:S(2)}, u32[]{:S(2)}) collective-permute-start(f32[32,1001]{1,0:T(8,128)S(1)} %get-tuple-element.27), channel_id=1, source_target_pairs={{0,3},{1,4},{2,5},{3,6},{4,7},{5,0},{6,1},{7,2},{8,11},{9,12},{10,... | collective-permute-start | bytes 384392 | tf_op jit(solution)/shard_map/ppermute | solution.py:52
  205.1 20.2 %collective-permute-start.25 = (f32[32,1001]{1,0:T(8,128)S(1)}, f32[32,1001]{1,0:T(8,128)S(1)}, u32[]{:S(2)}, u32[]{:S(2)}) collective-permute-start(f32[32,1001]{1,0:T(8,128)S(1)} %get-tuple-element.27), channel_id=1, source_target_pairs={{0,4},{1,5},{2,6},{3,7},{4,0},{5,1},{6,2},{7,3},{8,12},{9,13},{10,... | collective-permute-start | bytes 384392 | tf_op jit(solution)/shard_map/ppermute | solution.py:52
  209.9 19.3 %collective-permute-start.26 = (f32[32,1001]{1,0:T(8,128)S(1)}, f32[32,1001]{1,0:T(8,128)S(1)}, u32[]{:S(2)}, u32[]{:S(2)}) collective-permute-start(f32[32,1001]{1,0:T(8,128)S(1)} %get-tuple-element.27), channel_id=1, source_target_pairs={{0,5},{1,6},{2,7},{3,0},{4,1},{5,2},{6,3},{7,4},{8,13},{9,14},{10,... | collective-permute-start | bytes 384392 | tf_op jit(solution)/shard_map/ppermute | solution.py:52
  213.4 24.6 %collective-permute-start.27 = (f32[32,1001]{1,0:T(8,128)S(1)}, f32[32,1001]{1,0:T(8,128)S(1)}, u32[]{:S(2)}, u32[]{:S(2)}) collective-permute-start(f32[32,1001]{1,0:T(8,128)S(1)} %get-tuple-element.27), channel_id=1, source_target_pairs={{0,6},{1,7},{2,0},{3,1},{4,2},{5,3},{6,4},{7,5},{8,14},{9,15},{10,... | collective-permute-start | bytes 384392 | tf_op jit(solution)/shard_map/ppermute | solution.py:52
  218.8 21.6 %collective-permute-start.28 = (f32[32,1001]{1,0:T(8,128)S(1)}, f32[32,1001]{1,0:T(8,128)S(1)}, u32[]{:S(2)}, u32[]{:S(2)}) collective-permute-start(f32[32,1001]{1,0:T(8,128)S(1)} %get-tuple-element.27), channel_id=1, source_target_pairs={{0,7},{1,0},{2,1},{3,2},{4,3},{5,4},{6,5},{7,6},{8,15},{9,8},{10,9... | collective-permute-start | bytes 384392 | tf_op jit(solution)/shard_map/ppermute | solution.py:52
  252.4 6.9 %collective-permute-start.31 = (f32[32]{0:T(128)S(1)}, f32[32]{0:T(128)S(1)}, u32[]{:S(2)}, u32[]{:S(2)}) collective-permute-start(f32[32]{0:T(128)S(1)} %max.19), channel_id=1, source_target_pairs={{0,32},{8,40},{16,48},{24,56},{32,0},{40,8},{48,16},{56,24},{64,96... | collective-permute-start | bytes 392 | tf_op jit(solution)/shard_map/ppermute | solution.py:27
  271.1 9.3 %collective-permute-start.34 = (f32[32]{0:T(128)S(1)}, f32[32]{0:T(128)S(1)}, u32[]{:S(2)}, u32[]{:S(2)}) collective-permute-start(f32[32]{0:T(128)S(1)} %max.22), channel_id=1, source_target_pairs={{0,256},{8,264},{16,272},{24,280},{32,288},{40,296},{48,304},{56,3... | collective-permute-start | bytes 392 | tf_op jit(solution)/shard_map/ppermute | solution.py:27
  (9 other events, 275.8 us)
Sparse Core Ops, SparseCore 0:
  11.3 107.2 all-gather.1
  158.8 82.3 reduce-scatter.3

commit v5 on v3

--- a/solution.py
+++ b/solution.py
@@ -80,11 +80,17 @@
     request_ids = jnp.arange(requests, dtype=jnp.int32)
 
     own_kv = key_value
+    width = own_kv.shape[2]
+    seg_rows = -(-tok_rows // width)
+    seg_flat = jnp.pad(segment, (0, seg_rows * width - tok_rows)).astype(jnp.bfloat16)
+    packed = jnp.concatenate(
+        [own_kv.reshape(2 * tok_rows, width), seg_flat.reshape(seg_rows, width)], axis=0
+    )
     parts_kv, parts_seg = [], []
     for back in range(REACH, 0, -1):
-        kv_b, seg_b = from_behind((own_kv, segment), "req", back)
-        parts_kv.append(kv_b)
-        parts_seg.append(seg_b)
+        got = from_behind(packed, "req", back)
+        parts_kv.append(got[: 2 * tok_rows].reshape(own_kv.shape))
+        parts_seg.append(got[2 * tok_rows :].reshape(-1)[:tok_rows].astype(jnp.int32))
     parts_kv.append(own_kv)
     parts_seg.append(segment)
     next_first = from_behind(segment[:1], "req", -1)
@@ -152,13 +158,11 @@
     end_att, end_res = end_rows[:, : attended.shape[1]], end_rows[:, attended.shape[1] :]
 
     full_weight = lax.all_gather(out_weight, "req", axis=1, tiled=True)
-    end_part = jnp.dot(end_att, full_weight, preferred_element_type=jnp.float32)
-    end_part = end_part.astype(jnp.bfloat16)
-    attended, end_part = lax.optimization_barrier((attended, end_part))
-    projected = jnp.dot(attended, full_weight, preferred_element_type=jnp.float32)
-    own_share = lax.psum_scatter(
-        projected.astype(jnp.bfloat16), "tp", scatter_dimension=1, tiled=True
-    ).astype(jnp.float32)
+    both = jnp.dot(
+        jnp.concatenate([attended, end_att], axis=0), full_weight, preferred_element_type=jnp.float32
+    ).astype(jnp.bfloat16)
+    projected, end_part = both[:tok_rows], both[tok_rows:]
+    own_share = lax.psum_scatter(projected, "tp", scatter_dimension=1, tiled=True).astype(jnp.float32)
     hidden = (residual.astype(jnp.float32) + own_share).astype(jnp.bfloat16)
 
     end_sum = halving_scatter(end_part, "tp")

time: 287 us -> 278 us (0.969)
  matrix products: 29.6 us -> 18.7 us
  local copies, waits for them, and re-layouts: 17.4 us -> 23.8 us
  starting transfers between devices: 97.4 us -> 91.8 us
  other arithmetic: 16.1 us -> 19.8 us
  waiting for transfers between devices: 109 us -> 106 us
    ppermute x9 -> x5, starting transfers between devices: 31 us -> 16.9 us  [from_behind(): lax.ppermute(value, axis, [(source, source + steps) for source in range(i...]
    dot_general x2 -> x1, matrix products: 23.2 us -> 12.3 us  [local(): jnp.dot(jnp.concatenate([attended, end_att], axis=0), full_weight, prefer...]
    slice x0 -> x9, local copies, waits for them, and re-layouts: none -> 7.96 us  [the longest x3 4.12 us: local(): projected, end_part = (both[:tok_rows], both[tok_rows:])]
    ppermute x3, starting transfers between devices: 8.88 us -> 16.4 us  [halving_scatter(): lax.ppermute(give, axis, [(source, source ^ bit) for source in range(coun...]
    ppermute x15, waiting for transfers between devices: 75.6 us -> 69.4 us  [butterfly(): lax.ppermute(value, axis, [(source, source ^ stride) for source in range(...]
    unnamed x23 -> x19, local copies, waits for them, and re-layouts: 12.1 us -> 11.2 us
  transfers between devices with their start and end apart: 29 -> 25, of which waited for: 18 -> 19; matrix products, arithmetic and copies ran while one was open for 11% -> 13% of each run, Pallas kernels for 0% -> 0%
where the time goes in v5:
time: 278 us; the launch traced here: 275 us
  waiting for transfers between devices  106 us (38%)
  starting transfers between devices  91.8 us (33%)
  local copies, waits for them, and re-layouts  23.8 us (9%)
  other arithmetic  19.8 us (7%)
  matrix products  18.7 us (7%)
  between operations  15.3 us (6%)
    ppermute x15, waiting for transfers between devices, butterfly(): lax.ppermute(value, axis, [(source, source ^ stride) for source in range(...  69.4 us
    ppermute x15, starting transfers between devices, butterfly(): lax.ppermute(value, axis, [(source, source ^ stride) for source in range(...  58.4 us
    ppermute x3, waiting for transfers between devices, halving_scatter(): lax.ppermute(give, axis, [(source, source ^ bit) for source in range(coun...  33.8 us
    ppermute x5, starting transfers between devices, from_behind(): lax.ppermute(value, axis, [(source, source + steps) for source in range(i...  16.9 us
    ppermute x3, starting transfers between devices, halving_scatter(): lax.ppermute(give, axis, [(source, source ^ bit) for source in range(coun...  16.4 us
    dot_general x1, matrix products, local(): jnp.dot(jnp.concatenate([attended, end_att], axis=0), full_weight, prefer...  12.3 us
    unnamed x19, local copies, waits for them, and re-layouts  11.2 us
  transfers between devices with their start and end apart: 25, of which 19 were waited for; matrix products, arithmetic and copies ran while one was open for 13% of the time, Pallas kernels for 0%

profile of v5, /device:TPU:56, one launch (start us, length us, event | category | flops | bytes accessed | tf_op | source)
XLA Modules:
  0.0 275.5 jit_solution(7949531745178937012)
XLA Ops:
  9.6 5.6 %collective-permute-start = (bf16[514,128]{1,0:T(8,128)(2,1)S(1)}, bf16[514,128]{1,0:T(8,128)(2,1)}, u32[]{:S(2)}, u32[]{:S(2)}) collective-permute-start(bf16[514,128]{1,0:T(8,128)(2,1)S(1)} %pad_maximum_fusion), channel_id=1, source_target_pairs={{0,32},{8,40},{16,48},{24,56},{32,64},{40,72},{48,80},{56,88},{64,... | collective-permute-start | bytes 394760 | tf_op jit(solution)/shard_map/ppermute | solution.py:20
  17.5 3.6 %collective-permute-start.2 = (bf16[514,128]{1,0:T(8,128)(2,1)S(1)}, bf16[514,128]{1,0:T(8,128)(2,1)}, u32[]{:S(2)}, u32[]{:S(2)}) collective-permute-start(bf16[514,128]{1,0:T(8,128)(2,1)S(1)} %pad_maximum_fusion), channel_id=1, source_target_pairs={{0,16},{8,24},{16,32},{24,40},{32,48},{40,56},{48,64},{56,72},{64,... | collective-permute-start | bytes 394760 | tf_op jit(solution)/shard_map/ppermute | solution.py:20
  21.1 4.1 %collective-permute-start.3 = (bf16[514,128]{1,0:T(8,128)(2,1)S(1)}, bf16[514,128]{1,0:T(8,128)(2,1)}, u32[]{:S(2)}, u32[]{:S(2)}) collective-permute-start(bf16[514,128]{1,0:T(8,128)(2,1)S(1)} %pad_maximum_fusion), channel_id=1, source_target_pairs={{0,8},{8,16},{16,24},{24,32},{32,40},{40,48},{48,56},{56,64},{64,7... | collective-permute-start | bytes 394760 | tf_op jit(solution)/shard_map/ppermute | solution.py:20
  47.6 3.0 %fusion.27 = (bf16[1280,1,64]{2,0,1:T(8,128)(2,1)S(1)}, bf16[1280,1,64]{2,0,1:T(8,128)(2,1)S(1)}) fusion(f32[1280,1,128]{2,0,1:T(8,128)S(1)} %fusion.36, f32[64]{0:T(128)S(1)} %negate_power_fusion, f32[1280]{0:T(1024)S(1)} %convert_subtract_fusion), kind=kLoop, calls=%fused_computation.31 | loop fusion | flops 737280 | bytes 988416 | tf_op jit(solution)/shard_map/convert.15
  58.5 3.0 %collective-permute-start.5 = (bf16[32,1792]{1,0:T(8,128)(2,1)S(1)}, bf16[32,1792]{1,0:T(8,128)(2,1)S(1)}, u32[]{:S(2)}, u32[]{:S(2)}) collective-permute-start(bf16[32,1792]{1,0:T(8,128)(2,1)S(1)} %convolution_convert_fusion.1), channel_id=1, source_target_pairs={{0,8},{8,0},{16,24},{24,16},{32,40},{40,32},{48,56},{56,48},{64,72... | collective-permute-start | bytes 344072 | tf_op jit(solution)/shard_map/ppermute | solution.py:27
  65.3 4.5 %collective-permute-done.6 = bf16[32,1792]{1,0:T(8,128)(2,1)S(1)} collective-permute-done((bf16[32,1792]{1,0:T(8,128)(2,1)S(1)}, bf16[32,1792]{1,0:T(8,128)(2,1)S(1)}, u32[]{:S(2)}, u32[]{:S(2)}) %collective-permute-start.6) | collective-permute-done | bytes 114720 | tf_op jit(solution)/shard_map/ppermute | solution.py:27
  69.9 4.0 %collective-permute-start.7 = (bf16[32,1792]{1,0:T(8,128)(2,1)S(1)}, bf16[32,1792]{1,0:T(8,128)(2,1)S(1)}, u32[]{:S(2)}, u32[]{:S(2)}) collective-permute-start(bf16[32,1792]{1,0:T(8,128)(2,1)S(1)} %add.117), channel_id=1, source_target_pairs={{0,32},{8,40},{16,48},{24,56},{32,0},{40,8},{48,16},{56,24},{64,96... | collective-permute-start | bytes 344072 | tf_op jit(solution)/shard_map/ppermute | solution.py:27
  73.9 7.2 %collective-permute-done.7 = bf16[32,1792]{1,0:T(8,128)(2,1)S(1)} collective-permute-done((bf16[32,1792]{1,0:T(8,128)(2,1)S(1)}, bf16[32,1792]{1,0:T(8,128)(2,1)S(1)}, u32[]{:S(2)}, u32[]{:S(2)}) %collective-permute-start.7) | collective-permute-done | bytes 114720 | tf_op jit(solution)/shard_map/ppermute | solution.py:27
  81.1 4.9 %collective-permute-start.8 = (bf16[32,1792]{1,0:T(8,128)(2,1)S(1)}, bf16[32,1792]{1,0:T(8,128)(2,1)S(1)}, u32[]{:S(2)}, u32[]{:S(2)}) collective-permute-start(bf16[32,1792]{1,0:T(8,128)(2,1)S(1)} %add.118), channel_id=1, source_target_pairs={{0,64},{8,72},{16,80},{24,88},{32,96},{40,104},{48,112},{56,120},{... | collective-permute-start | bytes 344072 | tf_op jit(solution)/shard_map/ppermute | solution.py:27
  86.1 4.6 %collective-permute-done.8 = bf16[32,1792]{1,0:T(8,128)(2,1)S(1)} collective-permute-done((bf16[32,1792]{1,0:T(8,128)(2,1)S(1)}, bf16[32,1792]{1,0:T(8,128)(2,1)S(1)}, u32[]{:S(2)}, u32[]{:S(2)}) %collective-permute-start.8) | collective-permute-done | bytes 114720 | tf_op jit(solution)/shard_map/ppermute | solution.py:27
  90.7 8.8 %collective-permute-start.9 = (bf16[32,1792]{1,0:T(8,128)(2,1)S(1)}, bf16[32,1792]{1,0:T(8,128)(2,1)S(1)}, u32[]{:S(2)}, u32[]{:S(2)}) collective-permute-start(bf16[32,1792]{1,0:T(8,128)(2,1)S(1)} %add.119), channel_id=1, source_target_pairs={{0,128},{8,136},{16,144},{24,152},{32,160},{40,168},{48,176},{56,1... | collective-permute-start | bytes 344072 | tf_op jit(solution)/shard_map/ppermute | solution.py:27
  99.5 6.6 %collective-permute-done.9 = bf16[32,1792]{1,0:T(8,128)(2,1)S(1)} collective-permute-done((bf16[32,1792]{1,0:T(8,128)(2,1)S(1)}, bf16[32,1792]{1,0:T(8,128)(2,1)S(1)}, u32[]{:S(2)}, u32[]{:S(2)}) %collective-permute-start.9) | collective-permute-done | bytes 114720 | tf_op jit(solution)/shard_map/ppermute | solution.py:27
  106.2 8.1 %collective-permute-start.10 = (bf16[32,1792]{1,0:T(8,128)(2,1)S(1)}, bf16[32,1792]{1,0:T(8,128)(2,1)S(1)}, u32[]{:S(2)}, u32[]{:S(2)}) collective-permute-start(bf16[32,1792]{1,0:T(8,128)(2,1)S(1)} %add.120), channel_id=1, source_target_pairs={{0,256},{8,264},{16,272},{24,280},{32,288},{40,296},{48,304},{56,3... | collective-permute-start | bytes 344072 | tf_op jit(solution)/shard_map/ppermute | solution.py:27
  114.2 5.7 %collective-permute-done.10 = bf16[32,1792]{1,0:T(8,128)(2,1)S(1)} collective-permute-done((bf16[32,1792]{1,0:T(8,128)(2,1)S(1)}, bf16[32,1792]{1,0:T(8,128)(2,1)S(1)}, u32[]{:S(2)}, u32[]{:S(2)}) %collective-permute-start.10) | collective-permute-done | bytes 114720 | tf_op jit(solution)/shard_map/ppermute | solution.py:27
  122.3 12.3 %convolution_convert_fusion = bf16[288,7168]{1,0:T(8,128)(2,1)} fusion(bf16[896,7168]{0,1:T(8,128)(2,1)} %all-gather.2.cloned.1.call-done, bf16[32,896]{0,1:T(8,128)(2,1)S(1)} %copy.42, bf16[256,896]{0,1:T(8,128)(2,1)S(1)} %bitcast.121), kind=kOutput, calls=%fused_computation | convolution fusion | flops 3702472704 | bytes 17489920 | tf_op jit(solution)/shard_map/dot_general | solution.py:161
  134.6 4.1 %slice.135 = bf16[256,7168]{1,0:T(8,128)(2,1)} slice(bf16[288,7168]{1,0:T(8,128)(2,1)} %convolution_convert_fusion), slice={[0:256], [0:7168]} | slice | bytes 7340032 | tf_op jit(solution)/shard_map/slice | solution.py:164
  138.7 6.0 %copy.49 = bf16[256,7168]{0,1:T(8,128)(2,1)} copy(bf16[256,7168]{1,0:T(8,128)(2,1)} %slice.135) | data formatting | bytes 7340032
  145.1 5.9 %collective-permute-start.11 = (bf16[32,4,896]{2,0,1:T(8,128)(2,1)S(1)}, bf16[32,4,896]{2,0,1:T(8,128)(2,1)S(1)}, u32[]{:S(2)}, u32[]{:S(2)}) collective-permute-start(bf16[32,4,896]{2,0,1:T(8,128)(2,1)S(1)} %copy.54), channel_id=1, source_target_pairs={{0,4},{1,5},{2,6},{3,7},{4,0},{5,1},{6,2},{7,3},{8,12},{9,13},{10,... | collective-permute-start | bytes 688136 | tf_op jit(solution)/shard_map/ppermute | solution.py:46
  151.0 11.9 %collective-permute-done.11 = bf16[32,4,896]{2,0,1:T(8,128)(2,1)S(1)} collective-permute-done((bf16[32,4,896]{2,0,1:T(8,128)(2,1)S(1)}, bf16[32,4,896]{2,0,1:T(8,128)(2,1)S(1)}, u32[]{:S(2)}, u32[]{:S(2)}) %collective-permute-start.11) | collective-permute-done | bytes 229408 | tf_op jit(solution)/shard_map/ppermute | solution.py:46
  163.0 7.7 %collective-permute-start.12 = (f32[32,2,896]{2,0,1:T(8,128)S(1)}, f32[32,2,896]{2,0,1:T(8,128)S(1)}, u32[]{:S(2)}, u32[]{:S(2)}) collective-permute-start(f32[32,2,896]{2,0,1:T(8,128)S(1)} %constant_dynamic-slice_fusion.1), channel_id=1, source_target_pairs={{0,2},{1,3},{2,0},{3,1},{4,6},{5,7},{6,4},{7,5},{8,10},{9,11},{10,... | collective-permute-start | bytes 688136 | tf_op jit(solution)/shard_map/ppermute | solution.py:46
  170.8 15.0 %collective-permute-done.12 = f32[32,2,896]{2,0,1:T(8,128)S(1)} collective-permute-done((f32[32,2,896]{2,0,1:T(8,128)S(1)}, f32[32,2,896]{2,0,1:T(8,128)S(1)}, u32[]{:S(2)}, u32[]{:S(2)}) %collective-permute-start.12) | collective-permute-done | bytes 229408 | tf_op jit(solution)/shard_map/ppermute | solution.py:46
  188.6 6.9 %collective-permute-done.13 = f32[32,1,896]{2,0,1:T(8,128)S(1)} collective-permute-done((f32[32,1,896]{2,0,1:T(8,128)S(1)}, f32[32,1,896]{2,0,1:T(8,128)S(1)}, u32[]{:S(2)}, u32[]{:S(2)}) %collective-permute-start.13) | collective-permute-done | bytes 114720 | tf_op jit(solution)/shard_map/ppermute | solution.py:46
  198.9 8.2 %collective-permute-done.14 = f32[32,1001]{1,0:T(8,128)S(1)} collective-permute-done((f32[32,1001]{1,0:T(8,128)S(1)}, f32[32,1001]{1,0:T(8,128)S(1)}, u32[]{:S(2)}, u32[]{:S(2)}) %collective-permute-start.14) | collective-permute-done | bytes 128160 | tf_op jit(solution)/shard_map/ppermute | solution.py:27
  209.7 6.3 %collective-permute-done.15 = f32[32,1001]{1,0:T(8,128)S(1)} collective-permute-done((f32[32,1001]{1,0:T(8,128)S(1)}, f32[32,1001]{1,0:T(8,128)S(1)}, u32[]{:S(2)}, u32[]{:S(2)}) %collective-permute-start.15) | collective-permute-done | bytes 128160 | tf_op jit(solution)/shard_map/ppermute | solution.py:27
  216.1 3.3 %collective-permute-start.16 = (f32[32,1001]{1,0:T(8,128)S(1)}, f32[32,1001]{1,0:T(8,128)S(1)}, u32[]{:S(2)}, u32[]{:S(2)}) collective-permute-start(f32[32,1001]{1,0:T(8,128)S(1)} %add.137), channel_id=1, source_target_pairs={{0,4},{1,5},{2,6},{3,7},{4,0},{5,1},{6,2},{7,3},{8,12},{9,13},{10,... | collective-permute-start | bytes 384392 | tf_op jit(solution)/shard_map/ppermute | solution.py:27
  219.4 8.2 %collective-permute-done.16 = f32[32,1001]{1,0:T(8,128)S(1)} collective-permute-done((f32[32,1001]{1,0:T(8,128)S(1)}, f32[32,1001]{1,0:T(8,128)S(1)}, u32[]{:S(2)}, u32[]{:S(2)}) %collective-permute-start.16) | collective-permute-done | bytes 128160 | tf_op jit(solution)/shard_map/ppermute | solution.py:27
  236.9 3.5 %collective-permute-start.19 = (f32[32]{0:T(128)S(1)}, f32[32]{0:T(128)S(1)}, u32[]{:S(2)}, u32[]{:S(2)}) collective-permute-start(f32[32]{0:T(128)S(1)} %max.19), channel_id=1, source_target_pairs={{0,32},{8,40},{16,48},{24,56},{32,0},{40,8},{48,16},{56,24},{64,96... | collective-permute-start | bytes 392 | tf_op jit(solution)/shard_map/ppermute | solution.py:27
  240.4 3.4 %collective-permute-done.19 = f32[32]{0:T(128)S(1)} collective-permute-done((f32[32]{0:T(128)S(1)}, f32[32]{0:T(128)S(1)}, u32[]{:S(2)}, u32[]{:S(2)}) %collective-permute-start.19) | collective-permute-done | bytes 160 | tf_op jit(solution)/shard_map/ppermute | solution.py:27
  243.9 3.1 %collective-permute-start.20 = (f32[32]{0:T(128)S(1)}, f32[32]{0:T(128)S(1)}, u32[]{:S(2)}, u32[]{:S(2)}) collective-permute-start(f32[32]{0:T(128)S(1)} %max.20), channel_id=1, source_target_pairs={{0,64},{8,72},{16,80},{24,88},{32,96},{40,104},{48,112},{56,120},{... | collective-permute-start | bytes 392 | tf_op jit(solution)/shard_map/ppermute | solution.py:27
  251.8 3.8 %collective-permute-done.21 = f32[32]{0:T(128)S(1)} collective-permute-done((f32[32]{0:T(128)S(1)}, f32[32]{0:T(128)S(1)}, u32[]{:S(2)}, u32[]{:S(2)}) %collective-permute-start.21) | collective-permute-done | bytes 160 | tf_op jit(solution)/shard_map/ppermute | solution.py:27
  255.6 5.1 %collective-permute-start.22 = (f32[32]{0:T(128)S(1)}, f32[32]{0:T(128)S(1)}, u32[]{:S(2)}, u32[]{:S(2)}) collective-permute-start(f32[32]{0:T(128)S(1)} %max.22), channel_id=1, source_target_pairs={{0,256},{8,264},{16,272},{24,280},{32,288},{40,296},{48,304},{56,3... | collective-permute-start | bytes 392 | tf_op jit(solution)/shard_map/ppermute | solution.py:27
  261.5 3.5 %collective-permute-done.22 = f32[32]{0:T(128)S(1)} collective-permute-done((f32[32]{0:T(128)S(1)}, f32[32]{0:T(128)S(1)}, u32[]{:S(2)}, u32[]{:S(2)}) %collective-permute-start.22) | collective-permute-done | bytes 160 | tf_op jit(solution)/shard_map/ppermute | solution.py:27
  (110 shorter events, 68.0 us)
Async XLA Ops:
  7.2 188.6 %copy-start = (bf16[896,1000]{0,1:T(8,128)(2,1)S(1)}, bf16[896,1000]{0,1:T(8,128)(2,1)}, u32[]{:S(2)}) copy-start(bf16[896,1000]{0,1:T(8,128)(2,1)} %param.15) | copy-start | bytes 5376004
  7.2 35.2 %copy-start.2 = (s32[256]{0:T(256)S(1)}, s32[256]{0:T(256)}, u32[]{:S(2)}) copy-start(s32[256]{0:T(256)} %param.11) | copy-start | bytes 3076
  7.2 35.3 %copy-start.1 = (bf16[2,256,128]{2,1,0:T(8,128)(2,1)S(1)}, bf16[2,256,128]{2,1,0:T(8,128)(2,1)}, u32[]{:S(2)}) copy-start(bf16[2,256,128]{2,1,0:T(8,128)(2,1)} %param.10) | copy-start | bytes 393220
  7.2 115.1 %all-gather.2.cloned.1.call-start = ((), (), s32[]{:S(2)}) async-start(), calls=%async_computation.1 | async-start | bytes 13045760 | tf_op jit(solution)/shard_map/all_gather | solution.py:160
  7.9 257.5 %reduce-scatter.4.cloned.1.call-start = ((), (), s32[]{:S(2)}) async-start(), calls=%async_computation.2 | async-start | bytes 4128768
  9.6 26.4 %collective-permute-start = (bf16[514,128]{1,0:T(8,128)(2,1)S(1)}, bf16[514,128]{1,0:T(8,128)(2,1)}, u32[]{:S(2)}, u32[]{:S(2)}) collective-permute-start(bf16[514,128]{1,0:T(8,128)(2,1)S(1)} %pad_maximum_fusion), channel_id=1, source_target_pairs={{0,32},{8,40},{16,48},{24,56},{32,64},{40,72},{48,80},{56,88},{64,... | collective-permute-start | bytes 394760 | tf_op jit(solution)/shard_map/ppermute | solution.py:20
  15.2 21.7 %collective-permute-start.1 = (bf16[514,128]{1,0:T(8,128)(2,1)S(1)}, bf16[514,128]{1,0:T(8,128)(2,1)}, u32[]{:S(2)}, u32[]{:S(2)}) collective-permute-start(bf16[514,128]{1,0:T(8,128)(2,1)S(1)} %pad_maximum_fusion), channel_id=1, source_target_pairs={{0,24},{8,32},{16,40},{24,48},{32,56},{40,64},{48,72},{56,80},{64,... | collective-permute-start | bytes 394760 | tf_op jit(solution)/shard_map/ppermute | solution.py:20
  17.5 20.4 %collective-permute-start.2 = (bf16[514,128]{1,0:T(8,128)(2,1)S(1)}, bf16[514,128]{1,0:T(8,128)(2,1)}, u32[]{:S(2)}, u32[]{:S(2)}) collective-permute-start(bf16[514,128]{1,0:T(8,128)(2,1)S(1)} %pad_maximum_fusion), channel_id=1, source_target_pairs={{0,16},{8,24},{16,32},{24,40},{32,48},{40,56},{48,64},{56,72},{64,... | collective-permute-start | bytes 394760 | tf_op jit(solution)/shard_map/ppermute | solution.py:20
  21.1 17.7 %collective-permute-start.3 = (bf16[514,128]{1,0:T(8,128)(2,1)S(1)}, bf16[514,128]{1,0:T(8,128)(2,1)}, u32[]{:S(2)}, u32[]{:S(2)}) collective-permute-start(bf16[514,128]{1,0:T(8,128)(2,1)S(1)} %pad_maximum_fusion), channel_id=1, source_target_pairs={{0,8},{8,16},{16,24},{24,32},{32,40},{40,48},{48,56},{56,64},{64,7... | collective-permute-start | bytes 394760 | tf_op jit(solution)/shard_map/ppermute | solution.py:20
  26.4 6.8 %collective-permute-start.4 = (s32[1]{0:T(128)}, s32[1]{0:T(128)}, u32[]{:S(2)}, u32[]{:S(2)}) collective-permute-start(s32[1]{0:T(128)} %slice.109), channel_id=1, source_target_pairs={{8,0},{16,8},{24,16},{32,24},{40,32},{48,40},{56,48},{64,56},{72,6... | collective-permute-start | bytes 20 | tf_op jit(solution)/shard_map/ppermute | solution.py:20
  58.5 4.0 %collective-permute-start.5 = (bf16[32,1792]{1,0:T(8,128)(2,1)S(1)}, bf16[32,1792]{1,0:T(8,128)(2,1)S(1)}, u32[]{:S(2)}, u32[]{:S(2)}) collective-permute-start(bf16[32,1792]{1,0:T(8,128)(2,1)S(1)} %convolution_convert_fusion.1), channel_id=1, source_target_pairs={{0,8},{8,0},{16,24},{24,16},{32,40},{40,32},{48,56},{56,48},{64,72... | collective-permute-start | bytes 344072 | tf_op jit(solution)/shard_map/ppermute | solution.py:27
  62.5 7.3 %collective-permute-start.6 = (bf16[32,1792]{1,0:T(8,128)(2,1)S(1)}, bf16[32,1792]{1,0:T(8,128)(2,1)S(1)}, u32[]{:S(2)}, u32[]{:S(2)}) collective-permute-start(bf16[32,1792]{1,0:T(8,128)(2,1)S(1)} %add.116), channel_id=1, source_target_pairs={{0,16},{8,24},{16,0},{24,8},{32,48},{40,56},{48,32},{56,40},{64,80... | collective-permute-start | bytes 344072 | tf_op jit(solution)/shard_map/ppermute | solution.py:27
  69.9 11.2 %collective-permute-start.7 = (bf16[32,1792]{1,0:T(8,128)(2,1)S(1)}, bf16[32,1792]{1,0:T(8,128)(2,1)S(1)}, u32[]{:S(2)}, u32[]{:S(2)}) collective-permute-start(bf16[32,1792]{1,0:T(8,128)(2,1)S(1)} %add.117), channel_id=1, source_target_pairs={{0,32},{8,40},{16,48},{24,56},{32,0},{40,8},{48,16},{56,24},{64,96... | collective-permute-start | bytes 344072 | tf_op jit(solution)/shard_map/ppermute | solution.py:27
  81.1 9.6 %collective-permute-start.8 = (bf16[32,1792]{1,0:T(8,128)(2,1)S(1)}, bf16[32,1792]{1,0:T(8,128)(2,1)S(1)}, u32[]{:S(2)}, u32[]{:S(2)}) collective-permute-start(bf16[32,1792]{1,0:T(8,128)(2,1)S(1)} %add.118), channel_id=1, source_target_pairs={{0,64},{8,72},{16,80},{24,88},{32,96},{40,104},{48,112},{56,120},{... | collective-permute-start | bytes 344072 | tf_op jit(solution)/shard_map/ppermute | solution.py:27
  90.7 15.4 %collective-permute-start.9 = (bf16[32,1792]{1,0:T(8,128)(2,1)S(1)}, bf16[32,1792]{1,0:T(8,128)(2,1)S(1)}, u32[]{:S(2)}, u32[]{:S(2)}) collective-permute-start(bf16[32,1792]{1,0:T(8,128)(2,1)S(1)} %add.119), channel_id=1, source_target_pairs={{0,128},{8,136},{16,144},{24,152},{32,160},{40,168},{48,176},{56,1... | collective-permute-start | bytes 344072 | tf_op jit(solution)/shard_map/ppermute | solution.py:27
  106.2 13.8 %collective-permute-start.10 = (bf16[32,1792]{1,0:T(8,128)(2,1)S(1)}, bf16[32,1792]{1,0:T(8,128)(2,1)S(1)}, u32[]{:S(2)}, u32[]{:S(2)}) collective-permute-start(bf16[32,1792]{1,0:T(8,128)(2,1)S(1)} %add.120), channel_id=1, source_target_pairs={{0,256},{8,264},{16,272},{24,280},{32,288},{40,296},{48,304},{56,3... | collective-permute-start | bytes 344072 | tf_op jit(solution)/shard_map/ppermute | solution.py:27
  138.7 6.0 %slice-start = ((bf16[288,7168]{1,0:T(8,128)(2,1)}), bf16[32,7168]{1,0:T(8,128)(2,1)S(1)}, s32[]{:S(2)}) async-start(bf16[288,7168]{1,0:T(8,128)(2,1)} %convolution_convert_fusion), calls=%async_computation.3 | async-start | bytes 917504 | tf_op jit(solution)/shard_map/slice | solution.py:164
  138.7 49.9 %copy-start.3 = (bf16[896]{0:T(1024)(128)(2,1)S(1)}, bf16[896]{0:T(1024)(128)(2,1)}, u32[]{:S(2)}) copy-start(bf16[896]{0:T(1024)(128)(2,1)} %param.14) | copy-start | bytes 5380
  145.1 17.9 %collective-permute-start.11 = (bf16[32,4,896]{2,0,1:T(8,128)(2,1)S(1)}, bf16[32,4,896]{2,0,1:T(8,128)(2,1)S(1)}, u32[]{:S(2)}, u32[]{:S(2)}) collective-permute-start(bf16[32,4,896]{2,0,1:T(8,128)(2,1)S(1)} %copy.54), channel_id=1, source_target_pairs={{0,4},{1,5},{2,6},{3,7},{4,0},{5,1},{6,2},{7,3},{8,12},{9,13},{10,... | collective-permute-start | bytes 688136 | tf_op jit(solution)/shard_map/ppermute | solution.py:46
  163.0 22.7 %collective-permute-start.12 = (f32[32,2,896]{2,0,1:T(8,128)S(1)}, f32[32,2,896]{2,0,1:T(8,128)S(1)}, u32[]{:S(2)}, u32[]{:S(2)}) collective-permute-start(f32[32,2,896]{2,0,1:T(8,128)S(1)} %constant_dynamic-slice_fusion.1), channel_id=1, source_target_pairs={{0,2},{1,3},{2,0},{3,1},{4,6},{5,7},{6,4},{7,5},{8,10},{9,11},{10,... | collective-permute-start | bytes 688136 | tf_op jit(solution)/shard_map/ppermute | solution.py:46
  185.8 9.8 %collective-permute-start.13 = (f32[32,1,896]{2,0,1:T(8,128)S(1)}, f32[32,1,896]{2,0,1:T(8,128)S(1)}, u32[]{:S(2)}, u32[]{:S(2)}) collective-permute-start(f32[32,1,896]{2,0,1:T(8,128)S(1)} %constant_dynamic-slice_fusion), channel_id=1, source_target_pairs={{0,1},{1,0},{2,3},{3,2},{4,5},{5,4},{6,7},{7,6},{8,9},{9,8},{10,11... | collective-permute-start | bytes 344072 | tf_op jit(solution)/shard_map/ppermute | solution.py:46
  196.5 10.5 %collective-permute-start.14 = (f32[32,1001]{1,0:T(8,128)S(1)}, f32[32,1001]{1,0:T(8,128)S(1)}, u32[]{:S(2)}, u32[]{:S(2)}) collective-permute-start(f32[32,1001]{1,0:T(8,128)S(1)} %pad_maximum_fusion.1), channel_id=1, source_target_pairs={{0,1},{1,0},{2,3},{3,2},{4,5},{5,4},{6,7},{7,6},{8,9},{9,8},{10,11... | collective-permute-start | bytes 384392 | tf_op jit(solution)/shard_map/ppermute | solution.py:27
  207.1 8.9 %collective-permute-start.15 = (f32[32,1001]{1,0:T(8,128)S(1)}, f32[32,1001]{1,0:T(8,128)S(1)}, u32[]{:S(2)}, u32[]{:S(2)}) collective-permute-start(f32[32,1001]{1,0:T(8,128)S(1)} %fusion.62), channel_id=1, source_target_pairs={{0,2},{1,3},{2,0},{3,1},{4,6},{5,7},{6,4},{7,5},{8,10},{9,11},{10,... | collective-permute-start | bytes 384392 | tf_op jit(solution)/shard_map/ppermute | solution.py:27
  216.1 11.5 %collective-permute-start.16 = (f32[32,1001]{1,0:T(8,128)S(1)}, f32[32,1001]{1,0:T(8,128)S(1)}, u32[]{:S(2)}, u32[]{:S(2)}) collective-permute-start(f32[32,1001]{1,0:T(8,128)S(1)} %add.137), channel_id=1, source_target_pairs={{0,4},{1,5},{2,6},{3,7},{4,0},{5,1},{6,2},{7,3},{8,12},{9,13},{10,... | collective-permute-start | bytes 384392 | tf_op jit(solution)/shard_map/ppermute | solution.py:27
  228.5 3.0 %collective-permute-start.17 = (f32[32]{0:T(128)S(1)}, f32[32]{0:T(128)S(1)}, u32[]{:S(2)}, u32[]{:S(2)}) collective-permute-start(f32[32]{0:T(128)S(1)} %fusion.39), channel_id=1, source_target_pairs={{0,8},{8,0},{16,24},{24,16},{32,40},{40,32},{48,56},{56,48},{64,72... | collective-permute-start | bytes 392 | tf_op jit(solution)/shard_map/ppermute | solution.py:27
  231.5 5.4 %collective-permute-start.18 = (f32[32]{0:T(128)S(1)}, f32[32]{0:T(128)S(1)}, u32[]{:S(2)}, u32[]{:S(2)}) collective-permute-start(f32[32]{0:T(128)S(1)} %max.18), channel_id=1, source_target_pairs={{0,16},{8,24},{16,0},{24,8},{32,48},{40,56},{48,32},{56,40},{64,80... | collective-permute-start | bytes 392 | tf_op jit(solution)/shard_map/ppermute | solution.py:27
  236.9 6.9 %collective-permute-start.19 = (f32[32]{0:T(128)S(1)}, f32[32]{0:T(128)S(1)}, u32[]{:S(2)}, u32[]{:S(2)}) collective-permute-start(f32[32]{0:T(128)S(1)} %max.19), channel_id=1, source_target_pairs={{0,32},{8,40},{16,48},{24,56},{32,0},{40,8},{48,16},{56,24},{64,96... | collective-permute-start | bytes 392 | tf_op jit(solution)/shard_map/ppermute | solution.py:27
  243.9 5.4 %collective-permute-start.20 = (f32[32]{0:T(128)S(1)}, f32[32]{0:T(128)S(1)}, u32[]{:S(2)}, u32[]{:S(2)}) collective-permute-start(f32[32]{0:T(128)S(1)} %max.20), channel_id=1, source_target_pairs={{0,64},{8,72},{16,80},{24,88},{32,96},{40,104},{48,112},{56,120},{... | collective-permute-start | bytes 392 | tf_op jit(solution)/shard_map/ppermute | solution.py:27
  249.3 6.3 %collective-permute-start.21 = (f32[32]{0:T(128)S(1)}, f32[32]{0:T(128)S(1)}, u32[]{:S(2)}, u32[]{:S(2)}) collective-permute-start(f32[32]{0:T(128)S(1)} %max.21), channel_id=1, source_target_pairs={{0,128},{8,136},{16,144},{24,152},{32,160},{40,168},{48,176},{56,1... | collective-permute-start | bytes 392 | tf_op jit(solution)/shard_map/ppermute | solution.py:27
  255.6 9.3 %collective-permute-start.22 = (f32[32]{0:T(128)S(1)}, f32[32]{0:T(128)S(1)}, u32[]{:S(2)}, u32[]{:S(2)}) collective-permute-start(f32[32]{0:T(128)S(1)} %max.22), channel_id=1, source_target_pairs={{0,256},{8,264},{16,272},{24,280},{32,288},{40,296},{48,304},{56,3... | collective-permute-start | bytes 392 | tf_op jit(solution)/shard_map/ppermute | solution.py:27
Sparse Core Ops, SparseCore 0:
  11.3 110.9 all-gather.1
  144.8 66.1 reduce-scatter.3

commit v6 on v5

--- a/solution.py
+++ b/solution.py
@@ -162,10 +162,10 @@
         jnp.concatenate([attended, end_att], axis=0), full_weight, preferred_element_type=jnp.float32
     ).astype(jnp.bfloat16)
     projected, end_part = both[:tok_rows], both[tok_rows:]
+    end_sum = halving_scatter(end_part, "tp")
+    projected, end_sum = lax.optimization_barrier((projected, end_sum))
     own_share = lax.psum_scatter(projected, "tp", scatter_dimension=1, tiled=True).astype(jnp.float32)
     hidden = (residual.astype(jnp.float32) + own_share).astype(jnp.bfloat16)
-
-    end_sum = halving_scatter(end_part, "tp")
     last_state = (end_res.astype(jnp.float32) + end_sum).astype(jnp.bfloat16).astype(jnp.float32)
     scaled = (last_state * head_gain.astype(jnp.float32)).astype(jnp.bfloat16)
     square_part = jnp.sum(last_state * last_state, axis=1)

time: 278 us -> 266 us (0.957)
  waiting for transfers between devices: 106 us -> 88.4 us
  starting transfers between devices: 91.8 us -> 97.2 us
    ppermute x3, waiting for transfers between devices: 33.8 us -> 22.2 us  [halving_scatter(): lax.ppermute(give, axis, [(source, source ^ bit) for source in range(coun...]
    ppermute x15, starting transfers between devices: 58.4 us -> 67.3 us  [butterfly(): lax.ppermute(value, axis, [(source, source ^ stride) for source in range(...]
    ppermute x15, waiting for transfers between devices: 69.4 us -> 63.2 us  [butterfly(): lax.ppermute(value, axis, [(source, source ^ stride) for source in range(...]
    ppermute x3, starting transfers between devices: 16.4 us -> 12.9 us  [halving_scatter(): lax.ppermute(give, axis, [(source, source ^ bit) for source in range(coun...]
    unnamed x19 -> x21, local copies, waits for them, and re-layouts: 11.2 us -> 11.2 us
  transfers between devices with their start and end apart: 25 -> 25, of which waited for: 19 -> 19; matrix products, arithmetic and copies ran while one was open for 13% -> 15% of each run, Pallas kernels for 0% -> 0%
where the time goes in v6:
time: 266 us; the launch traced here: 263 us
  starting transfers between devices  97.2 us (37%)
  waiting for transfers between devices  88.4 us (33%)
  local copies, waits for them, and re-layouts  24.8 us (9%)
  other arithmetic  18.7 us (7%)
  matrix products  18.7 us (7%)
  between operations  15.3 us (6%)
    ppermute x15, starting transfers between devices, butterfly(): lax.ppermute(value, axis, [(source, source ^ stride) for source in range(...  67.3 us
    ppermute x15, waiting for transfers between devices, butterfly(): lax.ppermute(value, axis, [(source, source ^ stride) for source in range(...  63.2 us
    ppermute x3, waiting for transfers between devices, halving_scatter(): lax.ppermute(give, axis, [(source, source ^ bit) for source in range(coun...  22.2 us
    ppermute x5, starting transfers between devices, from_behind(): lax.ppermute(value, axis, [(source, source + steps) for source in range(i...  16.9 us
    ppermute x3, starting transfers between devices, halving_scatter(): lax.ppermute(give, axis, [(source, source ^ bit) for source in range(coun...  12.9 us
    dot_general x1, matrix products, local(): jnp.dot(jnp.concatenate([attended, end_att], axis=0), full_weight, prefer...  12.3 us
    unnamed x21, local copies, waits for them, and re-layouts  11.2 us
  transfers between devices with their start and end apart: 25, of which 19 were waited for; matrix products, arithmetic and copies ran while one was open for 15% of the time, Pallas kernels for 0%

profile of v6, /device:TPU:56, one launch (start us, length us, event | category | flops | bytes accessed | tf_op | source)
XLA Modules:
  0.0 263.1 jit_solution(16759483726243464018)
XLA Ops:
  9.6 5.6 %collective-permute-start = (bf16[514,128]{1,0:T(8,128)(2,1)S(1)}, bf16[514,128]{1,0:T(8,128)(2,1)}, u32[]{:S(2)}, u32[]{:S(2)}) collective-permute-start(bf16[514,128]{1,0:T(8,128)(2,1)S(1)} %pad_maximum_fusion), channel_id=1, source_target_pairs={{0,32},{8,40},{16,48},{24,56},{32,64},{40,72},{48,80},{56,88},{64,... | collective-permute-start | bytes 394760 | tf_op jit(solution)/shard_map/ppermute | solution.py:20
  17.5 3.6 %collective-permute-start.2 = (bf16[514,128]{1,0:T(8,128)(2,1)S(1)}, bf16[514,128]{1,0:T(8,128)(2,1)}, u32[]{:S(2)}, u32[]{:S(2)}) collective-permute-start(bf16[514,128]{1,0:T(8,128)(2,1)S(1)} %pad_maximum_fusion), channel_id=1, source_target_pairs={{0,16},{8,24},{16,32},{24,40},{32,48},{40,56},{48,64},{56,72},{64,... | collective-permute-start | bytes 394760 | tf_op jit(solution)/shard_map/ppermute | solution.py:20
  21.1 4.1 %collective-permute-start.3 = (bf16[514,128]{1,0:T(8,128)(2,1)S(1)}, bf16[514,128]{1,0:T(8,128)(2,1)}, u32[]{:S(2)}, u32[]{:S(2)}) collective-permute-start(bf16[514,128]{1,0:T(8,128)(2,1)S(1)} %pad_maximum_fusion), channel_id=1, source_target_pairs={{0,8},{8,16},{16,24},{24,32},{32,40},{40,48},{48,56},{56,64},{64,7... | collective-permute-start | bytes 394760 | tf_op jit(solution)/shard_map/ppermute | solution.py:20
  47.4 3.0 %fusion.27 = (bf16[1280,1,64]{2,0,1:T(8,128)(2,1)S(1)}, bf16[1280,1,64]{2,0,1:T(8,128)(2,1)S(1)}) fusion(f32[1280,1,128]{2,0,1:T(8,128)S(1)} %fusion.36, f32[64]{0:T(128)S(1)} %negate_power_fusion, f32[1280]{0:T(1024)S(1)} %convert_subtract_fusion), kind=kLoop, calls=%fused_computation.31 | loop fusion | flops 737280 | bytes 988416 | tf_op jit(solution)/shard_map/convert.15
  58.4 3.0 %collective-permute-start.5 = (bf16[32,1792]{1,0:T(8,128)(2,1)S(1)}, bf16[32,1792]{1,0:T(8,128)(2,1)S(1)}, u32[]{:S(2)}, u32[]{:S(2)}) collective-permute-start(bf16[32,1792]{1,0:T(8,128)(2,1)S(1)} %convolution_convert_fusion.1), channel_id=1, source_target_pairs={{0,8},{8,0},{16,24},{24,16},{32,40},{40,32},{48,56},{56,48},{64,72... | collective-permute-start | bytes 344072 | tf_op jit(solution)/shard_map/ppermute | solution.py:27
  65.2 4.5 %collective-permute-done.6 = bf16[32,1792]{1,0:T(8,128)(2,1)S(1)} collective-permute-done((bf16[32,1792]{1,0:T(8,128)(2,1)S(1)}, bf16[32,1792]{1,0:T(8,128)(2,1)S(1)}, u32[]{:S(2)}, u32[]{:S(2)}) %collective-permute-start.6) | collective-permute-done | bytes 114720 | tf_op jit(solution)/shard_map/ppermute | solution.py:27
  69.7 4.0 %collective-permute-start.7 = (bf16[32,1792]{1,0:T(8,128)(2,1)S(1)}, bf16[32,1792]{1,0:T(8,128)(2,1)S(1)}, u32[]{:S(2)}, u32[]{:S(2)}) collective-permute-start(bf16[32,1792]{1,0:T(8,128)(2,1)S(1)} %add.117), channel_id=1, source_target_pairs={{0,32},{8,40},{16,48},{24,56},{32,0},{40,8},{48,16},{56,24},{64,96... | collective-permute-start | bytes 344072 | tf_op jit(solution)/shard_map/ppermute | solution.py:27
  73.8 7.2 %collective-permute-done.7 = bf16[32,1792]{1,0:T(8,128)(2,1)S(1)} collective-permute-done((bf16[32,1792]{1,0:T(8,128)(2,1)S(1)}, bf16[32,1792]{1,0:T(8,128)(2,1)S(1)}, u32[]{:S(2)}, u32[]{:S(2)}) %collective-permute-start.7) | collective-permute-done | bytes 114720 | tf_op jit(solution)/shard_map/ppermute | solution.py:27
  81.0 4.9 %collective-permute-start.8 = (bf16[32,1792]{1,0:T(8,128)(2,1)S(1)}, bf16[32,1792]{1,0:T(8,128)(2,1)S(1)}, u32[]{:S(2)}, u32[]{:S(2)}) collective-permute-start(bf16[32,1792]{1,0:T(8,128)(2,1)S(1)} %add.118), channel_id=1, source_target_pairs={{0,64},{8,72},{16,80},{24,88},{32,96},{40,104},{48,112},{56,120},{... | collective-permute-start | bytes 344072 | tf_op jit(solution)/shard_map/ppermute | solution.py:27
  85.9 4.6 %collective-permute-done.8 = bf16[32,1792]{1,0:T(8,128)(2,1)S(1)} collective-permute-done((bf16[32,1792]{1,0:T(8,128)(2,1)S(1)}, bf16[32,1792]{1,0:T(8,128)(2,1)S(1)}, u32[]{:S(2)}, u32[]{:S(2)}) %collective-permute-start.8) | collective-permute-done | bytes 114720 | tf_op jit(solution)/shard_map/ppermute | solution.py:27
  90.6 8.7 %collective-permute-start.9 = (bf16[32,1792]{1,0:T(8,128)(2,1)S(1)}, bf16[32,1792]{1,0:T(8,128)(2,1)S(1)}, u32[]{:S(2)}, u32[]{:S(2)}) collective-permute-start(bf16[32,1792]{1,0:T(8,128)(2,1)S(1)} %add.119), channel_id=1, source_target_pairs={{0,128},{8,136},{16,144},{24,152},{32,160},{40,168},{48,176},{56,1... | collective-permute-start | bytes 344072 | tf_op jit(solution)/shard_map/ppermute | solution.py:27
  99.2 6.8 %collective-permute-done.9 = bf16[32,1792]{1,0:T(8,128)(2,1)S(1)} collective-permute-done((bf16[32,1792]{1,0:T(8,128)(2,1)S(1)}, bf16[32,1792]{1,0:T(8,128)(2,1)S(1)}, u32[]{:S(2)}, u32[]{:S(2)}) %collective-permute-start.9) | collective-permute-done | bytes 114720 | tf_op jit(solution)/shard_map/ppermute | solution.py:27
  106.0 7.9 %collective-permute-start.10 = (bf16[32,1792]{1,0:T(8,128)(2,1)S(1)}, bf16[32,1792]{1,0:T(8,128)(2,1)S(1)}, u32[]{:S(2)}, u32[]{:S(2)}) collective-permute-start(bf16[32,1792]{1,0:T(8,128)(2,1)S(1)} %add.120), channel_id=1, source_target_pairs={{0,256},{8,264},{16,272},{24,280},{32,288},{40,296},{48,304},{56,3... | collective-permute-start | bytes 344072 | tf_op jit(solution)/shard_map/ppermute | solution.py:27
  113.9 6.0 %collective-permute-done.10 = bf16[32,1792]{1,0:T(8,128)(2,1)S(1)} collective-permute-done((bf16[32,1792]{1,0:T(8,128)(2,1)S(1)}, bf16[32,1792]{1,0:T(8,128)(2,1)S(1)}, u32[]{:S(2)}, u32[]{:S(2)}) %collective-permute-start.10) | collective-permute-done | bytes 114720 | tf_op jit(solution)/shard_map/ppermute | solution.py:27
  122.4 12.3 %convolution_convert_fusion = bf16[288,7168]{1,0:T(8,128)(2,1)} fusion(bf16[896,7168]{0,1:T(8,128)(2,1)} %all-gather.2.cloned.1.call-done, bf16[32,896]{0,1:T(8,128)(2,1)S(1)} %copy.42, bf16[256,896]{0,1:T(8,128)(2,1)S(1)} %bitcast.117), kind=kOutput, calls=%fused_computation | convolution fusion | flops 3702472704 | bytes 17489920 | tf_op jit(solution)/shard_map/dot_general | solution.py:161
  136.1 5.8 %collective-permute-start.11 = (bf16[32,4,896]{2,0,1:T(8,128)(2,1)S(1)}, bf16[32,4,896]{2,0,1:T(8,128)(2,1)S(1)}, u32[]{:S(2)}, u32[]{:S(2)}) collective-permute-start(bf16[32,4,896]{2,0,1:T(8,128)(2,1)S(1)} %copy.54), channel_id=1, source_target_pairs={{0,4},{1,5},{2,6},{3,7},{4,0},{5,1},{6,2},{7,3},{8,12},{9,13},{10,... | collective-permute-start | bytes 688136 | tf_op jit(solution)/shard_map/ppermute | solution.py:46
  141.9 11.7 %collective-permute-done.11 = bf16[32,4,896]{2,0,1:T(8,128)(2,1)S(1)} collective-permute-done((bf16[32,4,896]{2,0,1:T(8,128)(2,1)S(1)}, bf16[32,4,896]{2,0,1:T(8,128)(2,1)S(1)}, u32[]{:S(2)}, u32[]{:S(2)}) %collective-permute-start.11) | collective-permute-done | bytes 229408 | tf_op jit(solution)/shard_map/ppermute | solution.py:46
  153.7 5.2 %collective-permute-start.12 = (f32[32,2,896]{2,0,1:T(8,128)S(1)}, f32[32,2,896]{2,0,1:T(8,128)S(1)}, u32[]{:S(2)}, u32[]{:S(2)}) collective-permute-start(f32[32,2,896]{2,0,1:T(8,128)S(1)} %constant_dynamic-slice_fusion.1), channel_id=1, source_target_pairs={{0,2},{1,3},{2,0},{3,1},{4,6},{5,7},{6,4},{7,5},{8,10},{9,11},{10,... | collective-permute-start | bytes 688136 | tf_op jit(solution)/shard_map/ppermute | solution.py:46
  158.9 9.5 %collective-permute-done.12 = f32[32,2,896]{2,0,1:T(8,128)S(1)} collective-permute-done((f32[32,2,896]{2,0,1:T(8,128)S(1)}, f32[32,2,896]{2,0,1:T(8,128)S(1)}, u32[]{:S(2)}, u32[]{:S(2)}) %collective-permute-start.12) | collective-permute-done | bytes 229408 | tf_op jit(solution)/shard_map/ppermute | solution.py:46
  170.5 4.1 %slice.135 = bf16[256,7168]{1,0:T(8,128)(2,1)} slice(bf16[288,7168]{1,0:T(8,128)(2,1)} %convolution_convert_fusion), slice={[0:256], [0:7168]} | slice | bytes 7340032 | tf_op jit(solution)/shard_map/slice | solution.py:164
  175.6 6.0 %copy.49 = bf16[256,7168]{0,1:T(8,128)(2,1)} copy(bf16[256,7168]{1,0:T(8,128)(2,1)} %slice.135) | data formatting | bytes 7340032
  182.5 2.9 %collective-permute-start.14 = (f32[32,1001]{1,0:T(8,128)S(1)}, f32[32,1001]{1,0:T(8,128)S(1)}, u32[]{:S(2)}, u32[]{:S(2)}) collective-permute-start(f32[32,1001]{1,0:T(8,128)S(1)} %pad_maximum_fusion.1), channel_id=1, source_target_pairs={{0,1},{1,0},{2,3},{3,2},{4,5},{5,4},{6,7},{7,6},{8,9},{9,8},{10,11... | collective-permute-start | bytes 384392 | tf_op jit(solution)/shard_map/ppermute | solution.py:27
  185.4 3.9 %collective-permute-done.14 = f32[32,1001]{1,0:T(8,128)S(1)} collective-permute-done((f32[32,1001]{1,0:T(8,128)S(1)}, f32[32,1001]{1,0:T(8,128)S(1)}, u32[]{:S(2)}, u32[]{:S(2)}) %collective-permute-start.14) | collective-permute-done | bytes 128160 | tf_op jit(solution)/shard_map/ppermute | solution.py:27
  189.5 4.1 %collective-permute-start.15 = (f32[32,1001]{1,0:T(8,128)S(1)}, f32[32,1001]{1,0:T(8,128)S(1)}, u32[]{:S(2)}, u32[]{:S(2)}) collective-permute-start(f32[32,1001]{1,0:T(8,128)S(1)} %fusion.60), channel_id=1, source_target_pairs={{0,2},{1,3},{2,0},{3,1},{4,6},{5,7},{6,4},{7,5},{8,10},{9,11},{10,... | collective-permute-start | bytes 384392 | tf_op jit(solution)/shard_map/ppermute | solution.py:27
  193.5 7.9 %collective-permute-done.15 = f32[32,1001]{1,0:T(8,128)S(1)} collective-permute-done((f32[32,1001]{1,0:T(8,128)S(1)}, f32[32,1001]{1,0:T(8,128)S(1)}, u32[]{:S(2)}, u32[]{:S(2)}) %collective-permute-start.15) | collective-permute-done | bytes 128160 | tf_op jit(solution)/shard_map/ppermute | solution.py:27
  201.4 4.7 %collective-permute-start.16 = (f32[32,1001]{1,0:T(8,128)S(1)}, f32[32,1001]{1,0:T(8,128)S(1)}, u32[]{:S(2)}, u32[]{:S(2)}) collective-permute-start(f32[32,1001]{1,0:T(8,128)S(1)} %add.137), channel_id=1, source_target_pairs={{0,4},{1,5},{2,6},{3,7},{4,0},{5,1},{6,2},{7,3},{8,12},{9,13},{10,... | collective-permute-start | bytes 384392 | tf_op jit(solution)/shard_map/ppermute | solution.py:27
  206.1 10.0 %collective-permute-done.16 = f32[32,1001]{1,0:T(8,128)S(1)} collective-permute-done((f32[32,1001]{1,0:T(8,128)S(1)}, f32[32,1001]{1,0:T(8,128)S(1)}, u32[]{:S(2)}, u32[]{:S(2)}) %collective-permute-start.16) | collective-permute-done | bytes 128160 | tf_op jit(solution)/shard_map/ppermute | solution.py:27
  220.1 3.4 %collective-permute-start.18 = (f32[32]{0:T(128)S(1)}, f32[32]{0:T(128)S(1)}, u32[]{:S(2)}, u32[]{:S(2)}) collective-permute-start(f32[32]{0:T(128)S(1)} %max.18), channel_id=1, source_target_pairs={{0,16},{8,24},{16,0},{24,8},{32,48},{40,56},{48,32},{56,40},{64,80... | collective-permute-start | bytes 392 | tf_op jit(solution)/shard_map/ppermute | solution.py:27
  225.5 4.9 %collective-permute-start.19 = (f32[32]{0:T(128)S(1)}, f32[32]{0:T(128)S(1)}, u32[]{:S(2)}, u32[]{:S(2)}) collective-permute-start(f32[32]{0:T(128)S(1)} %max.19), channel_id=1, source_target_pairs={{0,32},{8,40},{16,48},{24,56},{32,0},{40,8},{48,16},{56,24},{64,96... | collective-permute-start | bytes 392 | tf_op jit(solution)/shard_map/ppermute | solution.py:27
  232.4 4.0 %collective-permute-start.20 = (f32[32]{0:T(128)S(1)}, f32[32]{0:T(128)S(1)}, u32[]{:S(2)}, u32[]{:S(2)}) collective-permute-start(f32[32]{0:T(128)S(1)} %max.20), channel_id=1, source_target_pairs={{0,64},{8,72},{16,80},{24,88},{32,96},{40,104},{48,112},{56,120},{... | collective-permute-start | bytes 392 | tf_op jit(solution)/shard_map/ppermute | solution.py:27
  237.9 3.6 %collective-permute-start.21 = (f32[32]{0:T(128)S(1)}, f32[32]{0:T(128)S(1)}, u32[]{:S(2)}, u32[]{:S(2)}) collective-permute-start(f32[32]{0:T(128)S(1)} %max.21), channel_id=1, source_target_pairs={{0,128},{8,136},{16,144},{24,152},{32,160},{40,168},{48,176},{56,1... | collective-permute-start | bytes 392 | tf_op jit(solution)/shard_map/ppermute | solution.py:27
  244.2 6.7 %collective-permute-start.22 = (f32[32]{0:T(128)S(1)}, f32[32]{0:T(128)S(1)}, u32[]{:S(2)}, u32[]{:S(2)}) collective-permute-start(f32[32]{0:T(128)S(1)} %max.22), channel_id=1, source_target_pairs={{0,256},{8,264},{16,272},{24,280},{32,288},{40,296},{48,304},{56,3... | collective-permute-start | bytes 392 | tf_op jit(solution)/shard_map/ppermute | solution.py:27
  (112 shorter events, 63.3 us)
Async XLA Ops:
  7.2 174.6 %copy-start = (bf16[896,1000]{0,1:T(8,128)(2,1)S(1)}, bf16[896,1000]{0,1:T(8,128)(2,1)}, u32[]{:S(2)}) copy-start(bf16[896,1000]{0,1:T(8,128)(2,1)} %param.15) | copy-start | bytes 5376004
  7.2 35.1 %copy-start.3 = (s32[256]{0:T(256)S(1)}, s32[256]{0:T(256)}, u32[]{:S(2)}) copy-start(s32[256]{0:T(256)} %param.11) | copy-start | bytes 3076
  7.2 35.2 %copy-start.1 = (bf16[2,256,128]{2,1,0:T(8,128)(2,1)S(1)}, bf16[2,256,128]{2,1,0:T(8,128)(2,1)}, u32[]{:S(2)}) copy-start(bf16[2,256,128]{2,1,0:T(8,128)(2,1)} %param.10) | copy-start | bytes 393220
  7.2 115.2 %all-gather.2.cloned.1.call-start = ((), (), s32[]{:S(2)}) async-start(), calls=%async_computation.1 | async-start | bytes 13045760 | tf_op jit(solution)/shard_map/all_gather | solution.py:160
  7.9 246.2 %reduce-scatter.4.cloned.1.call-start = ((), (), s32[]{:S(2)}) async-start(), calls=%async_computation.2 | async-start | bytes 4128768
  9.6 26.3 %collective-permute-start = (bf16[514,128]{1,0:T(8,128)(2,1)S(1)}, bf16[514,128]{1,0:T(8,128)(2,1)}, u32[]{:S(2)}, u32[]{:S(2)}) collective-permute-start(bf16[514,128]{1,0:T(8,128)(2,1)S(1)} %pad_maximum_fusion), channel_id=1, source_target_pairs={{0,32},{8,40},{16,48},{24,56},{32,64},{40,72},{48,80},{56,88},{64,... | collective-permute-start | bytes 394760 | tf_op jit(solution)/shard_map/ppermute | solution.py:20
  15.2 21.7 %collective-permute-start.1 = (bf16[514,128]{1,0:T(8,128)(2,1)S(1)}, bf16[514,128]{1,0:T(8,128)(2,1)}, u32[]{:S(2)}, u32[]{:S(2)}) collective-permute-start(bf16[514,128]{1,0:T(8,128)(2,1)S(1)} %pad_maximum_fusion), channel_id=1, source_target_pairs={{0,24},{8,32},{16,40},{24,48},{32,56},{40,64},{48,72},{56,80},{64,... | collective-permute-start | bytes 394760 | tf_op jit(solution)/shard_map/ppermute | solution.py:20
  17.5 20.3 %collective-permute-start.2 = (bf16[514,128]{1,0:T(8,128)(2,1)S(1)}, bf16[514,128]{1,0:T(8,128)(2,1)}, u32[]{:S(2)}, u32[]{:S(2)}) collective-permute-start(bf16[514,128]{1,0:T(8,128)(2,1)S(1)} %pad_maximum_fusion), channel_id=1, source_target_pairs={{0,16},{8,24},{16,32},{24,40},{32,48},{40,56},{48,64},{56,72},{64,... | collective-permute-start | bytes 394760 | tf_op jit(solution)/shard_map/ppermute | solution.py:20
  21.1 17.6 %collective-permute-start.3 = (bf16[514,128]{1,0:T(8,128)(2,1)S(1)}, bf16[514,128]{1,0:T(8,128)(2,1)}, u32[]{:S(2)}, u32[]{:S(2)}) collective-permute-start(bf16[514,128]{1,0:T(8,128)(2,1)S(1)} %pad_maximum_fusion), channel_id=1, source_target_pairs={{0,8},{8,16},{16,24},{24,32},{32,40},{40,48},{48,56},{56,64},{64,7... | collective-permute-start | bytes 394760 | tf_op jit(solution)/shard_map/ppermute | solution.py:20
  26.4 6.8 %collective-permute-start.4 = (s32[1]{0:T(128)}, s32[1]{0:T(128)}, u32[]{:S(2)}, u32[]{:S(2)}) collective-permute-start(s32[1]{0:T(128)} %slice.109), channel_id=1, source_target_pairs={{8,0},{16,8},{24,16},{32,24},{40,32},{48,40},{56,48},{64,56},{72,6... | collective-permute-start | bytes 20 | tf_op jit(solution)/shard_map/ppermute | solution.py:20
  58.4 4.0 %collective-permute-start.5 = (bf16[32,1792]{1,0:T(8,128)(2,1)S(1)}, bf16[32,1792]{1,0:T(8,128)(2,1)S(1)}, u32[]{:S(2)}, u32[]{:S(2)}) collective-permute-start(bf16[32,1792]{1,0:T(8,128)(2,1)S(1)} %convolution_convert_fusion.1), channel_id=1, source_target_pairs={{0,8},{8,0},{16,24},{24,16},{32,40},{40,32},{48,56},{56,48},{64,72... | collective-permute-start | bytes 344072 | tf_op jit(solution)/shard_map/ppermute | solution.py:27
  62.4 7.3 %collective-permute-start.6 = (bf16[32,1792]{1,0:T(8,128)(2,1)S(1)}, bf16[32,1792]{1,0:T(8,128)(2,1)S(1)}, u32[]{:S(2)}, u32[]{:S(2)}) collective-permute-start(bf16[32,1792]{1,0:T(8,128)(2,1)S(1)} %add.116), channel_id=1, source_target_pairs={{0,16},{8,24},{16,0},{24,8},{32,48},{40,56},{48,32},{56,40},{64,80... | collective-permute-start | bytes 344072 | tf_op jit(solution)/shard_map/ppermute | solution.py:27
  69.7 11.2 %collective-permute-start.7 = (bf16[32,1792]{1,0:T(8,128)(2,1)S(1)}, bf16[32,1792]{1,0:T(8,128)(2,1)S(1)}, u32[]{:S(2)}, u32[]{:S(2)}) collective-permute-start(bf16[32,1792]{1,0:T(8,128)(2,1)S(1)} %add.117), channel_id=1, source_target_pairs={{0,32},{8,40},{16,48},{24,56},{32,0},{40,8},{48,16},{56,24},{64,96... | collective-permute-start | bytes 344072 | tf_op jit(solution)/shard_map/ppermute | solution.py:27
  81.0 9.5 %collective-permute-start.8 = (bf16[32,1792]{1,0:T(8,128)(2,1)S(1)}, bf16[32,1792]{1,0:T(8,128)(2,1)S(1)}, u32[]{:S(2)}, u32[]{:S(2)}) collective-permute-start(bf16[32,1792]{1,0:T(8,128)(2,1)S(1)} %add.118), channel_id=1, source_target_pairs={{0,64},{8,72},{16,80},{24,88},{32,96},{40,104},{48,112},{56,120},{... | collective-permute-start | bytes 344072 | tf_op jit(solution)/shard_map/ppermute | solution.py:27
  90.6 15.4 %collective-permute-start.9 = (bf16[32,1792]{1,0:T(8,128)(2,1)S(1)}, bf16[32,1792]{1,0:T(8,128)(2,1)S(1)}, u32[]{:S(2)}, u32[]{:S(2)}) collective-permute-start(bf16[32,1792]{1,0:T(8,128)(2,1)S(1)} %add.119), channel_id=1, source_target_pairs={{0,128},{8,136},{16,144},{24,152},{32,160},{40,168},{48,176},{56,1... | collective-permute-start | bytes 344072 | tf_op jit(solution)/shard_map/ppermute | solution.py:27
  106.0 13.8 %collective-permute-start.10 = (bf16[32,1792]{1,0:T(8,128)(2,1)S(1)}, bf16[32,1792]{1,0:T(8,128)(2,1)S(1)}, u32[]{:S(2)}, u32[]{:S(2)}) collective-permute-start(bf16[32,1792]{1,0:T(8,128)(2,1)S(1)} %add.120), channel_id=1, source_target_pairs={{0,256},{8,264},{16,272},{24,280},{32,288},{40,296},{48,304},{56,3... | collective-permute-start | bytes 344072 | tf_op jit(solution)/shard_map/ppermute | solution.py:27
  136.1 17.5 %collective-permute-start.11 = (bf16[32,4,896]{2,0,1:T(8,128)(2,1)S(1)}, bf16[32,4,896]{2,0,1:T(8,128)(2,1)S(1)}, u32[]{:S(2)}, u32[]{:S(2)}) collective-permute-start(bf16[32,4,896]{2,0,1:T(8,128)(2,1)S(1)} %copy.54), channel_id=1, source_target_pairs={{0,4},{1,5},{2,6},{3,7},{4,0},{5,1},{6,2},{7,3},{8,12},{9,13},{10,... | collective-permute-start | bytes 688136 | tf_op jit(solution)/shard_map/ppermute | solution.py:46
  153.7 14.8 %collective-permute-start.12 = (f32[32,2,896]{2,0,1:T(8,128)S(1)}, f32[32,2,896]{2,0,1:T(8,128)S(1)}, u32[]{:S(2)}, u32[]{:S(2)}) collective-permute-start(f32[32,2,896]{2,0,1:T(8,128)S(1)} %constant_dynamic-slice_fusion.1), channel_id=1, source_target_pairs={{0,2},{1,3},{2,0},{3,1},{4,6},{5,7},{6,4},{7,5},{8,10},{9,11},{10,... | collective-permute-start | bytes 688136 | tf_op jit(solution)/shard_map/ppermute | solution.py:46
  168.5 7.0 %collective-permute-start.13 = (f32[32,1,896]{2,0,1:T(8,128)S(1)}, f32[32,1,896]{2,0,1:T(8,128)S(1)}, u32[]{:S(2)}, u32[]{:S(2)}) collective-permute-start(f32[32,1,896]{2,0,1:T(8,128)S(1)} %constant_dynamic-slice_fusion), channel_id=1, source_target_pairs={{0,1},{1,0},{2,3},{3,2},{4,5},{5,4},{6,7},{7,6},{8,9},{9,8},{10,11... | collective-permute-start | bytes 344072 | tf_op jit(solution)/shard_map/ppermute | solution.py:46
  174.5 7.0 %copy-start.4 = (bf16[896]{0:T(1024)(128)(2,1)S(1)}, bf16[896]{0:T(1024)(128)(2,1)}, u32[]{:S(2)}) copy-start(bf16[896]{0:T(1024)(128)(2,1)} %param.14) | copy-start | bytes 5380
  175.5 79.8 %copy-start.2 = (bf16[256,896]{1,0:T(8,128)(2,1)S(1)}, bf16[256,896]{1,0:T(8,128)(2,1)}, u32[]{:S(2)}) copy-start(bf16[256,896]{1,0:T(8,128)(2,1)} %param.12) | copy-start | bytes 1376260
  182.5 6.9 %collective-permute-start.14 = (f32[32,1001]{1,0:T(8,128)S(1)}, f32[32,1001]{1,0:T(8,128)S(1)}, u32[]{:S(2)}, u32[]{:S(2)}) collective-permute-start(f32[32,1001]{1,0:T(8,128)S(1)} %pad_maximum_fusion.1), channel_id=1, source_target_pairs={{0,1},{1,0},{2,3},{3,2},{4,5},{5,4},{6,7},{7,6},{8,9},{9,8},{10,11... | collective-permute-start | bytes 384392 | tf_op jit(solution)/shard_map/ppermute | solution.py:27
  189.5 12.0 %collective-permute-start.15 = (f32[32,1001]{1,0:T(8,128)S(1)}, f32[32,1001]{1,0:T(8,128)S(1)}, u32[]{:S(2)}, u32[]{:S(2)}) collective-permute-start(f32[32,1001]{1,0:T(8,128)S(1)} %fusion.60), channel_id=1, source_target_pairs={{0,2},{1,3},{2,0},{3,1},{4,6},{5,7},{6,4},{7,5},{8,10},{9,11},{10,... | collective-permute-start | bytes 384392 | tf_op jit(solution)/shard_map/ppermute | solution.py:27
  201.4 14.7 %collective-permute-start.16 = (f32[32,1001]{1,0:T(8,128)S(1)}, f32[32,1001]{1,0:T(8,128)S(1)}, u32[]{:S(2)}, u32[]{:S(2)}) collective-permute-start(f32[32,1001]{1,0:T(8,128)S(1)} %add.137), channel_id=1, source_target_pairs={{0,4},{1,5},{2,6},{3,7},{4,0},{5,1},{6,2},{7,3},{8,12},{9,13},{10,... | collective-permute-start | bytes 384392 | tf_op jit(solution)/shard_map/ppermute | solution.py:27
  217.0 3.0 %collective-permute-start.17 = (f32[32]{0:T(128)S(1)}, f32[32]{0:T(128)S(1)}, u32[]{:S(2)}, u32[]{:S(2)}) collective-permute-start(f32[32]{0:T(128)S(1)} %fusion.39), channel_id=1, source_target_pairs={{0,8},{8,0},{16,24},{24,16},{32,40},{40,32},{48,56},{56,48},{64,72... | collective-permute-start | bytes 392 | tf_op jit(solution)/shard_map/ppermute | solution.py:27
  220.1 5.4 %collective-permute-start.18 = (f32[32]{0:T(128)S(1)}, f32[32]{0:T(128)S(1)}, u32[]{:S(2)}, u32[]{:S(2)}) collective-permute-start(f32[32]{0:T(128)S(1)} %max.18), channel_id=1, source_target_pairs={{0,16},{8,24},{16,0},{24,8},{32,48},{40,56},{48,32},{56,40},{64,80... | collective-permute-start | bytes 392 | tf_op jit(solution)/shard_map/ppermute | solution.py:27
  225.5 6.9 %collective-permute-start.19 = (f32[32]{0:T(128)S(1)}, f32[32]{0:T(128)S(1)}, u32[]{:S(2)}, u32[]{:S(2)}) collective-permute-start(f32[32]{0:T(128)S(1)} %max.19), channel_id=1, source_target_pairs={{0,32},{8,40},{16,48},{24,56},{32,0},{40,8},{48,16},{56,24},{64,96... | collective-permute-start | bytes 392 | tf_op jit(solution)/shard_map/ppermute | solution.py:27
  232.4 5.5 %collective-permute-start.20 = (f32[32]{0:T(128)S(1)}, f32[32]{0:T(128)S(1)}, u32[]{:S(2)}, u32[]{:S(2)}) collective-permute-start(f32[32]{0:T(128)S(1)} %max.20), channel_id=1, source_target_pairs={{0,64},{8,72},{16,80},{24,88},{32,96},{40,104},{48,112},{56,120},{... | collective-permute-start | bytes 392 | tf_op jit(solution)/shard_map/ppermute | solution.py:27
  237.9 6.3 %collective-permute-start.21 = (f32[32]{0:T(128)S(1)}, f32[32]{0:T(128)S(1)}, u32[]{:S(2)}, u32[]{:S(2)}) collective-permute-start(f32[32]{0:T(128)S(1)} %max.21), channel_id=1, source_target_pairs={{0,128},{8,136},{16,144},{24,152},{32,160},{40,168},{48,176},{56,1... | collective-permute-start | bytes 392 | tf_op jit(solution)/shard_map/ppermute | solution.py:27
  244.2 9.3 %collective-permute-start.22 = (f32[32]{0:T(128)S(1)}, f32[32]{0:T(128)S(1)}, u32[]{:S(2)}, u32[]{:S(2)}) collective-permute-start(f32[32]{0:T(128)S(1)} %max.22), channel_id=1, source_target_pairs={{0,256},{8,264},{16,272},{24,280},{32,288},{40,296},{48,304},{56,3... | collective-permute-start | bytes 392 | tf_op jit(solution)/shard_map/ppermute | solution.py:27
Sparse Core Ops, SparseCore 0:
  11.3 111.0 all-gather.1
  181.7 56.0 reduce-scatter.3

commit v7 on v6

--- a/solution.py
+++ b/solution.py
@@ -162,7 +162,7 @@
         jnp.concatenate([attended, end_att], axis=0), full_weight, preferred_element_type=jnp.float32
     ).astype(jnp.bfloat16)
     projected, end_part = both[:tok_rows], both[tok_rows:]
-    end_sum = halving_scatter(end_part, "tp")
+    end_sum = lax.psum_scatter(end_part, "tp", scatter_dimension=1, tiled=True).astype(jnp.float32)
     projected, end_sum = lax.optimization_barrier((projected, end_sum))
     own_share = lax.psum_scatter(projected, "tp", scatter_dimension=1, tiled=True).astype(jnp.float32)
     hidden = (residual.astype(jnp.float32) + own_share).astype(jnp.bfloat16)

time: 266 us -> 272 us (1.023)
  waiting for transfers between devices: 88.4 us -> 98 us
  starting transfers between devices: 97.2 us -> 90.1 us
    unnamed x3 -> x5, waiting for transfers between devices: 0.7 us -> 37.3 us
    ppermute x3 -> x0, waiting for transfers between devices: 22.2 us -> none  [halving_scatter(): lax.ppermute(give, axis, [(source, source ^ bit) for source in range(coun...]
    ppermute x3 -> x0, starting transfers between devices: 12.9 us -> none  [halving_scatter(): lax.ppermute(give, axis, [(source, source ^ bit) for source in range(coun...]
    ppermute x15, starting transfers between devices: 67.3 us -> 73.1 us  [butterfly(): lax.ppermute(value, axis, [(source, source ^ stride) for source in range(...]
    ppermute x15, waiting for transfers between devices: 63.2 us -> 58.5 us  [butterfly(): lax.ppermute(value, axis, [(source, source ^ stride) for source in range(...]
  transfers between devices with their start and end apart: 25 -> 23, of which waited for: 19 -> 17; matrix products, arithmetic and copies ran while one was open for 15% -> 15% of each run, Pallas kernels for 0% -> 0%
where the time goes in v7:
time: 272 us; the launch traced here: 267 us
  waiting for transfers between devices  98 us (36%)
  starting transfers between devices  90.1 us (33%)
  local copies, waits for them, and re-layouts  27.2 us (10%)
  matrix products  18.7 us (7%)
  other arithmetic  18.6 us (7%)
  between operations  14.9 us (5%)
    ppermute x15, starting transfers between devices, butterfly(): lax.ppermute(value, axis, [(source, source ^ stride) for source in range(...  73.1 us
    ppermute x15, waiting for transfers between devices, butterfly(): lax.ppermute(value, axis, [(source, source ^ stride) for source in range(...  58.5 us
    unnamed x5, waiting for transfers between devices  37.3 us
    ppermute x5, starting transfers between devices, from_behind(): lax.ppermute(value, axis, [(source, source + steps) for source in range(i...  16.9 us
    unnamed x21, local copies, waits for them, and re-layouts  13.9 us
    dot_general x1, matrix products, local(): jnp.dot(jnp.concatenate([attended, end_att], axis=0), full_weight, prefer...  12.3 us
  transfers between devices with their start and end apart: 23, of which 17 were waited for; matrix products, arithmetic and copies ran while one was open for 15% of the time, Pallas kernels for 0%

profile of v7, /device:TPU:56, one launch (start us, length us, event | category | flops | bytes accessed | tf_op | source)
XLA Modules:
  0.0 267.4 jit_solution(5447535462343089521)
XLA Ops:
  9.6 5.6 %collective-permute-start = (bf16[514,128]{1,0:T(8,128)(2,1)S(1)}, bf16[514,128]{1,0:T(8,128)(2,1)}, u32[]{:S(2)}, u32[]{:S(2)}) collective-permute-start(bf16[514,128]{1,0:T(8,128)(2,1)S(1)} %pad_maximum_fusion), channel_id=1, source_target_pairs={{0,32},{8,40},{16,48},{24,56},{32,64},{40,72},{48,80},{56,88},{64,... | collective-permute-start | bytes 394760 | tf_op jit(solution)/shard_map/ppermute | solution.py:20
  17.5 3.6 %collective-permute-start.2 = (bf16[514,128]{1,0:T(8,128)(2,1)S(1)}, bf16[514,128]{1,0:T(8,128)(2,1)}, u32[]{:S(2)}, u32[]{:S(2)}) collective-permute-start(bf16[514,128]{1,0:T(8,128)(2,1)S(1)} %pad_maximum_fusion), channel_id=1, source_target_pairs={{0,16},{8,24},{16,32},{24,40},{32,48},{40,56},{48,64},{56,72},{64,... | collective-permute-start | bytes 394760 | tf_op jit(solution)/shard_map/ppermute | solution.py:20
  21.1 4.1 %collective-permute-start.3 = (bf16[514,128]{1,0:T(8,128)(2,1)S(1)}, bf16[514,128]{1,0:T(8,128)(2,1)}, u32[]{:S(2)}, u32[]{:S(2)}) collective-permute-start(bf16[514,128]{1,0:T(8,128)(2,1)S(1)} %pad_maximum_fusion), channel_id=1, source_target_pairs={{0,8},{8,16},{16,24},{24,32},{32,40},{40,48},{48,56},{56,64},{64,7... | collective-permute-start | bytes 394760 | tf_op jit(solution)/shard_map/ppermute | solution.py:20
  47.5 3.0 %fusion.27 = (bf16[1280,1,64]{2,0,1:T(8,128)(2,1)S(1)}, bf16[1280,1,64]{2,0,1:T(8,128)(2,1)S(1)}) fusion(f32[1280,1,128]{2,0,1:T(8,128)S(1)} %fusion.36, f32[64]{0:T(128)S(1)} %negate_power_fusion, f32[1280]{0:T(1024)S(1)} %convert_subtract_fusion), kind=kLoop, calls=%fused_computation.31 | loop fusion | flops 737280 | bytes 988416 | tf_op jit(solution)/shard_map/convert.15
  54.3 2.5 fusion.13
  58.4 3.0 %collective-permute-start.5 = (bf16[32,1792]{1,0:T(8,128)(2,1)S(1)}, bf16[32,1792]{1,0:T(8,128)(2,1)S(1)}, u32[]{:S(2)}, u32[]{:S(2)}) collective-permute-start(bf16[32,1792]{1,0:T(8,128)(2,1)S(1)} %convolution_convert_fusion.1), channel_id=1, source_target_pairs={{0,8},{8,0},{16,24},{24,16},{32,40},{40,32},{48,56},{56,48},{64,72... | collective-permute-start | bytes 344072 | tf_op jit(solution)/shard_map/ppermute | solution.py:27
  62.4 2.7 %collective-permute-start.6 = (bf16[32,1792]{1,0:T(8,128)(2,1)S(1)}, bf16[32,1792]{1,0:T(8,128)(2,1)S(1)}, u32[]{:S(2)}, u32[]{:S(2)}) collective-permute-start(bf16[32,1792]{1,0:T(8,128)(2,1)S(1)} %add.77), channel_id=1, source_target_pairs={{0,16},{8,24},{16,0},{24,8},{32,48},{40,56},{48,32},{56,40},{64,80... | collective-permute-start | bytes 344072 | tf_op jit(solution)/shard_map/ppermute | solution.py:27
  65.2 4.6 %collective-permute-done.6 = bf16[32,1792]{1,0:T(8,128)(2,1)S(1)} collective-permute-done((bf16[32,1792]{1,0:T(8,128)(2,1)S(1)}, bf16[32,1792]{1,0:T(8,128)(2,1)S(1)}, u32[]{:S(2)}, u32[]{:S(2)}) %collective-permute-start.6) | collective-permute-done | bytes 114720 | tf_op jit(solution)/shard_map/ppermute | solution.py:27
  69.8 4.0 %collective-permute-start.7 = (bf16[32,1792]{1,0:T(8,128)(2,1)S(1)}, bf16[32,1792]{1,0:T(8,128)(2,1)S(1)}, u32[]{:S(2)}, u32[]{:S(2)}) collective-permute-start(bf16[32,1792]{1,0:T(8,128)(2,1)S(1)} %add.78), channel_id=1, source_target_pairs={{0,32},{8,40},{16,48},{24,56},{32,0},{40,8},{48,16},{56,24},{64,96... | collective-permute-start | bytes 344072 | tf_op jit(solution)/shard_map/ppermute | solution.py:27
  73.8 7.2 %collective-permute-done.7 = bf16[32,1792]{1,0:T(8,128)(2,1)S(1)} collective-permute-done((bf16[32,1792]{1,0:T(8,128)(2,1)S(1)}, bf16[32,1792]{1,0:T(8,128)(2,1)S(1)}, u32[]{:S(2)}, u32[]{:S(2)}) %collective-permute-start.7) | collective-permute-done | bytes 114720 | tf_op jit(solution)/shard_map/ppermute | solution.py:27
  81.0 4.9 %collective-permute-start.8 = (bf16[32,1792]{1,0:T(8,128)(2,1)S(1)}, bf16[32,1792]{1,0:T(8,128)(2,1)S(1)}, u32[]{:S(2)}, u32[]{:S(2)}) collective-permute-start(bf16[32,1792]{1,0:T(8,128)(2,1)S(1)} %add.79), channel_id=1, source_target_pairs={{0,64},{8,72},{16,80},{24,88},{32,96},{40,104},{48,112},{56,120},{... | collective-permute-start | bytes 344072 | tf_op jit(solution)/shard_map/ppermute | solution.py:27
  86.0 4.6 %collective-permute-done.8 = bf16[32,1792]{1,0:T(8,128)(2,1)S(1)} collective-permute-done((bf16[32,1792]{1,0:T(8,128)(2,1)S(1)}, bf16[32,1792]{1,0:T(8,128)(2,1)S(1)}, u32[]{:S(2)}, u32[]{:S(2)}) %collective-permute-start.8) | collective-permute-done | bytes 114720 | tf_op jit(solution)/shard_map/ppermute | solution.py:27
  90.6 8.7 %collective-permute-start.9 = (bf16[32,1792]{1,0:T(8,128)(2,1)S(1)}, bf16[32,1792]{1,0:T(8,128)(2,1)S(1)}, u32[]{:S(2)}, u32[]{:S(2)}) collective-permute-start(bf16[32,1792]{1,0:T(8,128)(2,1)S(1)} %add.80), channel_id=1, source_target_pairs={{0,128},{8,136},{16,144},{24,152},{32,160},{40,168},{48,176},{56,1... | collective-permute-start | bytes 344072 | tf_op jit(solution)/shard_map/ppermute | solution.py:27
  99.3 6.7 %collective-permute-done.9 = bf16[32,1792]{1,0:T(8,128)(2,1)S(1)} collective-permute-done((bf16[32,1792]{1,0:T(8,128)(2,1)S(1)}, bf16[32,1792]{1,0:T(8,128)(2,1)S(1)}, u32[]{:S(2)}, u32[]{:S(2)}) %collective-permute-start.9) | collective-permute-done | bytes 114720 | tf_op jit(solution)/shard_map/ppermute | solution.py:27
  106.1 7.9 %collective-permute-start.10 = (bf16[32,1792]{1,0:T(8,128)(2,1)S(1)}, bf16[32,1792]{1,0:T(8,128)(2,1)S(1)}, u32[]{:S(2)}, u32[]{:S(2)}) collective-permute-start(bf16[32,1792]{1,0:T(8,128)(2,1)S(1)} %add.81), channel_id=1, source_target_pairs={{0,256},{8,264},{16,272},{24,280},{32,288},{40,296},{48,304},{56,3... | collective-permute-start | bytes 344072 | tf_op jit(solution)/shard_map/ppermute | solution.py:27
  114.0 5.9 %collective-permute-done.10 = bf16[32,1792]{1,0:T(8,128)(2,1)S(1)} collective-permute-done((bf16[32,1792]{1,0:T(8,128)(2,1)S(1)}, bf16[32,1792]{1,0:T(8,128)(2,1)S(1)}, u32[]{:S(2)}, u32[]{:S(2)}) %collective-permute-start.10) | collective-permute-done | bytes 114720 | tf_op jit(solution)/shard_map/ppermute | solution.py:27
  122.3 12.3 %convolution_convert_fusion = bf16[288,7168]{1,0:T(8,128)(2,1)} fusion(bf16[896,7168]{0,1:T(8,128)(2,1)} %all-gather.2.cloned.1.call-done, bf16[32,896]{0,1:T(8,128)(2,1)S(1)} %copy.38, bf16[256,896]{0,1:T(8,128)(2,1)S(1)} %bitcast.115), kind=kOutput, calls=%fused_computation | convolution fusion | flops 3702472704 | bytes 17489920 | tf_op jit(solution)/shard_map/dot_general | solution.py:161
  137.4 4.1 %slice.135 = bf16[256,7168]{1,0:T(8,128)(2,1)} slice(bf16[288,7168]{1,0:T(8,128)(2,1)} %convolution_convert_fusion), slice={[0:256], [0:7168]} | slice | bytes 7340032 | tf_op jit(solution)/shard_map/slice | solution.py:164
  141.4 36.6 %reduce-scatter.7.cloned.1.call-done = bf16[896,32]{1,0:T(8,128)(2,1)} async-done(((bf16[7168,32]{1,0:T(8,128)(2,1)}), bf16[896,32]{1,0:T(8,128)(2,1)}) %reduce-scatter.7.cloned.1.call-update) | async-done | bytes 57360
  179.1 6.0 %copy.45 = bf16[256,7168]{0,1:T(8,128)(2,1)} copy(bf16[256,7168]{1,0:T(8,128)(2,1)} %slice.135) | data formatting | bytes 7340032
  186.1 2.6 collective-permute-start.11
  188.7 4.2 %collective-permute-done.11 = f32[32,1001]{1,0:T(8,128)S(1)} collective-permute-done((f32[32,1001]{1,0:T(8,128)S(1)}, f32[32,1001]{1,0:T(8,128)S(1)}, u32[]{:S(2)}, u32[]{:S(2)}) %collective-permute-start.11) | collective-permute-done | bytes 128160 | tf_op jit(solution)/shard_map/ppermute | solution.py:27
  193.0 5.5 %collective-permute-start.12 = (f32[32,1001]{1,0:T(8,128)S(1)}, f32[32,1001]{1,0:T(8,128)S(1)}, u32[]{:S(2)}, u32[]{:S(2)}) collective-permute-start(f32[32,1001]{1,0:T(8,128)S(1)} %fusion.60), channel_id=1, source_target_pairs={{0,2},{1,3},{2,0},{3,1},{4,6},{5,7},{6,4},{7,5},{8,10},{9,11},{10,... | collective-permute-start | bytes 384392 | tf_op jit(solution)/shard_map/ppermute | solution.py:27
  198.5 5.9 %collective-permute-done.12 = f32[32,1001]{1,0:T(8,128)S(1)} collective-permute-done((f32[32,1001]{1,0:T(8,128)S(1)}, f32[32,1001]{1,0:T(8,128)S(1)}, u32[]{:S(2)}, u32[]{:S(2)}) %collective-permute-start.12) | collective-permute-done | bytes 128160 | tf_op jit(solution)/shard_map/ppermute | solution.py:27
  204.4 9.1 %collective-permute-start.13 = (f32[32,1001]{1,0:T(8,128)S(1)}, f32[32,1001]{1,0:T(8,128)S(1)}, u32[]{:S(2)}, u32[]{:S(2)}) collective-permute-start(f32[32,1001]{1,0:T(8,128)S(1)} %add.86), channel_id=1, source_target_pairs={{0,4},{1,5},{2,6},{3,7},{4,0},{5,1},{6,2},{7,3},{8,12},{9,13},{10,... | collective-permute-start | bytes 384392 | tf_op jit(solution)/shard_map/ppermute | solution.py:27
  213.6 7.3 %collective-permute-done.13 = f32[32,1001]{1,0:T(8,128)S(1)} collective-permute-done((f32[32,1001]{1,0:T(8,128)S(1)}, f32[32,1001]{1,0:T(8,128)S(1)}, u32[]{:S(2)}, u32[]{:S(2)}) %collective-permute-start.13) | collective-permute-done | bytes 128160 | tf_op jit(solution)/shard_map/ppermute | solution.py:27
  224.8 3.1 %collective-permute-start.15 = (f32[32]{0:T(128)S(1)}, f32[32]{0:T(128)S(1)}, u32[]{:S(2)}, u32[]{:S(2)}) collective-permute-start(f32[32]{0:T(128)S(1)} %max.18), channel_id=1, source_target_pairs={{0,16},{8,24},{16,0},{24,8},{32,48},{40,56},{48,32},{56,40},{64,80... | collective-permute-start | bytes 392 | tf_op jit(solution)/shard_map/ppermute | solution.py:27
  230.2 4.5 %collective-permute-start.16 = (f32[32]{0:T(128)S(1)}, f32[32]{0:T(128)S(1)}, u32[]{:S(2)}, u32[]{:S(2)}) collective-permute-start(f32[32]{0:T(128)S(1)} %max.19), channel_id=1, source_target_pairs={{0,32},{8,40},{16,48},{24,56},{32,0},{40,8},{48,16},{56,24},{64,96... | collective-permute-start | bytes 392 | tf_op jit(solution)/shard_map/ppermute | solution.py:27
  234.7 2.4 collective-permute-done.16
  237.1 3.1 %collective-permute-start.17 = (f32[32]{0:T(128)S(1)}, f32[32]{0:T(128)S(1)}, u32[]{:S(2)}, u32[]{:S(2)}) collective-permute-start(f32[32]{0:T(128)S(1)} %max.20), channel_id=1, source_target_pairs={{0,64},{8,72},{16,80},{24,88},{32,96},{40,104},{48,112},{56,120},{... | collective-permute-start | bytes 392 | tf_op jit(solution)/shard_map/ppermute | solution.py:27
  242.6 4.5 %collective-permute-start.18 = (f32[32]{0:T(128)S(1)}, f32[32]{0:T(128)S(1)}, u32[]{:S(2)}, u32[]{:S(2)}) collective-permute-start(f32[32]{0:T(128)S(1)} %max.21), channel_id=1, source_target_pairs={{0,128},{8,136},{16,144},{24,152},{32,160},{40,168},{48,176},{56,1... | collective-permute-start | bytes 392 | tf_op jit(solution)/shard_map/ppermute | solution.py:27
  248.9 7.3 %collective-permute-start.19 = (f32[32]{0:T(128)S(1)}, f32[32]{0:T(128)S(1)}, u32[]{:S(2)}, u32[]{:S(2)}) collective-permute-start(f32[32]{0:T(128)S(1)} %max.22), channel_id=1, source_target_pairs={{0,256},{8,264},{16,272},{24,280},{32,288},{40,296},{48,304},{56,3... | collective-permute-start | bytes 392 | tf_op jit(solution)/shard_map/ppermute | solution.py:27
  (104 shorter events, 54.8 us)
Async XLA Ops:
  7.2 178.2 %copy-start = (bf16[896,1000]{0,1:T(8,128)(2,1)S(1)}, bf16[896,1000]{0,1:T(8,128)(2,1)}, u32[]{:S(2)}) copy-start(bf16[896,1000]{0,1:T(8,128)(2,1)} %param.15) | copy-start | bytes 5376004
  7.2 35.1 %copy-start.3 = (s32[256]{0:T(256)S(1)}, s32[256]{0:T(256)}, u32[]{:S(2)}) copy-start(s32[256]{0:T(256)} %param.11) | copy-start | bytes 3076
  7.2 35.2 %copy-start.1 = (bf16[2,256,128]{2,1,0:T(8,128)(2,1)S(1)}, bf16[2,256,128]{2,1,0:T(8,128)(2,1)}, u32[]{:S(2)}) copy-start(bf16[2,256,128]{2,1,0:T(8,128)(2,1)} %param.10) | copy-start | bytes 393220
  7.2 115.1 %all-gather.2.cloned.1.call-start = ((), (), s32[]{:S(2)}) async-start(), calls=%async_computation.2 | async-start | bytes 13045760 | tf_op jit(solution)/shard_map/all_gather | solution.py:160
  7.9 170.1 %reduce-scatter.7.cloned.1.call-start = ((), (), s32[]{:S(2)}) async-start(), calls=%async_computation.3 | async-start | bytes 2064384
  9.6 26.3 %collective-permute-start = (bf16[514,128]{1,0:T(8,128)(2,1)S(1)}, bf16[514,128]{1,0:T(8,128)(2,1)}, u32[]{:S(2)}, u32[]{:S(2)}) collective-permute-start(bf16[514,128]{1,0:T(8,128)(2,1)S(1)} %pad_maximum_fusion), channel_id=1, source_target_pairs={{0,32},{8,40},{16,48},{24,56},{32,64},{40,72},{48,80},{56,88},{64,... | collective-permute-start | bytes 394760 | tf_op jit(solution)/shard_map/ppermute | solution.py:20
  15.2 21.7 %collective-permute-start.1 = (bf16[514,128]{1,0:T(8,128)(2,1)S(1)}, bf16[514,128]{1,0:T(8,128)(2,1)}, u32[]{:S(2)}, u32[]{:S(2)}) collective-permute-start(bf16[514,128]{1,0:T(8,128)(2,1)S(1)} %pad_maximum_fusion), channel_id=1, source_target_pairs={{0,24},{8,32},{16,40},{24,48},{32,56},{40,64},{48,72},{56,80},{64,... | collective-permute-start | bytes 394760 | tf_op jit(solution)/shard_map/ppermute | solution.py:20
  17.5 20.3 %collective-permute-start.2 = (bf16[514,128]{1,0:T(8,128)(2,1)S(1)}, bf16[514,128]{1,0:T(8,128)(2,1)}, u32[]{:S(2)}, u32[]{:S(2)}) collective-permute-start(bf16[514,128]{1,0:T(8,128)(2,1)S(1)} %pad_maximum_fusion), channel_id=1, source_target_pairs={{0,16},{8,24},{16,32},{24,40},{32,48},{40,56},{48,64},{56,72},{64,... | collective-permute-start | bytes 394760 | tf_op jit(solution)/shard_map/ppermute | solution.py:20
  21.1 17.6 %collective-permute-start.3 = (bf16[514,128]{1,0:T(8,128)(2,1)S(1)}, bf16[514,128]{1,0:T(8,128)(2,1)}, u32[]{:S(2)}, u32[]{:S(2)}) collective-permute-start(bf16[514,128]{1,0:T(8,128)(2,1)S(1)} %pad_maximum_fusion), channel_id=1, source_target_pairs={{0,8},{8,16},{16,24},{24,32},{32,40},{40,48},{48,56},{56,64},{64,7... | collective-permute-start | bytes 394760 | tf_op jit(solution)/shard_map/ppermute | solution.py:20
  26.4 6.8 %collective-permute-start.4 = (s32[1]{0:T(128)}, s32[1]{0:T(128)}, u32[]{:S(2)}, u32[]{:S(2)}) collective-permute-start(s32[1]{0:T(128)} %slice.109), channel_id=1, source_target_pairs={{8,0},{16,8},{24,16},{32,24},{40,32},{48,40},{56,48},{64,56},{72,6... | collective-permute-start | bytes 20 | tf_op jit(solution)/shard_map/ppermute | solution.py:20
  58.4 4.0 %collective-permute-start.5 = (bf16[32,1792]{1,0:T(8,128)(2,1)S(1)}, bf16[32,1792]{1,0:T(8,128)(2,1)S(1)}, u32[]{:S(2)}, u32[]{:S(2)}) collective-permute-start(bf16[32,1792]{1,0:T(8,128)(2,1)S(1)} %convolution_convert_fusion.1), channel_id=1, source_target_pairs={{0,8},{8,0},{16,24},{24,16},{32,40},{40,32},{48,56},{56,48},{64,72... | collective-permute-start | bytes 344072 | tf_op jit(solution)/shard_map/ppermute | solution.py:27
  62.4 7.3 %collective-permute-start.6 = (bf16[32,1792]{1,0:T(8,128)(2,1)S(1)}, bf16[32,1792]{1,0:T(8,128)(2,1)S(1)}, u32[]{:S(2)}, u32[]{:S(2)}) collective-permute-start(bf16[32,1792]{1,0:T(8,128)(2,1)S(1)} %add.77), channel_id=1, source_target_pairs={{0,16},{8,24},{16,0},{24,8},{32,48},{40,56},{48,32},{56,40},{64,80... | collective-permute-start | bytes 344072 | tf_op jit(solution)/shard_map/ppermute | solution.py:27
  69.8 11.2 %collective-permute-start.7 = (bf16[32,1792]{1,0:T(8,128)(2,1)S(1)}, bf16[32,1792]{1,0:T(8,128)(2,1)S(1)}, u32[]{:S(2)}, u32[]{:S(2)}) collective-permute-start(bf16[32,1792]{1,0:T(8,128)(2,1)S(1)} %add.78), channel_id=1, source_target_pairs={{0,32},{8,40},{16,48},{24,56},{32,0},{40,8},{48,16},{56,24},{64,96... | collective-permute-start | bytes 344072 | tf_op jit(solution)/shard_map/ppermute | solution.py:27
  81.0 9.6 %collective-permute-start.8 = (bf16[32,1792]{1,0:T(8,128)(2,1)S(1)}, bf16[32,1792]{1,0:T(8,128)(2,1)S(1)}, u32[]{:S(2)}, u32[]{:S(2)}) collective-permute-start(bf16[32,1792]{1,0:T(8,128)(2,1)S(1)} %add.79), channel_id=1, source_target_pairs={{0,64},{8,72},{16,80},{24,88},{32,96},{40,104},{48,112},{56,120},{... | collective-permute-start | bytes 344072 | tf_op jit(solution)/shard_map/ppermute | solution.py:27
  90.6 15.4 %collective-permute-start.9 = (bf16[32,1792]{1,0:T(8,128)(2,1)S(1)}, bf16[32,1792]{1,0:T(8,128)(2,1)S(1)}, u32[]{:S(2)}, u32[]{:S(2)}) collective-permute-start(bf16[32,1792]{1,0:T(8,128)(2,1)S(1)} %add.80), channel_id=1, source_target_pairs={{0,128},{8,136},{16,144},{24,152},{32,160},{40,168},{48,176},{56,1... | collective-permute-start | bytes 344072 | tf_op jit(solution)/shard_map/ppermute | solution.py:27
  106.1 13.8 %collective-permute-start.10 = (bf16[32,1792]{1,0:T(8,128)(2,1)S(1)}, bf16[32,1792]{1,0:T(8,128)(2,1)S(1)}, u32[]{:S(2)}, u32[]{:S(2)}) collective-permute-start(bf16[32,1792]{1,0:T(8,128)(2,1)S(1)} %add.81), channel_id=1, source_target_pairs={{0,256},{8,264},{16,272},{24,280},{32,288},{40,296},{48,304},{56,3... | collective-permute-start | bytes 344072 | tf_op jit(solution)/shard_map/ppermute | solution.py:27
  137.3 121.4 %reduce-scatter.9.cloned.1.call-start = ((), (), s32[]{:S(2)}) async-start(), calls=%async_computation.4 | async-start | bytes 4128768
  141.4 43.7 %copy-start.4 = (bf16[896]{0:T(1024)(128)(2,1)S(1)}, bf16[896]{0:T(1024)(128)(2,1)}, u32[]{:S(2)}) copy-start(bf16[896]{0:T(1024)(128)(2,1)} %param.14) | copy-start | bytes 5380
  179.1 80.9 %copy-start.2 = (bf16[256,896]{1,0:T(8,128)(2,1)S(1)}, bf16[256,896]{1,0:T(8,128)(2,1)}, u32[]{:S(2)}) copy-start(bf16[256,896]{1,0:T(8,128)(2,1)} %param.12) | copy-start | bytes 1376260
  186.1 6.9 %collective-permute-start.11 = (f32[32,1001]{1,0:T(8,128)S(1)}, f32[32,1001]{1,0:T(8,128)S(1)}, u32[]{:S(2)}, u32[]{:S(2)}) collective-permute-start(f32[32,1001]{1,0:T(8,128)S(1)} %pad_maximum_fusion.1), channel_id=1, source_target_pairs={{0,1},{1,0},{2,3},{3,2},{4,5},{5,4},{6,7},{7,6},{8,9},{9,8},{10,11... | collective-permute-start | bytes 384392 | tf_op jit(solution)/shard_map/ppermute | solution.py:27
  193.0 11.4 %collective-permute-start.12 = (f32[32,1001]{1,0:T(8,128)S(1)}, f32[32,1001]{1,0:T(8,128)S(1)}, u32[]{:S(2)}, u32[]{:S(2)}) collective-permute-start(f32[32,1001]{1,0:T(8,128)S(1)} %fusion.60), channel_id=1, source_target_pairs={{0,2},{1,3},{2,0},{3,1},{4,6},{5,7},{6,4},{7,5},{8,10},{9,11},{10,... | collective-permute-start | bytes 384392 | tf_op jit(solution)/shard_map/ppermute | solution.py:27
  204.4 16.4 %collective-permute-start.13 = (f32[32,1001]{1,0:T(8,128)S(1)}, f32[32,1001]{1,0:T(8,128)S(1)}, u32[]{:S(2)}, u32[]{:S(2)}) collective-permute-start(f32[32,1001]{1,0:T(8,128)S(1)} %add.86), channel_id=1, source_target_pairs={{0,4},{1,5},{2,6},{3,7},{4,0},{5,1},{6,2},{7,3},{8,12},{9,13},{10,... | collective-permute-start | bytes 384392 | tf_op jit(solution)/shard_map/ppermute | solution.py:27
  221.8 3.0 %collective-permute-start.14 = (f32[32]{0:T(128)S(1)}, f32[32]{0:T(128)S(1)}, u32[]{:S(2)}, u32[]{:S(2)}) collective-permute-start(f32[32]{0:T(128)S(1)} %fusion.39), channel_id=1, source_target_pairs={{0,8},{8,0},{16,24},{24,16},{32,40},{40,32},{48,56},{56,48},{64,72... | collective-permute-start | bytes 392 | tf_op jit(solution)/shard_map/ppermute | solution.py:27
  224.8 5.4 %collective-permute-start.15 = (f32[32]{0:T(128)S(1)}, f32[32]{0:T(128)S(1)}, u32[]{:S(2)}, u32[]{:S(2)}) collective-permute-start(f32[32]{0:T(128)S(1)} %max.18), channel_id=1, source_target_pairs={{0,16},{8,24},{16,0},{24,8},{32,48},{40,56},{48,32},{56,40},{64,80... | collective-permute-start | bytes 392 | tf_op jit(solution)/shard_map/ppermute | solution.py:27
  230.2 6.9 %collective-permute-start.16 = (f32[32]{0:T(128)S(1)}, f32[32]{0:T(128)S(1)}, u32[]{:S(2)}, u32[]{:S(2)}) collective-permute-start(f32[32]{0:T(128)S(1)} %max.19), channel_id=1, source_target_pairs={{0,32},{8,40},{16,48},{24,56},{32,0},{40,8},{48,16},{56,24},{64,96... | collective-permute-start | bytes 392 | tf_op jit(solution)/shard_map/ppermute | solution.py:27
  237.1 5.4 %collective-permute-start.17 = (f32[32]{0:T(128)S(1)}, f32[32]{0:T(128)S(1)}, u32[]{:S(2)}, u32[]{:S(2)}) collective-permute-start(f32[32]{0:T(128)S(1)} %max.20), channel_id=1, source_target_pairs={{0,64},{8,72},{16,80},{24,88},{32,96},{40,104},{48,112},{56,120},{... | collective-permute-start | bytes 392 | tf_op jit(solution)/shard_map/ppermute | solution.py:27
  242.6 6.3 %collective-permute-start.18 = (f32[32]{0:T(128)S(1)}, f32[32]{0:T(128)S(1)}, u32[]{:S(2)}, u32[]{:S(2)}) collective-permute-start(f32[32]{0:T(128)S(1)} %max.21), channel_id=1, source_target_pairs={{0,128},{8,136},{16,144},{24,152},{32,160},{40,168},{48,176},{56,1... | collective-permute-start | bytes 392 | tf_op jit(solution)/shard_map/ppermute | solution.py:27
  248.9 9.3 %collective-permute-start.19 = (f32[32]{0:T(128)S(1)}, f32[32]{0:T(128)S(1)}, u32[]{:S(2)}, u32[]{:S(2)}) collective-permute-start(f32[32]{0:T(128)S(1)} %max.22), channel_id=1, source_target_pairs={{0,256},{8,264},{16,272},{24,280},{32,288},{40,296},{48,304},{56,3... | collective-permute-start | bytes 392 | tf_op jit(solution)/shard_map/ppermute | solution.py:27
Sparse Core Ops, SparseCore 0:
  11.3 110.9 all-gather.1
  137.4 40.5 reduce-scatter.6
  185.3 58.1 reduce-scatter.8

commit v8 on v6

--- a/solution.py
+++ b/solution.py
@@ -33,19 +33,18 @@
 def halving_scatter(value, axis):
     count = lax.axis_size(axis)
     index = lax.axis_index(axis)
-    rows = value.shape[0]
-    held = value.reshape(rows, count, value.shape[1] // count)
-    bit = count // 2
-    while bit >= 1:
-        if bit < count // 2:
-            held = held.astype(jnp.float32)
-        half = held.shape[1] // 2
+    rows, width = value.shape[0], value.shape[1] // count
+    held = value.reshape(rows, count, width)
+    bit = 1
+    while bit < count:
         mine = (index // bit) % 2
-        keep = lax.dynamic_slice_in_dim(held, mine * half, half, 1)
-        give = lax.dynamic_slice_in_dim(held, (1 - mine) * half, half, 1)
-        held = keep.astype(jnp.float32) + lax.ppermute(give, axis, [(source, source ^ bit) for source in range(count)]).astype(jnp.float32)
-        bit //= 2
-    return held.reshape(rows, -1)
+        pairs = held.reshape(rows, held.shape[1] // 2, 2, width)
+        keep = lax.dynamic_index_in_dim(pairs, mine, 2, keepdims=False)
+        give = lax.dynamic_index_in_dim(pairs, 1 - mine, 2, keepdims=False)
+        moved = lax.ppermute(give, axis, [(source, source ^ bit) for source in range(count)])
+        held = (keep.astype(jnp.float32) + moved.astype(jnp.float32)).astype(value.dtype)
+        bit *= 2
+    return held.reshape(rows, width).astype(jnp.float32)
 
 
 def rope_tables(positions, width):

time: 266 us -> 258 us (0.970)
  starting transfers between devices: 97.2 us -> 90.6 us
    ppermute x3, waiting for transfers between devices: 22.2 us -> 12.1 us  [halving_scatter(): lax.ppermute(give, axis, [(source, source ^ bit) for source in range(coun...]
    ppermute x15, waiting for transfers between devices: 63.2 us -> 70.9 us  [butterfly(): lax.ppermute(value, axis, [(source, source ^ stride) for source in range(...]
    ppermute x15, starting transfers between devices: 67.3 us -> 59.8 us  [butterfly(): lax.ppermute(value, axis, [(source, source ^ stride) for source in range(...]
    unnamed x21 -> x20, local copies, waits for them, and re-layouts: 11.2 us -> 11.2 us
  transfers between devices with their start and end apart: 25 -> 25, of which waited for: 19 -> 19; matrix products, arithmetic and copies ran while one was open for 15% -> 16% of each run, Pallas kernels for 0% -> 0%
where the time goes in v8:
time: 258 us; the launch traced here: 255 us
  starting transfers between devices  90.6 us (35%)
  waiting for transfers between devices  86.1 us (33%)
  local copies, waits for them, and re-layouts  25.8 us (10%)
  other arithmetic  18.7 us (7%)
  matrix products  18.7 us (7%)
  between operations  15.3 us (6%)
    ppermute x15, waiting for transfers between devices, butterfly(): lax.ppermute(value, axis, [(source, source ^ stride) for source in range(...  70.9 us
    ppermute x15, starting transfers between devices, butterfly(): lax.ppermute(value, axis, [(source, source ^ stride) for source in range(...  59.8 us
    ppermute x5, starting transfers between devices, from_behind(): lax.ppermute(value, axis, [(source, source + steps) for source in range(i...  16.9 us
    ppermute x3, starting transfers between devices, halving_scatter(): lax.ppermute(give, axis, [(source, source ^ bit) for source in range(coun...  13.8 us
    dot_general x1, matrix products, local(): jnp.dot(jnp.concatenate([attended, end_att], axis=0), full_weight, prefer...  12.3 us
    ppermute x3, waiting for transfers between devices, halving_scatter(): lax.ppermute(give, axis, [(source, source ^ bit) for source in range(coun...  12.1 us
    unnamed x20, local copies, waits for them, and re-layouts  11.2 us
  transfers between devices with their start and end apart: 25, of which 19 were waited for; matrix products, arithmetic and copies ran while one was open for 16% of the time, Pallas kernels for 0%

profile of v8, /device:TPU:56, one launch (start us, length us, event | category | flops | bytes accessed | tf_op | source)
XLA Modules:
  0.0 255.1 jit_solution(18387584890146171163)
XLA Ops:
  9.6 5.6 %collective-permute-start = (bf16[514,128]{1,0:T(8,128)(2,1)S(1)}, bf16[514,128]{1,0:T(8,128)(2,1)}, u32[]{:S(2)}, u32[]{:S(2)}) collective-permute-start(bf16[514,128]{1,0:T(8,128)(2,1)S(1)} %pad_maximum_fusion), channel_id=1, source_target_pairs={{0,32},{8,40},{16,48},{24,56},{32,64},{40,72},{48,80},{56,88},{64,... | collective-permute-start | bytes 394760 | tf_op jit(solution)/shard_map/ppermute | solution.py:20
  17.5 3.6 %collective-permute-start.2 = (bf16[514,128]{1,0:T(8,128)(2,1)S(1)}, bf16[514,128]{1,0:T(8,128)(2,1)}, u32[]{:S(2)}, u32[]{:S(2)}) collective-permute-start(bf16[514,128]{1,0:T(8,128)(2,1)S(1)} %pad_maximum_fusion), channel_id=1, source_target_pairs={{0,16},{8,24},{16,32},{24,40},{32,48},{40,56},{48,64},{56,72},{64,... | collective-permute-start | bytes 394760 | tf_op jit(solution)/shard_map/ppermute | solution.py:20
  21.1 4.1 %collective-permute-start.3 = (bf16[514,128]{1,0:T(8,128)(2,1)S(1)}, bf16[514,128]{1,0:T(8,128)(2,1)}, u32[]{:S(2)}, u32[]{:S(2)}) collective-permute-start(bf16[514,128]{1,0:T(8,128)(2,1)S(1)} %pad_maximum_fusion), channel_id=1, source_target_pairs={{0,8},{8,16},{16,24},{24,32},{32,40},{40,48},{48,56},{56,64},{64,7... | collective-permute-start | bytes 394760 | tf_op jit(solution)/shard_map/ppermute | solution.py:20
  58.4 3.0 %collective-permute-start.5 = (bf16[32,1792]{1,0:T(8,128)(2,1)S(1)}, bf16[32,1792]{1,0:T(8,128)(2,1)S(1)}, u32[]{:S(2)}, u32[]{:S(2)}) collective-permute-start(bf16[32,1792]{1,0:T(8,128)(2,1)S(1)} %convolution_convert_fusion.1), channel_id=1, source_target_pairs={{0,8},{8,0},{16,24},{24,16},{32,40},{40,32},{48,56},{56,48},{64,72... | collective-permute-start | bytes 344072 | tf_op jit(solution)/shard_map/ppermute | solution.py:27
  65.2 4.5 %collective-permute-done.6 = bf16[32,1792]{1,0:T(8,128)(2,1)S(1)} collective-permute-done((bf16[32,1792]{1,0:T(8,128)(2,1)S(1)}, bf16[32,1792]{1,0:T(8,128)(2,1)S(1)}, u32[]{:S(2)}, u32[]{:S(2)}) %collective-permute-start.6) | collective-permute-done | bytes 114720 | tf_op jit(solution)/shard_map/ppermute | solution.py:27
  69.7 4.0 %collective-permute-start.7 = (bf16[32,1792]{1,0:T(8,128)(2,1)S(1)}, bf16[32,1792]{1,0:T(8,128)(2,1)S(1)}, u32[]{:S(2)}, u32[]{:S(2)}) collective-permute-start(bf16[32,1792]{1,0:T(8,128)(2,1)S(1)} %add.122), channel_id=1, source_target_pairs={{0,32},{8,40},{16,48},{24,56},{32,0},{40,8},{48,16},{56,24},{64,96... | collective-permute-start | bytes 344072 | tf_op jit(solution)/shard_map/ppermute | solution.py:27
  73.8 7.2 %collective-permute-done.7 = bf16[32,1792]{1,0:T(8,128)(2,1)S(1)} collective-permute-done((bf16[32,1792]{1,0:T(8,128)(2,1)S(1)}, bf16[32,1792]{1,0:T(8,128)(2,1)S(1)}, u32[]{:S(2)}, u32[]{:S(2)}) %collective-permute-start.7) | collective-permute-done | bytes 114720 | tf_op jit(solution)/shard_map/ppermute | solution.py:27
  81.0 4.9 %collective-permute-start.8 = (bf16[32,1792]{1,0:T(8,128)(2,1)S(1)}, bf16[32,1792]{1,0:T(8,128)(2,1)S(1)}, u32[]{:S(2)}, u32[]{:S(2)}) collective-permute-start(bf16[32,1792]{1,0:T(8,128)(2,1)S(1)} %add.123), channel_id=1, source_target_pairs={{0,64},{8,72},{16,80},{24,88},{32,96},{40,104},{48,112},{56,120},{... | collective-permute-start | bytes 344072 | tf_op jit(solution)/shard_map/ppermute | solution.py:27
  85.9 4.6 %collective-permute-done.8 = bf16[32,1792]{1,0:T(8,128)(2,1)S(1)} collective-permute-done((bf16[32,1792]{1,0:T(8,128)(2,1)S(1)}, bf16[32,1792]{1,0:T(8,128)(2,1)S(1)}, u32[]{:S(2)}, u32[]{:S(2)}) %collective-permute-start.8) | collective-permute-done | bytes 114720 | tf_op jit(solution)/shard_map/ppermute | solution.py:27
  90.6 8.7 %collective-permute-start.9 = (bf16[32,1792]{1,0:T(8,128)(2,1)S(1)}, bf16[32,1792]{1,0:T(8,128)(2,1)S(1)}, u32[]{:S(2)}, u32[]{:S(2)}) collective-permute-start(bf16[32,1792]{1,0:T(8,128)(2,1)S(1)} %add.124), channel_id=1, source_target_pairs={{0,128},{8,136},{16,144},{24,152},{32,160},{40,168},{48,176},{56,1... | collective-permute-start | bytes 344072 | tf_op jit(solution)/shard_map/ppermute | solution.py:27
  99.2 6.8 %collective-permute-done.9 = bf16[32,1792]{1,0:T(8,128)(2,1)S(1)} collective-permute-done((bf16[32,1792]{1,0:T(8,128)(2,1)S(1)}, bf16[32,1792]{1,0:T(8,128)(2,1)S(1)}, u32[]{:S(2)}, u32[]{:S(2)}) %collective-permute-start.9) | collective-permute-done | bytes 114720 | tf_op jit(solution)/shard_map/ppermute | solution.py:27
  106.0 7.9 %collective-permute-start.10 = (bf16[32,1792]{1,0:T(8,128)(2,1)S(1)}, bf16[32,1792]{1,0:T(8,128)(2,1)S(1)}, u32[]{:S(2)}, u32[]{:S(2)}) collective-permute-start(bf16[32,1792]{1,0:T(8,128)(2,1)S(1)} %add.125), channel_id=1, source_target_pairs={{0,256},{8,264},{16,272},{24,280},{32,288},{40,296},{48,304},{56,3... | collective-permute-start | bytes 344072 | tf_op jit(solution)/shard_map/ppermute | solution.py:27
  113.9 6.0 %collective-permute-done.10 = bf16[32,1792]{1,0:T(8,128)(2,1)S(1)} collective-permute-done((bf16[32,1792]{1,0:T(8,128)(2,1)S(1)}, bf16[32,1792]{1,0:T(8,128)(2,1)S(1)}, u32[]{:S(2)}, u32[]{:S(2)}) %collective-permute-start.10) | collective-permute-done | bytes 114720 | tf_op jit(solution)/shard_map/ppermute | solution.py:27
  122.4 12.3 %convolution_convert_fusion = bf16[288,7168]{1,0:T(8,128)(2,1)} fusion(bf16[896,7168]{0,1:T(8,128)(2,1)} %all-gather.2.cloned.1.call-done, bf16[32,896]{0,1:T(8,128)(2,1)S(1)} %copy.44, bf16[256,896]{0,1:T(8,128)(2,1)S(1)} %bitcast.135), kind=kOutput, calls=%fused_computation | convolution fusion | flops 3702472704 | bytes 17489920 | tf_op jit(solution)/shard_map/dot_general | solution.py:160
  137.1 3.5 %collective-permute-start.11 = (bf16[32,4,896]{2,0,1:T(8,128)(2,1)S(1)}, bf16[32,4,896]{2,0,1:T(8,128)(2,1)S(1)}, u32[]{:S(2)}, u32[]{:S(2)}) collective-permute-start(bf16[32,4,896]{2,0,1:T(8,128)(2,1)S(1)} %bitcast.136), channel_id=1, source_target_pairs={{0,1},{1,0},{2,3},{3,2},{4,5},{5,4},{6,7},{7,6},{8,9},{9,8},{10,11... | collective-permute-start | bytes 688136 | tf_op jit(solution)/shard_map/ppermute | solution.py:44
  140.7 6.1 %collective-permute-done.11 = bf16[32,4,896]{2,0,1:T(8,128)(2,1)S(1)} collective-permute-done((bf16[32,4,896]{2,0,1:T(8,128)(2,1)S(1)}, bf16[32,4,896]{2,0,1:T(8,128)(2,1)S(1)}, u32[]{:S(2)}, u32[]{:S(2)}) %collective-permute-start.11) | collective-permute-done | bytes 229408 | tf_op jit(solution)/shard_map/ppermute | solution.py:44
  146.8 4.7 %collective-permute-start.12 = (bf16[32,2,896]{2,0,1:T(8,128)(2,1)S(1)}, bf16[32,2,896]{2,0,1:T(8,128)(2,1)S(1)}, u32[]{:S(2)}, u32[]{:S(2)}) collective-permute-start(bf16[32,2,896]{2,0,1:T(8,128)(2,1)S(1)} %dynamic-slice_bitcast_fusion), channel_id=1, source_target_pairs={{0,2},{1,3},{2,0},{3,1},{4,6},{5,7},{6,4},{7,5},{8,10},{9,11},{10,... | collective-permute-start | bytes 344072 | tf_op jit(solution)/shard_map/ppermute | solution.py:44
  151.6 5.2 %collective-permute-done.12 = bf16[32,2,896]{2,0,1:T(8,128)(2,1)S(1)} collective-permute-done((bf16[32,2,896]{2,0,1:T(8,128)(2,1)S(1)}, bf16[32,2,896]{2,0,1:T(8,128)(2,1)S(1)}, u32[]{:S(2)}, u32[]{:S(2)}) %collective-permute-start.12) | collective-permute-done | bytes 114720 | tf_op jit(solution)/shard_map/ppermute | solution.py:44
  156.8 5.6 %collective-permute-start.13 = (bf16[32,1,896]{2,0,1:T(8,128)(2,1)S(1)}, bf16[32,1,896]{2,0,1:T(8,128)(2,1)S(1)}, u32[]{:S(2)}, u32[]{:S(2)}) collective-permute-start(bf16[32,1,896]{2,0,1:T(8,128)(2,1)S(1)} %constant_dynamic-slice_fusion), channel_id=1, source_target_pairs={{0,4},{1,5},{2,6},{3,7},{4,0},{5,1},{6,2},{7,3},{8,12},{9,13},{10,... | collective-permute-start | bytes 172040 | tf_op jit(solution)/shard_map/ppermute | solution.py:44
  162.4 4.1 %slice.135 = bf16[256,7168]{1,0:T(8,128)(2,1)} slice(bf16[288,7168]{1,0:T(8,128)(2,1)} %convolution_convert_fusion), slice={[0:256], [0:7168]} | slice | bytes 7340032 | tf_op jit(solution)/shard_map/slice | solution.py:163
  167.4 6.0 %copy.52 = bf16[256,7168]{0,1:T(8,128)(2,1)} copy(bf16[256,7168]{1,0:T(8,128)(2,1)} %slice.135) | data formatting | bytes 7340032
  176.4 4.8 %collective-permute-done.14 = f32[32,1001]{1,0:T(8,128)S(1)} collective-permute-done((f32[32,1001]{1,0:T(8,128)S(1)}, f32[32,1001]{1,0:T(8,128)S(1)}, u32[]{:S(2)}, u32[]{:S(2)}) %collective-permute-start.14) | collective-permute-done | bytes 128160 | tf_op jit(solution)/shard_map/ppermute | solution.py:27
  181.3 3.4 %collective-permute-start.15 = (f32[32,1001]{1,0:T(8,128)S(1)}, f32[32,1001]{1,0:T(8,128)S(1)}, u32[]{:S(2)}, u32[]{:S(2)}) collective-permute-start(f32[32,1001]{1,0:T(8,128)S(1)} %fusion.64), channel_id=1, source_target_pairs={{0,2},{1,3},{2,0},{3,1},{4,6},{5,7},{6,4},{7,5},{8,10},{9,11},{10,... | collective-permute-start | bytes 384392 | tf_op jit(solution)/shard_map/ppermute | solution.py:27
  184.7 8.5 %collective-permute-done.15 = f32[32,1001]{1,0:T(8,128)S(1)} collective-permute-done((f32[32,1001]{1,0:T(8,128)S(1)}, f32[32,1001]{1,0:T(8,128)S(1)}, u32[]{:S(2)}, u32[]{:S(2)}) %collective-permute-start.15) | collective-permute-done | bytes 128160 | tf_op jit(solution)/shard_map/ppermute | solution.py:27
  193.2 5.9 %collective-permute-start.16 = (f32[32,1001]{1,0:T(8,128)S(1)}, f32[32,1001]{1,0:T(8,128)S(1)}, u32[]{:S(2)}, u32[]{:S(2)}) collective-permute-start(f32[32,1001]{1,0:T(8,128)S(1)} %add.142), channel_id=1, source_target_pairs={{0,4},{1,5},{2,6},{3,7},{4,0},{5,1},{6,2},{7,3},{8,12},{9,13},{10,... | collective-permute-start | bytes 384392 | tf_op jit(solution)/shard_map/ppermute | solution.py:27
  199.0 9.2 %collective-permute-done.16 = f32[32,1001]{1,0:T(8,128)S(1)} collective-permute-done((f32[32,1001]{1,0:T(8,128)S(1)}, f32[32,1001]{1,0:T(8,128)S(1)}, u32[]{:S(2)}, u32[]{:S(2)}) %collective-permute-start.16) | collective-permute-done | bytes 128160 | tf_op jit(solution)/shard_map/ppermute | solution.py:27
  217.6 3.1 %collective-permute-start.19 = (f32[32]{0:T(128)S(1)}, f32[32]{0:T(128)S(1)}, u32[]{:S(2)}, u32[]{:S(2)}) collective-permute-start(f32[32]{0:T(128)S(1)} %max.19), channel_id=1, source_target_pairs={{0,32},{8,40},{16,48},{24,56},{32,0},{40,8},{48,16},{56,24},{64,96... | collective-permute-start | bytes 392 | tf_op jit(solution)/shard_map/ppermute | solution.py:27
  220.7 3.8 %collective-permute-done.19 = f32[32]{0:T(128)S(1)} collective-permute-done((f32[32]{0:T(128)S(1)}, f32[32]{0:T(128)S(1)}, u32[]{:S(2)}, u32[]{:S(2)}) %collective-permute-start.19) | collective-permute-done | bytes 160 | tf_op jit(solution)/shard_map/ppermute | solution.py:27
  224.6 3.0 %collective-permute-start.20 = (f32[32]{0:T(128)S(1)}, f32[32]{0:T(128)S(1)}, u32[]{:S(2)}, u32[]{:S(2)}) collective-permute-start(f32[32]{0:T(128)S(1)} %max.20), channel_id=1, source_target_pairs={{0,64},{8,72},{16,80},{24,88},{32,96},{40,104},{48,112},{56,120},{... | collective-permute-start | bytes 392 | tf_op jit(solution)/shard_map/ppermute | solution.py:27
  231.9 4.4 %collective-permute-done.21 = f32[32]{0:T(128)S(1)} collective-permute-done((f32[32]{0:T(128)S(1)}, f32[32]{0:T(128)S(1)}, u32[]{:S(2)}, u32[]{:S(2)}) %collective-permute-start.21) | collective-permute-done | bytes 160 | tf_op jit(solution)/shard_map/ppermute | solution.py:27
  236.3 4.9 %collective-permute-start.22 = (f32[32]{0:T(128)S(1)}, f32[32]{0:T(128)S(1)}, u32[]{:S(2)}, u32[]{:S(2)}) collective-permute-start(f32[32]{0:T(128)S(1)} %max.22), channel_id=1, source_target_pairs={{0,256},{8,264},{16,272},{24,280},{32,288},{40,296},{48,304},{56,3... | collective-permute-start | bytes 392 | tf_op jit(solution)/shard_map/ppermute | solution.py:27
  242.0 3.7 %collective-permute-done.22 = f32[32]{0:T(128)S(1)} collective-permute-done((f32[32]{0:T(128)S(1)}, f32[32]{0:T(128)S(1)}, u32[]{:S(2)}, u32[]{:S(2)}) %collective-permute-start.22) | collective-permute-done | bytes 160 | tf_op jit(solution)/shard_map/ppermute | solution.py:27
  (112 shorter events, 66.8 us)
Async XLA Ops:
  7.2 166.5 %copy-start = (bf16[896,1000]{0,1:T(8,128)(2,1)S(1)}, bf16[896,1000]{0,1:T(8,128)(2,1)}, u32[]{:S(2)}) copy-start(bf16[896,1000]{0,1:T(8,128)(2,1)} %param.15) | copy-start | bytes 5376004
  7.2 35.1 %copy-start.3 = (s32[256]{0:T(256)S(1)}, s32[256]{0:T(256)}, u32[]{:S(2)}) copy-start(s32[256]{0:T(256)} %param.11) | copy-start | bytes 3076
  7.2 35.2 %copy-start.1 = (bf16[2,256,128]{2,1,0:T(8,128)(2,1)S(1)}, bf16[2,256,128]{2,1,0:T(8,128)(2,1)}, u32[]{:S(2)}) copy-start(bf16[2,256,128]{2,1,0:T(8,128)(2,1)} %param.10) | copy-start | bytes 393220
  7.2 115.2 %all-gather.2.cloned.1.call-start = ((), (), s32[]{:S(2)}) async-start(), calls=%async_computation.1 | async-start | bytes 13045760 | tf_op jit(solution)/shard_map/all_gather | solution.py:159
  7.9 238.2 %reduce-scatter.4.cloned.1.call-start = ((), (), s32[]{:S(2)}) async-start(), calls=%async_computation.2 | async-start | bytes 4128768
  9.6 26.3 %collective-permute-start = (bf16[514,128]{1,0:T(8,128)(2,1)S(1)}, bf16[514,128]{1,0:T(8,128)(2,1)}, u32[]{:S(2)}, u32[]{:S(2)}) collective-permute-start(bf16[514,128]{1,0:T(8,128)(2,1)S(1)} %pad_maximum_fusion), channel_id=1, source_target_pairs={{0,32},{8,40},{16,48},{24,56},{32,64},{40,72},{48,80},{56,88},{64,... | collective-permute-start | bytes 394760 | tf_op jit(solution)/shard_map/ppermute | solution.py:20
  15.2 21.7 %collective-permute-start.1 = (bf16[514,128]{1,0:T(8,128)(2,1)S(1)}, bf16[514,128]{1,0:T(8,128)(2,1)}, u32[]{:S(2)}, u32[]{:S(2)}) collective-permute-start(bf16[514,128]{1,0:T(8,128)(2,1)S(1)} %pad_maximum_fusion), channel_id=1, source_target_pairs={{0,24},{8,32},{16,40},{24,48},{32,56},{40,64},{48,72},{56,80},{64,... | collective-permute-start | bytes 394760 | tf_op jit(solution)/shard_map/ppermute | solution.py:20
  17.5 20.3 %collective-permute-start.2 = (bf16[514,128]{1,0:T(8,128)(2,1)S(1)}, bf16[514,128]{1,0:T(8,128)(2,1)}, u32[]{:S(2)}, u32[]{:S(2)}) collective-permute-start(bf16[514,128]{1,0:T(8,128)(2,1)S(1)} %pad_maximum_fusion), channel_id=1, source_target_pairs={{0,16},{8,24},{16,32},{24,40},{32,48},{40,56},{48,64},{56,72},{64,... | collective-permute-start | bytes 394760 | tf_op jit(solution)/shard_map/ppermute | solution.py:20
  21.1 17.6 %collective-permute-start.3 = (bf16[514,128]{1,0:T(8,128)(2,1)S(1)}, bf16[514,128]{1,0:T(8,128)(2,1)}, u32[]{:S(2)}, u32[]{:S(2)}) collective-permute-start(bf16[514,128]{1,0:T(8,128)(2,1)S(1)} %pad_maximum_fusion), channel_id=1, source_target_pairs={{0,8},{8,16},{16,24},{24,32},{32,40},{40,48},{48,56},{56,64},{64,7... | collective-permute-start | bytes 394760 | tf_op jit(solution)/shard_map/ppermute | solution.py:20
  26.4 6.8 %collective-permute-start.4 = (s32[1]{0:T(128)}, s32[1]{0:T(128)}, u32[]{:S(2)}, u32[]{:S(2)}) collective-permute-start(s32[1]{0:T(128)} %slice.109), channel_id=1, source_target_pairs={{8,0},{16,8},{24,16},{32,24},{40,32},{48,40},{56,48},{64,56},{72,6... | collective-permute-start | bytes 20 | tf_op jit(solution)/shard_map/ppermute | solution.py:20
  58.4 4.0 %collective-permute-start.5 = (bf16[32,1792]{1,0:T(8,128)(2,1)S(1)}, bf16[32,1792]{1,0:T(8,128)(2,1)S(1)}, u32[]{:S(2)}, u32[]{:S(2)}) collective-permute-start(bf16[32,1792]{1,0:T(8,128)(2,1)S(1)} %convolution_convert_fusion.1), channel_id=1, source_target_pairs={{0,8},{8,0},{16,24},{24,16},{32,40},{40,32},{48,56},{56,48},{64,72... | collective-permute-start | bytes 344072 | tf_op jit(solution)/shard_map/ppermute | solution.py:27
  62.4 7.3 %collective-permute-start.6 = (bf16[32,1792]{1,0:T(8,128)(2,1)S(1)}, bf16[32,1792]{1,0:T(8,128)(2,1)S(1)}, u32[]{:S(2)}, u32[]{:S(2)}) collective-permute-start(bf16[32,1792]{1,0:T(8,128)(2,1)S(1)} %add.121), channel_id=1, source_target_pairs={{0,16},{8,24},{16,0},{24,8},{32,48},{40,56},{48,32},{56,40},{64,80... | collective-permute-start | bytes 344072 | tf_op jit(solution)/shard_map/ppermute | solution.py:27
  69.7 11.2 %collective-permute-start.7 = (bf16[32,1792]{1,0:T(8,128)(2,1)S(1)}, bf16[32,1792]{1,0:T(8,128)(2,1)S(1)}, u32[]{:S(2)}, u32[]{:S(2)}) collective-permute-start(bf16[32,1792]{1,0:T(8,128)(2,1)S(1)} %add.122), channel_id=1, source_target_pairs={{0,32},{8,40},{16,48},{24,56},{32,0},{40,8},{48,16},{56,24},{64,96... | collective-permute-start | bytes 344072 | tf_op jit(solution)/shard_map/ppermute | solution.py:27
  81.0 9.5 %collective-permute-start.8 = (bf16[32,1792]{1,0:T(8,128)(2,1)S(1)}, bf16[32,1792]{1,0:T(8,128)(2,1)S(1)}, u32[]{:S(2)}, u32[]{:S(2)}) collective-permute-start(bf16[32,1792]{1,0:T(8,128)(2,1)S(1)} %add.123), channel_id=1, source_target_pairs={{0,64},{8,72},{16,80},{24,88},{32,96},{40,104},{48,112},{56,120},{... | collective-permute-start | bytes 344072 | tf_op jit(solution)/shard_map/ppermute | solution.py:27
  90.6 15.4 %collective-permute-start.9 = (bf16[32,1792]{1,0:T(8,128)(2,1)S(1)}, bf16[32,1792]{1,0:T(8,128)(2,1)S(1)}, u32[]{:S(2)}, u32[]{:S(2)}) collective-permute-start(bf16[32,1792]{1,0:T(8,128)(2,1)S(1)} %add.124), channel_id=1, source_target_pairs={{0,128},{8,136},{16,144},{24,152},{32,160},{40,168},{48,176},{56,1... | collective-permute-start | bytes 344072 | tf_op jit(solution)/shard_map/ppermute | solution.py:27
  106.0 13.8 %collective-permute-start.10 = (bf16[32,1792]{1,0:T(8,128)(2,1)S(1)}, bf16[32,1792]{1,0:T(8,128)(2,1)S(1)}, u32[]{:S(2)}, u32[]{:S(2)}) collective-permute-start(bf16[32,1792]{1,0:T(8,128)(2,1)S(1)} %add.125), channel_id=1, source_target_pairs={{0,256},{8,264},{16,272},{24,280},{32,288},{40,296},{48,304},{56,3... | collective-permute-start | bytes 344072 | tf_op jit(solution)/shard_map/ppermute | solution.py:27
  137.1 9.7 %collective-permute-start.11 = (bf16[32,4,896]{2,0,1:T(8,128)(2,1)S(1)}, bf16[32,4,896]{2,0,1:T(8,128)(2,1)S(1)}, u32[]{:S(2)}, u32[]{:S(2)}) collective-permute-start(bf16[32,4,896]{2,0,1:T(8,128)(2,1)S(1)} %bitcast.136), channel_id=1, source_target_pairs={{0,1},{1,0},{2,3},{3,2},{4,5},{5,4},{6,7},{7,6},{8,9},{9,8},{10,11... | collective-permute-start | bytes 688136 | tf_op jit(solution)/shard_map/ppermute | solution.py:44
  146.8 9.9 %collective-permute-start.12 = (bf16[32,2,896]{2,0,1:T(8,128)(2,1)S(1)}, bf16[32,2,896]{2,0,1:T(8,128)(2,1)S(1)}, u32[]{:S(2)}, u32[]{:S(2)}) collective-permute-start(bf16[32,2,896]{2,0,1:T(8,128)(2,1)S(1)} %dynamic-slice_bitcast_fusion), channel_id=1, source_target_pairs={{0,2},{1,3},{2,0},{3,1},{4,6},{5,7},{6,4},{7,5},{8,10},{9,11},{10,... | collective-permute-start | bytes 344072 | tf_op jit(solution)/shard_map/ppermute | solution.py:44
  156.8 10.6 %collective-permute-start.13 = (bf16[32,1,896]{2,0,1:T(8,128)(2,1)S(1)}, bf16[32,1,896]{2,0,1:T(8,128)(2,1)S(1)}, u32[]{:S(2)}, u32[]{:S(2)}) collective-permute-start(bf16[32,1,896]{2,0,1:T(8,128)(2,1)S(1)} %constant_dynamic-slice_fusion), channel_id=1, source_target_pairs={{0,4},{1,5},{2,6},{3,7},{4,0},{5,1},{6,2},{7,3},{8,12},{9,13},{10,... | collective-permute-start | bytes 172040 | tf_op jit(solution)/shard_map/ppermute | solution.py:44
  166.5 6.9 %copy-start.4 = (bf16[896]{0:T(1024)(128)(2,1)S(1)}, bf16[896]{0:T(1024)(128)(2,1)}, u32[]{:S(2)}) copy-start(bf16[896]{0:T(1024)(128)(2,1)} %param.14) | copy-start | bytes 5380
  167.4 80.0 %copy-start.2 = (bf16[256,896]{1,0:T(8,128)(2,1)S(1)}, bf16[256,896]{1,0:T(8,128)(2,1)}, u32[]{:S(2)}) copy-start(bf16[256,896]{1,0:T(8,128)(2,1)} %param.12) | copy-start | bytes 1376260
  174.4 6.9 %collective-permute-start.14 = (f32[32,1001]{1,0:T(8,128)S(1)}, f32[32,1001]{1,0:T(8,128)S(1)}, u32[]{:S(2)}, u32[]{:S(2)}) collective-permute-start(f32[32,1001]{1,0:T(8,128)S(1)} %pad_maximum_fusion.1), channel_id=1, source_target_pairs={{0,1},{1,0},{2,3},{3,2},{4,5},{5,4},{6,7},{7,6},{8,9},{9,8},{10,11... | collective-permute-start | bytes 384392 | tf_op jit(solution)/shard_map/ppermute | solution.py:27
  181.3 11.8 %collective-permute-start.15 = (f32[32,1001]{1,0:T(8,128)S(1)}, f32[32,1001]{1,0:T(8,128)S(1)}, u32[]{:S(2)}, u32[]{:S(2)}) collective-permute-start(f32[32,1001]{1,0:T(8,128)S(1)} %fusion.64), channel_id=1, source_target_pairs={{0,2},{1,3},{2,0},{3,1},{4,6},{5,7},{6,4},{7,5},{8,10},{9,11},{10,... | collective-permute-start | bytes 384392 | tf_op jit(solution)/shard_map/ppermute | solution.py:27
  193.2 15.1 %collective-permute-start.16 = (f32[32,1001]{1,0:T(8,128)S(1)}, f32[32,1001]{1,0:T(8,128)S(1)}, u32[]{:S(2)}, u32[]{:S(2)}) collective-permute-start(f32[32,1001]{1,0:T(8,128)S(1)} %add.142), channel_id=1, source_target_pairs={{0,4},{1,5},{2,6},{3,7},{4,0},{5,1},{6,2},{7,3},{8,12},{9,13},{10,... | collective-permute-start | bytes 384392 | tf_op jit(solution)/shard_map/ppermute | solution.py:27
  209.2 3.0 %collective-permute-start.17 = (f32[32]{0:T(128)S(1)}, f32[32]{0:T(128)S(1)}, u32[]{:S(2)}, u32[]{:S(2)}) collective-permute-start(f32[32]{0:T(128)S(1)} %fusion.41), channel_id=1, source_target_pairs={{0,8},{8,0},{16,24},{24,16},{32,40},{40,32},{48,56},{56,48},{64,72... | collective-permute-start | bytes 392 | tf_op jit(solution)/shard_map/ppermute | solution.py:27
  212.2 5.4 %collective-permute-start.18 = (f32[32]{0:T(128)S(1)}, f32[32]{0:T(128)S(1)}, u32[]{:S(2)}, u32[]{:S(2)}) collective-permute-start(f32[32]{0:T(128)S(1)} %max.18), channel_id=1, source_target_pairs={{0,16},{8,24},{16,0},{24,8},{32,48},{40,56},{48,32},{56,40},{64,80... | collective-permute-start | bytes 392 | tf_op jit(solution)/shard_map/ppermute | solution.py:27
  217.6 6.9 %collective-permute-start.19 = (f32[32]{0:T(128)S(1)}, f32[32]{0:T(128)S(1)}, u32[]{:S(2)}, u32[]{:S(2)}) collective-permute-start(f32[32]{0:T(128)S(1)} %max.19), channel_id=1, source_target_pairs={{0,32},{8,40},{16,48},{24,56},{32,0},{40,8},{48,16},{56,24},{64,96... | collective-permute-start | bytes 392 | tf_op jit(solution)/shard_map/ppermute | solution.py:27
  224.6 5.4 %collective-permute-start.20 = (f32[32]{0:T(128)S(1)}, f32[32]{0:T(128)S(1)}, u32[]{:S(2)}, u32[]{:S(2)}) collective-permute-start(f32[32]{0:T(128)S(1)} %max.20), channel_id=1, source_target_pairs={{0,64},{8,72},{16,80},{24,88},{32,96},{40,104},{48,112},{56,120},{... | collective-permute-start | bytes 392 | tf_op jit(solution)/shard_map/ppermute | solution.py:27
  230.0 6.3 %collective-permute-start.21 = (f32[32]{0:T(128)S(1)}, f32[32]{0:T(128)S(1)}, u32[]{:S(2)}, u32[]{:S(2)}) collective-permute-start(f32[32]{0:T(128)S(1)} %max.21), channel_id=1, source_target_pairs={{0,128},{8,136},{16,144},{24,152},{32,160},{40,168},{48,176},{56,1... | collective-permute-start | bytes 392 | tf_op jit(solution)/shard_map/ppermute | solution.py:27
  236.3 9.3 %collective-permute-start.22 = (f32[32]{0:T(128)S(1)}, f32[32]{0:T(128)S(1)}, u32[]{:S(2)}, u32[]{:S(2)}) collective-permute-start(f32[32]{0:T(128)S(1)} %max.22), channel_id=1, source_target_pairs={{0,256},{8,264},{16,272},{24,280},{32,288},{40,296},{48,304},{56,3... | collective-permute-start | bytes 392 | tf_op jit(solution)/shard_map/ppermute | solution.py:27
Sparse Core Ops, SparseCore 0:
  11.3 111.0 all-gather.1
  173.5 56.0 reduce-scatter.3

commit v9 on v8

--- a/solution.py
+++ b/solution.py
@@ -33,8 +33,8 @@
 def halving_scatter(value, axis):
     count = lax.axis_size(axis)
     index = lax.axis_index(axis)
-    rows, width = value.shape[0], value.shape[1] // count
-    held = value.reshape(rows, count, width)
+    rows, width = value.shape[1], value.shape[2]
+    held = jnp.moveaxis(value, 0, 1)
     bit = 1
     while bit < count:
         mine = (index // bit) % 2
@@ -157,13 +157,17 @@
     end_att, end_res = end_rows[:, : attended.shape[1]], end_rows[:, attended.shape[1] :]
 
     full_weight = lax.all_gather(out_weight, "req", axis=1, tiled=True)
-    both = jnp.dot(
-        jnp.concatenate([attended, end_att], axis=0), full_weight, preferred_element_type=jnp.float32
-    ).astype(jnp.bfloat16)
-    projected, end_part = both[:tok_rows], both[tok_rows:]
+    groups = lax.axis_size("tp")
+    both = jnp.einsum(
+        "tk,kgn->gtn",
+        jnp.concatenate([attended, end_att], axis=0),
+        full_weight.reshape(full_weight.shape[0], groups, -1),
+        preferred_element_type=jnp.float32,
+    ).astype(jnp.bfloat16)
+    projected, end_part = both[:, :tok_rows], both[:, tok_rows:]
     end_sum = halving_scatter(end_part, "tp")
     projected, end_sum = lax.optimization_barrier((projected, end_sum))
-    own_share = lax.psum_scatter(projected, "tp", scatter_dimension=1, tiled=True).astype(jnp.float32)
+    own_share = lax.psum_scatter(projected, "tp", scatter_dimension=0, tiled=True)[0].astype(jnp.float32)
     hidden = (residual.astype(jnp.float32) + own_share).astype(jnp.bfloat16)
     last_state = (end_res.astype(jnp.float32) + end_sum).astype(jnp.bfloat16).astype(jnp.float32)
     scaled = (last_state * head_gain.astype(jnp.float32)).astype(jnp.bfloat16)

time: 258 us -> 253 us (0.981)
  local copies, waits for them, and re-layouts: 25.8 us -> 18.1 us
    unnamed x20 -> x15, local copies, waits for them, and re-layouts: 11.2 us -> 3.92 us
where the time goes in v9:
time: 253 us; the launch traced here: 250 us
  starting transfers between devices  92.2 us (36%)
  waiting for transfers between devices  84 us (33%)
  matrix products  21 us (8%)
  other arithmetic  19.1 us (8%)
  local copies, waits for them, and re-layouts  18.1 us (7%)
  between operations  15.3 us (6%)
    ppermute x15, waiting for transfers between devices, butterfly(): lax.ppermute(value, axis, [(source, source ^ stride) for source in range(...  68.9 us
    ppermute x15, starting transfers between devices, butterfly(): lax.ppermute(value, axis, [(source, source ^ stride) for source in range(...  61.6 us
    ppermute x5, starting transfers between devices, from_behind(): lax.ppermute(value, axis, [(source, source + steps) for source in range(i...  16.9 us
    dot_general x1, matrix products, local(): jnp.einsum('tk,kgn->gtn', jnp.concatenate([attended, end_att], axis=0), f...  14.6 us
    ppermute x3, starting transfers between devices, halving_scatter(): lax.ppermute(give, axis, [(source, source ^ bit) for source in range(coun...  13.6 us
    ppermute x3, waiting for transfers between devices, halving_scatter(): lax.ppermute(give, axis, [(source, source ^ bit) for source in range(coun...  12.3 us
    slice x2, local copies, waits for them, and re-layouts, local(): projected, end_part = (both[:, :tok_rows], both[:, tok_rows:])  5.2 us
  transfers between devices with their start and end apart: 25, of which 19 were waited for; matrix products, arithmetic and copies ran while one was open for 16% of the time, Pallas kernels for 0%

profile of v9, /device:TPU:56, one launch (start us, length us, event | category | flops | bytes accessed | tf_op | source)
XLA Modules:
  0.0 249.8 jit_solution(17636056389491594181)
XLA Ops:
  9.6 4.9 %collective-permute-start = (bf16[514,128]{1,0:T(8,128)(2,1)S(1)}, bf16[514,128]{1,0:T(8,128)(2,1)S(1)}, u32[]{:S(2)}, u32[]{:S(2)}) collective-permute-start(bf16[514,128]{1,0:T(8,128)(2,1)S(1)} %pad_maximum_fusion), channel_id=1, source_target_pairs={{0,32},{8,40},{16,48},{24,56},{32,64},{40,72},{48,80},{56,88},{64,... | collective-permute-start | bytes 394760 | tf_op jit(solution)/shard_map/ppermute | solution.py:20
  16.8 4.2 %collective-permute-start.2 = (bf16[514,128]{1,0:T(8,128)(2,1)S(1)}, bf16[514,128]{1,0:T(8,128)(2,1)}, u32[]{:S(2)}, u32[]{:S(2)}) collective-permute-start(bf16[514,128]{1,0:T(8,128)(2,1)S(1)} %pad_maximum_fusion), channel_id=1, source_target_pairs={{0,16},{8,24},{16,32},{24,40},{32,48},{40,56},{48,64},{56,72},{64,... | collective-permute-start | bytes 394760 | tf_op jit(solution)/shard_map/ppermute | solution.py:20
  21.1 4.1 %collective-permute-start.3 = (bf16[514,128]{1,0:T(8,128)(2,1)S(1)}, bf16[514,128]{1,0:T(8,128)(2,1)}, u32[]{:S(2)}, u32[]{:S(2)}) collective-permute-start(bf16[514,128]{1,0:T(8,128)(2,1)S(1)} %pad_maximum_fusion), channel_id=1, source_target_pairs={{0,8},{8,16},{16,24},{24,32},{32,40},{40,48},{48,56},{56,64},{64,7... | collective-permute-start | bytes 394760 | tf_op jit(solution)/shard_map/ppermute | solution.py:20
  47.5 3.0 %fusion.25 = (bf16[1280,1,64]{2,0,1:T(8,128)(2,1)S(1)}, bf16[1280,1,64]{2,0,1:T(8,128)(2,1)S(1)}) fusion(f32[1280,1,128]{2,0,1:T(8,128)S(1)} %fusion.37, f32[64]{0:T(128)S(1)} %negate_power_fusion, f32[1280]{0:T(1024)S(1)} %convert_subtract_fusion), kind=kLoop, calls=%fused_computation.29 | loop fusion | flops 737280 | bytes 988416 | tf_op jit(solution)/shard_map/convert.19
  58.5 3.0 %collective-permute-start.5 = (bf16[32,1792]{1,0:T(8,128)(2,1)S(1)}, bf16[32,1792]{1,0:T(8,128)(2,1)S(1)}, u32[]{:S(2)}, u32[]{:S(2)}) collective-permute-start(bf16[32,1792]{1,0:T(8,128)(2,1)S(1)} %convolution_convert_fusion), channel_id=1, source_target_pairs={{0,8},{8,0},{16,24},{24,16},{32,40},{40,32},{48,56},{56,48},{64,72... | collective-permute-start | bytes 344072 | tf_op jit(solution)/shard_map/ppermute | solution.py:27
  65.2 4.6 %collective-permute-done.6 = bf16[32,1792]{1,0:T(8,128)(2,1)S(1)} collective-permute-done((bf16[32,1792]{1,0:T(8,128)(2,1)S(1)}, bf16[32,1792]{1,0:T(8,128)(2,1)S(1)}, u32[]{:S(2)}, u32[]{:S(2)}) %collective-permute-start.6) | collective-permute-done | bytes 114720 | tf_op jit(solution)/shard_map/ppermute | solution.py:27
  69.9 4.0 %collective-permute-start.7 = (bf16[32,1792]{1,0:T(8,128)(2,1)S(1)}, bf16[32,1792]{1,0:T(8,128)(2,1)S(1)}, u32[]{:S(2)}, u32[]{:S(2)}) collective-permute-start(bf16[32,1792]{1,0:T(8,128)(2,1)S(1)} %add.122), channel_id=1, source_target_pairs={{0,32},{8,40},{16,48},{24,56},{32,0},{40,8},{48,16},{56,24},{64,96... | collective-permute-start | bytes 344072 | tf_op jit(solution)/shard_map/ppermute | solution.py:27
  73.8 7.3 %collective-permute-done.7 = bf16[32,1792]{1,0:T(8,128)(2,1)S(1)} collective-permute-done((bf16[32,1792]{1,0:T(8,128)(2,1)S(1)}, bf16[32,1792]{1,0:T(8,128)(2,1)S(1)}, u32[]{:S(2)}, u32[]{:S(2)}) %collective-permute-start.7) | collective-permute-done | bytes 114720 | tf_op jit(solution)/shard_map/ppermute | solution.py:27
  81.1 4.9 %collective-permute-start.8 = (bf16[32,1792]{1,0:T(8,128)(2,1)S(1)}, bf16[32,1792]{1,0:T(8,128)(2,1)S(1)}, u32[]{:S(2)}, u32[]{:S(2)}) collective-permute-start(bf16[32,1792]{1,0:T(8,128)(2,1)S(1)} %add.123), channel_id=1, source_target_pairs={{0,64},{8,72},{16,80},{24,88},{32,96},{40,104},{48,112},{56,120},{... | collective-permute-start | bytes 344072 | tf_op jit(solution)/shard_map/ppermute | solution.py:27
  86.0 4.6 %collective-permute-done.8 = bf16[32,1792]{1,0:T(8,128)(2,1)S(1)} collective-permute-done((bf16[32,1792]{1,0:T(8,128)(2,1)S(1)}, bf16[32,1792]{1,0:T(8,128)(2,1)S(1)}, u32[]{:S(2)}, u32[]{:S(2)}) %collective-permute-start.8) | collective-permute-done | bytes 114720 | tf_op jit(solution)/shard_map/ppermute | solution.py:27
  90.7 8.7 %collective-permute-start.9 = (bf16[32,1792]{1,0:T(8,128)(2,1)S(1)}, bf16[32,1792]{1,0:T(8,128)(2,1)S(1)}, u32[]{:S(2)}, u32[]{:S(2)}) collective-permute-start(bf16[32,1792]{1,0:T(8,128)(2,1)S(1)} %add.124), channel_id=1, source_target_pairs={{0,128},{8,136},{16,144},{24,152},{32,160},{40,168},{48,176},{56,1... | collective-permute-start | bytes 344072 | tf_op jit(solution)/shard_map/ppermute | solution.py:27
  99.4 6.7 %collective-permute-done.9 = bf16[32,1792]{1,0:T(8,128)(2,1)S(1)} collective-permute-done((bf16[32,1792]{1,0:T(8,128)(2,1)S(1)}, bf16[32,1792]{1,0:T(8,128)(2,1)S(1)}, u32[]{:S(2)}, u32[]{:S(2)}) %collective-permute-start.9) | collective-permute-done | bytes 114720 | tf_op jit(solution)/shard_map/ppermute | solution.py:27
  106.2 7.9 %collective-permute-start.10 = (bf16[32,1792]{1,0:T(8,128)(2,1)S(1)}, bf16[32,1792]{1,0:T(8,128)(2,1)S(1)}, u32[]{:S(2)}, u32[]{:S(2)}) collective-permute-start(bf16[32,1792]{1,0:T(8,128)(2,1)S(1)} %add.125), channel_id=1, source_target_pairs={{0,256},{8,264},{16,272},{24,280},{32,288},{40,296},{48,304},{56,3... | collective-permute-start | bytes 344072 | tf_op jit(solution)/shard_map/ppermute | solution.py:27
  114.1 5.8 %collective-permute-done.10 = bf16[32,1792]{1,0:T(8,128)(2,1)S(1)} collective-permute-done((bf16[32,1792]{1,0:T(8,128)(2,1)S(1)}, bf16[32,1792]{1,0:T(8,128)(2,1)S(1)}, u32[]{:S(2)}, u32[]{:S(2)}) %collective-permute-start.10) | collective-permute-done | bytes 114720 | tf_op jit(solution)/shard_map/ppermute | solution.py:27
  122.4 14.6 %convert_bitcast_fusion = bf16[8,288,896]{2,1,0:T(8,128)(2,1)} fusion(bf16[896,8,896]{0,2,1:T(8,128)(2,1)} %bitcast.147, bf16[32,896]{1,0:T(8,128)(2,1)S(1)} %slice.111, bf16[256,896]{1,0:T(8,128)(2,1)S(1)} %copy.33), kind=kOutput, calls=%fused_computation.9 | convolution fusion | flops 3702472704 | bytes 17489920 | tf_op jit(solution)/shard_map/tk,kgn->gtn/dot_general | solution.py:161
  138.1 3.4 %collective-permute-start.11 = (bf16[32,4,896]{2,0,1:T(8,128)(2,1)S(1)}, bf16[32,4,896]{2,0,1:T(8,128)(2,1)S(1)}, u32[]{:S(2)}, u32[]{:S(2)}) collective-permute-start(bf16[32,4,896]{2,0,1:T(8,128)(2,1)S(1)} %dynamic-slice_bitcast_fusion), channel_id=1, source_target_pairs={{0,1},{1,0},{2,3},{3,2},{4,5},{5,4},{6,7},{7,6},{8,9},{9,8},{10,11... | collective-permute-start | bytes 688136 | tf_op jit(solution)/shard_map/ppermute | solution.py:44
  141.5 6.2 %collective-permute-done.11 = bf16[32,4,896]{2,0,1:T(8,128)(2,1)S(1)} collective-permute-done((bf16[32,4,896]{2,0,1:T(8,128)(2,1)S(1)}, bf16[32,4,896]{2,0,1:T(8,128)(2,1)S(1)}, u32[]{:S(2)}, u32[]{:S(2)}) %collective-permute-start.11) | collective-permute-done | bytes 229408 | tf_op jit(solution)/shard_map/ppermute | solution.py:44
  147.9 4.6 %collective-permute-start.12 = (bf16[32,2,896]{2,0,1:T(8,128)(2,1)S(1)}, bf16[32,2,896]{2,0,1:T(8,128)(2,1)S(1)}, u32[]{:S(2)}, u32[]{:S(2)}) collective-permute-start(bf16[32,2,896]{2,0,1:T(8,128)(2,1)S(1)} %dynamic-slice_bitcast_fusion.1), channel_id=1, source_target_pairs={{0,2},{1,3},{2,0},{3,1},{4,6},{5,7},{6,4},{7,5},{8,10},{9,11},{10,... | collective-permute-start | bytes 344072 | tf_op jit(solution)/shard_map/ppermute | solution.py:44
  152.5 5.3 %collective-permute-done.12 = bf16[32,2,896]{2,0,1:T(8,128)(2,1)S(1)} collective-permute-done((bf16[32,2,896]{2,0,1:T(8,128)(2,1)S(1)}, bf16[32,2,896]{2,0,1:T(8,128)(2,1)S(1)}, u32[]{:S(2)}, u32[]{:S(2)}) %collective-permute-start.12) | collective-permute-done | bytes 114720 | tf_op jit(solution)/shard_map/ppermute | solution.py:44
  157.8 5.7 %collective-permute-start.13 = (bf16[32,1,896]{2,0,1:T(8,128)(2,1)S(1)}, bf16[32,1,896]{2,0,1:T(8,128)(2,1)S(1)}, u32[]{:S(2)}, u32[]{:S(2)}) collective-permute-start(bf16[32,1,896]{2,0,1:T(8,128)(2,1)S(1)} %constant_dynamic-slice_fusion), channel_id=1, source_target_pairs={{0,4},{1,5},{2,6},{3,7},{4,0},{5,1},{6,2},{7,3},{8,12},{9,13},{10,... | collective-permute-start | bytes 172040 | tf_op jit(solution)/shard_map/ppermute | solution.py:44
  163.5 4.1 %slice.135 = bf16[8,256,896]{2,1,0:T(8,128)(2,1)} slice(bf16[8,288,896]{2,1,0:T(8,128)(2,1)} %convert_bitcast_fusion), slice={[0:8], [0:256], [0:896]} | slice | bytes 7340032 | tf_op jit(solution)/shard_map/slice | solution.py:167
  171.3 4.9 %collective-permute-done.14 = f32[32,1001]{1,0:T(8,128)S(1)} collective-permute-done((f32[32,1001]{1,0:T(8,128)S(1)}, f32[32,1001]{1,0:T(8,128)S(1)}, u32[]{:S(2)}, u32[]{:S(2)}) %collective-permute-start.14) | collective-permute-done | bytes 128160 | tf_op jit(solution)/shard_map/ppermute | solution.py:27
  176.3 3.2 %collective-permute-start.15 = (f32[32,1001]{1,0:T(8,128)S(1)}, f32[32,1001]{1,0:T(8,128)S(1)}, u32[]{:S(2)}, u32[]{:S(2)}) collective-permute-start(f32[32,1001]{1,0:T(8,128)S(1)} %fusion.64), channel_id=1, source_target_pairs={{0,2},{1,3},{2,0},{3,1},{4,6},{5,7},{6,4},{7,5},{8,10},{9,11},{10,... | collective-permute-start | bytes 384392 | tf_op jit(solution)/shard_map/ppermute | solution.py:27
  179.6 8.6 %collective-permute-done.15 = f32[32,1001]{1,0:T(8,128)S(1)} collective-permute-done((f32[32,1001]{1,0:T(8,128)S(1)}, f32[32,1001]{1,0:T(8,128)S(1)}, u32[]{:S(2)}, u32[]{:S(2)}) %collective-permute-start.15) | collective-permute-done | bytes 128160 | tf_op jit(solution)/shard_map/ppermute | solution.py:27
  188.2 5.7 %collective-permute-start.16 = (f32[32,1001]{1,0:T(8,128)S(1)}, f32[32,1001]{1,0:T(8,128)S(1)}, u32[]{:S(2)}, u32[]{:S(2)}) collective-permute-start(f32[32,1001]{1,0:T(8,128)S(1)} %add.142), channel_id=1, source_target_pairs={{0,4},{1,5},{2,6},{3,7},{4,0},{5,1},{6,2},{7,3},{8,12},{9,13},{10,... | collective-permute-start | bytes 384392 | tf_op jit(solution)/shard_map/ppermute | solution.py:27
  193.8 9.3 %collective-permute-done.16 = f32[32,1001]{1,0:T(8,128)S(1)} collective-permute-done((f32[32,1001]{1,0:T(8,128)S(1)}, f32[32,1001]{1,0:T(8,128)S(1)}, u32[]{:S(2)}, u32[]{:S(2)}) %collective-permute-start.16) | collective-permute-done | bytes 128160 | tf_op jit(solution)/shard_map/ppermute | solution.py:27
  212.5 3.8 %collective-permute-start.19 = (f32[32]{0:T(128)S(1)}, f32[32]{0:T(128)S(1)}, u32[]{:S(2)}, u32[]{:S(2)}) collective-permute-start(f32[32]{0:T(128)S(1)} %max.19), channel_id=1, source_target_pairs={{0,32},{8,40},{16,48},{24,56},{32,0},{40,8},{48,16},{56,24},{64,96... | collective-permute-start | bytes 392 | tf_op jit(solution)/shard_map/ppermute | solution.py:27
  216.3 3.1 %collective-permute-done.19 = f32[32]{0:T(128)S(1)} collective-permute-done((f32[32]{0:T(128)S(1)}, f32[32]{0:T(128)S(1)}, u32[]{:S(2)}, u32[]{:S(2)}) %collective-permute-start.19) | collective-permute-done | bytes 160 | tf_op jit(solution)/shard_map/ppermute | solution.py:27
  219.4 3.4 %collective-permute-start.20 = (f32[32]{0:T(128)S(1)}, f32[32]{0:T(128)S(1)}, u32[]{:S(2)}, u32[]{:S(2)}) collective-permute-start(f32[32]{0:T(128)S(1)} %max.20), channel_id=1, source_target_pairs={{0,64},{8,72},{16,80},{24,88},{32,96},{40,104},{48,112},{56,120},{... | collective-permute-start | bytes 392 | tf_op jit(solution)/shard_map/ppermute | solution.py:27
  226.9 4.3 %collective-permute-done.21 = f32[32]{0:T(128)S(1)} collective-permute-done((f32[32]{0:T(128)S(1)}, f32[32]{0:T(128)S(1)}, u32[]{:S(2)}, u32[]{:S(2)}) %collective-permute-start.21) | collective-permute-done | bytes 160 | tf_op jit(solution)/shard_map/ppermute | solution.py:27
  231.2 5.7 %collective-permute-start.22 = (f32[32]{0:T(128)S(1)}, f32[32]{0:T(128)S(1)}, u32[]{:S(2)}, u32[]{:S(2)}) collective-permute-start(f32[32]{0:T(128)S(1)} %max.22), channel_id=1, source_target_pairs={{0,256},{8,264},{16,272},{24,280},{32,288},{40,296},{48,304},{56,3... | collective-permute-start | bytes 392 | tf_op jit(solution)/shard_map/ppermute | solution.py:27
  237.6 2.9 %collective-permute-done.22 = f32[32]{0:T(128)S(1)} collective-permute-done((f32[32]{0:T(128)S(1)}, f32[32]{0:T(128)S(1)}, u32[]{:S(2)}, u32[]{:S(2)}) %collective-permute-start.22) | collective-permute-done | bytes 160 | tf_op jit(solution)/shard_map/ppermute | solution.py:27
  (106 shorter events, 61.9 us)
Async XLA Ops:
  7.2 161.5 %copy-start = (bf16[896,1000]{0,1:T(8,128)(2,1)S(1)}, bf16[896,1000]{0,1:T(8,128)(2,1)}, u32[]{:S(2)}) copy-start(bf16[896,1000]{0,1:T(8,128)(2,1)} %param.15) | copy-start | bytes 5376004
  7.2 39.2 %copy-start.2 = (s32[256]{0:T(256)S(1)}, s32[256]{0:T(256)}, u32[]{:S(2)}) copy-start(s32[256]{0:T(256)} %param.11) | copy-start | bytes 3076
  7.2 115.2 %all-gather.2.cloned.1.call-start = ((), (), s32[]{:S(2)}) async-start(), calls=%async_computation.1 | async-start | bytes 13045760 | tf_op jit(solution)/shard_map/all_gather | solution.py:159
  7.9 233.1 %reduce-scatter.2.cloned.1.call-start = ((), (), s32[]{:S(2)}) async-start(), calls=%async_computation.2 | async-start | bytes 4128768 | tf_op jit(solution)/shard_map/reduce_scatter | solution.py:170
  9.6 26.4 %collective-permute-start = (bf16[514,128]{1,0:T(8,128)(2,1)S(1)}, bf16[514,128]{1,0:T(8,128)(2,1)S(1)}, u32[]{:S(2)}, u32[]{:S(2)}) collective-permute-start(bf16[514,128]{1,0:T(8,128)(2,1)S(1)} %pad_maximum_fusion), channel_id=1, source_target_pairs={{0,32},{8,40},{16,48},{24,56},{32,64},{40,72},{48,80},{56,88},{64,... | collective-permute-start | bytes 394760 | tf_op jit(solution)/shard_map/ppermute | solution.py:20
  14.5 21.4 %collective-permute-start.1 = (bf16[514,128]{1,0:T(8,128)(2,1)S(1)}, bf16[514,128]{1,0:T(8,128)(2,1)}, u32[]{:S(2)}, u32[]{:S(2)}) collective-permute-start(bf16[514,128]{1,0:T(8,128)(2,1)S(1)} %pad_maximum_fusion), channel_id=1, source_target_pairs={{0,24},{8,32},{16,40},{24,48},{32,56},{40,64},{48,72},{56,80},{64,... | collective-permute-start | bytes 394760 | tf_op jit(solution)/shard_map/ppermute | solution.py:20
  16.8 20.1 %collective-permute-start.2 = (bf16[514,128]{1,0:T(8,128)(2,1)S(1)}, bf16[514,128]{1,0:T(8,128)(2,1)}, u32[]{:S(2)}, u32[]{:S(2)}) collective-permute-start(bf16[514,128]{1,0:T(8,128)(2,1)S(1)} %pad_maximum_fusion), channel_id=1, source_target_pairs={{0,16},{8,24},{16,32},{24,40},{32,48},{40,56},{48,64},{56,72},{64,... | collective-permute-start | bytes 394760 | tf_op jit(solution)/shard_map/ppermute | solution.py:20
  21.1 16.7 %collective-permute-start.3 = (bf16[514,128]{1,0:T(8,128)(2,1)S(1)}, bf16[514,128]{1,0:T(8,128)(2,1)}, u32[]{:S(2)}, u32[]{:S(2)}) collective-permute-start(bf16[514,128]{1,0:T(8,128)(2,1)S(1)} %pad_maximum_fusion), channel_id=1, source_target_pairs={{0,8},{8,16},{16,24},{24,32},{32,40},{40,48},{48,56},{56,64},{64,7... | collective-permute-start | bytes 394760 | tf_op jit(solution)/shard_map/ppermute | solution.py:20
  26.4 6.8 %collective-permute-start.4 = (s32[1]{0:T(128)}, s32[1]{0:T(128)}, u32[]{:S(2)}, u32[]{:S(2)}) collective-permute-start(s32[1]{0:T(128)} %slice.109), channel_id=1, source_target_pairs={{8,0},{16,8},{24,16},{32,24},{40,32},{48,40},{56,48},{64,56},{72,6... | collective-permute-start | bytes 20 | tf_op jit(solution)/shard_map/ppermute | solution.py:20
  58.5 4.0 %collective-permute-start.5 = (bf16[32,1792]{1,0:T(8,128)(2,1)S(1)}, bf16[32,1792]{1,0:T(8,128)(2,1)S(1)}, u32[]{:S(2)}, u32[]{:S(2)}) collective-permute-start(bf16[32,1792]{1,0:T(8,128)(2,1)S(1)} %convolution_convert_fusion), channel_id=1, source_target_pairs={{0,8},{8,0},{16,24},{24,16},{32,40},{40,32},{48,56},{56,48},{64,72... | collective-permute-start | bytes 344072 | tf_op jit(solution)/shard_map/ppermute | solution.py:27
  62.5 7.3 %collective-permute-start.6 = (bf16[32,1792]{1,0:T(8,128)(2,1)S(1)}, bf16[32,1792]{1,0:T(8,128)(2,1)S(1)}, u32[]{:S(2)}, u32[]{:S(2)}) collective-permute-start(bf16[32,1792]{1,0:T(8,128)(2,1)S(1)} %add.121), channel_id=1, source_target_pairs={{0,16},{8,24},{16,0},{24,8},{32,48},{40,56},{48,32},{56,40},{64,80... | collective-permute-start | bytes 344072 | tf_op jit(solution)/shard_map/ppermute | solution.py:27
  69.9 11.2 %collective-permute-start.7 = (bf16[32,1792]{1,0:T(8,128)(2,1)S(1)}, bf16[32,1792]{1,0:T(8,128)(2,1)S(1)}, u32[]{:S(2)}, u32[]{:S(2)}) collective-permute-start(bf16[32,1792]{1,0:T(8,128)(2,1)S(1)} %add.122), channel_id=1, source_target_pairs={{0,32},{8,40},{16,48},{24,56},{32,0},{40,8},{48,16},{56,24},{64,96... | collective-permute-start | bytes 344072 | tf_op jit(solution)/shard_map/ppermute | solution.py:27
  81.1 9.5 %collective-permute-start.8 = (bf16[32,1792]{1,0:T(8,128)(2,1)S(1)}, bf16[32,1792]{1,0:T(8,128)(2,1)S(1)}, u32[]{:S(2)}, u32[]{:S(2)}) collective-permute-start(bf16[32,1792]{1,0:T(8,128)(2,1)S(1)} %add.123), channel_id=1, source_target_pairs={{0,64},{8,72},{16,80},{24,88},{32,96},{40,104},{48,112},{56,120},{... | collective-permute-start | bytes 344072 | tf_op jit(solution)/shard_map/ppermute | solution.py:27
  90.7 15.4 %collective-permute-start.9 = (bf16[32,1792]{1,0:T(8,128)(2,1)S(1)}, bf16[32,1792]{1,0:T(8,128)(2,1)S(1)}, u32[]{:S(2)}, u32[]{:S(2)}) collective-permute-start(bf16[32,1792]{1,0:T(8,128)(2,1)S(1)} %add.124), channel_id=1, source_target_pairs={{0,128},{8,136},{16,144},{24,152},{32,160},{40,168},{48,176},{56,1... | collective-permute-start | bytes 344072 | tf_op jit(solution)/shard_map/ppermute | solution.py:27
  106.2 13.8 %collective-permute-start.10 = (bf16[32,1792]{1,0:T(8,128)(2,1)S(1)}, bf16[32,1792]{1,0:T(8,128)(2,1)S(1)}, u32[]{:S(2)}, u32[]{:S(2)}) collective-permute-start(bf16[32,1792]{1,0:T(8,128)(2,1)S(1)} %add.125), channel_id=1, source_target_pairs={{0,256},{8,264},{16,272},{24,280},{32,288},{40,296},{48,304},{56,3... | collective-permute-start | bytes 344072 | tf_op jit(solution)/shard_map/ppermute | solution.py:27
  137.0 31.5 %copy-start.3 = (bf16[896]{0:T(1024)(128)(2,1)S(1)}, bf16[896]{0:T(1024)(128)(2,1)}, u32[]{:S(2)}) copy-start(bf16[896]{0:T(1024)(128)(2,1)} %param.14) | copy-start | bytes 5380
  138.1 9.7 %collective-permute-start.11 = (bf16[32,4,896]{2,0,1:T(8,128)(2,1)S(1)}, bf16[32,4,896]{2,0,1:T(8,128)(2,1)S(1)}, u32[]{:S(2)}, u32[]{:S(2)}) collective-permute-start(bf16[32,4,896]{2,0,1:T(8,128)(2,1)S(1)} %dynamic-slice_bitcast_fusion), channel_id=1, source_target_pairs={{0,1},{1,0},{2,3},{3,2},{4,5},{5,4},{6,7},{7,6},{8,9},{9,8},{10,11... | collective-permute-start | bytes 688136 | tf_op jit(solution)/shard_map/ppermute | solution.py:44
  147.8 93.2 %copy-start.1 = (bf16[256,896]{1,0:T(8,128)(2,1)S(1)}, bf16[256,896]{1,0:T(8,128)(2,1)}, u32[]{:S(2)}) copy-start(bf16[256,896]{1,0:T(8,128)(2,1)} %param.12) | copy-start | bytes 1376260
  147.9 9.9 %collective-permute-start.12 = (bf16[32,2,896]{2,0,1:T(8,128)(2,1)S(1)}, bf16[32,2,896]{2,0,1:T(8,128)(2,1)S(1)}, u32[]{:S(2)}, u32[]{:S(2)}) collective-permute-start(bf16[32,2,896]{2,0,1:T(8,128)(2,1)S(1)} %dynamic-slice_bitcast_fusion.1), channel_id=1, source_target_pairs={{0,2},{1,3},{2,0},{3,1},{4,6},{5,7},{6,4},{7,5},{8,10},{9,11},{10,... | collective-permute-start | bytes 344072 | tf_op jit(solution)/shard_map/ppermute | solution.py:44
  157.8 10.6 %collective-permute-start.13 = (bf16[32,1,896]{2,0,1:T(8,128)(2,1)S(1)}, bf16[32,1,896]{2,0,1:T(8,128)(2,1)S(1)}, u32[]{:S(2)}, u32[]{:S(2)}) collective-permute-start(bf16[32,1,896]{2,0,1:T(8,128)(2,1)S(1)} %constant_dynamic-slice_fusion), channel_id=1, source_target_pairs={{0,4},{1,5},{2,6},{3,7},{4,0},{5,1},{6,2},{7,3},{8,12},{9,13},{10,... | collective-permute-start | bytes 172040 | tf_op jit(solution)/shard_map/ppermute | solution.py:44
  169.4 6.9 %collective-permute-start.14 = (f32[32,1001]{1,0:T(8,128)S(1)}, f32[32,1001]{1,0:T(8,128)S(1)}, u32[]{:S(2)}, u32[]{:S(2)}) collective-permute-start(f32[32,1001]{1,0:T(8,128)S(1)} %pad_maximum_fusion.1), channel_id=1, source_target_pairs={{0,1},{1,0},{2,3},{3,2},{4,5},{5,4},{6,7},{7,6},{8,9},{9,8},{10,11... | collective-permute-start | bytes 384392 | tf_op jit(solution)/shard_map/ppermute | solution.py:27
  176.3 11.8 %collective-permute-start.15 = (f32[32,1001]{1,0:T(8,128)S(1)}, f32[32,1001]{1,0:T(8,128)S(1)}, u32[]{:S(2)}, u32[]{:S(2)}) collective-permute-start(f32[32,1001]{1,0:T(8,128)S(1)} %fusion.64), channel_id=1, source_target_pairs={{0,2},{1,3},{2,0},{3,1},{4,6},{5,7},{6,4},{7,5},{8,10},{9,11},{10,... | collective-permute-start | bytes 384392 | tf_op jit(solution)/shard_map/ppermute | solution.py:27
  188.2 15.0 %collective-permute-start.16 = (f32[32,1001]{1,0:T(8,128)S(1)}, f32[32,1001]{1,0:T(8,128)S(1)}, u32[]{:S(2)}, u32[]{:S(2)}) collective-permute-start(f32[32,1001]{1,0:T(8,128)S(1)} %add.142), channel_id=1, source_target_pairs={{0,4},{1,5},{2,6},{3,7},{4,0},{5,1},{6,2},{7,3},{8,12},{9,13},{10,... | collective-permute-start | bytes 384392 | tf_op jit(solution)/shard_map/ppermute | solution.py:27
  204.0 3.0 %collective-permute-start.17 = (f32[32]{0:T(128)S(1)}, f32[32]{0:T(128)S(1)}, u32[]{:S(2)}, u32[]{:S(2)}) collective-permute-start(f32[32]{0:T(128)S(1)} %fusion.41), channel_id=1, source_target_pairs={{0,8},{8,0},{16,24},{24,16},{32,40},{40,32},{48,56},{56,48},{64,72... | collective-permute-start | bytes 392 | tf_op jit(solution)/shard_map/ppermute | solution.py:27
  207.1 5.4 %collective-permute-start.18 = (f32[32]{0:T(128)S(1)}, f32[32]{0:T(128)S(1)}, u32[]{:S(2)}, u32[]{:S(2)}) collective-permute-start(f32[32]{0:T(128)S(1)} %max.18), channel_id=1, source_target_pairs={{0,16},{8,24},{16,0},{24,8},{32,48},{40,56},{48,32},{56,40},{64,80... | collective-permute-start | bytes 392 | tf_op jit(solution)/shard_map/ppermute | solution.py:27
  212.5 6.9 %collective-permute-start.19 = (f32[32]{0:T(128)S(1)}, f32[32]{0:T(128)S(1)}, u32[]{:S(2)}, u32[]{:S(2)}) collective-permute-start(f32[32]{0:T(128)S(1)} %max.19), channel_id=1, source_target_pairs={{0,32},{8,40},{16,48},{24,56},{32,0},{40,8},{48,16},{56,24},{64,96... | collective-permute-start | bytes 392 | tf_op jit(solution)/shard_map/ppermute | solution.py:27
  219.4 5.4 %collective-permute-start.20 = (f32[32]{0:T(128)S(1)}, f32[32]{0:T(128)S(1)}, u32[]{:S(2)}, u32[]{:S(2)}) collective-permute-start(f32[32]{0:T(128)S(1)} %max.20), channel_id=1, source_target_pairs={{0,64},{8,72},{16,80},{24,88},{32,96},{40,104},{48,112},{56,120},{... | collective-permute-start | bytes 392 | tf_op jit(solution)/shard_map/ppermute | solution.py:27
  224.8 6.3 %collective-permute-start.21 = (f32[32]{0:T(128)S(1)}, f32[32]{0:T(128)S(1)}, u32[]{:S(2)}, u32[]{:S(2)}) collective-permute-start(f32[32]{0:T(128)S(1)} %max.21), channel_id=1, source_target_pairs={{0,128},{8,136},{16,144},{24,152},{32,160},{40,168},{48,176},{56,1... | collective-permute-start | bytes 392 | tf_op jit(solution)/shard_map/ppermute | solution.py:27
  231.2 9.3 %collective-permute-start.22 = (f32[32]{0:T(128)S(1)}, f32[32]{0:T(128)S(1)}, u32[]{:S(2)}, u32[]{:S(2)}) collective-permute-start(f32[32]{0:T(128)S(1)} %max.22), channel_id=1, source_target_pairs={{0,256},{8,264},{16,272},{24,280},{32,288},{40,296},{48,304},{56,3... | collective-permute-start | bytes 392 | tf_op jit(solution)/shard_map/ppermute | solution.py:27
Sparse Core Ops, SparseCore 0:
  11.3 111.0 all-gather.1
  168.5 56.0 reduce-scatter.1

commit v10 on v9

--- a/solution.py
+++ b/solution.py
@@ -164,18 +164,19 @@
         full_weight.reshape(full_weight.shape[0], groups, -1),
         preferred_element_type=jnp.float32,
     ).astype(jnp.bfloat16)
-    projected, end_part = both[:, :tok_rows], both[:, tok_rows:]
+    end_part = both[:, tok_rows:]
     end_sum = halving_scatter(end_part, "tp")
-    projected, end_sum = lax.optimization_barrier((projected, end_sum))
-    own_share = lax.psum_scatter(projected, "tp", scatter_dimension=0, tiled=True)[0].astype(jnp.float32)
+    both, end_sum = lax.optimization_barrier((both, end_sum))
+    own_share = lax.psum_scatter(both, "tp", scatter_dimension=0, tiled=True)[0, :tok_rows]
+    own_share = own_share.astype(jnp.float32)
     hidden = (residual.astype(jnp.float32) + own_share).astype(jnp.bfloat16)
     last_state = (end_res.astype(jnp.float32) + end_sum).astype(jnp.bfloat16).astype(jnp.float32)
     scaled = (last_state * head_gain.astype(jnp.float32)).astype(jnp.bfloat16)
     square_part = jnp.sum(last_state * last_state, axis=1)
     logit_part = jnp.dot(scaled, vocab_weight, preferred_element_type=jnp.float32)
     summed = butterfly(
-        jnp.concatenate([logit_part, square_part[:, None]], axis=1), "tp", jnp.add
-    )
+        jnp.concatenate([logit_part, square_part[:, None]], axis=1).astype(jnp.bfloat16), "tp", jnp.add
+    ).astype(jnp.float32)
     raw_logits, square_sum = summed[:, :-1], summed[:, -1]
     mean_square = square_sum / D
     last_norm = jnp.sqrt(mean_square)

time: 253 us -> 246 us (0.972)
  waiting for transfers between devices: 84 us -> 73.2 us
  starting transfers between devices: 92.2 us -> 99.4 us
  local copies, waits for them, and re-layouts: 18.1 us -> 14 us
    ppermute x15, waiting for transfers between devices: 68.9 us -> 54.7 us  [butterfly(): lax.ppermute(value, axis, [(source, source ^ stride) for source in range(...]
    ppermute x15, starting transfers between devices: 61.6 us -> 68.8 us  [butterfly(): lax.ppermute(value, axis, [(source, source ^ stride) for source in range(...]
    slice x2 -> x1, local copies, waits for them, and re-layouts: 5.2 us -> 1.06 us  [local(): end_part = both[:, tok_rows:]]
    ppermute x3, waiting for transfers between devices: 12.3 us -> 15.7 us  [halving_scatter(): lax.ppermute(give, axis, [(source, source ^ bit) for source in range(coun...]
  transfers between devices with their start and end apart: 25 -> 25, of which waited for: 19 -> 19; matrix products, arithmetic and copies ran while one was open for 16% -> 15% of each run, Pallas kernels for 0% -> 0%
where the time goes in v10:
time: 246 us; the launch traced here: 242 us
  starting transfers between devices  99.4 us (40%)
  waiting for transfers between devices  73.2 us (30%)
  matrix products  21 us (9%)
  other arithmetic  19.3 us (8%)
  between operations  15.3 us (6%)
  local copies, waits for them, and re-layouts  14 us (6%)
    ppermute x15, starting transfers between devices, butterfly(): lax.ppermute(value, axis, [(source, source ^ stride) for source in range(...  68.8 us
    ppermute x15, waiting for transfers between devices, butterfly(): lax.ppermute(value, axis, [(source, source ^ stride) for source in range(...  54.7 us
    ppermute x5, starting transfers between devices, from_behind(): lax.ppermute(value, axis, [(source, source + steps) for source in range(i...  16.9 us
    ppermute x3, waiting for transfers between devices, halving_scatter(): lax.ppermute(give, axis, [(source, source ^ bit) for source in range(coun...  15.7 us
    dot_general x1, matrix products, local(): jnp.einsum('tk,kgn->gtn', jnp.concatenate([attended, end_att], axis=0), f...  14.6 us
    ppermute x3, starting transfers between devices, halving_scatter(): lax.ppermute(give, axis, [(source, source ^ bit) for source in range(coun...  13.6 us
  transfers between devices with their start and end apart: 25, of which 19 were waited for; matrix products, arithmetic and copies ran while one was open for 15% of the time, Pallas kernels for 0%

profile of v10, /device:TPU:56, one launch (start us, length us, event | category | flops | bytes accessed | tf_op | source)
XLA Modules:
  0.0 242.1 jit_solution(498460092143860313)
XLA Ops:
  9.6 4.9 %collective-permute-start = (bf16[514,128]{1,0:T(8,128)(2,1)S(1)}, bf16[514,128]{1,0:T(8,128)(2,1)S(1)}, u32[]{:S(2)}, u32[]{:S(2)}) collective-permute-start(bf16[514,128]{1,0:T(8,128)(2,1)S(1)} %pad_maximum_fusion), channel_id=1, source_target_pairs={{0,32},{8,40},{16,48},{24,56},{32,64},{40,72},{48,80},{56,88},{64,... | collective-permute-start | bytes 394760 | tf_op jit(solution)/shard_map/ppermute | solution.py:20
  16.8 4.2 %collective-permute-start.2 = (bf16[514,128]{1,0:T(8,128)(2,1)S(1)}, bf16[514,128]{1,0:T(8,128)(2,1)}, u32[]{:S(2)}, u32[]{:S(2)}) collective-permute-start(bf16[514,128]{1,0:T(8,128)(2,1)S(1)} %pad_maximum_fusion), channel_id=1, source_target_pairs={{0,16},{8,24},{16,32},{24,40},{32,48},{40,56},{48,64},{56,72},{64,... | collective-permute-start | bytes 394760 | tf_op jit(solution)/shard_map/ppermute | solution.py:20
  21.1 4.1 %collective-permute-start.3 = (bf16[514,128]{1,0:T(8,128)(2,1)S(1)}, bf16[514,128]{1,0:T(8,128)(2,1)}, u32[]{:S(2)}, u32[]{:S(2)}) collective-permute-start(bf16[514,128]{1,0:T(8,128)(2,1)S(1)} %pad_maximum_fusion), channel_id=1, source_target_pairs={{0,8},{8,16},{16,24},{24,32},{32,40},{40,48},{48,56},{56,64},{64,7... | collective-permute-start | bytes 394760 | tf_op jit(solution)/shard_map/ppermute | solution.py:20
  47.5 3.0 %fusion.25 = (bf16[1280,1,64]{2,0,1:T(8,128)(2,1)S(1)}, bf16[1280,1,64]{2,0,1:T(8,128)(2,1)S(1)}) fusion(f32[1280,1,128]{2,0,1:T(8,128)S(1)} %fusion.37, f32[64]{0:T(128)S(1)} %negate_power_fusion, f32[1280]{0:T(1024)S(1)} %convert_subtract_fusion), kind=kLoop, calls=%fused_computation.30 | loop fusion | flops 737280 | bytes 988416 | tf_op jit(solution)/shard_map/convert.22
  58.5 3.0 %collective-permute-start.5 = (bf16[32,1792]{1,0:T(8,128)(2,1)S(1)}, bf16[32,1792]{1,0:T(8,128)(2,1)S(1)}, u32[]{:S(2)}, u32[]{:S(2)}) collective-permute-start(bf16[32,1792]{1,0:T(8,128)(2,1)S(1)} %convolution_convert_fusion), channel_id=1, source_target_pairs={{0,8},{8,0},{16,24},{24,16},{32,40},{40,32},{48,56},{56,48},{64,72... | collective-permute-start | bytes 344072 | tf_op jit(solution)/shard_map/ppermute | solution.py:27
  62.5 2.8 %collective-permute-start.6 = (bf16[32,1792]{1,0:T(8,128)(2,1)S(1)}, bf16[32,1792]{1,0:T(8,128)(2,1)S(1)}, u32[]{:S(2)}, u32[]{:S(2)}) collective-permute-start(bf16[32,1792]{1,0:T(8,128)(2,1)S(1)} %add.121), channel_id=1, source_target_pairs={{0,16},{8,24},{16,0},{24,8},{32,48},{40,56},{48,32},{56,40},{64,80... | collective-permute-start | bytes 344072 | tf_op jit(solution)/shard_map/ppermute | solution.py:27
  65.2 4.5 %collective-permute-done.6 = bf16[32,1792]{1,0:T(8,128)(2,1)S(1)} collective-permute-done((bf16[32,1792]{1,0:T(8,128)(2,1)S(1)}, bf16[32,1792]{1,0:T(8,128)(2,1)S(1)}, u32[]{:S(2)}, u32[]{:S(2)}) %collective-permute-start.6) | collective-permute-done | bytes 114720 | tf_op jit(solution)/shard_map/ppermute | solution.py:27
  69.8 4.0 %collective-permute-start.7 = (bf16[32,1792]{1,0:T(8,128)(2,1)S(1)}, bf16[32,1792]{1,0:T(8,128)(2,1)S(1)}, u32[]{:S(2)}, u32[]{:S(2)}) collective-permute-start(bf16[32,1792]{1,0:T(8,128)(2,1)S(1)} %add.122), channel_id=1, source_target_pairs={{0,32},{8,40},{16,48},{24,56},{32,0},{40,8},{48,16},{56,24},{64,96... | collective-permute-start | bytes 344072 | tf_op jit(solution)/shard_map/ppermute | solution.py:27
  73.9 7.2 %collective-permute-done.7 = bf16[32,1792]{1,0:T(8,128)(2,1)S(1)} collective-permute-done((bf16[32,1792]{1,0:T(8,128)(2,1)S(1)}, bf16[32,1792]{1,0:T(8,128)(2,1)S(1)}, u32[]{:S(2)}, u32[]{:S(2)}) %collective-permute-start.7) | collective-permute-done | bytes 114720 | tf_op jit(solution)/shard_map/ppermute | solution.py:27
  81.1 4.9 %collective-permute-start.8 = (bf16[32,1792]{1,0:T(8,128)(2,1)S(1)}, bf16[32,1792]{1,0:T(8,128)(2,1)S(1)}, u32[]{:S(2)}, u32[]{:S(2)}) collective-permute-start(bf16[32,1792]{1,0:T(8,128)(2,1)S(1)} %add.123), channel_id=1, source_target_pairs={{0,64},{8,72},{16,80},{24,88},{32,96},{40,104},{48,112},{56,120},{... | collective-permute-start | bytes 344072 | tf_op jit(solution)/shard_map/ppermute | solution.py:27
  86.0 4.6 %collective-permute-done.8 = bf16[32,1792]{1,0:T(8,128)(2,1)S(1)} collective-permute-done((bf16[32,1792]{1,0:T(8,128)(2,1)S(1)}, bf16[32,1792]{1,0:T(8,128)(2,1)S(1)}, u32[]{:S(2)}, u32[]{:S(2)}) %collective-permute-start.8) | collective-permute-done | bytes 114720 | tf_op jit(solution)/shard_map/ppermute | solution.py:27
  90.7 8.7 %collective-permute-start.9 = (bf16[32,1792]{1,0:T(8,128)(2,1)S(1)}, bf16[32,1792]{1,0:T(8,128)(2,1)S(1)}, u32[]{:S(2)}, u32[]{:S(2)}) collective-permute-start(bf16[32,1792]{1,0:T(8,128)(2,1)S(1)} %add.124), channel_id=1, source_target_pairs={{0,128},{8,136},{16,144},{24,152},{32,160},{40,168},{48,176},{56,1... | collective-permute-start | bytes 344072 | tf_op jit(solution)/shard_map/ppermute | solution.py:27
  99.5 6.7 %collective-permute-done.9 = bf16[32,1792]{1,0:T(8,128)(2,1)S(1)} collective-permute-done((bf16[32,1792]{1,0:T(8,128)(2,1)S(1)}, bf16[32,1792]{1,0:T(8,128)(2,1)S(1)}, u32[]{:S(2)}, u32[]{:S(2)}) %collective-permute-start.9) | collective-permute-done | bytes 114720 | tf_op jit(solution)/shard_map/ppermute | solution.py:27
  106.2 7.9 %collective-permute-start.10 = (bf16[32,1792]{1,0:T(8,128)(2,1)S(1)}, bf16[32,1792]{1,0:T(8,128)(2,1)S(1)}, u32[]{:S(2)}, u32[]{:S(2)}) collective-permute-start(bf16[32,1792]{1,0:T(8,128)(2,1)S(1)} %add.125), channel_id=1, source_target_pairs={{0,256},{8,264},{16,272},{24,280},{32,288},{40,296},{48,304},{56,3... | collective-permute-start | bytes 344072 | tf_op jit(solution)/shard_map/ppermute | solution.py:27
  114.2 5.8 %collective-permute-done.10 = bf16[32,1792]{1,0:T(8,128)(2,1)S(1)} collective-permute-done((bf16[32,1792]{1,0:T(8,128)(2,1)S(1)}, bf16[32,1792]{1,0:T(8,128)(2,1)S(1)}, u32[]{:S(2)}, u32[]{:S(2)}) %collective-permute-start.10) | collective-permute-done | bytes 114720 | tf_op jit(solution)/shard_map/ppermute | solution.py:27
  122.4 14.6 %convert_bitcast_fusion = bf16[8,288,896]{2,1,0:T(8,128)(2,1)} fusion(bf16[896,8,896]{0,2,1:T(8,128)(2,1)} %bitcast.151, bf16[32,896]{1,0:T(8,128)(2,1)S(1)} %slice.111, bf16[256,896]{1,0:T(8,128)(2,1)S(1)} %copy.33), kind=kOutput, calls=%fused_computation.9 | convolution fusion | flops 3702472704 | bytes 17489920 | tf_op jit(solution)/shard_map/tk,kgn->gtn/dot_general | solution.py:161
  138.0 3.4 %collective-permute-start.11 = (bf16[32,4,896]{2,0,1:T(8,128)(2,1)S(1)}, bf16[32,4,896]{2,0,1:T(8,128)(2,1)S(1)}, u32[]{:S(2)}, u32[]{:S(2)}) collective-permute-start(bf16[32,4,896]{2,0,1:T(8,128)(2,1)S(1)} %dynamic-slice_bitcast_fusion), channel_id=1, source_target_pairs={{0,1},{1,0},{2,3},{3,2},{4,5},{5,4},{6,7},{7,6},{8,9},{9,8},{10,11... | collective-permute-start | bytes 688136 | tf_op jit(solution)/shard_map/ppermute | solution.py:44
  141.4 6.2 %collective-permute-done.11 = bf16[32,4,896]{2,0,1:T(8,128)(2,1)S(1)} collective-permute-done((bf16[32,4,896]{2,0,1:T(8,128)(2,1)S(1)}, bf16[32,4,896]{2,0,1:T(8,128)(2,1)S(1)}, u32[]{:S(2)}, u32[]{:S(2)}) %collective-permute-start.11) | collective-permute-done | bytes 229408 | tf_op jit(solution)/shard_map/ppermute | solution.py:44
  147.8 4.4 %collective-permute-start.12 = (bf16[32,2,896]{2,0,1:T(8,128)(2,1)S(1)}, bf16[32,2,896]{2,0,1:T(8,128)(2,1)S(1)}, u32[]{:S(2)}, u32[]{:S(2)}) collective-permute-start(bf16[32,2,896]{2,0,1:T(8,128)(2,1)S(1)} %dynamic-slice_bitcast_fusion.1), channel_id=1, source_target_pairs={{0,2},{1,3},{2,0},{3,1},{4,6},{5,7},{6,4},{7,5},{8,10},{9,11},{10,... | collective-permute-start | bytes 344072 | tf_op jit(solution)/shard_map/ppermute | solution.py:44
  152.2 5.3 %collective-permute-done.12 = bf16[32,2,896]{2,0,1:T(8,128)(2,1)S(1)} collective-permute-done((bf16[32,2,896]{2,0,1:T(8,128)(2,1)S(1)}, bf16[32,2,896]{2,0,1:T(8,128)(2,1)S(1)}, u32[]{:S(2)}, u32[]{:S(2)}) %collective-permute-start.12) | collective-permute-done | bytes 114720 | tf_op jit(solution)/shard_map/ppermute | solution.py:44
  157.6 5.8 %collective-permute-start.13 = (bf16[32,1,896]{2,0,1:T(8,128)(2,1)S(1)}, bf16[32,1,896]{2,0,1:T(8,128)(2,1)S(1)}, u32[]{:S(2)}, u32[]{:S(2)}) collective-permute-start(bf16[32,1,896]{2,0,1:T(8,128)(2,1)S(1)} %constant_dynamic-slice_fusion), channel_id=1, source_target_pairs={{0,4},{1,5},{2,6},{3,7},{4,0},{5,1},{6,2},{7,3},{8,12},{9,13},{10,... | collective-permute-start | bytes 172040 | tf_op jit(solution)/shard_map/ppermute | solution.py:44
  163.4 4.2 %collective-permute-done.13 = bf16[32,1,896]{2,0,1:T(8,128)(2,1)S(1)} collective-permute-done((bf16[32,1,896]{2,0,1:T(8,128)(2,1)S(1)}, bf16[32,1,896]{2,0,1:T(8,128)(2,1)S(1)}, u32[]{:S(2)}, u32[]{:S(2)}) %collective-permute-start.13) | collective-permute-done | bytes 57376 | tf_op jit(solution)/shard_map/ppermute | solution.py:44
  171.1 3.6 %collective-permute-done.14 = bf16[32,1001]{1,0:T(8,128)(2,1)S(1)} collective-permute-done((bf16[32,1001]{1,0:T(8,128)(2,1)S(1)}, bf16[32,1001]{1,0:T(8,128)(2,1)S(1)}, u32[]{:S(2)}, u32[]{:S(2)}) %collective-permute-start.14) | collective-permute-done | bytes 64096 | tf_op jit(solution)/shard_map/ppermute | solution.py:27
  174.8 3.9 %collective-permute-start.15 = (bf16[32,1001]{1,0:T(8,128)(2,1)S(1)}, bf16[32,1001]{1,0:T(8,128)(2,1)S(1)}, u32[]{:S(2)}, u32[]{:S(2)}) collective-permute-start(bf16[32,1001]{1,0:T(8,128)(2,1)S(1)} %fusion.63), channel_id=1, source_target_pairs={{0,2},{1,3},{2,0},{3,1},{4,6},{5,7},{6,4},{7,5},{8,10},{9,11},{10,... | collective-permute-start | bytes 192200 | tf_op jit(solution)/shard_map/ppermute | solution.py:27
  178.7 4.0 %collective-permute-done.15 = bf16[32,1001]{1,0:T(8,128)(2,1)S(1)} collective-permute-done((bf16[32,1001]{1,0:T(8,128)(2,1)S(1)}, bf16[32,1001]{1,0:T(8,128)(2,1)S(1)}, u32[]{:S(2)}, u32[]{:S(2)}) %collective-permute-start.15) | collective-permute-done | bytes 64096 | tf_op jit(solution)/shard_map/ppermute | solution.py:27
  182.7 7.3 %collective-permute-start.16 = (bf16[32,1001]{1,0:T(8,128)(2,1)S(1)}, bf16[32,1001]{1,0:T(8,128)(2,1)S(1)}, u32[]{:S(2)}, u32[]{:S(2)}) collective-permute-start(bf16[32,1001]{1,0:T(8,128)(2,1)S(1)} %add.142), channel_id=1, source_target_pairs={{0,4},{1,5},{2,6},{3,7},{4,0},{5,1},{6,2},{7,3},{8,12},{9,13},{10,... | collective-permute-start | bytes 192200 | tf_op jit(solution)/shard_map/ppermute | solution.py:27
  190.0 4.4 %collective-permute-done.16 = bf16[32,1001]{1,0:T(8,128)(2,1)S(1)} collective-permute-done((bf16[32,1001]{1,0:T(8,128)(2,1)S(1)}, bf16[32,1001]{1,0:T(8,128)(2,1)S(1)}, u32[]{:S(2)}, u32[]{:S(2)}) %collective-permute-start.16) | collective-permute-done | bytes 64096 | tf_op jit(solution)/shard_map/ppermute | solution.py:27
  198.4 3.6 %collective-permute-start.18 = (f32[32]{0:T(128)S(1)}, f32[32]{0:T(128)S(1)}, u32[]{:S(2)}, u32[]{:S(2)}) collective-permute-start(f32[32]{0:T(128)S(1)} %max.18), channel_id=1, source_target_pairs={{0,16},{8,24},{16,0},{24,8},{32,48},{40,56},{48,32},{56,40},{64,80... | collective-permute-start | bytes 392 | tf_op jit(solution)/shard_map/ppermute | solution.py:27
  203.8 4.9 %collective-permute-start.19 = (f32[32]{0:T(128)S(1)}, f32[32]{0:T(128)S(1)}, u32[]{:S(2)}, u32[]{:S(2)}) collective-permute-start(f32[32]{0:T(128)S(1)} %max.19), channel_id=1, source_target_pairs={{0,32},{8,40},{16,48},{24,56},{32,0},{40,8},{48,16},{56,24},{64,96... | collective-permute-start | bytes 392 | tf_op jit(solution)/shard_map/ppermute | solution.py:27
  210.7 4.8 %collective-permute-start.20 = (f32[32]{0:T(128)S(1)}, f32[32]{0:T(128)S(1)}, u32[]{:S(2)}, u32[]{:S(2)}) collective-permute-start(f32[32]{0:T(128)S(1)} %max.20), channel_id=1, source_target_pairs={{0,64},{8,72},{16,80},{24,88},{32,96},{40,104},{48,112},{56,120},{... | collective-permute-start | bytes 392 | tf_op jit(solution)/shard_map/ppermute | solution.py:27
  219.7 3.6 %collective-permute-done.21 = f32[32]{0:T(128)S(1)} collective-permute-done((f32[32]{0:T(128)S(1)}, f32[32]{0:T(128)S(1)}, u32[]{:S(2)}, u32[]{:S(2)}) %collective-permute-start.21) | collective-permute-done | bytes 160 | tf_op jit(solution)/shard_map/ppermute | solution.py:27
  223.4 5.8 %collective-permute-start.22 = (f32[32]{0:T(128)S(1)}, f32[32]{0:T(128)S(1)}, u32[]{:S(2)}, u32[]{:S(2)}) collective-permute-start(f32[32]{0:T(128)S(1)} %max.22), channel_id=1, source_target_pairs={{0,256},{8,264},{16,272},{24,280},{32,288},{40,296},{48,304},{56,3... | collective-permute-start | bytes 392 | tf_op jit(solution)/shard_map/ppermute | solution.py:27
  (103 shorter events, 60.4 us)
Async XLA Ops:
  7.2 160.7 %copy-start = (bf16[896,1000]{0,1:T(8,128)(2,1)S(1)}, bf16[896,1000]{0,1:T(8,128)(2,1)}, u32[]{:S(2)}) copy-start(bf16[896,1000]{0,1:T(8,128)(2,1)} %param.15) | copy-start | bytes 5376004
  7.2 39.2 %copy-start.1 = (s32[256]{0:T(256)S(1)}, s32[256]{0:T(256)}, u32[]{:S(2)}) copy-start(s32[256]{0:T(256)} %param.11) | copy-start | bytes 3076
  7.2 115.2 %all-gather.2.cloned.1.call-start = ((), (), s32[]{:S(2)}) async-start(), calls=%async_computation.1 | async-start | bytes 13045760 | tf_op jit(solution)/shard_map/all_gather | solution.py:159
  7.9 225.3 %reduce-scatter.2.cloned.1.call-start = ((), (), s32[]{:S(2)}) async-start(), calls=%async_computation.2 | async-start | bytes 4644864 | tf_op jit(solution)/shard_map/reduce_scatter | solution.py:170
  9.6 26.4 %collective-permute-start = (bf16[514,128]{1,0:T(8,128)(2,1)S(1)}, bf16[514,128]{1,0:T(8,128)(2,1)S(1)}, u32[]{:S(2)}, u32[]{:S(2)}) collective-permute-start(bf16[514,128]{1,0:T(8,128)(2,1)S(1)} %pad_maximum_fusion), channel_id=1, source_target_pairs={{0,32},{8,40},{16,48},{24,56},{32,64},{40,72},{48,80},{56,88},{64,... | collective-permute-start | bytes 394760 | tf_op jit(solution)/shard_map/ppermute | solution.py:20
  14.5 21.4 %collective-permute-start.1 = (bf16[514,128]{1,0:T(8,128)(2,1)S(1)}, bf16[514,128]{1,0:T(8,128)(2,1)}, u32[]{:S(2)}, u32[]{:S(2)}) collective-permute-start(bf16[514,128]{1,0:T(8,128)(2,1)S(1)} %pad_maximum_fusion), channel_id=1, source_target_pairs={{0,24},{8,32},{16,40},{24,48},{32,56},{40,64},{48,72},{56,80},{64,... | collective-permute-start | bytes 394760 | tf_op jit(solution)/shard_map/ppermute | solution.py:20
  16.8 20.1 %collective-permute-start.2 = (bf16[514,128]{1,0:T(8,128)(2,1)S(1)}, bf16[514,128]{1,0:T(8,128)(2,1)}, u32[]{:S(2)}, u32[]{:S(2)}) collective-permute-start(bf16[514,128]{1,0:T(8,128)(2,1)S(1)} %pad_maximum_fusion), channel_id=1, source_target_pairs={{0,16},{8,24},{16,32},{24,40},{32,48},{40,56},{48,64},{56,72},{64,... | collective-permute-start | bytes 394760 | tf_op jit(solution)/shard_map/ppermute | solution.py:20
  21.1 16.8 %collective-permute-start.3 = (bf16[514,128]{1,0:T(8,128)(2,1)S(1)}, bf16[514,128]{1,0:T(8,128)(2,1)}, u32[]{:S(2)}, u32[]{:S(2)}) collective-permute-start(bf16[514,128]{1,0:T(8,128)(2,1)S(1)} %pad_maximum_fusion), channel_id=1, source_target_pairs={{0,8},{8,16},{16,24},{24,32},{32,40},{40,48},{48,56},{56,64},{64,7... | collective-permute-start | bytes 394760 | tf_op jit(solution)/shard_map/ppermute | solution.py:20
  26.4 6.8 %collective-permute-start.4 = (s32[1]{0:T(128)}, s32[1]{0:T(128)}, u32[]{:S(2)}, u32[]{:S(2)}) collective-permute-start(s32[1]{0:T(128)} %slice.109), channel_id=1, source_target_pairs={{8,0},{16,8},{24,16},{32,24},{40,32},{48,40},{56,48},{64,56},{72,6... | collective-permute-start | bytes 20 | tf_op jit(solution)/shard_map/ppermute | solution.py:20
  58.5 3.9 %collective-permute-start.5 = (bf16[32,1792]{1,0:T(8,128)(2,1)S(1)}, bf16[32,1792]{1,0:T(8,128)(2,1)S(1)}, u32[]{:S(2)}, u32[]{:S(2)}) collective-permute-start(bf16[32,1792]{1,0:T(8,128)(2,1)S(1)} %convolution_convert_fusion), channel_id=1, source_target_pairs={{0,8},{8,0},{16,24},{24,16},{32,40},{40,32},{48,56},{56,48},{64,72... | collective-permute-start | bytes 344072 | tf_op jit(solution)/shard_map/ppermute | solution.py:27
  62.5 7.3 %collective-permute-start.6 = (bf16[32,1792]{1,0:T(8,128)(2,1)S(1)}, bf16[32,1792]{1,0:T(8,128)(2,1)S(1)}, u32[]{:S(2)}, u32[]{:S(2)}) collective-permute-start(bf16[32,1792]{1,0:T(8,128)(2,1)S(1)} %add.121), channel_id=1, source_target_pairs={{0,16},{8,24},{16,0},{24,8},{32,48},{40,56},{48,32},{56,40},{64,80... | collective-permute-start | bytes 344072 | tf_op jit(solution)/shard_map/ppermute | solution.py:27
  69.8 11.2 %collective-permute-start.7 = (bf16[32,1792]{1,0:T(8,128)(2,1)S(1)}, bf16[32,1792]{1,0:T(8,128)(2,1)S(1)}, u32[]{:S(2)}, u32[]{:S(2)}) collective-permute-start(bf16[32,1792]{1,0:T(8,128)(2,1)S(1)} %add.122), channel_id=1, source_target_pairs={{0,32},{8,40},{16,48},{24,56},{32,0},{40,8},{48,16},{56,24},{64,96... | collective-permute-start | bytes 344072 | tf_op jit(solution)/shard_map/ppermute | solution.py:27
  81.1 9.6 %collective-permute-start.8 = (bf16[32,1792]{1,0:T(8,128)(2,1)S(1)}, bf16[32,1792]{1,0:T(8,128)(2,1)S(1)}, u32[]{:S(2)}, u32[]{:S(2)}) collective-permute-start(bf16[32,1792]{1,0:T(8,128)(2,1)S(1)} %add.123), channel_id=1, source_target_pairs={{0,64},{8,72},{16,80},{24,88},{32,96},{40,104},{48,112},{56,120},{... | collective-permute-start | bytes 344072 | tf_op jit(solution)/shard_map/ppermute | solution.py:27
  90.7 15.4 %collective-permute-start.9 = (bf16[32,1792]{1,0:T(8,128)(2,1)S(1)}, bf16[32,1792]{1,0:T(8,128)(2,1)S(1)}, u32[]{:S(2)}, u32[]{:S(2)}) collective-permute-start(bf16[32,1792]{1,0:T(8,128)(2,1)S(1)} %add.124), channel_id=1, source_target_pairs={{0,128},{8,136},{16,144},{24,152},{32,160},{40,168},{48,176},{56,1... | collective-permute-start | bytes 344072 | tf_op jit(solution)/shard_map/ppermute | solution.py:27
  106.2 13.7 %collective-permute-start.10 = (bf16[32,1792]{1,0:T(8,128)(2,1)S(1)}, bf16[32,1792]{1,0:T(8,128)(2,1)S(1)}, u32[]{:S(2)}, u32[]{:S(2)}) collective-permute-start(bf16[32,1792]{1,0:T(8,128)(2,1)S(1)} %add.125), channel_id=1, source_target_pairs={{0,256},{8,264},{16,272},{24,280},{32,288},{40,296},{48,304},{56,3... | collective-permute-start | bytes 344072 | tf_op jit(solution)/shard_map/ppermute | solution.py:27
  122.4 45.3 %copy-start.2 = (bf16[896]{0:T(1024)(128)(2,1)S(1)}, bf16[896]{0:T(1024)(128)(2,1)}, u32[]{:S(2)}) copy-start(bf16[896]{0:T(1024)(128)(2,1)} %param.14) | copy-start | bytes 5380
  138.0 9.7 %collective-permute-start.11 = (bf16[32,4,896]{2,0,1:T(8,128)(2,1)S(1)}, bf16[32,4,896]{2,0,1:T(8,128)(2,1)S(1)}, u32[]{:S(2)}, u32[]{:S(2)}) collective-permute-start(bf16[32,4,896]{2,0,1:T(8,128)(2,1)S(1)} %dynamic-slice_bitcast_fusion), channel_id=1, source_target_pairs={{0,1},{1,0},{2,3},{3,2},{4,5},{5,4},{6,7},{7,6},{8,9},{9,8},{10,11... | collective-permute-start | bytes 688136 | tf_op jit(solution)/shard_map/ppermute | solution.py:44
  147.8 9.7 %collective-permute-start.12 = (bf16[32,2,896]{2,0,1:T(8,128)(2,1)S(1)}, bf16[32,2,896]{2,0,1:T(8,128)(2,1)S(1)}, u32[]{:S(2)}, u32[]{:S(2)}) collective-permute-start(bf16[32,2,896]{2,0,1:T(8,128)(2,1)S(1)} %dynamic-slice_bitcast_fusion.1), channel_id=1, source_target_pairs={{0,2},{1,3},{2,0},{3,1},{4,6},{5,7},{6,4},{7,5},{8,10},{9,11},{10,... | collective-permute-start | bytes 344072 | tf_op jit(solution)/shard_map/ppermute | solution.py:44
  157.6 10.0 %collective-permute-start.13 = (bf16[32,1,896]{2,0,1:T(8,128)(2,1)S(1)}, bf16[32,1,896]{2,0,1:T(8,128)(2,1)S(1)}, u32[]{:S(2)}, u32[]{:S(2)}) collective-permute-start(bf16[32,1,896]{2,0,1:T(8,128)(2,1)S(1)} %constant_dynamic-slice_fusion), channel_id=1, source_target_pairs={{0,4},{1,5},{2,6},{3,7},{4,0},{5,1},{6,2},{7,3},{8,12},{9,13},{10,... | collective-permute-start | bytes 172040 | tf_op jit(solution)/shard_map/ppermute | solution.py:44
  168.6 6.2 %collective-permute-start.14 = (bf16[32,1001]{1,0:T(8,128)(2,1)S(1)}, bf16[32,1001]{1,0:T(8,128)(2,1)S(1)}, u32[]{:S(2)}, u32[]{:S(2)}) collective-permute-start(bf16[32,1001]{1,0:T(8,128)(2,1)S(1)} %pad_maximum_fusion.2), channel_id=1, source_target_pairs={{0,1},{1,0},{2,3},{3,2},{4,5},{5,4},{6,7},{7,6},{8,9},{9,8},{10,11... | collective-permute-start | bytes 192200 | tf_op jit(solution)/shard_map/ppermute | solution.py:27
  174.8 7.9 %collective-permute-start.15 = (bf16[32,1001]{1,0:T(8,128)(2,1)S(1)}, bf16[32,1001]{1,0:T(8,128)(2,1)S(1)}, u32[]{:S(2)}, u32[]{:S(2)}) collective-permute-start(bf16[32,1001]{1,0:T(8,128)(2,1)S(1)} %fusion.63), channel_id=1, source_target_pairs={{0,2},{1,3},{2,0},{3,1},{4,6},{5,7},{6,4},{7,5},{8,10},{9,11},{10,... | collective-permute-start | bytes 192200 | tf_op jit(solution)/shard_map/ppermute | solution.py:27
  182.7 11.7 %collective-permute-start.16 = (bf16[32,1001]{1,0:T(8,128)(2,1)S(1)}, bf16[32,1001]{1,0:T(8,128)(2,1)S(1)}, u32[]{:S(2)}, u32[]{:S(2)}) collective-permute-start(bf16[32,1001]{1,0:T(8,128)(2,1)S(1)} %add.142), channel_id=1, source_target_pairs={{0,4},{1,5},{2,6},{3,7},{4,0},{5,1},{6,2},{7,3},{8,12},{9,13},{10,... | collective-permute-start | bytes 192200 | tf_op jit(solution)/shard_map/ppermute | solution.py:27
  195.3 3.0 %collective-permute-start.17 = (f32[32]{0:T(128)S(1)}, f32[32]{0:T(128)S(1)}, u32[]{:S(2)}, u32[]{:S(2)}) collective-permute-start(f32[32]{0:T(128)S(1)} %fusion.41), channel_id=1, source_target_pairs={{0,8},{8,0},{16,24},{24,16},{32,40},{40,32},{48,56},{56,48},{64,72... | collective-permute-start | bytes 392 | tf_op jit(solution)/shard_map/ppermute | solution.py:27
  198.4 5.4 %collective-permute-start.18 = (f32[32]{0:T(128)S(1)}, f32[32]{0:T(128)S(1)}, u32[]{:S(2)}, u32[]{:S(2)}) collective-permute-start(f32[32]{0:T(128)S(1)} %max.18), channel_id=1, source_target_pairs={{0,16},{8,24},{16,0},{24,8},{32,48},{40,56},{48,32},{56,40},{64,80... | collective-permute-start | bytes 392 | tf_op jit(solution)/shard_map/ppermute | solution.py:27
  203.8 6.9 %collective-permute-start.19 = (f32[32]{0:T(128)S(1)}, f32[32]{0:T(128)S(1)}, u32[]{:S(2)}, u32[]{:S(2)}) collective-permute-start(f32[32]{0:T(128)S(1)} %max.19), channel_id=1, source_target_pairs={{0,32},{8,40},{16,48},{24,56},{32,0},{40,8},{48,16},{56,24},{64,96... | collective-permute-start | bytes 392 | tf_op jit(solution)/shard_map/ppermute | solution.py:27
  210.7 6.3 %collective-permute-start.20 = (f32[32]{0:T(128)S(1)}, f32[32]{0:T(128)S(1)}, u32[]{:S(2)}, u32[]{:S(2)}) collective-permute-start(f32[32]{0:T(128)S(1)} %max.20), channel_id=1, source_target_pairs={{0,64},{8,72},{16,80},{24,88},{32,96},{40,104},{48,112},{56,120},{... | collective-permute-start | bytes 392 | tf_op jit(solution)/shard_map/ppermute | solution.py:27
  217.1 6.3 %collective-permute-start.21 = (f32[32]{0:T(128)S(1)}, f32[32]{0:T(128)S(1)}, u32[]{:S(2)}, u32[]{:S(2)}) collective-permute-start(f32[32]{0:T(128)S(1)} %max.21), channel_id=1, source_target_pairs={{0,128},{8,136},{16,144},{24,152},{32,160},{40,168},{48,176},{56,1... | collective-permute-start | bytes 392 | tf_op jit(solution)/shard_map/ppermute | solution.py:27
  223.4 9.3 %collective-permute-start.22 = (f32[32]{0:T(128)S(1)}, f32[32]{0:T(128)S(1)}, u32[]{:S(2)}, u32[]{:S(2)}) collective-permute-start(f32[32]{0:T(128)S(1)} %max.22), channel_id=1, source_target_pairs={{0,256},{8,264},{16,272},{24,280},{32,288},{40,296},{48,304},{56,3... | collective-permute-start | bytes 392 | tf_op jit(solution)/shard_map/ppermute | solution.py:27
Sparse Core Ops, SparseCore 0:
  11.3 111.0 all-gather.1
  167.7 56.7 reduce-scatter.1

commit v11 on v10

--- a/solution.py
+++ b/solution.py
@@ -1,12 +1,13 @@
 import jax
 import jax.numpy as jnp
 from jax import lax
-from jax.sharding import PartitionSpec as P
+from jax.sharding import Mesh, PartitionSpec as P
 
 D = 7168
 HD = 128
 GROUP = 7
 REACH = 4
+REQ = ("z", "x", "c")
 
 
 theta = 5000000.0
@@ -73,9 +74,9 @@
 def local(queries, key_value, segment, residual, out_weight, head_gain, vocab_weight):
     tok_rows = segment.shape[0]
     heads_kv = key_value.shape[2] // HD
-    requests = lax.axis_size("req") // 2
-    devices_req = lax.axis_size("req")
-    device = lax.axis_index("req")
+    requests = lax.axis_size(REQ) // 2
+    devices_req = lax.axis_size(REQ)
+    device = lax.axis_index(REQ)
     request_ids = jnp.arange(requests, dtype=jnp.int32)
 
     own_kv = key_value
@@ -87,12 +88,12 @@
     )
     parts_kv, parts_seg = [], []
     for back in range(REACH, 0, -1):
-        got = from_behind(packed, "req", back)
+        got = from_behind(packed, REQ, back)
         parts_kv.append(got[: 2 * tok_rows].reshape(own_kv.shape))
         parts_seg.append(got[2 * tok_rows :].reshape(-1)[:tok_rows].astype(jnp.int32))
     parts_kv.append(own_kv)
     parts_seg.append(segment)
-    next_first = from_behind(segment[:1], "req", -1)
+    next_first = from_behind(segment[:1], REQ, -1)
     window = jnp.concatenate(parts_kv, axis=1)
     seg_window = jnp.concatenate(parts_seg, axis=0)
     span = window.shape[1]
@@ -152,18 +153,23 @@
         (((0,), (0,)), ((), ())),
         preferred_element_type=jnp.float32,
     ).astype(jnp.bfloat16)
-    end_rows = butterfly(end_rows, "req", jnp.add)
+    end_rows = butterfly(end_rows, REQ, jnp.add)
     attended, end_rows = lax.optimization_barrier((attended, end_rows))
     end_att, end_res = end_rows[:, : attended.shape[1]], end_rows[:, attended.shape[1] :]
 
-    full_weight = lax.all_gather(out_weight, "req", axis=1, tiled=True)
     groups = lax.axis_size("tp")
+    chip_half = lax.all_gather(out_weight, ("z", "x"), axis=1, tiled=True)
+    halves = lax.all_gather(chip_half, "c", axis=0, tiled=False)
+    cores, k_rows = halves.shape[0], halves.shape[1]
+    per_group = halves.shape[2] // (groups * out_weight.shape[1])
+    halves = halves.reshape(cores, k_rows, groups, per_group, out_weight.shape[1])
     both = jnp.einsum(
-        "tk,kgn->gtn",
+        "tk,ckgin->gticn",
         jnp.concatenate([attended, end_att], axis=0),
-        full_weight.reshape(full_weight.shape[0], groups, -1),
+        halves,
         preferred_element_type=jnp.float32,
     ).astype(jnp.bfloat16)
+    both = both.reshape(groups, both.shape[1], -1)
     end_part = both[:, tok_rows:]
     end_sum = halving_scatter(end_part, "tp")
     both, end_sum = lax.optimization_barrier((both, end_sum))
@@ -181,24 +187,26 @@
     mean_square = square_sum / D
     last_norm = jnp.sqrt(mean_square)
     local_top = jnp.max(raw_logits * lax.rsqrt(mean_square + eps)[:, None], axis=1)
-    top_logit = butterfly(local_top, "req", jnp.maximum)
+    top_logit = butterfly(local_top, REQ, jnp.maximum)
     return (hidden, key_cache, last_norm, top_logit)
 
 
 def solution(mesh):
+    req_size = mesh.shape["req"]
+    split = Mesh(mesh.devices.reshape(req_size // 8, 4, 2, mesh.shape["tp"]), REQ + ("tp",))
     placed = (
-        P("req", "tp"),
-        P(None, "req", "tp"),
-        P("req"),
-        P("req", "tp"),
-        P("tp", "req"),
+        P(REQ, "tp"),
+        P(None, REQ, "tp"),
+        P(REQ),
+        P(REQ, "tp"),
+        P("tp", REQ),
         P("tp"),
-        P("tp", "req"),
+        P("tp", REQ),
     )
     return jax.shard_map(
         local,
-        mesh=mesh,
+        mesh=split,
         in_specs=placed,
-        out_specs=(P("req", "tp"), P("req", "tp"), P(), P()),
+        out_specs=(P(REQ, "tp"), P(REQ, "tp"), P(), P()),
         check_vma=False,
     )

time: 246 us -> 375 us (1.52)
  waiting for transfers between devices: 73.2 us -> 166 us
  local copies, waits for them, and re-layouts: 14 us -> 63.7 us
  starting transfers between devices: 99.4 us -> 90.3 us
    all_gather x1 -> x2, waiting for transfers between devices: 2.14 us -> 103 us  [the longest x1 103 us: local(): chip_half = lax.all_gather(out_weight, ('z', 'x'), axis=1, tiled=True)]
    reshape x0 -> x2, local copies, waits for them, and re-layouts: none -> 40.2 us  [the longest x1 24.7 us: local(): halves.reshape(cores, k_rows, groups, per_group, out_weight.shape[1])]
    convert_element_type x0 -> x1, local copies, waits for them, and re-layouts: none -> 9.38 us  [local(): both = jnp.einsum('tk,ckgin->gticn', jnp.concatenate([attended, end_att],...]
    ppermute x15, waiting for transfers between devices: 54.7 us -> 47.8 us  [butterfly(): lax.ppermute(value, axis, [(source, source ^ stride) for source in range(...]
    ppermute x15, starting transfers between devices: 68.8 us -> 63.1 us  [butterfly(): lax.ppermute(value, axis, [(source, source ^ stride) for source in range(...]
  transfers between devices with their start and end apart: 25 -> 26, of which waited for: 19 -> 19; matrix products, arithmetic and copies ran while one was open for 15% -> 10% of each run, Pallas kernels for 0% -> 0%
where the time goes in v11:
time: 375 us; the launch traced here: 373 us
  waiting for transfers between devices  166 us (44%)
  starting transfers between devices  90.3 us (24%)
  local copies, waits for them, and re-layouts  63.7 us (17%)
  other arithmetic  19.2 us (5%)
  matrix products  18.3 us (5%)
  between operations  15 us (4%)
    all_gather x1, waiting for transfers between devices, local(): chip_half = lax.all_gather(out_weight, ('z', 'x'), axis=1, tiled=True)  103 us
    ppermute x15, starting transfers between devices, butterfly(): lax.ppermute(value, axis, [(source, source ^ stride) for source in range(...  63.1 us
    ppermute x15, waiting for transfers between devices, butterfly(): lax.ppermute(value, axis, [(source, source ^ stride) for source in range(...  47.8 us
    reshape x1, local copies, waits for them, and re-layouts, local(): halves.reshape(cores, k_rows, groups, per_group, out_weight.shape[1])  24.7 us
    reshape x1, local copies, waits for them, and re-layouts, local(): both = both.reshape(groups, both.shape[1], -1)  15.5 us
    ppermute x3, waiting for transfers between devices, halving_scatter(): lax.ppermute(give, axis, [(source, source ^ bit) for source in range(coun...  15.1 us
    ppermute x5, starting transfers between devices, from_behind(): lax.ppermute(value, axis, [(source, source + steps) for source in range(i...  14.4 us
    ppermute x3, starting transfers between devices, halving_scatter(): lax.ppermute(give, axis, [(source, source ^ bit) for source in range(coun...  12.7 us
  transfers between devices with their start and end apart: 26, of which 19 were waited for; matrix products, arithmetic and copies ran while one was open for 10% of the time, Pallas kernels for 0%

profile of v11, /device:TPU:56, one launch (start us, length us, event | category | flops | bytes accessed | tf_op | source)
XLA Modules:
  0.0 372.8 jit_solution(6426506884844975606)
XLA Ops:
  8.0 102.5 %all-gather.4.cloned.1.call-done = bf16[896,3584]{0,1:T(8,128)(2,1)} async-done(((bf16[896,112]{0,1:T(8,128)(2,1)}), bf16[896,3584]{0,1:T(8,128)(2,1)}) %all-gather.4.cloned.1.call-update) | async-done | bytes 6422544 | tf_op jit(solution)/shard_map/all_gather | solution.py:161
  112.2 4.0 %collective-permute-start = (bf16[514,128]{1,0:T(8,128)(2,1)S(1)}, bf16[514,128]{1,0:T(8,128)(2,1)}, u32[]{:S(2)}, u32[]{:S(2)}) collective-permute-start(bf16[514,128]{1,0:T(8,128)(2,1)S(1)} %pad_maximum_fusion), channel_id=1, source_target_pairs={{0,32},{8,40},{16,48},{24,56},{32,64},{40,72},{48,80},{56,88},{64,... | collective-permute-start | bytes 394760 | tf_op jit(solution)/shard_map/ppermute | solution.py:21
  121.0 4.4 %collective-permute-start.3 = (bf16[514,128]{1,0:T(8,128)(2,1)S(1)}, bf16[514,128]{1,0:T(8,128)(2,1)}, u32[]{:S(2)}, u32[]{:S(2)}) collective-permute-start(bf16[514,128]{1,0:T(8,128)(2,1)S(1)} %pad_maximum_fusion), channel_id=1, source_target_pairs={{0,8},{8,16},{16,24},{24,32},{32,40},{40,48},{48,56},{56,64},{64,7... | collective-permute-start | bytes 394760 | tf_op jit(solution)/shard_map/ppermute | solution.py:21
  147.1 3.0 fusion.29
  158.0 3.0 collective-permute-start.5
  164.8 4.5 %collective-permute-done.6 = bf16[32,1792]{1,0:T(8,128)(2,1)S(1)} collective-permute-done((bf16[32,1792]{1,0:T(8,128)(2,1)S(1)}, bf16[32,1792]{1,0:T(8,128)(2,1)S(1)}, u32[]{:S(2)}, u32[]{:S(2)}) %collective-permute-start.6) | collective-permute-done | bytes 114720 | tf_op jit(solution)/shard_map/ppermute | solution.py:28
  169.4 3.6 collective-permute-start.7
  172.9 4.6 %collective-permute-done.7 = bf16[32,1792]{1,0:T(8,128)(2,1)S(1)} collective-permute-done((bf16[32,1792]{1,0:T(8,128)(2,1)S(1)}, bf16[32,1792]{1,0:T(8,128)(2,1)S(1)}, u32[]{:S(2)}, u32[]{:S(2)}) %collective-permute-start.7) | collective-permute-done | bytes 114720 | tf_op jit(solution)/shard_map/ppermute | solution.py:28
  177.6 4.6 %collective-permute-start.8 = (bf16[32,1792]{1,0:T(8,128)(2,1)S(1)}, bf16[32,1792]{1,0:T(8,128)(2,1)S(1)}, u32[]{:S(2)}, u32[]{:S(2)}) collective-permute-start(bf16[32,1792]{1,0:T(8,128)(2,1)S(1)} %add.131), channel_id=1, source_target_pairs={{0,64},{8,72},{16,80},{24,88},{32,96},{40,104},{48,112},{56,120},{... | collective-permute-start | bytes 344072 | tf_op jit(solution)/shard_map/ppermute | solution.py:28
  184.9 5.0 %collective-permute-start.9 = (bf16[32,1792]{1,0:T(8,128)(2,1)S(1)}, bf16[32,1792]{1,0:T(8,128)(2,1)S(1)}, u32[]{:S(2)}, u32[]{:S(2)}) collective-permute-start(bf16[32,1792]{1,0:T(8,128)(2,1)S(1)} %add.132), channel_id=1, source_target_pairs={{0,128},{8,136},{16,144},{24,152},{32,160},{40,168},{48,176},{56,1... | collective-permute-start | bytes 344072 | tf_op jit(solution)/shard_map/ppermute | solution.py:28
  192.8 7.6 %collective-permute-start.10 = (bf16[32,1792]{1,0:T(8,128)(2,1)S(1)}, bf16[32,1792]{1,0:T(8,128)(2,1)S(1)}, u32[]{:S(2)}, u32[]{:S(2)}) collective-permute-start(bf16[32,1792]{1,0:T(8,128)(2,1)S(1)} %add.133), channel_id=1, source_target_pairs={{0,256},{8,264},{16,272},{24,280},{32,288},{40,296},{48,304},{56,3... | collective-permute-start | bytes 344072 | tf_op jit(solution)/shard_map/ppermute | solution.py:28
  200.4 3.5 collective-permute-done.10
  205.0 24.7 %reshape.392 = bf16[2,896,8,4,112]{1,0,4,3,2:T(2,128)(2,1)} reshape(bf16[1792,3584]{0,1:T(8,128)(2,1)} %all-gather.6.cloned.1.call-done) | data formatting | bytes 25690112 | tf_op jit(solution)/shard_map/reshape | solution.py:165
  229.7 11.9 %convert_bitcast_fusion = bf16[8,288,4,2,112]{4,1,2,0,3:T(8,128)(2,1)} fusion(bf16[2,896,8,4,112]{1,0,4,3,2:T(2,128)(2,1)} %reshape.392, bf16[32,896]{1,0:T(8,128)(2,1)S(1)} %slice.111, bf16[256,896]{1,0:T(8,128)(2,1)S(1)} %copy-done.2), kind=kOutput, calls=%fused_computation.8 | convolution fusion | flops 3702472704 | bytes 17489920 | tf_op jit(solution)/shard_map/tk,ckgin->gticn/dot_general | solution.py:166
  241.6 9.4 %copy.36 = bf16[8,288,4,2,112]{4,3,2,1,0:T(2,128)(2,1)} copy(bf16[8,288,4,2,112]{4,1,2,0,3:T(8,128)(2,1)} %convert_bitcast_fusion) | data formatting | bytes 8257536 | tf_op jit(solution)/shard_map/convert_element_type | solution.py:171
  251.0 15.5 %reshape.393 = bf16[8,288,896]{2,1,0:T(8,128)(2,1)} reshape(bf16[8,288,4,2,112]{4,3,2,1,0:T(2,128)(2,1)} %copy.36) | data formatting | bytes 8257536 | tf_op jit(solution)/shard_map/reshape | solution.py:172
  267.5 3.3 collective-permute-start.11
  270.9 4.5 %collective-permute-done.11 = bf16[32,4,896]{2,0,1:T(8,128)(2,1)S(1)} collective-permute-done((bf16[32,4,896]{2,0,1:T(8,128)(2,1)S(1)}, bf16[32,4,896]{2,0,1:T(8,128)(2,1)S(1)}, u32[]{:S(2)}, u32[]{:S(2)}) %collective-permute-start.11) | collective-permute-done | bytes 229408 | tf_op jit(solution)/shard_map/ppermute | solution.py:45
  275.6 5.0 %collective-permute-start.12 = (bf16[32,2,896]{2,0,1:T(8,128)(2,1)S(1)}, bf16[32,2,896]{2,0,1:T(8,128)(2,1)S(1)}, u32[]{:S(2)}, u32[]{:S(2)}) collective-permute-start(bf16[32,2,896]{2,0,1:T(8,128)(2,1)S(1)} %dynamic-slice_bitcast_fusion.1), channel_id=1, source_target_pairs={{0,2},{1,3},{2,0},{3,1},{4,6},{5,7},{6,4},{7,5},{8,10},{9,11},{10,... | collective-permute-start | bytes 344072 | tf_op jit(solution)/shard_map/ppermute | solution.py:45
  280.6 4.6 %collective-permute-done.12 = bf16[32,2,896]{2,0,1:T(8,128)(2,1)S(1)} collective-permute-done((bf16[32,2,896]{2,0,1:T(8,128)(2,1)S(1)}, bf16[32,2,896]{2,0,1:T(8,128)(2,1)S(1)}, u32[]{:S(2)}, u32[]{:S(2)}) %collective-permute-start.12) | collective-permute-done | bytes 114720 | tf_op jit(solution)/shard_map/ppermute | solution.py:45
  285.2 4.3 %collective-permute-start.13 = (bf16[32,1,896]{2,0,1:T(8,128)(2,1)S(1)}, bf16[32,1,896]{2,0,1:T(8,128)(2,1)S(1)}, u32[]{:S(2)}, u32[]{:S(2)}) collective-permute-start(bf16[32,1,896]{2,0,1:T(8,128)(2,1)S(1)} %constant_dynamic-slice_fusion), channel_id=1, source_target_pairs={{0,4},{1,5},{2,6},{3,7},{4,0},{5,1},{6,2},{7,3},{8,12},{9,13},{10,... | collective-permute-start | bytes 172040 | tf_op jit(solution)/shard_map/ppermute | solution.py:45
  289.5 6.0 %collective-permute-done.13 = bf16[32,1,896]{2,0,1:T(8,128)(2,1)S(1)} collective-permute-done((bf16[32,1,896]{2,0,1:T(8,128)(2,1)S(1)}, bf16[32,1,896]{2,0,1:T(8,128)(2,1)S(1)}, u32[]{:S(2)}, u32[]{:S(2)}) %collective-permute-start.13) | collective-permute-done | bytes 57376 | tf_op jit(solution)/shard_map/ppermute | solution.py:45
  298.5 4.2 %collective-permute-done.14 = bf16[32,1001]{1,0:T(8,128)(2,1)S(1)} collective-permute-done((bf16[32,1001]{1,0:T(8,128)(2,1)S(1)}, bf16[32,1001]{1,0:T(8,128)(2,1)S(1)}, u32[]{:S(2)}, u32[]{:S(2)}) %collective-permute-start.14) | collective-permute-done | bytes 64096 | tf_op jit(solution)/shard_map/ppermute | solution.py:28
  302.8 3.2 collective-permute-start.15
  306.0 4.5 %collective-permute-done.15 = bf16[32,1001]{1,0:T(8,128)(2,1)S(1)} collective-permute-done((bf16[32,1001]{1,0:T(8,128)(2,1)S(1)}, bf16[32,1001]{1,0:T(8,128)(2,1)S(1)}, u32[]{:S(2)}, u32[]{:S(2)}) %collective-permute-start.15) | collective-permute-done | bytes 64096 | tf_op jit(solution)/shard_map/ppermute | solution.py:28
  310.5 6.0 %collective-permute-start.16 = (bf16[32,1001]{1,0:T(8,128)(2,1)S(1)}, bf16[32,1001]{1,0:T(8,128)(2,1)S(1)}, u32[]{:S(2)}, u32[]{:S(2)}) collective-permute-start(bf16[32,1001]{1,0:T(8,128)(2,1)S(1)} %add.150), channel_id=1, source_target_pairs={{0,4},{1,5},{2,6},{3,7},{4,0},{5,1},{6,2},{7,3},{8,12},{9,13},{10,... | collective-permute-start | bytes 192200 | tf_op jit(solution)/shard_map/ppermute | solution.py:28
  316.5 5.8 %collective-permute-done.16 = bf16[32,1001]{1,0:T(8,128)(2,1)S(1)} collective-permute-done((bf16[32,1001]{1,0:T(8,128)(2,1)S(1)}, bf16[32,1001]{1,0:T(8,128)(2,1)S(1)}, u32[]{:S(2)}, u32[]{:S(2)}) %collective-permute-start.16) | collective-permute-done | bytes 64096 | tf_op jit(solution)/shard_map/ppermute | solution.py:28
  331.6 5.1 %collective-permute-start.19 = (f32[32]{0:T(128)S(1)}, f32[32]{0:T(128)S(1)}, u32[]{:S(2)}, u32[]{:S(2)}) collective-permute-start(f32[32]{0:T(128)S(1)} %max.19), channel_id=1, source_target_pairs={{0,32},{8,40},{16,48},{24,56},{32,0},{40,8},{48,16},{56,24},{64,96... | collective-permute-start | bytes 392 | tf_op jit(solution)/shard_map/ppermute | solution.py:28
  338.6 3.7 collective-permute-start.20
  344.0 8.8 %collective-permute-start.21 = (f32[32]{0:T(128)S(1)}, f32[32]{0:T(128)S(1)}, u32[]{:S(2)}, u32[]{:S(2)}) collective-permute-start(f32[32]{0:T(128)S(1)} %max.21), channel_id=1, source_target_pairs={{0,128},{8,136},{16,144},{24,152},{32,160},{40,168},{48,176},{56,1... | collective-permute-start | bytes 392 | tf_op jit(solution)/shard_map/ppermute | solution.py:28
  354.3 3.4 collective-permute-start.22
  358.5 5.2 %collective-permute-done.22 = f32[32]{0:T(128)S(1)} collective-permute-done((f32[32]{0:T(128)S(1)}, f32[32]{0:T(128)S(1)}, u32[]{:S(2)}, u32[]{:S(2)}) %collective-permute-start.22) | collective-permute-done | bytes 160 | tf_op jit(solution)/shard_map/ppermute | solution.py:28
  (113 shorter events, 68.3 us)
Async XLA Ops:
  7.2 288.7 %copy-start = (bf16[896,1000]{0,1:T(8,128)(2,1)S(1)}, bf16[896,1000]{0,1:T(8,128)(2,1)}, u32[]{:S(2)}) copy-start(bf16[896,1000]{0,1:T(8,128)(2,1)} %param.15) | copy-start | bytes 5376004
  7.2 126.3 %copy-start.3 = (s32[256]{0:T(256)S(1)}, s32[256]{0:T(256)}, u32[]{:S(2)}) copy-start(s32[256]{0:T(256)} %param.11) | copy-start | bytes 3076
  7.2 134.9 %copy-start.1 = (bf16[2,256,128]{2,1,0:T(8,128)(2,1)S(1)}, bf16[2,256,128]{2,1,0:T(8,128)(2,1)}, u32[]{:S(2)}) copy-start(bf16[2,256,128]{2,1,0:T(8,128)(2,1)} %param.10) | copy-start | bytes 393220
  7.2 103.3 %all-gather.4.cloned.1.call-start = ((), (), s32[]{:S(2)}) async-start(), calls=%async_computation.1 | async-start | bytes 6623232 | tf_op jit(solution)/shard_map/all_gather | solution.py:161
  7.9 197.0 %all-gather.6.cloned.1.call-start = ((), (), s32[]{:S(2)}) async-start(), calls=%async_computation.3 | async-start | bytes 19267584 | tf_op jit(solution)/shard_map/all_gather | solution.py:162
  110.6 253.6 %reduce-scatter.2.cloned.1.call-start = ((), (), s32[]{:S(2)}) async-start(), calls=%async_computation.2 | async-start | bytes 4644864 | tf_op jit(solution)/shard_map/reduce_scatter | solution.py:176
  112.2 23.4 %collective-permute-start = (bf16[514,128]{1,0:T(8,128)(2,1)S(1)}, bf16[514,128]{1,0:T(8,128)(2,1)}, u32[]{:S(2)}, u32[]{:S(2)}) collective-permute-start(bf16[514,128]{1,0:T(8,128)(2,1)S(1)} %pad_maximum_fusion), channel_id=1, source_target_pairs={{0,32},{8,40},{16,48},{24,56},{32,64},{40,72},{48,80},{56,88},{64,... | collective-permute-start | bytes 394760 | tf_op jit(solution)/shard_map/ppermute | solution.py:21
  116.2 20.3 %collective-permute-start.1 = (bf16[514,128]{1,0:T(8,128)(2,1)S(1)}, bf16[514,128]{1,0:T(8,128)(2,1)}, u32[]{:S(2)}, u32[]{:S(2)}) collective-permute-start(bf16[514,128]{1,0:T(8,128)(2,1)S(1)} %pad_maximum_fusion), channel_id=1, source_target_pairs={{0,24},{8,32},{16,40},{24,48},{32,56},{40,64},{48,72},{56,80},{64,... | collective-permute-start | bytes 394760 | tf_op jit(solution)/shard_map/ppermute | solution.py:21
  118.1 19.3 %collective-permute-start.2 = (bf16[514,128]{1,0:T(8,128)(2,1)S(1)}, bf16[514,128]{1,0:T(8,128)(2,1)}, u32[]{:S(2)}, u32[]{:S(2)}) collective-permute-start(bf16[514,128]{1,0:T(8,128)(2,1)S(1)} %pad_maximum_fusion), channel_id=1, source_target_pairs={{0,16},{8,24},{16,32},{24,40},{32,48},{40,56},{48,64},{56,72},{64,... | collective-permute-start | bytes 394760 | tf_op jit(solution)/shard_map/ppermute | solution.py:21
  121.0 17.4 %collective-permute-start.3 = (bf16[514,128]{1,0:T(8,128)(2,1)S(1)}, bf16[514,128]{1,0:T(8,128)(2,1)}, u32[]{:S(2)}, u32[]{:S(2)}) collective-permute-start(bf16[514,128]{1,0:T(8,128)(2,1)S(1)} %pad_maximum_fusion), channel_id=1, source_target_pairs={{0,8},{8,16},{16,24},{24,32},{32,40},{40,48},{48,56},{56,64},{64,7... | collective-permute-start | bytes 394760 | tf_op jit(solution)/shard_map/ppermute | solution.py:21
  126.6 6.9 %collective-permute-start.4 = (s32[1]{0:T(128)}, s32[1]{0:T(128)}, u32[]{:S(2)}, u32[]{:S(2)}) collective-permute-start(s32[1]{0:T(128)} %slice.109), channel_id=1, source_target_pairs={{8,0},{16,8},{24,16},{32,24},{40,32},{48,40},{56,48},{64,56},{72,6... | collective-permute-start | bytes 20 | tf_op jit(solution)/shard_map/ppermute | solution.py:21
  158.0 4.0 %collective-permute-start.5 = (bf16[32,1792]{1,0:T(8,128)(2,1)S(1)}, bf16[32,1792]{1,0:T(8,128)(2,1)S(1)}, u32[]{:S(2)}, u32[]{:S(2)}) collective-permute-start(bf16[32,1792]{1,0:T(8,128)(2,1)S(1)} %convolution_convert_fusion), channel_id=1, source_target_pairs={{0,8},{8,0},{16,24},{24,16},{32,40},{40,32},{48,56},{56,48},{64,72... | collective-permute-start | bytes 344072 | tf_op jit(solution)/shard_map/ppermute | solution.py:28
  162.0 7.3 %collective-permute-start.6 = (bf16[32,1792]{1,0:T(8,128)(2,1)S(1)}, bf16[32,1792]{1,0:T(8,128)(2,1)S(1)}, u32[]{:S(2)}, u32[]{:S(2)}) collective-permute-start(bf16[32,1792]{1,0:T(8,128)(2,1)S(1)} %add.129), channel_id=1, source_target_pairs={{0,16},{8,24},{16,0},{24,8},{32,48},{40,56},{48,32},{56,40},{64,80... | collective-permute-start | bytes 344072 | tf_op jit(solution)/shard_map/ppermute | solution.py:28
  169.4 8.2 %collective-permute-start.7 = (bf16[32,1792]{1,0:T(8,128)(2,1)S(1)}, bf16[32,1792]{1,0:T(8,128)(2,1)S(1)}, u32[]{:S(2)}, u32[]{:S(2)}) collective-permute-start(bf16[32,1792]{1,0:T(8,128)(2,1)S(1)} %add.130), channel_id=1, source_target_pairs={{0,32},{8,40},{16,48},{24,56},{32,0},{40,8},{48,16},{56,24},{64,96... | collective-permute-start | bytes 344072 | tf_op jit(solution)/shard_map/ppermute | solution.py:28
  177.6 7.3 %collective-permute-start.8 = (bf16[32,1792]{1,0:T(8,128)(2,1)S(1)}, bf16[32,1792]{1,0:T(8,128)(2,1)S(1)}, u32[]{:S(2)}, u32[]{:S(2)}) collective-permute-start(bf16[32,1792]{1,0:T(8,128)(2,1)S(1)} %add.131), channel_id=1, source_target_pairs={{0,64},{8,72},{16,80},{24,88},{32,96},{40,104},{48,112},{56,120},{... | collective-permute-start | bytes 344072 | tf_op jit(solution)/shard_map/ppermute | solution.py:28
  184.9 7.8 %collective-permute-start.9 = (bf16[32,1792]{1,0:T(8,128)(2,1)S(1)}, bf16[32,1792]{1,0:T(8,128)(2,1)S(1)}, u32[]{:S(2)}, u32[]{:S(2)}) collective-permute-start(bf16[32,1792]{1,0:T(8,128)(2,1)S(1)} %add.132), channel_id=1, source_target_pairs={{0,128},{8,136},{16,144},{24,152},{32,160},{40,168},{48,176},{56,1... | collective-permute-start | bytes 344072 | tf_op jit(solution)/shard_map/ppermute | solution.py:28
  192.8 11.2 %collective-permute-start.10 = (bf16[32,1792]{1,0:T(8,128)(2,1)S(1)}, bf16[32,1792]{1,0:T(8,128)(2,1)S(1)}, u32[]{:S(2)}, u32[]{:S(2)}) collective-permute-start(bf16[32,1792]{1,0:T(8,128)(2,1)S(1)} %add.133), channel_id=1, source_target_pairs={{0,256},{8,264},{16,272},{24,280},{32,288},{40,296},{48,304},{56,3... | collective-permute-start | bytes 344072 | tf_op jit(solution)/shard_map/ppermute | solution.py:28
  205.0 24.7 %copy-start.2 = (bf16[256,896]{1,0:T(8,128)(2,1)S(1)}, bf16[256,896]{1,0:T(8,128)(2,1)}, u32[]{:S(2)}) copy-start(bf16[256,896]{1,0:T(8,128)(2,1)} %copy.34) | copy-start | bytes 1376260
  251.0 44.6 %copy-start.4 = (bf16[896]{0:T(1024)(128)(2,1)S(1)}, bf16[896]{0:T(1024)(128)(2,1)}, u32[]{:S(2)}) copy-start(bf16[896]{0:T(1024)(128)(2,1)} %param.14) | copy-start | bytes 5380
  267.5 7.9 %collective-permute-start.11 = (bf16[32,4,896]{2,0,1:T(8,128)(2,1)S(1)}, bf16[32,4,896]{2,0,1:T(8,128)(2,1)S(1)}, u32[]{:S(2)}, u32[]{:S(2)}) collective-permute-start(bf16[32,4,896]{2,0,1:T(8,128)(2,1)S(1)} %dynamic-slice_bitcast_fusion), channel_id=1, source_target_pairs={{0,1},{1,0},{2,3},{3,2},{4,5},{5,4},{6,7},{7,6},{8,9},{9,8},{10,11... | collective-permute-start | bytes 688136 | tf_op jit(solution)/shard_map/ppermute | solution.py:45
  275.6 9.6 %collective-permute-start.12 = (bf16[32,2,896]{2,0,1:T(8,128)(2,1)S(1)}, bf16[32,2,896]{2,0,1:T(8,128)(2,1)S(1)}, u32[]{:S(2)}, u32[]{:S(2)}) collective-permute-start(bf16[32,2,896]{2,0,1:T(8,128)(2,1)S(1)} %dynamic-slice_bitcast_fusion.1), channel_id=1, source_target_pairs={{0,2},{1,3},{2,0},{3,1},{4,6},{5,7},{6,4},{7,5},{8,10},{9,11},{10,... | collective-permute-start | bytes 344072 | tf_op jit(solution)/shard_map/ppermute | solution.py:45
  285.2 10.4 %collective-permute-start.13 = (bf16[32,1,896]{2,0,1:T(8,128)(2,1)S(1)}, bf16[32,1,896]{2,0,1:T(8,128)(2,1)S(1)}, u32[]{:S(2)}, u32[]{:S(2)}) collective-permute-start(bf16[32,1,896]{2,0,1:T(8,128)(2,1)S(1)} %constant_dynamic-slice_fusion), channel_id=1, source_target_pairs={{0,4},{1,5},{2,6},{3,7},{4,0},{5,1},{6,2},{7,3},{8,12},{9,13},{10,... | collective-permute-start | bytes 172040 | tf_op jit(solution)/shard_map/ppermute | solution.py:45
  296.6 6.2 %collective-permute-start.14 = (bf16[32,1001]{1,0:T(8,128)(2,1)S(1)}, bf16[32,1001]{1,0:T(8,128)(2,1)S(1)}, u32[]{:S(2)}, u32[]{:S(2)}) collective-permute-start(bf16[32,1001]{1,0:T(8,128)(2,1)S(1)} %pad_maximum_fusion.2), channel_id=1, source_target_pairs={{0,1},{1,0},{2,3},{3,2},{4,5},{5,4},{6,7},{7,6},{8,9},{9,8},{10,11... | collective-permute-start | bytes 192200 | tf_op jit(solution)/shard_map/ppermute | solution.py:28
  302.8 7.6 %collective-permute-start.15 = (bf16[32,1001]{1,0:T(8,128)(2,1)S(1)}, bf16[32,1001]{1,0:T(8,128)(2,1)S(1)}, u32[]{:S(2)}, u32[]{:S(2)}) collective-permute-start(bf16[32,1001]{1,0:T(8,128)(2,1)S(1)} %fusion.66), channel_id=1, source_target_pairs={{0,2},{1,3},{2,0},{3,1},{4,6},{5,7},{6,4},{7,5},{8,10},{9,11},{10,... | collective-permute-start | bytes 192200 | tf_op jit(solution)/shard_map/ppermute | solution.py:28
  310.5 11.8 %collective-permute-start.16 = (bf16[32,1001]{1,0:T(8,128)(2,1)S(1)}, bf16[32,1001]{1,0:T(8,128)(2,1)S(1)}, u32[]{:S(2)}, u32[]{:S(2)}) collective-permute-start(bf16[32,1001]{1,0:T(8,128)(2,1)S(1)} %add.150), channel_id=1, source_target_pairs={{0,4},{1,5},{2,6},{3,7},{4,0},{5,1},{6,2},{7,3},{8,12},{9,13},{10,... | collective-permute-start | bytes 192200 | tf_op jit(solution)/shard_map/ppermute | solution.py:28
  323.2 3.0 collective-permute-start.17
  326.2 5.4 %collective-permute-start.18 = (f32[32]{0:T(128)S(1)}, f32[32]{0:T(128)S(1)}, u32[]{:S(2)}, u32[]{:S(2)}) collective-permute-start(f32[32]{0:T(128)S(1)} %max.18), channel_id=1, source_target_pairs={{0,16},{8,24},{16,0},{24,8},{32,48},{40,56},{48,32},{56,40},{64,80... | collective-permute-start | bytes 392 | tf_op jit(solution)/shard_map/ppermute | solution.py:28
  331.6 6.9 %collective-permute-start.19 = (f32[32]{0:T(128)S(1)}, f32[32]{0:T(128)S(1)}, u32[]{:S(2)}, u32[]{:S(2)}) collective-permute-start(f32[32]{0:T(128)S(1)} %max.19), channel_id=1, source_target_pairs={{0,32},{8,40},{16,48},{24,56},{32,0},{40,8},{48,16},{56,24},{64,96... | collective-permute-start | bytes 392 | tf_op jit(solution)/shard_map/ppermute | solution.py:28
  338.6 5.4 %collective-permute-start.20 = (f32[32]{0:T(128)S(1)}, f32[32]{0:T(128)S(1)}, u32[]{:S(2)}, u32[]{:S(2)}) collective-permute-start(f32[32]{0:T(128)S(1)} %max.20), channel_id=1, source_target_pairs={{0,64},{8,72},{16,80},{24,88},{32,96},{40,104},{48,112},{56,120},{... | collective-permute-start | bytes 392 | tf_op jit(solution)/shard_map/ppermute | solution.py:28
  344.0 10.3 %collective-permute-start.21 = (f32[32]{0:T(128)S(1)}, f32[32]{0:T(128)S(1)}, u32[]{:S(2)}, u32[]{:S(2)}) collective-permute-start(f32[32]{0:T(128)S(1)} %max.21), channel_id=1, source_target_pairs={{0,128},{8,136},{16,144},{24,152},{32,160},{40,168},{48,176},{56,1... | collective-permute-start | bytes 392 | tf_op jit(solution)/shard_map/ppermute | solution.py:28
  354.3 9.3 %collective-permute-start.22 = (f32[32]{0:T(128)S(1)}, f32[32]{0:T(128)S(1)}, u32[]{:S(2)}, u32[]{:S(2)}) collective-permute-start(f32[32]{0:T(128)S(1)} %max.22), channel_id=1, source_target_pairs={{0,256},{8,264},{16,272},{24,280},{32,288},{40,296},{48,304},{56,3... | collective-permute-start | bytes 392 | tf_op jit(solution)/shard_map/ppermute | solution.py:28
Sparse Core Ops, SparseCore 0:
  11.2 99.2 all-gather.3
  112.6 29.8 all-gather.5
  295.7 56.9 reduce-scatter.1

commit v12 on v10

--- a/solution.py
+++ b/solution.py
@@ -92,7 +92,6 @@
         parts_seg.append(got[2 * tok_rows :].reshape(-1)[:tok_rows].astype(jnp.int32))
     parts_kv.append(own_kv)
     parts_seg.append(segment)
-    next_first = from_behind(segment[:1], "req", -1)
     window = jnp.concatenate(parts_kv, axis=1)
     seg_window = jnp.concatenate(parts_seg, axis=0)
     span = window.shape[1]
@@ -141,18 +140,22 @@
     )
     context = context / jnp.transpose(total, (2, 0, 1))[..., None]
     attended = context.astype(jnp.bfloat16).reshape(tok_rows, heads_kv * GROUP * HD)
-    following = jnp.concatenate([segment[1:], next_first])
-    is_last_dev = device == devices_req - 1
-    is_end = following != segment
-    is_end = is_end.at[tok_rows - 1].set(is_end[tok_rows - 1] | is_last_dev)
+    is_end = jnp.concatenate([segment[1:] != segment[:-1], jnp.ones((1,), bool)])
     select = (is_end[:, None] & (segment[:, None] == request_ids[None, :])).astype(jnp.bfloat16)
+    held = jnp.any(segment[:, None] == request_ids[None, :], axis=0)
+    tag = jnp.where(held, device, -1).astype(jnp.bfloat16)
     end_rows = lax.dot_general(
         select,
         jnp.concatenate([attended, residual], axis=1),
         (((0,), (0,)), ((), ())),
         preferred_element_type=jnp.float32,
     ).astype(jnp.bfloat16)
-    end_rows = butterfly(end_rows, "req", jnp.add)
+    end_rows = jnp.concatenate([end_rows, tag[:, None]], axis=1)
+
+    def latest(mine, other):
+        return jnp.where(other[:, -1:] > mine[:, -1:], other, mine)
+
+    end_rows = butterfly(end_rows, "req", latest)[:, :-1]
     attended, end_rows = lax.optimization_barrier((attended, end_rows))
     end_att, end_res = end_rows[:, : attended.shape[1]], end_rows[:, attended.shape[1] :]
 

time: 246 us -> 240 us (0.976); the launches traced: 242 us -> 239 us
  waiting for transfers between devices: 73.2 us -> 93.8 us
  starting transfers between devices: 99.4 us -> 79.9 us
  matrix products: 21 us -> 17.5 us
    ppermute x15, starting transfers between devices: 68.8 us -> 53 us  [butterfly(): lax.ppermute(value, axis, [(source, source ^ stride) for source in range(...]
    ppermute x15, waiting for transfers between devices: 54.7 us -> 67.4 us  [butterfly(): lax.ppermute(value, axis, [(source, source ^ stride) for source in range(...]
    all_gather x1, waiting for transfers between devices: 2.14 us -> 7.7 us  [local(): full_weight = lax.all_gather(out_weight, 'req', axis=1, tiled=True)]
    dot_general x1, matrix products: 14.6 us -> 11.2 us  [local(): jnp.einsum('tk,kgn->gtn', jnp.concatenate([attended, end_att], axis=0), f...]
    slice x3 -> x0, local copies, waits for them, and re-layouts: 2.53 us -> none  [the longest x1 1.19 us: local(): next_first = from_behind(segment[:1], 'req', -1)]
    ppermute x5 -> x4, starting transfers between devices: 16.9 us -> 15.6 us  [from_behind(): lax.ppermute(value, axis, [(source, source + steps) for source in range(i...]
  transfers between devices with their start and end apart: 25 -> 24, of which waited for: 19 -> 19; matrix products, arithmetic and copies ran while one was open for 15% -> 15% of each run, Pallas kernels for 0% -> 0%
where the time goes in v12:
time: 240 us; the launch traced here: 239 us
  waiting for transfers between devices  93.8 us (39%)
  starting transfers between devices  79.9 us (33%)
  other arithmetic  20.6 us (9%)
  matrix products  17.5 us (7%)
  between operations  14.6 us (6%)
  local copies, waits for them, and re-layouts  12.2 us (5%)
    ppermute x15, waiting for transfers between devices, butterfly(): lax.ppermute(value, axis, [(source, source ^ stride) for source in range(...  67.4 us
    ppermute x15, starting transfers between devices, butterfly(): lax.ppermute(value, axis, [(source, source ^ stride) for source in range(...  53 us
    ppermute x3, waiting for transfers between devices, halving_scatter(): lax.ppermute(give, axis, [(source, source ^ bit) for source in range(coun...  18 us
    ppermute x4, starting transfers between devices, from_behind(): lax.ppermute(value, axis, [(source, source + steps) for source in range(i...  15.6 us
    ppermute x3, starting transfers between devices, halving_scatter(): lax.ppermute(give, axis, [(source, source ^ bit) for source in range(coun...  11.2 us
    dot_general x1, matrix products, local(): jnp.einsum('tk,kgn->gtn', jnp.concatenate([attended, end_att], axis=0), f...  11.2 us
    all_gather x1, waiting for transfers between devices, local(): full_weight = lax.all_gather(out_weight, 'req', axis=1, tiled=True)  7.7 us
  transfers between devices with their start and end apart: 24, of which 19 were waited for; matrix products, arithmetic and copies ran while one was open for 15% of the time, Pallas kernels for 0%

profile of v12, /device:TPU:56, one launch (start us, length us, event | category | flops | bytes accessed | tf_op | source)
XLA Modules:
  0.0 238.6 jit_solution(11665168954545086751)
XLA Ops:
  9.6 4.9 %collective-permute-start = (bf16[514,128]{1,0:T(8,128)(2,1)S(1)}, bf16[514,128]{1,0:T(8,128)(2,1)S(1)}, u32[]{:S(2)}, u32[]{:S(2)}) collective-permute-start(bf16[514,128]{1,0:T(8,128)(2,1)S(1)} %pad_maximum_fusion), channel_id=1, source_target_pairs={{0,32},{8,40},{16,48},{24,56},{32,64},{40,72},{48,80},{56,88},{64,... | collective-permute-start | bytes 394760 | tf_op jit(solution)/shard_map/ppermute | solution.py:20
  16.8 4.2 %collective-permute-start.2 = (bf16[514,128]{1,0:T(8,128)(2,1)S(1)}, bf16[514,128]{1,0:T(8,128)(2,1)}, u32[]{:S(2)}, u32[]{:S(2)}) collective-permute-start(bf16[514,128]{1,0:T(8,128)(2,1)S(1)} %pad_maximum_fusion), channel_id=1, source_target_pairs={{0,16},{8,24},{16,32},{24,40},{32,48},{40,56},{48,64},{56,72},{64,... | collective-permute-start | bytes 394760 | tf_op jit(solution)/shard_map/ppermute | solution.py:20
  21.1 4.1 %collective-permute-start.3 = (bf16[514,128]{1,0:T(8,128)(2,1)S(1)}, bf16[514,128]{1,0:T(8,128)(2,1)}, u32[]{:S(2)}, u32[]{:S(2)}) collective-permute-start(bf16[514,128]{1,0:T(8,128)(2,1)S(1)} %pad_maximum_fusion), channel_id=1, source_target_pairs={{0,8},{8,16},{16,24},{24,32},{32,40},{40,48},{48,56},{56,64},{64,7... | collective-permute-start | bytes 394760 | tf_op jit(solution)/shard_map/ppermute | solution.py:20
  43.3 3.0 %fusion.25 = (bf16[1280,1,64]{2,0,1:T(8,128)(2,1)S(1)}, bf16[1280,1,64]{2,0,1:T(8,128)(2,1)S(1)}) fusion(f32[1280,1,128]{2,0,1:T(8,128)S(1)} %fusion.37, f32[64]{0:T(128)S(1)} %negate_power_fusion, f32[1280]{0:T(1024)S(1)} %convert_subtract_fusion), kind=kLoop, calls=%fused_computation.30 | loop fusion | flops 737280 | bytes 988416 | tf_op jit(solution)/shard_map/convert.22
  60.0 4.9 %collective-permute-done.5 = bf16[32,1793]{1,0:T(8,128)(2,1)S(1)} collective-permute-done((bf16[32,1793]{1,0:T(8,128)(2,1)S(1)}, bf16[32,1793]{1,0:T(8,128)(2,1)S(1)}, u32[]{:S(2)}, u32[]{:S(2)}) %collective-permute-start.5) | collective-permute-done | bytes 114784 | tf_op jit(solution)/shard_map/ppermute | solution.py:27
  65.1 4.1 %collective-permute-start.6 = (bf16[32,1793]{1,0:T(8,128)(2,1)S(1)}, bf16[32,1793]{1,0:T(8,128)(2,1)S(1)}, u32[]{:S(2)}, u32[]{:S(2)}) collective-permute-start(bf16[32,1793]{1,0:T(8,128)(2,1)S(1)} %broadcast_select_fusion.3), channel_id=1, source_target_pairs={{0,32},{8,40},{16,48},{24,56},{32,0},{40,8},{48,16},{56,24},{64,96... | collective-permute-start | bytes 344264 | tf_op jit(solution)/shard_map/ppermute | solution.py:27
  69.2 4.2 %collective-permute-done.6 = bf16[32,1793]{1,0:T(8,128)(2,1)S(1)} collective-permute-done((bf16[32,1793]{1,0:T(8,128)(2,1)S(1)}, bf16[32,1793]{1,0:T(8,128)(2,1)S(1)}, u32[]{:S(2)}, u32[]{:S(2)}) %collective-permute-start.6) | collective-permute-done | bytes 114784 | tf_op jit(solution)/shard_map/ppermute | solution.py:27
  73.6 4.6 %collective-permute-start.7 = (bf16[32,1793]{1,0:T(8,128)(2,1)S(1)}, bf16[32,1793]{1,0:T(8,128)(2,1)S(1)}, u32[]{:S(2)}, u32[]{:S(2)}) collective-permute-start(bf16[32,1793]{1,0:T(8,128)(2,1)S(1)} %broadcast_select_fusion.2), channel_id=1, source_target_pairs={{0,64},{8,72},{16,80},{24,88},{32,96},{40,104},{48,112},{56,120},{... | collective-permute-start | bytes 344264 | tf_op jit(solution)/shard_map/ppermute | solution.py:27
  78.2 5.2 %collective-permute-done.7 = bf16[32,1793]{1,0:T(8,128)(2,1)S(1)} collective-permute-done((bf16[32,1793]{1,0:T(8,128)(2,1)S(1)}, bf16[32,1793]{1,0:T(8,128)(2,1)S(1)}, u32[]{:S(2)}, u32[]{:S(2)}) %collective-permute-start.7) | collective-permute-done | bytes 114784 | tf_op jit(solution)/shard_map/ppermute | solution.py:27
  83.6 7.3 %collective-permute-start.8 = (bf16[32,1793]{1,0:T(8,128)(2,1)S(1)}, bf16[32,1793]{1,0:T(8,128)(2,1)S(1)}, u32[]{:S(2)}, u32[]{:S(2)}) collective-permute-start(bf16[32,1793]{1,0:T(8,128)(2,1)S(1)} %broadcast_select_fusion.1), channel_id=1, source_target_pairs={{0,128},{8,136},{16,144},{24,152},{32,160},{40,168},{48,176},{56,1... | collective-permute-start | bytes 344264 | tf_op jit(solution)/shard_map/ppermute | solution.py:27
  90.9 7.8 %collective-permute-done.8 = bf16[32,1793]{1,0:T(8,128)(2,1)S(1)} collective-permute-done((bf16[32,1793]{1,0:T(8,128)(2,1)S(1)}, bf16[32,1793]{1,0:T(8,128)(2,1)S(1)}, u32[]{:S(2)}, u32[]{:S(2)}) %collective-permute-start.8) | collective-permute-done | bytes 114784 | tf_op jit(solution)/shard_map/ppermute | solution.py:27
  98.9 6.5 %collective-permute-start.9 = (bf16[32,1793]{1,0:T(8,128)(2,1)S(1)}, bf16[32,1793]{1,0:T(8,128)(2,1)S(1)}, u32[]{:S(2)}, u32[]{:S(2)}) collective-permute-start(bf16[32,1793]{1,0:T(8,128)(2,1)S(1)} %broadcast_select_fusion), channel_id=1, source_target_pairs={{0,256},{8,264},{16,272},{24,280},{32,288},{40,296},{48,304},{56,3... | collective-permute-start | bytes 344264 | tf_op jit(solution)/shard_map/ppermute | solution.py:27
  105.4 8.2 %collective-permute-done.9 = bf16[32,1793]{1,0:T(8,128)(2,1)S(1)} collective-permute-done((bf16[32,1793]{1,0:T(8,128)(2,1)S(1)}, bf16[32,1793]{1,0:T(8,128)(2,1)S(1)}, u32[]{:S(2)}, u32[]{:S(2)}) %collective-permute-start.9) | collective-permute-done | bytes 114784 | tf_op jit(solution)/shard_map/ppermute | solution.py:27
  114.8 7.7 %all-gather.2.cloned.1.call-done = bf16[896,7168]{0,1:T(8,128)(2,1)} async-done(((bf16[896,112]{0,1:T(8,128)(2,1)}), bf16[896,7168]{0,1:T(8,128)(2,1)}) %all-gather.2.cloned.1.call-update) | async-done | bytes 12845072 | tf_op jit(solution)/shard_map/all_gather | solution.py:162
  122.5 11.2 %convert_bitcast_fusion = bf16[8,288,896]{2,1,0:T(8,128)(2,1)} fusion(bf16[896,8,896]{0,2,1:T(8,128)(2,1)} %bitcast.151, bf16[32,896]{1,0:T(8,128)(2,1)S(1)} %slice.145, bf16[256,896]{1,0:T(8,128)(2,1)} %copy.39), kind=kOutput, calls=%fused_computation.9 | convolution fusion | flops 3702472704 | bytes 17489920 | tf_op jit(solution)/shard_map/tk,kgn->gtn/dot_general | solution.py:164
  134.8 3.2 %collective-permute-start.10 = (bf16[32,4,896]{2,0,1:T(8,128)(2,1)S(1)}, bf16[32,4,896]{2,0,1:T(8,128)(2,1)S(1)}, u32[]{:S(2)}, u32[]{:S(2)}) collective-permute-start(bf16[32,4,896]{2,0,1:T(8,128)(2,1)S(1)} %dynamic-slice_bitcast_fusion), channel_id=1, source_target_pairs={{0,1},{1,0},{2,3},{3,2},{4,5},{5,4},{6,7},{7,6},{8,9},{9,8},{10,11... | collective-permute-start | bytes 688136 | tf_op jit(solution)/shard_map/ppermute | solution.py:44
  138.0 6.4 %collective-permute-done.10 = bf16[32,4,896]{2,0,1:T(8,128)(2,1)S(1)} collective-permute-done((bf16[32,4,896]{2,0,1:T(8,128)(2,1)S(1)}, bf16[32,4,896]{2,0,1:T(8,128)(2,1)S(1)}, u32[]{:S(2)}, u32[]{:S(2)}) %collective-permute-start.10) | collective-permute-done | bytes 229408 | tf_op jit(solution)/shard_map/ppermute | solution.py:44
  144.5 3.9 %collective-permute-start.11 = (bf16[32,2,896]{2,0,1:T(8,128)(2,1)S(1)}, bf16[32,2,896]{2,0,1:T(8,128)(2,1)S(1)}, u32[]{:S(2)}, u32[]{:S(2)}) collective-permute-start(bf16[32,2,896]{2,0,1:T(8,128)(2,1)S(1)} %dynamic-slice_bitcast_fusion.1), channel_id=1, source_target_pairs={{0,2},{1,3},{2,0},{3,1},{4,6},{5,7},{6,4},{7,5},{8,10},{9,11},{10,... | collective-permute-start | bytes 344072 | tf_op jit(solution)/shard_map/ppermute | solution.py:44
  148.5 5.8 %collective-permute-done.11 = bf16[32,2,896]{2,0,1:T(8,128)(2,1)S(1)} collective-permute-done((bf16[32,2,896]{2,0,1:T(8,128)(2,1)S(1)}, bf16[32,2,896]{2,0,1:T(8,128)(2,1)S(1)}, u32[]{:S(2)}, u32[]{:S(2)}) %collective-permute-start.11) | collective-permute-done | bytes 114720 | tf_op jit(solution)/shard_map/ppermute | solution.py:44
  154.3 4.1 %collective-permute-start.12 = (bf16[32,1,896]{2,0,1:T(8,128)(2,1)S(1)}, bf16[32,1,896]{2,0,1:T(8,128)(2,1)S(1)}, u32[]{:S(2)}, u32[]{:S(2)}) collective-permute-start(bf16[32,1,896]{2,0,1:T(8,128)(2,1)S(1)} %constant_dynamic-slice_fusion), channel_id=1, source_target_pairs={{0,4},{1,5},{2,6},{3,7},{4,0},{5,1},{6,2},{7,3},{8,12},{9,13},{10,... | collective-permute-start | bytes 172040 | tf_op jit(solution)/shard_map/ppermute | solution.py:44
  158.5 5.9 %collective-permute-done.12 = bf16[32,1,896]{2,0,1:T(8,128)(2,1)S(1)} collective-permute-done((bf16[32,1,896]{2,0,1:T(8,128)(2,1)S(1)}, bf16[32,1,896]{2,0,1:T(8,128)(2,1)S(1)}, u32[]{:S(2)}, u32[]{:S(2)}) %collective-permute-start.12) | collective-permute-done | bytes 57376 | tf_op jit(solution)/shard_map/ppermute | solution.py:44
  167.3 4.2 %collective-permute-done.13 = bf16[32,1001]{1,0:T(8,128)(2,1)S(1)} collective-permute-done((bf16[32,1001]{1,0:T(8,128)(2,1)S(1)}, bf16[32,1001]{1,0:T(8,128)(2,1)S(1)}, u32[]{:S(2)}, u32[]{:S(2)}) %collective-permute-start.13) | collective-permute-done | bytes 64096 | tf_op jit(solution)/shard_map/ppermute | solution.py:27
  171.6 3.3 %collective-permute-start.14 = (bf16[32,1001]{1,0:T(8,128)(2,1)S(1)}, bf16[32,1001]{1,0:T(8,128)(2,1)S(1)}, u32[]{:S(2)}, u32[]{:S(2)}) collective-permute-start(bf16[32,1001]{1,0:T(8,128)(2,1)S(1)} %fusion.64), channel_id=1, source_target_pairs={{0,2},{1,3},{2,0},{3,1},{4,6},{5,7},{6,4},{7,5},{8,10},{9,11},{10,... | collective-permute-start | bytes 192200 | tf_op jit(solution)/shard_map/ppermute | solution.py:27
  174.8 5.0 %collective-permute-done.14 = bf16[32,1001]{1,0:T(8,128)(2,1)S(1)} collective-permute-done((bf16[32,1001]{1,0:T(8,128)(2,1)S(1)}, bf16[32,1001]{1,0:T(8,128)(2,1)S(1)}, u32[]{:S(2)}, u32[]{:S(2)}) %collective-permute-start.14) | collective-permute-done | bytes 64096 | tf_op jit(solution)/shard_map/ppermute | solution.py:27
  179.8 4.4 %collective-permute-start.15 = (bf16[32,1001]{1,0:T(8,128)(2,1)S(1)}, bf16[32,1001]{1,0:T(8,128)(2,1)S(1)}, u32[]{:S(2)}, u32[]{:S(2)}) collective-permute-start(bf16[32,1001]{1,0:T(8,128)(2,1)S(1)} %add.116), channel_id=1, source_target_pairs={{0,4},{1,5},{2,6},{3,7},{4,0},{5,1},{6,2},{7,3},{8,12},{9,13},{10,... | collective-permute-start | bytes 192200 | tf_op jit(solution)/shard_map/ppermute | solution.py:27
  184.2 7.6 %collective-permute-done.15 = bf16[32,1001]{1,0:T(8,128)(2,1)S(1)} collective-permute-done((bf16[32,1001]{1,0:T(8,128)(2,1)S(1)}, bf16[32,1001]{1,0:T(8,128)(2,1)S(1)}, u32[]{:S(2)}, u32[]{:S(2)}) %collective-permute-start.15) | collective-permute-done | bytes 64096 | tf_op jit(solution)/shard_map/ppermute | solution.py:27
  201.2 3.2 %collective-permute-start.18 = (f32[32]{0:T(128)S(1)}, f32[32]{0:T(128)S(1)}, u32[]{:S(2)}, u32[]{:S(2)}) collective-permute-start(f32[32]{0:T(128)S(1)} %max.19), channel_id=1, source_target_pairs={{0,32},{8,40},{16,48},{24,56},{32,0},{40,8},{48,16},{56,24},{64,96... | collective-permute-start | bytes 392 | tf_op jit(solution)/shard_map/ppermute | solution.py:27
  204.4 3.7 %collective-permute-done.18 = f32[32]{0:T(128)S(1)} collective-permute-done((f32[32]{0:T(128)S(1)}, f32[32]{0:T(128)S(1)}, u32[]{:S(2)}, u32[]{:S(2)}) %collective-permute-start.18) | collective-permute-done | bytes 160 | tf_op jit(solution)/shard_map/ppermute | solution.py:27
  210.1 3.5 %collective-permute-done.19 = f32[32]{0:T(128)S(1)} collective-permute-done((f32[32]{0:T(128)S(1)}, f32[32]{0:T(128)S(1)}, u32[]{:S(2)}, u32[]{:S(2)}) %collective-permute-start.19) | collective-permute-done | bytes 160 | tf_op jit(solution)/shard_map/ppermute | solution.py:27
  215.6 4.3 %collective-permute-done.20 = f32[32]{0:T(128)S(1)} collective-permute-done((f32[32]{0:T(128)S(1)}, f32[32]{0:T(128)S(1)}, u32[]{:S(2)}, u32[]{:S(2)}) %collective-permute-start.20) | collective-permute-done | bytes 160 | tf_op jit(solution)/shard_map/ppermute | solution.py:27
  219.9 4.9 %collective-permute-start.21 = (f32[32]{0:T(128)S(1)}, f32[32]{0:T(128)S(1)}, u32[]{:S(2)}, u32[]{:S(2)}) collective-permute-start(f32[32]{0:T(128)S(1)} %max.22), channel_id=1, source_target_pairs={{0,256},{8,264},{16,272},{24,280},{32,288},{40,296},{48,304},{56,3... | collective-permute-start | bytes 392 | tf_op jit(solution)/shard_map/ppermute | solution.py:27
  225.6 3.7 %collective-permute-done.21 = f32[32]{0:T(128)S(1)} collective-permute-done((f32[32]{0:T(128)S(1)}, f32[32]{0:T(128)S(1)}, u32[]{:S(2)}, u32[]{:S(2)}) %collective-permute-start.21) | collective-permute-done | bytes 160 | tf_op jit(solution)/shard_map/ppermute | solution.py:27
  (108 shorter events, 59.0 us)
Async XLA Ops:
  7.2 157.4 %copy-start = (bf16[896,1000]{0,1:T(8,128)(2,1)S(1)}, bf16[896,1000]{0,1:T(8,128)(2,1)}, u32[]{:S(2)}) copy-start(bf16[896,1000]{0,1:T(8,128)(2,1)} %param.13) | copy-start | bytes 5376004
  7.2 35.0 %copy-start.1 = (s32[256]{0:T(256)S(1)}, s32[256]{0:T(256)}, u32[]{:S(2)}) copy-start(s32[256]{0:T(256)} %param.9) | copy-start | bytes 3076
  7.2 115.3 %all-gather.2.cloned.1.call-start = ((), (), s32[]{:S(2)}) async-start(), calls=%async_computation.1 | async-start | bytes 13045760 | tf_op jit(solution)/shard_map/all_gather | solution.py:162
  7.9 221.8 %reduce-scatter.2.cloned.1.call-start = ((), (), s32[]{:S(2)}) async-start(), calls=%async_computation.2 | async-start | bytes 4644864 | tf_op jit(solution)/shard_map/reduce_scatter | solution.py:173
  9.6 22.2 %collective-permute-start = (bf16[514,128]{1,0:T(8,128)(2,1)S(1)}, bf16[514,128]{1,0:T(8,128)(2,1)S(1)}, u32[]{:S(2)}, u32[]{:S(2)}) collective-permute-start(bf16[514,128]{1,0:T(8,128)(2,1)S(1)} %pad_maximum_fusion), channel_id=1, source_target_pairs={{0,32},{8,40},{16,48},{24,56},{32,64},{40,72},{48,80},{56,88},{64,... | collective-permute-start | bytes 394760 | tf_op jit(solution)/shard_map/ppermute | solution.py:20
  14.5 17.3 %collective-permute-start.1 = (bf16[514,128]{1,0:T(8,128)(2,1)S(1)}, bf16[514,128]{1,0:T(8,128)(2,1)}, u32[]{:S(2)}, u32[]{:S(2)}) collective-permute-start(bf16[514,128]{1,0:T(8,128)(2,1)S(1)} %pad_maximum_fusion), channel_id=1, source_target_pairs={{0,24},{8,32},{16,40},{24,48},{32,56},{40,64},{48,72},{56,80},{64,... | collective-permute-start | bytes 394760 | tf_op jit(solution)/shard_map/ppermute | solution.py:20
  16.8 15.9 %collective-permute-start.2 = (bf16[514,128]{1,0:T(8,128)(2,1)S(1)}, bf16[514,128]{1,0:T(8,128)(2,1)}, u32[]{:S(2)}, u32[]{:S(2)}) collective-permute-start(bf16[514,128]{1,0:T(8,128)(2,1)S(1)} %pad_maximum_fusion), channel_id=1, source_target_pairs={{0,16},{8,24},{16,32},{24,40},{32,48},{40,56},{48,64},{56,72},{64,... | collective-permute-start | bytes 394760 | tf_op jit(solution)/shard_map/ppermute | solution.py:20
  21.1 12.6 %collective-permute-start.3 = (bf16[514,128]{1,0:T(8,128)(2,1)S(1)}, bf16[514,128]{1,0:T(8,128)(2,1)}, u32[]{:S(2)}, u32[]{:S(2)}) collective-permute-start(bf16[514,128]{1,0:T(8,128)(2,1)S(1)} %pad_maximum_fusion), channel_id=1, source_target_pairs={{0,8},{8,16},{16,24},{24,32},{32,40},{40,48},{48,56},{56,64},{64,7... | collective-permute-start | bytes 394760 | tf_op jit(solution)/shard_map/ppermute | solution.py:20
  54.1 3.2 %collective-permute-start.4 = (bf16[32,1793]{1,0:T(8,128)(2,1)S(1)}, bf16[32,1793]{1,0:T(8,128)(2,1)S(1)}, u32[]{:S(2)}, u32[]{:S(2)}) collective-permute-start(bf16[32,1793]{1,0:T(8,128)(2,1)S(1)} %pad_maximum_fusion.1), channel_id=1, source_target_pairs={{0,8},{8,0},{16,24},{24,16},{32,40},{40,32},{48,56},{56,48},{64,72... | collective-permute-start | bytes 344264 | tf_op jit(solution)/shard_map/ppermute | solution.py:27
  57.6 7.3 %collective-permute-start.5 = (bf16[32,1793]{1,0:T(8,128)(2,1)S(1)}, bf16[32,1793]{1,0:T(8,128)(2,1)S(1)}, u32[]{:S(2)}, u32[]{:S(2)}) collective-permute-start(bf16[32,1793]{1,0:T(8,128)(2,1)S(1)} %broadcast_select_fusion.4), channel_id=1, source_target_pairs={{0,16},{8,24},{16,0},{24,8},{32,48},{40,56},{48,32},{56,40},{64,80... | collective-permute-start | bytes 344264 | tf_op jit(solution)/shard_map/ppermute | solution.py:27
  65.1 8.3 %collective-permute-start.6 = (bf16[32,1793]{1,0:T(8,128)(2,1)S(1)}, bf16[32,1793]{1,0:T(8,128)(2,1)S(1)}, u32[]{:S(2)}, u32[]{:S(2)}) collective-permute-start(bf16[32,1793]{1,0:T(8,128)(2,1)S(1)} %broadcast_select_fusion.3), channel_id=1, source_target_pairs={{0,32},{8,40},{16,48},{24,56},{32,0},{40,8},{48,16},{56,24},{64,96... | collective-permute-start | bytes 344264 | tf_op jit(solution)/shard_map/ppermute | solution.py:27
  73.6 9.8 %collective-permute-start.7 = (bf16[32,1793]{1,0:T(8,128)(2,1)S(1)}, bf16[32,1793]{1,0:T(8,128)(2,1)S(1)}, u32[]{:S(2)}, u32[]{:S(2)}) collective-permute-start(bf16[32,1793]{1,0:T(8,128)(2,1)S(1)} %broadcast_select_fusion.2), channel_id=1, source_target_pairs={{0,64},{8,72},{16,80},{24,88},{32,96},{40,104},{48,112},{56,120},{... | collective-permute-start | bytes 344264 | tf_op jit(solution)/shard_map/ppermute | solution.py:27
  83.6 15.1 %collective-permute-start.8 = (bf16[32,1793]{1,0:T(8,128)(2,1)S(1)}, bf16[32,1793]{1,0:T(8,128)(2,1)S(1)}, u32[]{:S(2)}, u32[]{:S(2)}) collective-permute-start(bf16[32,1793]{1,0:T(8,128)(2,1)S(1)} %broadcast_select_fusion.1), channel_id=1, source_target_pairs={{0,128},{8,136},{16,144},{24,152},{32,160},{40,168},{48,176},{56,1... | collective-permute-start | bytes 344264 | tf_op jit(solution)/shard_map/ppermute | solution.py:27
  98.9 14.7 %collective-permute-start.9 = (bf16[32,1793]{1,0:T(8,128)(2,1)S(1)}, bf16[32,1793]{1,0:T(8,128)(2,1)S(1)}, u32[]{:S(2)}, u32[]{:S(2)}) collective-permute-start(bf16[32,1793]{1,0:T(8,128)(2,1)S(1)} %broadcast_select_fusion), channel_id=1, source_target_pairs={{0,256},{8,264},{16,272},{24,280},{32,288},{40,296},{48,304},{56,3... | collective-permute-start | bytes 344264 | tf_op jit(solution)/shard_map/ppermute | solution.py:27
  122.5 41.9 %copy-start.2 = (bf16[896]{0:T(1024)(128)(2,1)S(1)}, bf16[896]{0:T(1024)(128)(2,1)}, u32[]{:S(2)}) copy-start(bf16[896]{0:T(1024)(128)(2,1)} %param.12) | copy-start | bytes 5380
  134.8 9.7 %collective-permute-start.10 = (bf16[32,4,896]{2,0,1:T(8,128)(2,1)S(1)}, bf16[32,4,896]{2,0,1:T(8,128)(2,1)S(1)}, u32[]{:S(2)}, u32[]{:S(2)}) collective-permute-start(bf16[32,4,896]{2,0,1:T(8,128)(2,1)S(1)} %dynamic-slice_bitcast_fusion), channel_id=1, source_target_pairs={{0,1},{1,0},{2,3},{3,2},{4,5},{5,4},{6,7},{7,6},{8,9},{9,8},{10,11... | collective-permute-start | bytes 688136 | tf_op jit(solution)/shard_map/ppermute | solution.py:44
  144.5 9.7 %collective-permute-start.11 = (bf16[32,2,896]{2,0,1:T(8,128)(2,1)S(1)}, bf16[32,2,896]{2,0,1:T(8,128)(2,1)S(1)}, u32[]{:S(2)}, u32[]{:S(2)}) collective-permute-start(bf16[32,2,896]{2,0,1:T(8,128)(2,1)S(1)} %dynamic-slice_bitcast_fusion.1), channel_id=1, source_target_pairs={{0,2},{1,3},{2,0},{3,1},{4,6},{5,7},{6,4},{7,5},{8,10},{9,11},{10,... | collective-permute-start | bytes 344072 | tf_op jit(solution)/shard_map/ppermute | solution.py:44
  154.3 10.0 %collective-permute-start.12 = (bf16[32,1,896]{2,0,1:T(8,128)(2,1)S(1)}, bf16[32,1,896]{2,0,1:T(8,128)(2,1)S(1)}, u32[]{:S(2)}, u32[]{:S(2)}) collective-permute-start(bf16[32,1,896]{2,0,1:T(8,128)(2,1)S(1)} %constant_dynamic-slice_fusion), channel_id=1, source_target_pairs={{0,4},{1,5},{2,6},{3,7},{4,0},{5,1},{6,2},{7,3},{8,12},{9,13},{10,... | collective-permute-start | bytes 172040 | tf_op jit(solution)/shard_map/ppermute | solution.py:44
  165.3 6.2 %collective-permute-start.13 = (bf16[32,1001]{1,0:T(8,128)(2,1)S(1)}, bf16[32,1001]{1,0:T(8,128)(2,1)S(1)}, u32[]{:S(2)}, u32[]{:S(2)}) collective-permute-start(bf16[32,1001]{1,0:T(8,128)(2,1)S(1)} %pad_maximum_fusion.3), channel_id=1, source_target_pairs={{0,1},{1,0},{2,3},{3,2},{4,5},{5,4},{6,7},{7,6},{8,9},{9,8},{10,11... | collective-permute-start | bytes 192200 | tf_op jit(solution)/shard_map/ppermute | solution.py:27
  171.6 8.2 %collective-permute-start.14 = (bf16[32,1001]{1,0:T(8,128)(2,1)S(1)}, bf16[32,1001]{1,0:T(8,128)(2,1)S(1)}, u32[]{:S(2)}, u32[]{:S(2)}) collective-permute-start(bf16[32,1001]{1,0:T(8,128)(2,1)S(1)} %fusion.64), channel_id=1, source_target_pairs={{0,2},{1,3},{2,0},{3,1},{4,6},{5,7},{6,4},{7,5},{8,10},{9,11},{10,... | collective-permute-start | bytes 192200 | tf_op jit(solution)/shard_map/ppermute | solution.py:27
  179.8 12.0 %collective-permute-start.15 = (bf16[32,1001]{1,0:T(8,128)(2,1)S(1)}, bf16[32,1001]{1,0:T(8,128)(2,1)S(1)}, u32[]{:S(2)}, u32[]{:S(2)}) collective-permute-start(bf16[32,1001]{1,0:T(8,128)(2,1)S(1)} %add.116), channel_id=1, source_target_pairs={{0,4},{1,5},{2,6},{3,7},{4,0},{5,1},{6,2},{7,3},{8,12},{9,13},{10,... | collective-permute-start | bytes 192200 | tf_op jit(solution)/shard_map/ppermute | solution.py:27
  192.8 3.0 %collective-permute-start.16 = (f32[32]{0:T(128)S(1)}, f32[32]{0:T(128)S(1)}, u32[]{:S(2)}, u32[]{:S(2)}) collective-permute-start(f32[32]{0:T(128)S(1)} %fusion.41), channel_id=1, source_target_pairs={{0,8},{8,0},{16,24},{24,16},{32,40},{40,32},{48,56},{56,48},{64,72... | collective-permute-start | bytes 392 | tf_op jit(solution)/shard_map/ppermute | solution.py:27
  195.8 5.4 %collective-permute-start.17 = (f32[32]{0:T(128)S(1)}, f32[32]{0:T(128)S(1)}, u32[]{:S(2)}, u32[]{:S(2)}) collective-permute-start(f32[32]{0:T(128)S(1)} %max.18), channel_id=1, source_target_pairs={{0,16},{8,24},{16,0},{24,8},{32,48},{40,56},{48,32},{56,40},{64,80... | collective-permute-start | bytes 392 | tf_op jit(solution)/shard_map/ppermute | solution.py:27
  201.2 6.9 %collective-permute-start.18 = (f32[32]{0:T(128)S(1)}, f32[32]{0:T(128)S(1)}, u32[]{:S(2)}, u32[]{:S(2)}) collective-permute-start(f32[32]{0:T(128)S(1)} %max.19), channel_id=1, source_target_pairs={{0,32},{8,40},{16,48},{24,56},{32,0},{40,8},{48,16},{56,24},{64,96... | collective-permute-start | bytes 392 | tf_op jit(solution)/shard_map/ppermute | solution.py:27
  208.1 5.4 %collective-permute-start.19 = (f32[32]{0:T(128)S(1)}, f32[32]{0:T(128)S(1)}, u32[]{:S(2)}, u32[]{:S(2)}) collective-permute-start(f32[32]{0:T(128)S(1)} %max.20), channel_id=1, source_target_pairs={{0,64},{8,72},{16,80},{24,88},{32,96},{40,104},{48,112},{56,120},{... | collective-permute-start | bytes 392 | tf_op jit(solution)/shard_map/ppermute | solution.py:27
  213.6 6.3 %collective-permute-start.20 = (f32[32]{0:T(128)S(1)}, f32[32]{0:T(128)S(1)}, u32[]{:S(2)}, u32[]{:S(2)}) collective-permute-start(f32[32]{0:T(128)S(1)} %max.21), channel_id=1, source_target_pairs={{0,128},{8,136},{16,144},{24,152},{32,160},{40,168},{48,176},{56,1... | collective-permute-start | bytes 392 | tf_op jit(solution)/shard_map/ppermute | solution.py:27
  219.9 9.3 %collective-permute-start.21 = (f32[32]{0:T(128)S(1)}, f32[32]{0:T(128)S(1)}, u32[]{:S(2)}, u32[]{:S(2)}) collective-permute-start(f32[32]{0:T(128)S(1)} %max.22), channel_id=1, source_target_pairs={{0,256},{8,264},{16,272},{24,280},{32,288},{40,296},{48,304},{56,3... | collective-permute-start | bytes 392 | tf_op jit(solution)/shard_map/ppermute | solution.py:27
Sparse Core Ops, SparseCore 0:
  11.3 111.1 all-gather.1
  164.5 56.8 reduce-scatter.1
